TPU v7x, 32 devices: a whole 2x2x4 slice. The times are simulated.
32 devices in a mesh: tm: 8 (over z, x), row: 4 (over y, core).
Axes of the slice: x: 2, y: 2, z: 4, core: 2. Of those that a mesh axis runs over, the one named last changes fastest.
Arguments:
- coupling: bfloat16 [8, 4096, 2048], P('tm', 'row'), as said below
- row_scale: float32 [8, 4096], P('tm', 'row'), may hold values from 0.1 to 10
- block_mask: int32 [8, 32, 16], P('tm', 'row'), may hold values 0 or 1
- link_map: int32 [8, 16], P('tm'), may hold values from 0 to 15, each once within a row
- tile_order: int32 [16], replicated, may hold values from 0 to 15, each once
- link_diag: float32 [8, 2048], P('tm'), may hold values from 0.1 to 1
Outputs:
- schur_rows: float32 [8, 2048, 2048], P('tm', 'row')
- chain_complement: float32 [8, 3, 128, 128], P('tm')
Inputs may be any that keep to these rules, and one draw needn't show every extreme that they name: `coupling`: entries lie within 6 / sqrt(4096) of zero. Each row of link_map lists every linking block once. tile_order lists every linking block once.
All inputs are finite; a program needn't handle non-finite values. No bound on the sum of `block_mask` on one device may be relied on, other than what follows from the above.
Results may differ from a plain program's by a relative error of at most 0.0011.
Values may be sent and summed in bfloat16 or wider, within the bound.
No kernel may reach another device: no remote copies, remote signals or barrier semaphores. Data moves between devices by JAX's collectives and lax.ppermute only.
A program may use at most 128 MiB of HBM per device.

v0:
```python
import jax
import jax.numpy as jnp
from jax import lax
from jax.sharding import PartitionSpec as P

L = 2048
BLK = 128


HIGHEST = lax.Precision.HIGHEST


def join_segments(earlier_seg, later_seg):
    top_one, cross_one, bottom_one, empty_one = earlier_seg
    top_two, cross_two, bottom_two, empty_two = later_seg
    both_empty = empty_one * empty_two
    middle = bottom_one + top_two
    middle = 0.5 * (middle + middle.T) + both_empty * jnp.eye(middle.shape[0], dtype=jnp.float32)
    factor = jnp.linalg.cholesky(middle)
    half_width = top_one.shape[0]
    solved = jax.scipy.linalg.cho_solve(
        (factor, True), jnp.concatenate([cross_one.T, cross_two], axis=1)
    )
    solve_one = solved[:, :half_width]
    solve_two = solved[:, half_width:]
    top_new = top_one - jnp.dot(cross_one, solve_one, precision=HIGHEST)
    cross_new = -jnp.dot(cross_one, solve_two, precision=HIGHEST)
    bottom_new = bottom_two - jnp.dot(cross_two.T, solve_two, precision=HIGHEST)
    first_empty = empty_one > 0.5
    second_empty = empty_two > 0.5
    top_out = jnp.where(first_empty, top_two, jnp.where(second_empty, top_one, top_new))
    cross_out = jnp.where(first_empty, cross_two, jnp.where(second_empty, cross_one, cross_new))
    bottom_out = jnp.where(first_empty, bottom_two, jnp.where(second_empty, bottom_one, bottom_new))
    return (top_out, cross_out, bottom_out, both_empty)


def contract_rows(left_cols, right_cols):
    return lax.dot_general(
        left_cols, right_cols, (((0,), (0,)), ((), ())), preferred_element_type=jnp.float32
    )


def local(coupling, row_scale, block_mask, link_map, tile_order, link_diag):
    local_slab = coupling[0]
    row_weights = row_scale[0]
    live_blocks = block_mask[0]
    block_map = link_map[0]
    diagonal = link_diag[0]
    slab_height = local_slab.shape[0]
    block_count = L // BLK
    owners = lax.axis_size("row")
    own_blocks = block_count // owners
    own_rows = own_blocks * BLK
    my_index = lax.axis_index("row")
    masked = (
        local_slab.reshape(slab_height // BLK, BLK, block_count, BLK)
        * live_blocks.astype(jnp.bfloat16)[:, None, :, None]
    ).reshape(slab_height, block_count, BLK)
    block_ids = jnp.arange(block_count, dtype=jnp.int32)
    source = jnp.sum(
        block_ids[None, :] * (block_map[None, :] == block_ids[:, None]).astype(jnp.int32), axis=1
    )
    global_cols = jnp.take(masked, source, axis=1).reshape(slab_height, L)
    my_blocks = lax.dynamic_slice_in_dim(tile_order, my_index * own_blocks, own_blocks)
    left_cols = jnp.take(masked, jnp.take(source, tile_order), axis=1).reshape(slab_height, L)
    scaled = (row_weights[:, None] * global_cols.astype(jnp.float32)).astype(jnp.bfloat16)
    owned = lax.psum_scatter(
        contract_rows(left_cols, scaled), "row", scatter_dimension=0, tiled=True
    )
    local_rows = jnp.arange(own_rows, dtype=jnp.int32)
    target = jnp.repeat(my_blocks, BLK) * BLK + local_rows % BLK
    column_ids = jnp.arange(L, dtype=jnp.int32)
    owned = owned + jnp.where(
        column_ids[None, :] == target[:, None], jnp.take(diagonal, target)[:, None], 0.0
    )

    def pick_rows(wanted):
        where_held = jnp.sum(block_ids * (tile_order == wanted).astype(jnp.int32))
        local_block = where_held - my_index * own_blocks
        is_held = (local_block >= 0) & (local_block < own_blocks)
        rows_here = lax.dynamic_slice_in_dim(
            owned, jnp.clip(local_block, 0, own_blocks - 1) * BLK, BLK
        )
        return jnp.where(is_held, rows_here, 0.0)

    first_rows = pick_rows(0)
    final_rows = pick_rows(block_count - 1)
    pieces = (first_rows[:, :BLK], first_rows[:, L - BLK :], final_rows[:, L - BLK :])
    summed = lax.psum((pieces[0], pieces[1], pieces[2]), "row")
    own_segment = (summed[0], summed[1], summed[2], jnp.zeros((), jnp.float32))
    stacked = jnp.stack(own_segment[:3])[None]
    every_segment = lax.all_gather(stacked, "tm", axis=0, tiled=True)
    segment_count = every_segment.shape[0]
    empty_flags = jnp.zeros((segment_count,), jnp.float32)
    prefixes = lax.associative_scan(
        jax.vmap(join_segments),
        (every_segment[:, 0], every_segment[:, 1], every_segment[:, 2], empty_flags),
    )
    position = lax.axis_index("tm")
    chain_out = jnp.stack(
        [lax.dynamic_index_in_dim(member, position, 0, False) for member in prefixes[:3]]
    )[None]
    return (owned[None], chain_out)


def solution(mesh):
    placed = (
        P("tm", "row", None),
        P("tm", "row"),
        P("tm", "row", None),
        P("tm", None),
        P(),
        P("tm", None),
    )
    return jax.shard_map(
        local,
        mesh=mesh,
        in_specs=placed,
        out_specs=(P("tm", "row", None), P("tm", None, None, None)),
        check_vma=False,
    )
```

profile of v0, /device:TPU:0, one launch (start us, length us, event | category | flops | bytes accessed | tf_op | source)
XLA Modules:
  0.0 581.4 jit_solution(10147022563122233437)
XLA Ops:
  7.2 6.4 %copy.204 = bf16[1,1024,2048]{1,2,0:T(8,128)(2,1)} copy(bf16[1,1024,2048]{2,1,0:T(8,128)(2,1)} %param.11) | data formatting | bytes 8388608 | tf_op args[0]
  13.6 6.4 %copy.206 = bf16[1024,16,128]{2,0,1:T(8,128)(2,1)} copy(bf16[1024,16,128]{0,2,1:T(8,128)(2,1)} %bitcast.199) | data formatting | bytes 8388608 | tf_op jit(solution)/shard_map/reshape;squeeze | solution.py:56
  21.7 5.8 %broadcast_multiply_fusion = bf16[1024,16,128]{2,0,1:T(8,128)(2,1)} fusion(bf16[1024,16,128]{2,0,1:T(8,128)(2,1)} %copy.206, bf16[1024,16]{0,1:T(8,128)(2,1)S(1)} %bitcast.215), kind=kLoop, calls=%fused_computation.8 | loop fusion | flops 2097152 | bytes 8421376 | tf_op jit(solution)/shard_map/mul | solution.py:56
  27.6 5.2 gather_fusion.2
  32.8 4.6 select_bitcast_fusion
  37.3 6.4 %copy.207 = bf16[1024,16,128]{0,2,1:T(8,128)(2,1)} copy(bf16[1024,16,128]{2,0,1:T(8,128)(2,1)} %select_bitcast_fusion) | data formatting | bytes 8388608 | tf_op jit(solution)/shard_map/jit(_take)/select_n | solution.py:65
  43.7 5.2 gather_fusion.3
  49.0 5.7 multiply_convert_fusion
  54.6 6.4 %copy.208 = bf16[1024,16,128]{0,2,1:T(8,128)(2,1)} copy(bf16[1024,16,128]{2,0,1:T(8,128)(2,1)} %multiply_convert_fusion) | data formatting | bytes 8388608 | tf_op jit(solution)/shard_map/convert_element_type | solution.py:66
  61.0 15.2 %fusion.103 = f32[2048,2048]{1,0:T(8,128)} fusion(bf16[1024,2048]{0,1:T(8,128)(2,1)} %bitcast.200, bf16[1024,2048]{0,1:T(8,128)(2,1)} %bitcast.201), kind=kOutput, calls=%fused_computation.217 | convolution fusion | flops 8589934592 | bytes 25165824 | tf_op jit(solution)/shard_map/dot_general | solution.py:38
  77.7 3.1 gather_fusion.1
  81.0 124.1 %reduce-scatter.2.cloned.1.call-done = f32[512,2048]{1,0:T(8,128)} async-done(((f32[2048,2048]{1,0:T(8,128)}), f32[512,2048]{1,0:T(8,128)}) %reduce-scatter.2.cloned.1.call-update) | async-done | bytes 4194320 | tf_op jit(solution)/shard_map/reduce_scatter | solution.py:67
  205.2 2.8 select_add_fusion
  209.7 31.8 %all-reduce.21.cloned.1.call-done = (f32[1,128,128]{2,1,0:T(8,128)}, f32[1,128,128]{2,1,0:T(8,128)}, f32[1,128,128]{2,1,0:T(8,128)}) async-done(((f32[1,128,128]{2,1,0:T(8,128)}, f32[1,128,128]{2,1,0:T(8,128)}, f32[1,128,128]{2,1,0:T(8,128)}), (f32[1,128,128]{2,1,0:T(8,128)}, f32[1,128,128]{2,1,0:T(8,128)}, f32[1,128,128]{2,1,0:T(8,128)})) %all-reduce.21.cloned.1.call-update) | async-done | bytes 196624 | tf_op jit(solution)/shard_map/psum | solution.py:89
  241.5 1.6 pad_maximum_fusion.3
  243.1 4.8 fusion.113
  247.9 40.5 %all-gather.3.cloned.1.call-done = f32[24,128,128]{2,1,0:T(8,128)} async-done(((f32[3,128,128]{2,1,0:T(8,128)}), f32[24,128,128]{2,1,0:T(8,128)}) %all-gather.3.cloned.1.call-update) | async-done | bytes 1572880 | tf_op jit(solution)/shard_map/all_gather | solution.py:92
  288.4 1.5 fusion.95
  291.0 46.9 %custom-call.41 = f32[4,128,128]{2,1,0:T(8,128)S(1)} custom-call(f32[4,128,128]{2,1,0:T(8,128)S(1)} %copy.216), custom_call_target="Cholesky" | custom-call | tf_op jit(solution)/shard_map/vmap(jit(cholesky))/cholesky | solution.py:19
  338.2 39.3 %custom-call.42 = f32[4,1,128,128]{2,3,1,0:T(8,128)S(1)} custom-call(f32[4,1,128,128]{3,2,1,0:T(8,128)S(1)} %select_bitcast_fusion.1), custom_call_target="InvertDiagBlocksLowerTriangular" | custom-call | tf_op jit(solution)/shard_map/vmap(jit(_cho_solve))/triangular_solve | solution.py:21
  381.7 23.5 %custom-call.43 = f32[2,128,128]{2,1,0:T(8,128)S(1)} custom-call(f32[2,128,128]{2,1,0:T(8,128)S(1)} %fusion.44), custom_call_target="Cholesky" | custom-call | tf_op jit(solution)/shard_map/vmap(jit(cholesky))/cholesky | solution.py:19
  405.4 28.4 %custom-call.44 = f32[2,1,128,128]{2,3,1,0:T(8,128)S(1)} custom-call(f32[2,1,128,128]{3,2,1,0:T(8,128)S(1)} %select_bitcast_fusion.3), custom_call_target="InvertDiagBlocksLowerTriangular" | custom-call | tf_op jit(solution)/shard_map/vmap(jit(_cho_solve))/triangular_solve | solution.py:21
  436.7 11.7 %custom-call.49 = f32[1,128,128]{2,1,0:T(8,128)S(1)} custom-call(f32[1,128,128]{2,1,0:T(8,128)S(1)} %fusion.66), custom_call_target="Cholesky" | custom-call | tf_op jit(solution)/shard_map/vmap(jit(cholesky))/cholesky | solution.py:19
  449.8 9.8 %custom-call.50 = f32[1,1,128,128]{2,3,1,0:T(8,128)S(1)} custom-call(f32[1,1,128,128]{3,2,1,0:T(8,128)S(1)} %fusion.48), custom_call_target="InvertDiagBlocksLowerTriangular" | custom-call | tf_op jit(solution)/shard_map/vmap(jit(_cho_solve))/triangular_solve | solution.py:21
  463.1 11.9 %custom-call.51 = f32[1,128,128]{2,1,0:T(8,128)S(1)} custom-call(f32[1,128,128]{2,1,0:T(8,128)S(1)} %fusion.59), custom_call_target="Cholesky" | custom-call | tf_op jit(solution)/shard_map/vmap(jit(cholesky))/cholesky | solution.py:19
  476.2 9.8 %custom-call.52 = f32[1,1,128,128]{2,3,1,0:T(8,128)S(1)} custom-call(f32[1,1,128,128]{3,2,1,0:T(8,128)S(1)} %fusion.49), custom_call_target="InvertDiagBlocksLowerTriangular" | custom-call | tf_op jit(solution)/shard_map/vmap(jit(_cho_solve))/triangular_solve | solution.py:21
  489.7 1.6 fusion.94
  494.5 35.2 %custom-call.45 = f32[3,128,128]{2,1,0:T(8,128)S(1)} custom-call(f32[3,128,128]{2,1,0:T(8,128)S(1)} %fusion.30), custom_call_target="Cholesky" | custom-call | tf_op jit(solution)/shard_map/vmap(jit(cholesky))/cholesky | solution.py:19
  531.4 29.5 %custom-call.46 = f32[3,1,128,128]{2,3,1,0:T(8,128)S(1)} custom-call(f32[3,1,128,128]{3,2,1,0:T(8,128)S(1)} %select_bitcast_fusion.2), custom_call_target="InvertDiagBlocksLowerTriangular" | custom-call | tf_op jit(solution)/shard_map/vmap(jit(_cho_solve))/triangular_solve | solution.py:21
  560.9 1.5 fusion.10
  567.6 2.1 pad.77
  569.7 2.1 pad.76
  (169 shorter events, 34.3 us)
Async XLA Ops:
  7.2 70.6 %copy-start = (f32[1,2048]{1,0:T(1,128)S(1)}, f32[1,2048]{1,0:T(1,128)}, u32[]{:S(2)}) copy-start(f32[1,2048]{1,0:T(1,128)} %param.16) | copy-start | bytes 24580
  7.2 198.0 %reduce-scatter.2.cloned.1.call-start = ((), (), s32[]{:S(2)}) async-start(), calls=%async_computation.1 | async-start | bytes 20971520 | tf_op jit(solution)/shard_map/reduce_scatter | solution.py:67
  13.6 6.4 %copy-start.7 = (s32[1,8,16]{2,1,0:T(8,128)S(1)}, s32[1,8,16]{2,1,0:T(8,128)}, u32[]{:S(2)}) copy-start(s32[1,8,16]{2,1,0:T(8,128)} %param.13) | copy-start | bytes 1540
  13.6 6.6 %copy-start.9 = (s32[1,16]{1,0:T(1,128)S(1)}, s32[1,16]{1,0:T(1,128)}, u32[]{:S(2)}) copy-start(s32[1,16]{1,0:T(1,128)} %param.14) | copy-start | bytes 196
  13.6 6.8 %copy-start.8 = (s32[16]{0:T(128)S(1)}, s32[16]{0:T(128)}, u32[]{:S(2)}) copy-start(s32[16]{0:T(128)} %param.15) | copy-start | bytes 196
  43.7 5.2 copy-start.6
  76.2 165.3 %all-reduce.21.cloned.1.call-start = ((), (), s32[]{:S(2)}) async-start(), calls=%async_computation.3 | async-start | bytes 393216 | tf_op jit(solution)/shard_map/psum | solution.py:89
  209.4 79.1 %all-gather.3.cloned.1.call-start = ((), (), s32[]{:S(2)}) async-start(), calls=%async_computation.2 | async-start | bytes 1769472 | tf_op jit(solution)/shard_map/all_gather | solution.py:92
  243.1 162.1 %copy-start.3 = (pred[128,128]{1,0:T(8,128)(4,1)}, pred[128,128]{1,0:T(8,128)(4,1)S(1)}, u32[]{:S(2)}) copy-start(pred[128,128]{1,0:T(8,128)(4,1)S(1)} %iota_compare_fusion.3) | copy-start | bytes 49156
  243.1 162.2 %copy-start.1 = (pred[128,128]{1,0:T(8,128)(4,1)}, pred[128,128]{1,0:T(8,128)(4,1)S(1)}, u32[]{:S(2)}) copy-start(pred[128,128]{1,0:T(8,128)(4,1)S(1)} %iota_compare_fusion.4) | copy-start | bytes 49156
  493.0 71.2 %copy-start.4 = (f32[1,128,128]{2,1,0:T(8,128)S(1)}, f32[1,128,128]{2,1,0:T(8,128)}, u32[]{:S(2)}) copy-start(f32[1,128,128]{2,1,0:T(8,128)} %get-tuple-element.42) | copy-start | bytes 196612
  494.1 70.6 %copy-start.2 = (f32[1,128,128]{1,2,0:T(8,128)S(1)}, f32[1,128,128]{1,2,0:T(8,128)}, u32[]{:S(2)}) copy-start(f32[1,128,128]{1,2,0:T(8,128)} %get-tuple-element.34) | copy-start | bytes 196612
  564.4 7.4 %copy-start.5 = (f32[1,1,128,128]{3,2,1,0:T(8,128)S(1)}, f32[1,1,128,128]{3,2,1,0:T(8,128)}, u32[]{:S(2)}) copy-start(f32[1,1,128,128]{3,2,1,0:T(8,128)} %get-tuple-element.22) | copy-start | bytes 196612
Sparse Core Ops, SparseCore 0:
  76.3 128.8 reduce-scatter.1
  209.5 31.9 all-reduce.20
  244.2 44.1 all-gather.2
where the time goes:
time: 590 us; the launch traced here: 581 us
  other arithmetic  284 us (48%)
  waiting for transfers between devices  197 us (33%)
  local copies, waits for them, and re-layouts  57.1 us (10%)
  matrix products  26.8 us (5%)
  between operations  16.4 us (3%)
    another operation x16, other arithmetic, join_segments(): factor = jnp.linalg.cholesky(middle)  132 us
    reduce_scatter x1, waiting for transfers between devices, local(): lax.psum_scatter(contract_rows(left_cols, scaled), 'row', scatter_dimensi...  124 us
    another operation x11, other arithmetic, join_segments(): jax.scipy.linalg.cho_solve((factor, True), jnp.concatenate([cross_one.T,...  119 us
    all_gather x1, waiting for transfers between devices, local(): every_segment = lax.all_gather(stacked, 'tm', axis=0, tiled=True)  40.5 us
    psum x1, waiting for transfers between devices, local(): summed = lax.psum((pieces[0], pieces[1], pieces[2]), 'row')  31.8 us
    dot_general x1, matrix products, contract_rows(): lax.dot_general(left_cols, right_cols, (((0,), (0,)), ((), ())), preferre...  15.2 us
  transfers between devices with their start and end apart: 3, of which 3 were waited for; matrix products, arithmetic and copies ran while one was open for 1% of the time, Pallas kernels for 0%

commit v1 on v0

v1 whole, which is shorter than its diff:
```python
import jax
import jax.numpy as jnp
from jax import lax
from jax.sharding import PartitionSpec as P

L = 2048
BLK = 128


HIGHEST = lax.Precision.HIGHEST


def join_segments(earlier_seg, later_seg):
    top_one, cross_one, bottom_one = earlier_seg
    top_two, cross_two, bottom_two = later_seg
    middle = bottom_one + top_two
    middle = 0.5 * (middle + middle.T)
    factor = jnp.linalg.cholesky(middle)
    half_width = top_one.shape[0]
    solved = jax.scipy.linalg.cho_solve(
        (factor, True), jnp.concatenate([cross_one.T, cross_two], axis=1)
    )
    solve_one = solved[:, :half_width]
    solve_two = solved[:, half_width:]
    top_new = top_one - jnp.dot(cross_one, solve_one, precision=HIGHEST)
    cross_new = -jnp.dot(cross_one, solve_two, precision=HIGHEST)
    bottom_new = bottom_two - jnp.dot(cross_two.T, solve_two, precision=HIGHEST)
    return (top_new, cross_new, bottom_new)


def contract_rows(left_cols, right_cols):
    return lax.dot_general(
        left_cols, right_cols, (((0,), (0,)), ((), ())), preferred_element_type=jnp.float32
    )


def local(coupling, row_scale, block_mask, link_map, tile_order, link_diag):
    local_slab = coupling[0]
    row_weights = row_scale[0]
    live_blocks = block_mask[0]
    block_map = link_map[0]
    diagonal = link_diag[0]
    slab_height = local_slab.shape[0]
    block_count = L // BLK
    owners = lax.axis_size("row")
    own_blocks = block_count // owners
    own_rows = own_blocks * BLK
    my_index = lax.axis_index("row")
    block_ids = jnp.arange(block_count, dtype=jnp.int32)
    source = jnp.sum(
        block_ids[None, :] * (block_map[None, :] == block_ids[:, None]).astype(jnp.int32), axis=1
    )

    def edge_cols(global_block):
        local_block = source[global_block]
        cols = lax.dynamic_slice_in_dim(local_slab, local_block * BLK, BLK, axis=1)
        live = lax.dynamic_index_in_dim(live_blocks, local_block, 1, False)
        cols = (cols.reshape(slab_height // BLK, BLK, BLK) * live.astype(jnp.bfloat16)[:, None, None])
        cols = cols.reshape(slab_height, BLK)
        weighted = (row_weights[:, None] * cols.astype(jnp.float32)).astype(jnp.bfloat16)
        return cols, weighted

    first_cols, first_scaled = edge_cols(0)
    final_cols, final_scaled = edge_cols(block_count - 1)
    part_pieces = jnp.stack(
        [
            contract_rows(first_cols, first_scaled),
            contract_rows(first_cols, final_scaled),
            contract_rows(final_cols, final_scaled),
        ]
    )
    summed = lax.psum(part_pieces, "row")
    eye = jnp.eye(BLK, dtype=jnp.float32)
    segment = (
        summed[0] + eye * diagonal[:BLK][None, :],
        summed[1],
        summed[2] + eye * diagonal[L - BLK :][None, :],
    )

    times = lax.axis_size("tm")
    position = lax.axis_index("tm")
    running = segment
    shift = 1
    while shift < times:
        pairs = [(src, src + shift) for src in range(times - shift)]
        earlier = tuple(lax.ppermute(piece, "tm", pairs) for piece in running)
        joined = join_segments(earlier, running)
        take = position >= shift
        running = tuple(jnp.where(take, new, old) for new, old in zip(joined, running))
        shift *= 2
    chain_out = jnp.stack(running)[None]

    masked = (
        local_slab.reshape(slab_height // BLK, BLK, block_count, BLK)
        * live_blocks.astype(jnp.bfloat16)[:, None, :, None]
    ).reshape(slab_height, block_count, BLK)
    global_cols = jnp.take(masked, source, axis=1).reshape(slab_height, L)
    my_blocks = lax.dynamic_slice_in_dim(tile_order, my_index * own_blocks, own_blocks)
    left_cols = jnp.take(masked, jnp.take(source, tile_order), axis=1).reshape(slab_height, L)
    scaled = (row_weights[:, None] * global_cols.astype(jnp.float32)).astype(jnp.bfloat16)
    owned = lax.psum_scatter(
        contract_rows(left_cols, scaled), "row", scatter_dimension=0, tiled=True
    )
    local_rows = jnp.arange(own_rows, dtype=jnp.int32)
    target = jnp.repeat(my_blocks, BLK) * BLK + local_rows % BLK
    column_ids = jnp.arange(L, dtype=jnp.int32)
    owned = owned + jnp.where(
        column_ids[None, :] == target[:, None], jnp.take(diagonal, target)[:, None], 0.0
    )
    return (owned[None], chain_out)


def solution(mesh):
    placed = (
        P("tm", "row", None),
        P("tm", "row"),
        P("tm", "row", None),
        P("tm", None),
        P(),
        P("tm", None),
    )
    return jax.shard_map(
        local,
        mesh=mesh,
        in_specs=placed,
        out_specs=(P("tm", "row", None), P("tm", None, None, None)),
        check_vma=False,
    )
```

time: 590 us -> 232 us (0.39); the launches traced: 581 us -> 230 us
  other arithmetic: 284 us -> 94.7 us
  waiting for transfers between devices: 197 us -> 16.7 us
  starting transfers between devices: 0.38 us -> 29.3 us
  local copies, waits for them, and re-layouts: 57.1 us -> 43 us
    reduce_scatter x1, waiting for transfers between devices: 124 us -> 14.9 us  [local(): lax.psum_scatter(contract_rows(left_cols, scaled), 'row', scatter_dimensi...]
    another operation x16 -> x9, other arithmetic: 132 us -> 37.2 us  [join_segments(): factor = jnp.linalg.cholesky(middle)]
    another operation x11 -> x6, other arithmetic: 119 us -> 31.4 us  [join_segments(): jax.scipy.linalg.cho_solve((factor, True), jnp.concatenate([cross_one.T,...]
    all_gather x1 -> x0, waiting for transfers between devices: 40.5 us -> none  [local(): every_segment = lax.all_gather(stacked, 'tm', axis=0, tiled=True)]
    psum x1, waiting for transfers between devices: 31.8 us -> 0.01 us  [local(): summed = lax.psum(part_pieces, 'row')]
    ppermute x0 -> x9, starting transfers between devices: none -> 29.2 us  [local(): earlier = tuple((lax.ppermute(piece, 'tm', pairs) for piece in running))]
    dot_general x1 -> x4, matrix products: 15.2 us -> 20.5 us  [contract_rows(): lax.dot_general(left_cols, right_cols, (((0,), (0,)), ((), ())), preferre...]
  transfers between devices with their start and end apart: 3 -> 11, of which waited for: 3 -> 3; matrix products, arithmetic and copies ran while one was open for 1% -> 65% of each run, Pallas kernels for 0% -> 0%
where the time goes in v1:
time: 232 us; the launch traced here: 230 us
  other arithmetic  94.7 us (41%)
  local copies, waits for them, and re-layouts  43 us (19%)
  starting transfers between devices  29.3 us (13%)
  matrix products  26.5 us (11%)
  between operations  19.8 us (9%)
  waiting for transfers between devices  16.7 us (7%)
    another operation x9, other arithmetic, join_segments(): factor = jnp.linalg.cholesky(middle)  37.2 us
    another operation x6, other arithmetic, join_segments(): jax.scipy.linalg.cho_solve((factor, True), jnp.concatenate([cross_one.T,...  31.4 us
    ppermute x9, starting transfers between devices, local(): earlier = tuple((lax.ppermute(piece, 'tm', pairs) for piece in running))  29.2 us
    dot_general x4, matrix products, contract_rows(): lax.dot_general(left_cols, right_cols, (((0,), (0,)), ((), ())), preferre...  20.5 us
    reduce_scatter x1, waiting for transfers between devices, local(): lax.psum_scatter(contract_rows(left_cols, scaled), 'row', scatter_dimensi...  14.9 us
    unnamed x10, local copies, waits for them, and re-layouts  6.91 us
    convert_element_type x1, local copies, waits for them, and re-layouts, local(): (row_weights[:, None] * global_cols.astype(jnp.float32)).astype(jnp.bfloa...  6.4 us
    select_n x1, local copies, waits for them, and re-layouts, local(): jnp.take(masked, jnp.take(source, tile_order), axis=1)  6.4 us
  transfers between devices with their start and end apart: 11, of which 3 were waited for; matrix products, arithmetic and copies ran while one was open for 65% of the time, Pallas kernels for 0%

profile of v1, /device:TPU:0, one launch (start us, length us, event | category | flops | bytes accessed | tf_op | source)
XLA Modules:
  0.0 230.0 jit_solution(5900160344904309961)
XLA Ops:
  14.8 1.8 convolution_bitcast_fusion
  16.6 1.8 convolution_bitcast_fusion.1
  18.4 1.8 convolution_bitcast_fusion.2
  21.0 6.4 %copy.56 = bf16[1,1024,2048]{1,2,0:T(8,128)(2,1)} copy(bf16[1,1024,2048]{2,1,0:T(8,128)(2,1)} %param.11) | data formatting | bytes 8388608 | tf_op args[0]
  27.4 6.4 %copy.58 = bf16[1024,16,128]{2,0,1:T(8,128)(2,1)} copy(bf16[1024,16,128]{0,2,1:T(8,128)(2,1)} %bitcast.139) | data formatting | bytes 8388608 | tf_op jit(solution)/shard_map/reshape;squeeze | solution.py:94
  34.7 5.8 %broadcast_multiply_fusion = bf16[1024,16,128]{2,0,1:T(8,128)(2,1)} fusion(bf16[1024,16,128]{2,0,1:T(8,128)(2,1)} %copy.58, bf16[1024,16]{0,1:T(8,128)(2,1)S(1)} %bitcast.145), kind=kLoop, calls=%fused_computation.8 | loop fusion | flops 2097152 | bytes 8421376 | tf_op jit(solution)/shard_map/mul | solution.py:94
  40.5 5.2 %gather_fusion.2 = bf16[16,1024,128]{2,1,0:T(8,128)(2,1)} fusion(bf16[1024,16,128]{2,0,1:T(8,128)(2,1)} %broadcast_multiply_fusion, s32[1024]{0:T(1024)S(1)} %pad_clamp_fusion.2), kind=kCustom, calls=%fused_computation.clone | custom fusion | bytes 8388672 | tf_op jit(solution)/shard_map/jit(_take)/gather | solution.py:99
  45.7 4.6 %select_bitcast_fusion = bf16[1024,16,128]{2,0,1:T(8,128)(2,1)} fusion(bf16[16,1024,128]{2,1,0:T(8,128)(2,1)} %gather_fusion.2, pred[16]{0:T(512)(128)(4,1)S(1)} %get-tuple-element.11), kind=kLoop, calls=%fused_computation.5 | loop fusion | flops 2097152 | bytes 8388624 | tf_op jit(solution)/shard_map/jit(_take)/select_n | solution.py:99
  50.3 6.4 %copy.59 = bf16[1024,16,128]{0,2,1:T(8,128)(2,1)} copy(bf16[1024,16,128]{2,0,1:T(8,128)(2,1)} %select_bitcast_fusion) | data formatting | bytes 8388608 | tf_op jit(solution)/shard_map/jit(_take)/select_n | solution.py:99
  56.7 5.2 %gather_fusion.3 = bf16[16,1024,128]{2,1,0:T(8,128)(2,1)} fusion(bf16[1024,16,128]{2,0,1:T(8,128)(2,1)} %broadcast_multiply_fusion, s32[1024]{0:T(1024)S(1)} %pad_clamp_fusion.1), kind=kCustom, calls=%fused_computation.1.clone | custom fusion | bytes 8388672 | tf_op jit(solution)/shard_map/jit(_take)/gather | solution.py:97
  62.0 5.6 %multiply_convert_fusion = bf16[1024,16,128]{2,0,1:T(8,128)(2,1)} fusion(bf16[16,1024,128]{2,1,0:T(8,128)(2,1)} %gather_fusion.3, f32[1024]{0:T(1024)S(1)} %bitcast.152, pred[16]{0:T(512)(128)(4,1)S(1)} %compare_and_fusion), kind=kLoop, calls=%fused_computation.4 | loop fusion | flops 8388608 | bytes 8392720 | tf_op jit(solution)/shard_map/convert_element_type | solution.py:100
  67.6 6.4 %copy.60 = bf16[1024,16,128]{0,2,1:T(8,128)(2,1)} copy(bf16[1024,16,128]{2,0,1:T(8,128)(2,1)} %multiply_convert_fusion) | data formatting | bytes 8388608 | tf_op jit(solution)/shard_map/convert_element_type | solution.py:100
  74.0 15.2 %fusion.82 = f32[2048,2048]{1,0:T(8,128)} fusion(bf16[1024,2048]{0,1:T(8,128)(2,1)} %bitcast.140, bf16[1024,2048]{0,1:T(8,128)(2,1)} %bitcast.141), kind=kOutput, calls=%fused_computation.153 | convolution fusion | flops 8589934592 | bytes 25165824 | tf_op jit(solution)/shard_map/dot_general | solution.py:32
  89.9 3.1 %gather_fusion.1 = f32[512]{0:T(512)S(1)} fusion(f32[2048]{0:T(1024)S(1)} %bitcast.138, s32[1024]{0:T(1024)S(1)} %pad_clamp_fusion), kind=kCustom, calls=%fused_computation.3 | custom fusion | bytes 6144 | tf_op jit(solution)/shard_map/jit(_take)/gather | solution.py:108
  94.0 4.8 %collective-permute-start.2 = (f32[128,128]{1,0:T(8,128)S(1)}, f32[128,128]{1,0:T(8,128)S(1)}, u32[]{:S(2)}, u32[]{:S(2)}) collective-permute-start(f32[128,128]{1,0:T(8,128)S(1)} %fusion.42), channel_id=1, source_target_pairs={{0,4},{4,8},{8,12},{12,16},{16,20},{20,24},{24,28},{1,5},{5,9},{9,... | collective-permute-start | bytes 196616 | tf_op jit(solution)/shard_map/ppermute | solution.py:86
  99.8 3.7 %collective-permute-start.1 = (f32[128,128]{0,1:T(8,128)S(1)}, f32[128,128]{0,1:T(8,128)S(1)}, u32[]{:S(2)}, u32[]{:S(2)}) collective-permute-start(f32[128,128]{0,1:T(8,128)S(1)} %copy.61), channel_id=1, source_target_pairs={{0,4},{4,8},{8,12},{12,16},{16,20},{20,24},{24,28},{1,5},{5,9},{9,... | collective-permute-start | bytes 196616 | tf_op jit(solution)/shard_map/ppermute | solution.py:86
  104.7 11.7 %cholesky.59 = f32[128,128]{1,0:T(8,128)S(1)} custom-call(f32[128,128]{1,0:T(8,128)S(1)} %copy.65), custom_call_target="Cholesky" | custom-call | tf_op jit(solution)/shard_map/jit(cholesky)/cholesky | solution.py:18
  117.8 9.8 %custom-call.9 = f32[1,128,128]{1,2,0:T(8,128)S(1)} custom-call(f32[1,128,128]{2,1,0:T(8,128)S(1)} %fusion.34), custom_call_target="InvertDiagBlocksLowerTriangular" | custom-call | tf_op jit(solution)/shard_map/jit(_cho_solve)/triangular_solve | solution.py:20
  129.3 3.5 %collective-permute-start.5 = (f32[128,128]{1,0:T(8,128)S(1)}, f32[128,128]{1,0:T(8,128)S(1)}, u32[]{:S(2)}, u32[]{:S(2)}) collective-permute-start(f32[128,128]{1,0:T(8,128)S(1)} %fusion.6), channel_id=1, source_target_pairs={{0,8},{4,12},{8,16},{12,20},{16,24},{20,28},{1,9},{5,13},{9,17},{1... | collective-permute-start | bytes 196616 | tf_op jit(solution)/shard_map/ppermute | solution.py:86
  132.8 3.4 %collective-permute-start = (f32[128,128]{1,0:T(8,128)S(1)}, f32[128,128]{1,0:T(8,128)S(1)}, u32[]{:S(2)}, u32[]{:S(2)}) collective-permute-start(f32[128,128]{1,0:T(8,128)S(1)} %get-tuple-element.10), channel_id=1, source_target_pairs={{0,4},{4,8},{8,12},{12,16},{16,20},{20,24},{24,28},{1,5},{5,9},{9,... | collective-permute-start | bytes 196616 | tf_op jit(solution)/shard_map/ppermute | solution.py:86
  137.5 3.7 %collective-permute-start.4 = (f32[128,128]{0,1:T(8,128)S(1)}, f32[128,128]{0,1:T(8,128)S(1)}, u32[]{:S(2)}, u32[]{:S(2)}) collective-permute-start(f32[128,128]{0,1:T(8,128)S(1)} %copy.67), channel_id=1, source_target_pairs={{0,8},{4,12},{8,16},{12,20},{16,24},{20,28},{1,9},{5,13},{9,17},{1... | collective-permute-start | bytes 196616 | tf_op jit(solution)/shard_map/ppermute | solution.py:86
  141.7 11.7 %cholesky.70 = f32[128,128]{1,0:T(8,128)S(1)} custom-call(f32[128,128]{1,0:T(8,128)S(1)} %fusion.51), custom_call_target="Cholesky" | custom-call | tf_op jit(solution)/shard_map/jit(cholesky)/cholesky | solution.py:18
  154.8 9.8 %custom-call.10 = f32[1,128,128]{1,2,0:T(8,128)S(1)} custom-call(f32[1,128,128]{2,1,0:T(8,128)S(1)} %fusion.35), custom_call_target="InvertDiagBlocksLowerTriangular" | custom-call | tf_op jit(solution)/shard_map/jit(_cho_solve)/triangular_solve | solution.py:20
  165.6 2.2 collective-permute-start.7
  168.1 1.3 collective-permute-start.8
  169.4 1.7 collective-permute-start.3
  171.3 1.3 collective-permute-done.3
  173.0 11.7 %cholesky.81 = f32[128,128]{1,0:T(8,128)S(1)} custom-call(f32[128,128]{1,0:T(8,128)S(1)} %fusion.47), custom_call_target="Cholesky" | custom-call | tf_op jit(solution)/shard_map/jit(cholesky)/cholesky | solution.py:18
  186.1 9.8 %custom-call.11 = f32[1,128,128]{1,2,0:T(8,128)S(1)} custom-call(f32[1,128,128]{2,1,0:T(8,128)S(1)} %fusion.36), custom_call_target="InvertDiagBlocksLowerTriangular" | custom-call | tf_op jit(solution)/shard_map/jit(_cho_solve)/triangular_solve | solution.py:20
  195.9 5.0 %collective-permute-start.6 = (f32[128,128]{1,0:T(8,128)S(1)}, f32[128,128]{1,0:T(8,128)S(1)}, u32[]{:S(2)}, u32[]{:S(2)}) collective-permute-start(f32[128,128]{1,0:T(8,128)S(1)} %get-tuple-element.8), channel_id=1, source_target_pairs={{0,16},{4,20},{8,24},{12,28},{1,17},{5,21},{9,25},{13,29},{2,18},{... | collective-permute-start | bytes 196616 | tf_op jit(solution)/shard_map/ppermute | solution.py:86
  203.5 14.9 %reduce-scatter.2.cloned.1.call-done = f32[512,2048]{1,0:T(8,128)} async-done(((f32[2048,2048]{1,0:T(8,128)}), f32[512,2048]{1,0:T(8,128)}) %reduce-scatter.2.cloned.1.call-update) | async-done | bytes 4194320 | tf_op jit(solution)/shard_map/reduce_scatter | solution.py:101
  218.4 4.8 %add_bitcast_fusion = f32[1,512,2048]{2,1,0:T(8,128)} fusion(f32[512,2048]{1,0:T(8,128)} %reduce-scatter.2.cloned.1.call-done, f32[512]{0:T(512)S(1)} %and_select_fusion.1, s32[512]{0:T(512)S(1)} %fusion.65), kind=kLoop, calls=%fused_computation.6 | loop fusion | flops 3145728 | bytes 8392704 | tf_op jit(solution)/shard_map/broadcast_in_dim | solution.py:110
  (92 shorter events, 19.7 us)
Async XLA Ops:
  7.2 86.0 %all-reduce.2.cloned.1.call-start = ((), (), s32[]{:S(2)}) async-start(), calls=%async_computation.2 | async-start | bytes 393216 | tf_op jit(solution)/shard_map/psum | solution.py:72
  20.9 6.5 %copy-start.1 = (s32[1,8,16]{2,1,0:T(8,128)S(1)}, s32[1,8,16]{2,1,0:T(8,128)}, u32[]{:S(2)}) copy-start(s32[1,8,16]{2,1,0:T(8,128)} %param.13) | copy-start | bytes 1540
  20.9 197.5 %reduce-scatter.2.cloned.1.call-start = ((), (), s32[]{:S(2)}) async-start(), calls=%async_computation.1 | async-start | bytes 20971520 | tf_op jit(solution)/shard_map/reduce_scatter | solution.py:101
  27.4 6.6 %copy-start.3 = (s32[16]{0:T(128)S(1)}, s32[16]{0:T(128)}, u32[]{:S(2)}) copy-start(s32[16]{0:T(128)} %param.15) | copy-start | bytes 196
  56.7 5.2 %copy-start.2 = (f32[1,1024]{1,0:T(1,128)S(1)}, f32[1,1024]{1,0:T(1,128)}, u32[]{:S(2)}) copy-start(f32[1,1024]{1,0:T(1,128)} %param.12) | copy-start | bytes 12292
  89.2 0.7 copy-start
  94.0 9.5 %collective-permute-start.2 = (f32[128,128]{1,0:T(8,128)S(1)}, f32[128,128]{1,0:T(8,128)S(1)}, u32[]{:S(2)}, u32[]{:S(2)}) collective-permute-start(f32[128,128]{1,0:T(8,128)S(1)} %fusion.42), channel_id=1, source_target_pairs={{0,4},{4,8},{8,12},{12,16},{16,20},{20,24},{24,28},{1,5},{5,9},{9,... | collective-permute-start | bytes 196616 | tf_op jit(solution)/shard_map/ppermute | solution.py:86
  99.8 27.8 %collective-permute-start.1 = (f32[128,128]{0,1:T(8,128)S(1)}, f32[128,128]{0,1:T(8,128)S(1)}, u32[]{:S(2)}, u32[]{:S(2)}) collective-permute-start(f32[128,128]{0,1:T(8,128)S(1)} %copy.61), channel_id=1, source_target_pairs={{0,4},{4,8},{8,12},{12,16},{16,20},{20,24},{24,28},{1,5},{5,9},{9,... | collective-permute-start | bytes 196616 | tf_op jit(solution)/shard_map/ppermute | solution.py:86
  129.3 11.9 %collective-permute-start.5 = (f32[128,128]{1,0:T(8,128)S(1)}, f32[128,128]{1,0:T(8,128)S(1)}, u32[]{:S(2)}, u32[]{:S(2)}) collective-permute-start(f32[128,128]{1,0:T(8,128)S(1)} %fusion.6), channel_id=1, source_target_pairs={{0,8},{4,12},{8,16},{12,20},{16,24},{20,28},{1,9},{5,13},{9,17},{1... | collective-permute-start | bytes 196616 | tf_op jit(solution)/shard_map/ppermute | solution.py:86
  132.8 8.4 %collective-permute-start = (f32[128,128]{1,0:T(8,128)S(1)}, f32[128,128]{1,0:T(8,128)S(1)}, u32[]{:S(2)}, u32[]{:S(2)}) collective-permute-start(f32[128,128]{1,0:T(8,128)S(1)} %get-tuple-element.10), channel_id=1, source_target_pairs={{0,4},{4,8},{8,12},{12,16},{16,20},{20,24},{24,28},{1,5},{5,9},{9,... | collective-permute-start | bytes 196616 | tf_op jit(solution)/shard_map/ppermute | solution.py:86
  137.5 27.1 %collective-permute-start.4 = (f32[128,128]{0,1:T(8,128)S(1)}, f32[128,128]{0,1:T(8,128)S(1)}, u32[]{:S(2)}, u32[]{:S(2)}) collective-permute-start(f32[128,128]{0,1:T(8,128)S(1)} %copy.67), channel_id=1, source_target_pairs={{0,8},{4,12},{8,16},{12,20},{16,24},{20,28},{1,9},{5,13},{9,17},{1... | collective-permute-start | bytes 196616 | tf_op jit(solution)/shard_map/ppermute | solution.py:86
  165.6 35.3 %collective-permute-start.7 = (f32[128,128]{0,1:T(8,128)S(1)}, f32[128,128]{0,1:T(8,128)S(1)}, u32[]{:S(2)}, u32[]{:S(2)}) collective-permute-start(f32[128,128]{0,1:T(8,128)S(1)} %copy.71), channel_id=1, source_target_pairs={{0,16},{4,20},{8,24},{12,28},{1,17},{5,21},{9,25},{13,29},{2,18},{... | collective-permute-start | bytes 196616 | tf_op jit(solution)/shard_map/ppermute | solution.py:86
  168.1 3.3 %collective-permute-start.8 = (f32[128,128]{1,0:T(8,128)S(1)}, f32[128,128]{1,0:T(8,128)S(1)}, u32[]{:S(2)}, u32[]{:S(2)}) collective-permute-start(f32[128,128]{1,0:T(8,128)S(1)} %fusion.4), channel_id=1, source_target_pairs={{0,16},{4,20},{8,24},{12,28},{1,17},{5,21},{9,25},{13,29},{2,18},{... | collective-permute-start | bytes 196616 | tf_op jit(solution)/shard_map/ppermute | solution.py:86
  169.4 3.3 %collective-permute-start.3 = (f32[128,128]{1,0:T(8,128)S(1)}, f32[128,128]{1,0:T(8,128)S(1)}, u32[]{:S(2)}, u32[]{:S(2)}) collective-permute-start(f32[128,128]{1,0:T(8,128)S(1)} %get-tuple-element.18), channel_id=1, source_target_pairs={{0,8},{4,12},{8,16},{12,20},{16,24},{20,28},{1,9},{5,13},{9,17},{1... | collective-permute-start | bytes 196616 | tf_op jit(solution)/shard_map/ppermute | solution.py:86
  195.9 6.9 %collective-permute-start.6 = (f32[128,128]{1,0:T(8,128)S(1)}, f32[128,128]{1,0:T(8,128)S(1)}, u32[]{:S(2)}, u32[]{:S(2)}) collective-permute-start(f32[128,128]{1,0:T(8,128)S(1)} %get-tuple-element.8), channel_id=1, source_target_pairs={{0,16},{4,20},{8,24},{12,28},{1,17},{5,21},{9,25},{13,29},{2,18},{... | collective-permute-start | bytes 196616 | tf_op jit(solution)/shard_map/ppermute | solution.py:86
Sparse Core Ops, SparseCore 0:
  21.0 34.4 all-reduce.1
  89.3 129.0 reduce-scatter.1

commit v2 on v1

--- a/solution.py
+++ b/solution.py
@@ -2,9 +2,69 @@
 import jax.numpy as jnp
 from jax import lax
 from jax.sharding import PartitionSpec as P
+from jax.experimental import pallas as pl
+from jax.experimental.pallas import tpu as pltpu
 
 L = 2048
 BLK = 128
+
+
+def gram_kernel(src_left, src_right, tile_ref, mask_ref, flag_ref, g_ref, w_ref, diag_ref,
+                out_ref, s_ref, lt_ref):
+    k = pl.program_id(0)
+    row_blocks = g_ref.shape[0] // BLK
+    col_blocks = g_ref.shape[1] // BLK
+
+    @pl.when(k == 0)
+    def _():
+        def fill(j, carry):
+            src = src_right[j]
+            c0 = pl.multiple_of(src * BLK, BLK)
+            d0 = pl.multiple_of(j * BLK, BLK)
+            for rb in range(row_blocks):
+                live = mask_ref[rb * col_blocks + src].astype(jnp.float32)
+                vals = g_ref[rb * BLK:(rb + 1) * BLK, pl.ds(c0, BLK)].astype(jnp.float32)
+                wts = w_ref[rb * BLK:(rb + 1) * BLK, :]
+                s_ref[rb * BLK:(rb + 1) * BLK, pl.ds(d0, BLK)] = (wts * (vals * live)).astype(jnp.bfloat16)
+            return carry
+        lax.fori_loop(0, col_blocks, fill, 0)
+
+    src = src_left[k]
+    c0 = pl.multiple_of(src * BLK, BLK)
+    for rb in range(row_blocks):
+        live = mask_ref[rb * col_blocks + src].astype(jnp.float32)
+        vals = g_ref[rb * BLK:(rb + 1) * BLK, pl.ds(c0, BLK)].astype(jnp.float32) * live
+        lt_ref[:, rb * BLK:(rb + 1) * BLK] = vals.T.astype(jnp.bfloat16)
+    out_ref[...] = jnp.dot(lt_ref[...], s_ref[...], preferred_element_type=jnp.float32)
+    blk = tile_ref[k]
+    e0 = pl.multiple_of(blk * BLK, BLK)
+    rows = lax.broadcasted_iota(jnp.int32, (BLK, BLK), 0)
+    cols = lax.broadcasted_iota(jnp.int32, (BLK, BLK), 1)
+    dvals = diag_ref[pl.ds(blk, 1), :] * flag_ref[0].astype(jnp.float32)
+    out_ref[:, pl.ds(e0, BLK)] += jnp.where(rows == cols, dvals, 0.0)
+
+
+def gram_rows(slab, weights, live_blocks, src_left, src_right, tile_order, diagonal, flag):
+    height = slab.shape[0]
+    col_blocks = L // BLK
+    grid_spec = pltpu.PrefetchScalarGridSpec(
+        num_scalar_prefetch=5,
+        grid=(col_blocks,),
+        in_specs=[
+            pl.BlockSpec((height, L), lambda k, *_: (0, 0)),
+            pl.BlockSpec((height, 1), lambda k, *_: (0, 0)),
+            pl.BlockSpec((col_blocks, BLK), lambda k, *_: (0, 0)),
+        ],
+        out_specs=pl.BlockSpec((BLK, L), lambda k, *_: (k, 0)),
+        scratch_shapes=[pltpu.VMEM((height, L), jnp.bfloat16), pltpu.VMEM((BLK, height), jnp.bfloat16)],
+    )
+    return pl.pallas_call(
+        gram_kernel,
+        grid_spec=grid_spec,
+        out_shape=jax.ShapeDtypeStruct((L, L), jnp.float32),
+        compiler_params=pltpu.CompilerParams(vmem_limit_bytes=56 * 1024 * 1024),
+    )(src_left, src_right, tile_order, live_blocks.reshape(-1), flag.reshape(1),
+      slab, weights.reshape(height, 1), diagonal.reshape(col_blocks, BLK))
 
 
 HIGHEST = lax.Precision.HIGHEST
@@ -42,9 +102,6 @@
     diagonal = link_diag[0]
     slab_height = local_slab.shape[0]
     block_count = L // BLK
-    owners = lax.axis_size("row")
-    own_blocks = block_count // owners
-    own_rows = own_blocks * BLK
     my_index = lax.axis_index("row")
     block_ids = jnp.arange(block_count, dtype=jnp.int32)
     source = jnp.sum(
@@ -83,30 +140,20 @@
     shift = 1
     while shift < times:
         pairs = [(src, src + shift) for src in range(times - shift)]
-        earlier = tuple(lax.ppermute(piece, "tm", pairs) for piece in running)
+        moved = lax.ppermute(jnp.stack(running), "tm", pairs)
+        earlier = (moved[0], moved[1], moved[2])
         joined = join_segments(earlier, running)
         take = position >= shift
         running = tuple(jnp.where(take, new, old) for new, old in zip(joined, running))
         shift *= 2
     chain_out = jnp.stack(running)[None]
 
-    masked = (
-        local_slab.reshape(slab_height // BLK, BLK, block_count, BLK)
-        * live_blocks.astype(jnp.bfloat16)[:, None, :, None]
-    ).reshape(slab_height, block_count, BLK)
-    global_cols = jnp.take(masked, source, axis=1).reshape(slab_height, L)
-    my_blocks = lax.dynamic_slice_in_dim(tile_order, my_index * own_blocks, own_blocks)
-    left_cols = jnp.take(masked, jnp.take(source, tile_order), axis=1).reshape(slab_height, L)
-    scaled = (row_weights[:, None] * global_cols.astype(jnp.float32)).astype(jnp.bfloat16)
-    owned = lax.psum_scatter(
-        contract_rows(left_cols, scaled), "row", scatter_dimension=0, tiled=True
+    flag = (my_index == 0).astype(jnp.int32)
+    partial = gram_rows(
+        local_slab, row_weights, live_blocks, jnp.take(source, tile_order), source,
+        tile_order, diagonal, flag,
     )
-    local_rows = jnp.arange(own_rows, dtype=jnp.int32)
-    target = jnp.repeat(my_blocks, BLK) * BLK + local_rows % BLK
-    column_ids = jnp.arange(L, dtype=jnp.int32)
-    owned = owned + jnp.where(
-        column_ids[None, :] == target[:, None], jnp.take(diagonal, target)[:, None], 0.0
-    )
+    owned = lax.psum_scatter(partial, "row", scatter_dimension=0, tiled=True)
     return (owned[None], chain_out)
 
 

time: 232 us -> 193 us (0.83)
  local copies, waits for them, and re-layouts: 43 us -> 4.98 us
  waiting for transfers between devices: 16.7 us -> 46 us
  Pallas kernels: 0 us -> 21.8 us
  other arithmetic: 94.7 us -> 74.1 us
  matrix products: 26.5 us -> 11.1 us
  starting transfers between devices: 29.3 us -> 14.5 us
    pallas_call x0 -> x1, Pallas kernels: none -> 21.8 us  [gram_rows(): pl.pallas_call(gram_kernel, grid_spec=grid_spec, out_shape=jax.ShapeDtype...]
    dot_general x4 -> x3, matrix products: 20.5 us -> 5.6 us  [contract_rows(): lax.dot_general(left_cols, right_cols, (((0,), (0,)), ((), ())), preferre...]
    ppermute x9 -> x3, starting transfers between devices: 29.2 us -> 14.4 us  [local(): moved = lax.ppermute(jnp.stack(running), 'tm', pairs)]
    reduce_scatter x1, waiting for transfers between devices: 14.9 us -> 28.7 us  [local(): owned = lax.psum_scatter(partial, 'row', scatter_dimension=0, tiled=True)]
    gather x3 -> x0, local copies, waits for them, and re-layouts: 13.5 us -> none  [the longest x1 5.2 us: local(): global_cols = jnp.take(masked, source, axis=1).reshape(slab_height, L)]
    psum x1, waiting for transfers between devices: 0.01 us -> 8.45 us  [local(): summed = lax.psum(part_pieces, 'row')]
    ppermute x9 -> x3, waiting for transfers between devices: 1.74 us -> 8.9 us  [local(): moved = lax.ppermute(jnp.stack(running), 'tm', pairs)]
    unnamed x10 -> x8, local copies, waits for them, and re-layouts: 6.91 us -> 0.02 us
  transfers between devices with their start and end apart: 11 -> 5, of which waited for: 3 -> 5; matrix products, arithmetic and copies ran while one was open for 65% -> 42% of each run, Pallas kernels for 0% -> 11%
where the time goes in v2:
time: 193 us; the launch traced here: 192 us
  other arithmetic  74.1 us (38%)
  waiting for transfers between devices  46 us (24%)
  Pallas kernels  21.8 us (11%)
  between operations  19.7 us (10%)
  starting transfers between devices  14.5 us (8%)
  matrix products  11.1 us (6%)
  local copies, waits for them, and re-layouts  4.98 us (3%)
    another operation x9, other arithmetic, join_segments(): factor = jnp.linalg.cholesky(middle)  37.2 us
    another operation x6, other arithmetic, join_segments(): jax.scipy.linalg.cho_solve((factor, True), jnp.concatenate([cross_one.T,...  31.4 us
    reduce_scatter x1, waiting for transfers between devices, local(): owned = lax.psum_scatter(partial, 'row', scatter_dimension=0, tiled=True)  28.7 us
    pallas_call x1, Pallas kernels, gram_rows(): pl.pallas_call(gram_kernel, grid_spec=grid_spec, out_shape=jax.ShapeDtype...  21.8 us
    ppermute x3, starting transfers between devices, local(): moved = lax.ppermute(jnp.stack(running), 'tm', pairs)  14.4 us
    ppermute x3, waiting for transfers between devices, local(): moved = lax.ppermute(jnp.stack(running), 'tm', pairs)  8.9 us
    psum x1, waiting for transfers between devices, local(): summed = lax.psum(part_pieces, 'row')  8.45 us
    dot_general x3, matrix products, contract_rows(): lax.dot_general(left_cols, right_cols, (((0,), (0,)), ((), ())), preferre...  5.6 us
  transfers between devices with their start and end apart: 5, of which 5 were waited for; matrix products, arithmetic and copies ran while one was open for 42% of the time, Pallas kernels for 11%

profile of v2, /device:TPU:0, one launch (start us, length us, event | category | flops | bytes accessed | tf_op | source)
XLA Modules:
  0.0 192.3 jit_solution(9096600565683990793)
XLA Ops:
  7.2 0.8 select_reduce_fusion.3.src_right
  13.8 1.0 fusion.100
  14.8 1.9 convolution_bitcast_fusion
  16.7 1.9 convolution_bitcast_fusion.1
  18.6 1.9 convolution_bitcast_fusion.2
  20.5 0.7 pad_maximum_fusion
  21.2 0.7 compare_select_fusion
  21.9 0.7 gather_fusion
  23.8 1.0 copy.56.w_ref
  24.8 21.8 %shard_map.80 = f32[2048,2048]{1,0:T(8,128)} custom-call(s32[16]{0:T(128)} %and_select_fusion.src_left, s32[16]{0:T(128)} %copy-done, s32[16]{0:T(128)} %tile_ref.1, s32[128]{0:T(128)} %reshape_squeeze.9.mask_ref, s32[1]{0:T(128)} %bitcast.1.flag_ref, bf16[1024,2048]{1,0:T(8,128)(2,1)} %bitcast.171, f32[1024,1]{1,0:T(8,128)} %copy.56.w_ref, f32[16,128]{1,0:T(8,128)} %bitcast.178), custom_call_target="tpu_custom_call" | custom-call | tf_op jit(solution)/shard_map/pallas_call | solution.py:61
  46.6 0.7 slice_bitcast_fusion.12
  47.3 8.4 %all-reduce.2.cloned.1.call-done = f32[3,128,128]{1,2,0:T(8,128)} async-done(((f32[3,128,128]{1,2,0:T(8,128)}), f32[3,128,128]{1,2,0:T(8,128)}) %all-reduce.2.cloned.1.call-update) | async-done | bytes 196624 | tf_op jit(solution)/shard_map/psum | solution.py:129
  55.8 1.0 slice_bitcast_fusion.7
  56.9 3.4 %collective-permute-start = (f32[3,128,128]{2,1,0:T(8,128)S(1)}, f32[3,128,128]{2,1,0:T(8,128)S(1)}, u32[]{:S(2)}, u32[]{:S(2)}) collective-permute-start(f32[3,128,128]{2,1,0:T(8,128)S(1)} %copy.60), channel_id=1, source_target_pairs={{0,4},{4,8},{8,12},{12,16},{16,20},{20,24},{24,28},{1,5},{5,9},{9,... | collective-permute-start | bytes 589832 | tf_op jit(solution)/shard_map/ppermute | solution.py:143
  60.5 3.0 %collective-permute-done = f32[3,128,128]{2,1,0:T(8,128)S(1)} collective-permute-done((f32[3,128,128]{2,1,0:T(8,128)S(1)}, f32[3,128,128]{2,1,0:T(8,128)S(1)}, u32[]{:S(2)}, u32[]{:S(2)}) %collective-permute-start) | collective-permute-done | bytes 196640 | tf_op jit(solution)/shard_map/ppermute | solution.py:143
  63.8 11.7 %cholesky.59 = f32[128,128]{1,0:T(8,128)S(1)} custom-call(f32[128,128]{1,0:T(8,128)S(1)} %copy.65), custom_call_target="Cholesky" | custom-call | tf_op jit(solution)/shard_map/jit(cholesky)/cholesky | solution.py:78
  76.2 0.7 fusion.33
  76.9 9.8 %custom-call.9 = f32[1,128,128]{1,2,0:T(8,128)S(1)} custom-call(f32[1,128,128]{2,1,0:T(8,128)S(1)} %fusion.33), custom_call_target="InvertDiagBlocksLowerTriangular" | custom-call | tf_op jit(solution)/shard_map/jit(_cho_solve)/triangular_solve | solution.py:80
  87.3 1.1 fusion.7
  88.8 1.0 fusion.6
  89.8 5.5 %collective-permute-start.1 = (f32[3,128,128]{2,1,0:T(8,128)S(1)}, f32[3,128,128]{2,1,0:T(8,128)S(1)}, u32[]{:S(2)}, u32[]{:S(2)}) collective-permute-start(f32[3,128,128]{2,1,0:T(8,128)S(1)} %pad_maximum_fusion.2), channel_id=1, source_target_pairs={{0,8},{4,12},{8,16},{12,20},{16,24},{20,28},{1,9},{5,13},{9,17},{1... | collective-permute-start | bytes 589832 | tf_op jit(solution)/shard_map/ppermute | solution.py:143
  95.3 3.0 %collective-permute-done.1 = f32[3,128,128]{2,1,0:T(8,128)S(1)} collective-permute-done((f32[3,128,128]{2,1,0:T(8,128)S(1)}, f32[3,128,128]{2,1,0:T(8,128)S(1)}, u32[]{:S(2)}, u32[]{:S(2)}) %collective-permute-start.1) | collective-permute-done | bytes 196640 | tf_op jit(solution)/shard_map/ppermute | solution.py:143
  98.6 11.7 %cholesky.70 = f32[128,128]{1,0:T(8,128)S(1)} custom-call(f32[128,128]{1,0:T(8,128)S(1)} %fusion.65), custom_call_target="Cholesky" | custom-call | tf_op jit(solution)/shard_map/jit(cholesky)/cholesky | solution.py:78
  111.0 0.7 fusion.34
  111.6 9.8 %custom-call.10 = f32[1,128,128]{1,2,0:T(8,128)S(1)} custom-call(f32[1,128,128]{2,1,0:T(8,128)S(1)} %fusion.34), custom_call_target="InvertDiagBlocksLowerTriangular" | custom-call | tf_op jit(solution)/shard_map/jit(_cho_solve)/triangular_solve | solution.py:80
  122.9 5.6 %collective-permute-start.2 = (f32[3,128,128]{2,1,0:T(8,128)S(1)}, f32[3,128,128]{2,1,0:T(8,128)S(1)}, u32[]{:S(2)}, u32[]{:S(2)}) collective-permute-start(f32[3,128,128]{2,1,0:T(8,128)S(1)} %pad_maximum_fusion.3), channel_id=1, source_target_pairs={{0,16},{4,20},{8,24},{12,28},{1,17},{5,21},{9,25},{13,29},{2,18},{... | collective-permute-start | bytes 589832 | tf_op jit(solution)/shard_map/ppermute | solution.py:143
  128.4 3.0 %collective-permute-done.2 = f32[3,128,128]{2,1,0:T(8,128)S(1)} collective-permute-done((f32[3,128,128]{2,1,0:T(8,128)S(1)}, f32[3,128,128]{2,1,0:T(8,128)S(1)}, u32[]{:S(2)}, u32[]{:S(2)}) %collective-permute-start.2) | collective-permute-done | bytes 196640 | tf_op jit(solution)/shard_map/ppermute | solution.py:143
  131.8 11.7 %cholesky.81 = f32[128,128]{1,0:T(8,128)S(1)} custom-call(f32[128,128]{1,0:T(8,128)S(1)} %fusion.55), custom_call_target="Cholesky" | custom-call | tf_op jit(solution)/shard_map/jit(cholesky)/cholesky | solution.py:78
  144.2 0.7 fusion.35
  144.8 9.8 %custom-call.11 = f32[1,128,128]{1,2,0:T(8,128)S(1)} custom-call(f32[1,128,128]{2,1,0:T(8,128)S(1)} %fusion.35), custom_call_target="InvertDiagBlocksLowerTriangular" | custom-call | tf_op jit(solution)/shard_map/jit(_cho_solve)/triangular_solve | solution.py:80
  156.1 0.7 maximum_bitcast_fusion
  156.8 28.7 %reduce-scatter.2.cloned.1.call-done = f32[512,2048]{1,0:T(8,128)} async-done(((f32[2048,2048]{1,0:T(8,128)}), f32[512,2048]{1,0:T(8,128)}) %reduce-scatter.2.cloned.1.call-update) | async-done | bytes 4194320 | tf_op jit(solution)/shard_map/reduce_scatter | solution.py:156
  (66 shorter events, 8.8 us)
Async XLA Ops:
  7.2 16.0 %copy-start.1 = (s32[1,8,16]{2,1,0:T(8,128)S(1)}, s32[1,8,16]{2,1,0:T(8,128)}, u32[]{:S(2)}) copy-start(s32[1,8,16]{2,1,0:T(8,128)} %param.11) | copy-start | bytes 1540
  7.2 16.6 %copy-start.2 = (f32[1,1024]{1,0:T(1,128)S(1)}, f32[1,1024]{1,0:T(1,128)}, u32[]{:S(2)}) copy-start(f32[1,1024]{1,0:T(1,128)} %param.10) | copy-start | bytes 12292
  7.2 15.4 %copy-start.3 = (s32[16]{0:T(128)S(1)}, s32[16]{0:T(128)}, u32[]{:S(2)}) copy-start(s32[16]{0:T(128)} %tile_ref.1) | copy-start | bytes 196
  7.2 48.6 %all-reduce.2.cloned.1.call-start = ((), (), s32[]{:S(2)}) async-start(), calls=%async_computation.2 | async-start | bytes 393216 | tf_op jit(solution)/shard_map/psum | solution.py:129
  8.0 16.8 %copy-start = (s32[16]{0:T(128)}, s32[16]{0:T(128)S(1)}, u32[]{:S(2)}) copy-start(s32[16]{0:T(128)S(1)} %select_reduce_fusion.3.src_right) | copy-start | bytes 196
  21.2 164.2 %reduce-scatter.2.cloned.1.call-start = ((), (), s32[]{:S(2)}) async-start(), calls=%async_computation.1 | async-start | bytes 20971520 | tf_op jit(solution)/shard_map/reduce_scatter | solution.py:156
  56.9 6.5 %collective-permute-start = (f32[3,128,128]{2,1,0:T(8,128)S(1)}, f32[3,128,128]{2,1,0:T(8,128)S(1)}, u32[]{:S(2)}, u32[]{:S(2)}) collective-permute-start(f32[3,128,128]{2,1,0:T(8,128)S(1)} %copy.60), channel_id=1, source_target_pairs={{0,4},{4,8},{8,12},{12,16},{16,20},{20,24},{24,28},{1,5},{5,9},{9,... | collective-permute-start | bytes 589832 | tf_op jit(solution)/shard_map/ppermute | solution.py:143
  89.8 8.5 %collective-permute-start.1 = (f32[3,128,128]{2,1,0:T(8,128)S(1)}, f32[3,128,128]{2,1,0:T(8,128)S(1)}, u32[]{:S(2)}, u32[]{:S(2)}) collective-permute-start(f32[3,128,128]{2,1,0:T(8,128)S(1)} %pad_maximum_fusion.2), channel_id=1, source_target_pairs={{0,8},{4,12},{8,16},{12,20},{16,24},{20,28},{1,9},{5,13},{9,17},{1... | collective-permute-start | bytes 589832 | tf_op jit(solution)/shard_map/ppermute | solution.py:143
  122.9 8.5 %collective-permute-start.2 = (f32[3,128,128]{2,1,0:T(8,128)S(1)}, f32[3,128,128]{2,1,0:T(8,128)S(1)}, u32[]{:S(2)}, u32[]{:S(2)}) collective-permute-start(f32[3,128,128]{2,1,0:T(8,128)S(1)} %pad_maximum_fusion.3), channel_id=1, source_target_pairs={{0,16},{4,20},{8,24},{12,28},{1,17},{5,21},{9,25},{13,29},{2,18},{... | collective-permute-start | bytes 589832 | tf_op jit(solution)/shard_map/ppermute | solution.py:143
Sparse Core Ops, SparseCore 0:
  21.3 34.4 all-reduce.1
  59.1 126.2 reduce-scatter.1

commit v3 on v2

--- a/solution.py
+++ b/solution.py
@@ -9,8 +9,12 @@
 BLK = 128
 
 
-def gram_kernel(src_left, src_right, tile_ref, mask_ref, flag_ref, g_ref, w_ref, diag_ref,
-                out_ref, s_ref, lt_ref):
+def contrib_kernel(src_left, src_right, tile_ref, mask_ref, flag_ref, g_ref, w_ref, diag_ref, *rest):
+    if len(rest) == 4:
+        acc_ref, out_ref, s_ref, lt_ref = rest
+    else:
+        acc_ref = None
+        out_ref, s_ref, lt_ref = rest
     k = pl.program_id(0)
     row_blocks = g_ref.shape[0] // BLK
     col_blocks = g_ref.shape[1] // BLK
@@ -35,36 +39,48 @@
         live = mask_ref[rb * col_blocks + src].astype(jnp.float32)
         vals = g_ref[rb * BLK:(rb + 1) * BLK, pl.ds(c0, BLK)].astype(jnp.float32) * live
         lt_ref[:, rb * BLK:(rb + 1) * BLK] = vals.T.astype(jnp.bfloat16)
-    out_ref[...] = jnp.dot(lt_ref[...], s_ref[...], preferred_element_type=jnp.float32)
-    blk = tile_ref[k]
-    e0 = pl.multiple_of(blk * BLK, BLK)
-    rows = lax.broadcasted_iota(jnp.int32, (BLK, BLK), 0)
-    cols = lax.broadcasted_iota(jnp.int32, (BLK, BLK), 1)
-    dvals = diag_ref[pl.ds(blk, 1), :] * flag_ref[0].astype(jnp.float32)
-    out_ref[:, pl.ds(e0, BLK)] += jnp.where(rows == cols, dvals, 0.0)
-
-
-def gram_rows(slab, weights, live_blocks, src_left, src_right, tile_order, diagonal, flag):
+    term = jnp.dot(lt_ref[...], s_ref[...], preferred_element_type=jnp.float32)
+    if acc_ref is None:
+        out_ref[...] = term
+        blk = tile_ref[k]
+        e0 = pl.multiple_of(blk * BLK, BLK)
+        rows = lax.broadcasted_iota(jnp.int32, (BLK, BLK), 0)
+        cols = lax.broadcasted_iota(jnp.int32, (BLK, BLK), 1)
+        dvals = diag_ref[pl.ds(blk, 1), :] * flag_ref[0].astype(jnp.float32)
+        out_ref[:, pl.ds(e0, BLK)] += jnp.where(rows == cols, dvals, 0.0)
+    else:
+        out_ref[...] = acc_ref[...] + term
+
+
+def gram_contrib(slab, weights, live_blocks, src_left, src_right, own_tiles, diagonal, acc=None):
     height = slab.shape[0]
     col_blocks = L // BLK
+    out_blocks = src_left.shape[0]
+    in_specs = [
+        pl.BlockSpec((height, L), lambda k, *_: (0, 0)),
+        pl.BlockSpec((height, 1), lambda k, *_: (0, 0)),
+        pl.BlockSpec((col_blocks, BLK), lambda k, *_: (0, 0)),
+    ]
+    operands = [slab, weights.reshape(height, 1), diagonal.reshape(col_blocks, BLK)]
+    aliases = {}
+    if acc is not None:
+        in_specs.append(pl.BlockSpec((BLK, L), lambda k, *_: (k, 0)))
+        operands.append(acc)
+        aliases = {8: 0}
     grid_spec = pltpu.PrefetchScalarGridSpec(
         num_scalar_prefetch=5,
-        grid=(col_blocks,),
-        in_specs=[
-            pl.BlockSpec((height, L), lambda k, *_: (0, 0)),
-            pl.BlockSpec((height, 1), lambda k, *_: (0, 0)),
-            pl.BlockSpec((col_blocks, BLK), lambda k, *_: (0, 0)),
-        ],
+        grid=(out_blocks,),
+        in_specs=in_specs,
         out_specs=pl.BlockSpec((BLK, L), lambda k, *_: (k, 0)),
         scratch_shapes=[pltpu.VMEM((height, L), jnp.bfloat16), pltpu.VMEM((BLK, height), jnp.bfloat16)],
     )
     return pl.pallas_call(
-        gram_kernel,
+        contrib_kernel,
         grid_spec=grid_spec,
-        out_shape=jax.ShapeDtypeStruct((L, L), jnp.float32),
+        out_shape=jax.ShapeDtypeStruct((out_blocks * BLK, L), jnp.float32),
+        input_output_aliases=aliases,
         compiler_params=pltpu.CompilerParams(vmem_limit_bytes=56 * 1024 * 1024),
-    )(src_left, src_right, tile_order, live_blocks.reshape(-1), flag.reshape(1),
-      slab, weights.reshape(height, 1), diagonal.reshape(col_blocks, BLK))
+    )(src_left, src_right, own_tiles, live_blocks.reshape(-1), jnp.ones((1,), jnp.int32), *operands)
 
 
 HIGHEST = lax.Precision.HIGHEST
@@ -148,12 +164,26 @@
         shift *= 2
     chain_out = jnp.stack(running)[None]
 
-    flag = (my_index == 0).astype(jnp.int32)
-    partial = gram_rows(
-        local_slab, row_weights, live_blocks, jnp.take(source, tile_order), source,
-        tile_order, diagonal, flag,
-    )
-    owned = lax.psum_scatter(partial, "row", scatter_dimension=0, tiled=True)
+    owners = lax.axis_size("row")
+    own_blocks = block_count // owners
+    own_tiles = lax.dynamic_slice_in_dim(tile_order, my_index * own_blocks, own_blocks)
+    left_src = jnp.take(source, own_tiles)
+    every_weight = lax.all_gather(row_weights, "row", axis=0, tiled=False)
+    every_mask = lax.all_gather(live_blocks, "row", axis=0, tiled=False)
+    peers = []
+    for step in range(1, owners):
+        pairs = [(src, src ^ step) for src in range(owners)]
+        peers.append((lax.ppermute(local_slab, "row", pairs), my_index ^ step))
+    owned = gram_contrib(
+        local_slab, row_weights, live_blocks, left_src, source, own_tiles, diagonal
+    )
+    for slab, where_from in peers:
+        owned = gram_contrib(
+            slab,
+            lax.dynamic_index_in_dim(every_weight, where_from, 0, False),
+            lax.dynamic_index_in_dim(every_mask, where_from, 0, False),
+            left_src, source, own_tiles, diagonal, owned,
+        )
     return (owned[None], chain_out)
 
 

time: 193 us -> 344 us (1.78)
  blocking collectives: 0 us -> 136 us
  Pallas kernels: 21.8 us -> 46.1 us
  waiting for transfers between devices: 46 us -> 32.6 us
  local copies, waits for them, and re-layouts: 4.98 us -> 10.8 us
    all_gather x0 -> x2, blocking collectives: none -> 136 us  [the longest x1 130 us: local(): every_weight = lax.all_gather(row_weights, 'row', axis=0, tiled=False)]
    reduce_scatter x1 -> x0, waiting for transfers between devices: 28.7 us -> none  [local(): owned = lax.psum_scatter(partial, 'row', scatter_dimension=0, tiled=True)]
    pallas_call x1 -> x4, Pallas kernels: 21.8 us -> 46.1 us  [gram_contrib(): pl.pallas_call(contrib_kernel, grid_spec=grid_spec, out_shape=jax.ShapeDt...]
    psum x1, waiting for transfers between devices: 8.45 us -> 32.6 us  [local(): summed = lax.psum(part_pieces, 'row')]
    ppermute x3, waiting for transfers between devices: 8.9 us -> 0.01 us  [local(): moved = lax.ppermute(jnp.stack(running), 'tm', pairs)]
    reshape x0 -> x7, local copies, waits for them, and re-layouts: none -> 5.17 us  [the longest x4 3.16 us: gram_contrib(): weights.reshape(height, 1)]
  transfers between devices with their start and end apart: 5 -> 7, of which waited for: 5 -> 1; matrix products, arithmetic and copies ran while one was open for 42% -> 27% of each run, Pallas kernels for 11% -> 10%
where the time goes in v3:
time: 344 us; the launch traced here: 343 us
  blocking collectives  136 us (40%)
  other arithmetic  73.5 us (21%)
  Pallas kernels  46.1 us (13%)
  waiting for transfers between devices  32.6 us (9%)
  between operations  19.7 us (6%)
  starting transfers between devices  15.1 us (4%)
  local copies, waits for them, and re-layouts  10.8 us (3%)
  matrix products  9.47 us (3%)
    all_gather x1, blocking collectives, local(): every_weight = lax.all_gather(row_weights, 'row', axis=0, tiled=False)  130 us
    pallas_call x4, Pallas kernels, gram_contrib(): pl.pallas_call(contrib_kernel, grid_spec=grid_spec, out_shape=jax.ShapeDt...  46.1 us
    another operation x9, other arithmetic, join_segments(): factor = jnp.linalg.cholesky(middle)  37.2 us
    psum x1, waiting for transfers between devices, local(): summed = lax.psum(part_pieces, 'row')  32.6 us
    another operation x6, other arithmetic, join_segments(): jax.scipy.linalg.cho_solve((factor, True), jnp.concatenate([cross_one.T,...  31.4 us
    ppermute x3, starting transfers between devices, local(): moved = lax.ppermute(jnp.stack(running), 'tm', pairs)  11.8 us
  transfers between devices with their start and end apart: 7, of which 1 were waited for; matrix products, arithmetic and copies ran while one was open for 27% of the time, Pallas kernels for 10%

profile of v3, /device:TPU:0, one launch (start us, length us, event | category | flops | bytes accessed | tf_op | source)
XLA Modules:
  0.0 343.1 jit_solution(18429590029881774241)
XLA Ops:
  7.8 2.6 collective-permute-start.1
  10.4 0.8 select_reduce_fusion.3.src_right
  17.0 1.0 fusion.103
  18.0 1.9 convolution_bitcast_fusion
  19.9 1.9 convolution_bitcast_fusion.1
  21.8 1.9 convolution_bitcast_fusion.2
  23.7 0.7 pad_maximum_fusion
  24.4 0.7 slice_bitcast_fusion.12
  25.1 1.3 reshape_squeeze.13.mask_ref
  26.4 32.6 %all-reduce.2.cloned.1.call-done = f32[3,128,128]{1,2,0:T(8,128)} async-done(((f32[3,128,128]{1,2,0:T(8,128)}), f32[3,128,128]{1,2,0:T(8,128)}) %all-reduce.2.cloned.1.call-update) | async-done | bytes 196624 | tf_op jit(solution)/shard_map/psum | solution.py:145
  59.0 1.0 slice_bitcast_fusion.7
  60.2 3.4 collective-permute-start.3
  64.4 1.0 copy.90.w_ref
  65.4 130.4 %all-gather = f32[4,1,1024]{2,1,0:T(1,128)S(1)} all-gather(f32[1,1,1024]{2,1,0:T(1,128)S(1)} %bitcast.196), channel_id=1, replica_groups=mesh['tm'=8,'row'=4] {'row'}, dimensions={0}, use_global_device_ids=true | all-gather | bytes 20480 | tf_op jit(solution)/shard_map/all_gather | solution.py:171
  196.3 11.7 %cholesky.59 = f32[128,128]{1,0:T(8,128)S(1)} custom-call(f32[128,128]{1,0:T(8,128)S(1)} %copy.102), custom_call_target="Cholesky" | custom-call | tf_op jit(solution)/shard_map/jit(cholesky)/cholesky | solution.py:94
  209.4 9.8 %custom-call.9 = f32[1,128,128]{1,2,0:T(8,128)S(1)} custom-call(f32[1,128,128]{2,1,0:T(8,128)S(1)} %fusion.33), custom_call_target="InvertDiagBlocksLowerTriangular" | custom-call | tf_op jit(solution)/shard_map/jit(_cho_solve)/triangular_solve | solution.py:96
  220.6 3.7 %collective-permute-start.4 = (f32[3,128,128]{2,1,0:T(8,128)S(1)}, f32[3,128,128]{2,1,0:T(8,128)S(1)}, u32[]{:S(2)}, u32[]{:S(2)}) collective-permute-start(f32[3,128,128]{2,1,0:T(8,128)S(1)} %pad_maximum_fusion.2), channel_id=1, source_target_pairs={{0,8},{4,12},{8,16},{12,20},{16,24},{20,28},{1,9},{5,13},{9,17},{1... | collective-permute-start | bytes 589832 | tf_op jit(solution)/shard_map/ppermute | solution.py:159
  224.4 1.0 copy.91.w_ref
  225.4 5.4 %all_gather.6 = s32[4,8,16]{2,1,0:T(8,128)S(1)} all-gather(s32[1,8,16]{2,1,0:T(8,128)S(1)} %copy-done.2), channel_id=1, replica_groups=mesh['tm'=8,'row'=4] {'row'}, dimensions={0}, use_global_device_ids=true | all-gather | bytes 2560 | tf_op jit(solution)/shard_map/all_gather | solution.py:172
  231.4 1.1 copy.92.w_ref
  233.2 1.1 copy.93.w_ref
  234.2 0.7 reshape.209.mask_ref
  235.2 11.7 %cholesky.70 = f32[128,128]{1,0:T(8,128)S(1)} custom-call(f32[128,128]{1,0:T(8,128)S(1)} %fusion.65), custom_call_target="Cholesky" | custom-call | tf_op jit(solution)/shard_map/jit(cholesky)/cholesky | solution.py:94
  248.2 9.8 %custom-call.10 = f32[1,128,128]{1,2,0:T(8,128)S(1)} custom-call(f32[1,128,128]{2,1,0:T(8,128)S(1)} %fusion.34), custom_call_target="InvertDiagBlocksLowerTriangular" | custom-call | tf_op jit(solution)/shard_map/jit(_cho_solve)/triangular_solve | solution.py:96
  259.5 4.7 %collective-permute-start.5 = (f32[3,128,128]{2,1,0:T(8,128)S(1)}, f32[3,128,128]{2,1,0:T(8,128)S(1)}, u32[]{:S(2)}, u32[]{:S(2)}) collective-permute-start(f32[3,128,128]{2,1,0:T(8,128)S(1)} %pad_maximum_fusion.3), channel_id=1, source_target_pairs={{0,16},{4,20},{8,24},{12,28},{1,17},{5,21},{9,25},{13,29},{2,18},{... | collective-permute-start | bytes 589832 | tf_op jit(solution)/shard_map/ppermute | solution.py:159
  264.7 10.8 %shard_map.80.rest_0_ = f32[512,2048]{1,0:T(8,128)} custom-call(s32[4]{0:T(128)} %and_select_fusion.src_left, s32[16]{0:T(128)} %copy-done, s32[4]{0:T(128)} %copy-done.4, s32[128]{0:T(128)} %reshape_squeeze.13.mask_ref, s32[1]{0:T(128)} %constant.99.clone.1.flag_ref, bf16[1024,2048]{1,0:T(8,128)(2,1)} %bitcast.181, f32[1024,1]{1,0:T(8,128)} %copy.90.w_ref, ...), custom_call_target="tpu_custom_call" | custom-call | tf_op jit(solution)/shard_map/pallas_call | solution.py:77
  275.9 11.7 %cholesky.81 = f32[128,128]{1,0:T(8,128)S(1)} custom-call(f32[128,128]{1,0:T(8,128)S(1)} %fusion.55), custom_call_target="Cholesky" | custom-call | tf_op jit(solution)/shard_map/jit(cholesky)/cholesky | solution.py:94
  289.0 9.8 %custom-call.11 = f32[1,128,128]{1,2,0:T(8,128)S(1)} custom-call(f32[1,128,128]{2,1,0:T(8,128)S(1)} %fusion.35), custom_call_target="InvertDiagBlocksLowerTriangular" | custom-call | tf_op jit(solution)/shard_map/jit(_cho_solve)/triangular_solve | solution.py:96
  300.2 0.7 maximum_bitcast_fusion
  300.9 11.8 %shard_map.81.rest_0_ = f32[512,2048]{1,0:T(8,128)} custom-call(s32[4]{0:T(128)} %and_select_fusion.src_left, s32[16]{0:T(128)} %copy-done, s32[4]{0:T(128)} %copy-done.4, s32[128]{0:T(128)} %reshape.213.mask_ref, s32[1]{0:T(128)} %constant.99.clone.1.flag_ref, bf16[1024,2048]{1,0:T(8,128)(2,1)} %collective-permute-done.2.g_ref, ...), custom_call_target="tpu_custom_call", output_to_operand_aliasing={{}: (8, {})} | custom-call | tf_op jit(solution)/shard_map/pallas_call | solution.py:77
  312.7 11.8 %shard_map.82.rest_0_ = f32[512,2048]{1,0:T(8,128)} custom-call(s32[4]{0:T(128)} %and_select_fusion.src_left, s32[16]{0:T(128)} %copy-done, s32[4]{0:T(128)} %copy-done.4, s32[128]{0:T(128)} %reshape.211.mask_ref, s32[1]{0:T(128)} %constant.99.clone.1.flag_ref, bf16[1024,2048]{1,0:T(8,128)(2,1)} %collective-permute-done.1.g_ref, ...), custom_call_target="tpu_custom_call", output_to_operand_aliasing={{}: (8, {})} | custom-call | tf_op jit(solution)/shard_map/pallas_call | solution.py:77
  324.5 11.8 %shard_map.83 = f32[512,2048]{1,0:T(8,128)} custom-call(s32[4]{0:T(128)} %and_select_fusion.src_left, s32[16]{0:T(128)} %copy-done, s32[4]{0:T(128)} %copy-done.4, s32[128]{0:T(128)} %reshape.209.mask_ref, s32[1]{0:T(128)} %constant.99.clone.1.flag_ref, bf16[1024,2048]{1,0:T(8,128)(2,1)} %collective-permute-done.g_ref, ...), custom_call_target="tpu_custom_call", output_to_operand_aliasing={{}: (8, {})} | custom-call | tf_op jit(solution)/shard_map/pallas_call | solution.py:77
  (86 shorter events, 13.2 us)
Async XLA Ops:
  7.2 57.2 %copy-start.3 = (f32[1,1024]{1,0:T(1,128)S(1)}, f32[1,1024]{1,0:T(1,128)}, u32[]{:S(2)}) copy-start(f32[1,1024]{1,0:T(1,128)} %param.10) | copy-start | bytes 12292
  7.2 56.4 %copy-start.5 = (s32[16]{0:T(128)S(1)}, s32[16]{0:T(128)}, u32[]{:S(2)}) copy-start(s32[16]{0:T(128)} %param.13) | copy-start | bytes 196
  7.2 51.8 %all-reduce.2.cloned.1.call-start = ((), (), s32[]{:S(2)}) async-start(), calls=%async_computation | async-start | bytes 393216 | tf_op jit(solution)/shard_map/psum | solution.py:145
  7.2 293.6 %collective-permute-start.2 = (bf16[1024,2048]{1,0:T(8,128)(2,1)}, bf16[1024,2048]{1,0:T(8,128)(2,1)}, u32[]{:S(2)}, u32[]{:S(2)}) collective-permute-start(bf16[1024,2048]{1,0:T(8,128)(2,1)} %bitcast.178), channel_id=1, source_target_pairs={{0,1},{1,0},{2,3},{3,2},{4,5},{5,4},{6,7},{7,6},{8,9},{9,8},{10,11... | collective-permute-start | bytes 12582920 | tf_op jit(solution)/shard_map/ppermute | solution.py:176
  7.8 304.9 %collective-permute-start.1 = (bf16[1024,2048]{1,0:T(8,128)(2,1)}, bf16[1024,2048]{1,0:T(8,128)(2,1)}, u32[]{:S(2)}, u32[]{:S(2)}) collective-permute-start(bf16[1024,2048]{1,0:T(8,128)(2,1)} %bitcast.179), channel_id=1, source_target_pairs={{0,2},{1,3},{2,0},{3,1},{4,6},{5,7},{6,4},{7,5},{8,10},{9,11},{10,... | collective-permute-start | bytes 12582920 | tf_op jit(solution)/shard_map/ppermute | solution.py:176
  10.3 314.1 %collective-permute-start = (bf16[1024,2048]{1,0:T(8,128)(2,1)}, bf16[1024,2048]{1,0:T(8,128)(2,1)}, u32[]{:S(2)}, u32[]{:S(2)}) collective-permute-start(bf16[1024,2048]{1,0:T(8,128)(2,1)} %bitcast.180), channel_id=1, source_target_pairs={{0,3},{1,2},{2,1},{3,0},{4,7},{5,6},{6,5},{7,4},{8,11},{9,10},{10,... | collective-permute-start | bytes 12582920 | tf_op jit(solution)/shard_map/ppermute | solution.py:176
  11.2 208.6 %copy-start = (s32[16]{0:T(128)}, s32[16]{0:T(128)S(1)}, u32[]{:S(2)}) copy-start(s32[16]{0:T(128)S(1)} %select_reduce_fusion.3.src_right) | copy-start | bytes 196
  21.8 203.7 %copy-start.2 = (s32[1,8,16]{2,1,0:T(8,128)S(1)}, s32[1,8,16]{2,1,0:T(8,128)}, u32[]{:S(2)}) copy-start(s32[1,8,16]{2,1,0:T(8,128)} %param.11) | copy-start | bytes 1540
  59.0 160.8 %copy-start.1 = (f32[3,128,128]{1,2,0:T(8,128)S(1)}, f32[3,128,128]{1,2,0:T(8,128)}, u32[]{:S(2)}) copy-start(f32[3,128,128]{1,2,0:T(8,128)} %all-reduce.2.cloned.1.call-done) | copy-start | bytes 589828
  60.2 135.7 %collective-permute-start.3 = (f32[3,128,128]{2,1,0:T(8,128)S(1)}, f32[3,128,128]{2,1,0:T(8,128)S(1)}, u32[]{:S(2)}, u32[]{:S(2)}) collective-permute-start(f32[3,128,128]{2,1,0:T(8,128)S(1)} %copy.97), channel_id=1, source_target_pairs={{0,4},{4,8},{8,12},{12,16},{16,20},{20,24},{24,28},{1,5},{5,9},{9,... | collective-permute-start | bytes 589832 | tf_op jit(solution)/shard_map/ppermute | solution.py:159
  63.7 200.5 %copy-start.4 = (s32[4]{0:T(128)}, s32[4]{0:T(128)S(1)}, u32[]{:S(2)}) copy-start(s32[4]{0:T(128)S(1)} %get-tuple-element.7.tile_ref) | copy-start | bytes 52
  220.6 14.3 %collective-permute-start.4 = (f32[3,128,128]{2,1,0:T(8,128)S(1)}, f32[3,128,128]{2,1,0:T(8,128)S(1)}, u32[]{:S(2)}, u32[]{:S(2)}) collective-permute-start(f32[3,128,128]{2,1,0:T(8,128)S(1)} %pad_maximum_fusion.2), channel_id=1, source_target_pairs={{0,8},{4,12},{8,16},{12,20},{16,24},{20,28},{1,9},{5,13},{9,17},{1... | collective-permute-start | bytes 589832 | tf_op jit(solution)/shard_map/ppermute | solution.py:159
  259.5 16.1 %collective-permute-start.5 = (f32[3,128,128]{2,1,0:T(8,128)S(1)}, f32[3,128,128]{2,1,0:T(8,128)S(1)}, u32[]{:S(2)}, u32[]{:S(2)}) collective-permute-start(f32[3,128,128]{2,1,0:T(8,128)S(1)} %pad_maximum_fusion.3), channel_id=1, source_target_pairs={{0,16},{4,20},{8,24},{12,28},{1,17},{5,21},{9,25},{13,29},{2,18},{... | collective-permute-start | bytes 589832 | tf_op jit(solution)/shard_map/ppermute | solution.py:159
Sparse Core Ops, SparseCore 0:
  24.5 34.4 all-reduce.1

commit v4 on v3

--- a/solution.py
+++ b/solution.py
@@ -168,21 +168,49 @@
     own_blocks = block_count // owners
     own_tiles = lax.dynamic_slice_in_dim(tile_order, my_index * own_blocks, own_blocks)
     left_src = jnp.take(source, own_tiles)
-    every_weight = lax.all_gather(row_weights, "row", axis=0, tiled=False)
-    every_mask = lax.all_gather(live_blocks, "row", axis=0, tiled=False)
-    peers = []
-    for step in range(1, owners):
-        pairs = [(src, src ^ step) for src in range(owners)]
-        peers.append((lax.ppermute(local_slab, "row", pairs), my_index ^ step))
+    packed_side = jnp.concatenate(
+        [row_weights, live_blocks.reshape(-1).astype(jnp.float32)]
+    )
+
+    def unpack_side(side, chunk, chunks):
+        rows = slab_height // chunks
+        weights = lax.slice_in_dim(side, chunk * rows, (chunk + 1) * rows)
+        live = side[slab_height:].reshape(slab_height // BLK, block_count).astype(jnp.int32)
+        live = lax.slice_in_dim(live, chunk * (rows // BLK), (chunk + 1) * (rows // BLK))
+        return weights, live
+
+    def exchange(value, step):
+        return lax.ppermute(value, "row", [(src, src ^ step) for src in range(owners)])
+
+    chunks = 2
+    chunk_rows = slab_height // chunks
+    own_slabs = [lax.slice_in_dim(local_slab, c * chunk_rows, (c + 1) * chunk_rows) for c in range(chunks)]
+    if owners == 4:
+        neighbour = (exchange(local_slab, 1), exchange(packed_side, 1), 1)
+        across_side = exchange(packed_side, 2)
+        across = [exchange(piece, 2) for piece in own_slabs]
+        forwarded = [exchange(piece, 1) for piece in across]
+        forwarded_side = exchange(across_side, 1)
+        arrivals = [neighbour]
+        arrivals += [(piece, across_side, c, chunks) for c, piece in enumerate(across)]
+        arrivals += [(piece, forwarded_side, c, chunks) for c, piece in enumerate(forwarded)]
+    else:
+        arrivals = [
+            (exchange(local_slab, step), exchange(packed_side, step), 0, 1)
+            for step in range(1, owners)
+        ]
     owned = gram_contrib(
         local_slab, row_weights, live_blocks, left_src, source, own_tiles, diagonal
     )
-    for slab, where_from in peers:
+    for arrival in arrivals:
+        if len(arrival) == 3:
+            slab, side, _ = arrival
+            weights, live = unpack_side(side, 0, 1)
+        else:
+            slab, side, chunk, count = arrival
+            weights, live = unpack_side(side, chunk, count)
         owned = gram_contrib(
-            slab,
-            lax.dynamic_index_in_dim(every_weight, where_from, 0, False),
-            lax.dynamic_index_in_dim(every_mask, where_from, 0, False),
-            left_src, source, own_tiles, diagonal, owned,
+            slab, weights, live, left_src, source, own_tiles, diagonal, owned,
         )
     return (owned[None], chain_out)
 

time: 344 us -> 218 us (0.63)
  blocking collectives: 136 us -> 0 us
  waiting for transfers between devices: 32.6 us -> 14.6 us
  Pallas kernels: 46.1 us -> 60.5 us
  starting transfers between devices: 15.1 us -> 20.6 us
  local copies, waits for them, and re-layouts: 10.8 us -> 15.7 us
    all_gather x2 -> x0, blocking collectives: 136 us -> none  [the longest x1 130 us: local(): every_weight = lax.all_gather(row_weights, 'row', axis=0, tiled=False)]
    psum x1, waiting for transfers between devices: 32.6 us -> 8.34 us  [local(): summed = lax.psum(part_pieces, 'row')]
    pallas_call x4 -> x6, Pallas kernels: 46.1 us -> 60.5 us  [gram_contrib(): pl.pallas_call(contrib_kernel, grid_spec=grid_spec, out_shape=jax.ShapeDt...]
    ppermute x3, waiting for transfers between devices: 0.01 us -> 6.25 us  [local(): moved = lax.ppermute(jnp.stack(running), 'tm', pairs)]
    slice x0 -> x6, local copies, waits for them, and re-layouts: none -> 6.08 us  [the longest x1 4.79 us: local(): lax.slice_in_dim(local_slab, c * chunk_rows, (c + 1) * chunk_rows)]
  transfers between devices with their start and end apart: 7 -> 12, of which waited for: 1 -> 4; matrix products, arithmetic and copies ran while one was open for 27% -> 46% of each run, Pallas kernels for 10% -> 24%
where the time goes in v4:
time: 218 us; the launch traced here: 215 us
  other arithmetic  74.8 us (34%)
  Pallas kernels  60.5 us (28%)
  starting transfers between devices  20.6 us (9%)
  between operations  19.8 us (9%)
  local copies, waits for them, and re-layouts  15.7 us (7%)
  waiting for transfers between devices  14.6 us (7%)
  matrix products  9.49 us (4%)
    pallas_call x6, Pallas kernels, gram_contrib(): pl.pallas_call(contrib_kernel, grid_spec=grid_spec, out_shape=jax.ShapeDt...  60.5 us
    another operation x9, other arithmetic, join_segments(): factor = jnp.linalg.cholesky(middle)  37.2 us
    another operation x6, other arithmetic, join_segments(): jax.scipy.linalg.cho_solve((factor, True), jnp.concatenate([cross_one.T,...  31.4 us
    ppermute x3, starting transfers between devices, local(): moved = lax.ppermute(jnp.stack(running), 'tm', pairs)  14.7 us
    psum x1, waiting for transfers between devices, local(): summed = lax.psum(part_pieces, 'row')  8.34 us
    ppermute x3, waiting for transfers between devices, local(): moved = lax.ppermute(jnp.stack(running), 'tm', pairs)  6.25 us
    ppermute x8, starting transfers between devices, exchange(): lax.ppermute(value, 'row', [(src, src ^ step) for src in range(owners)])  5.84 us
    dot_general x3, matrix products, contract_rows(): lax.dot_general(left_cols, right_cols, (((0,), (0,)), ((), ())), preferre...  5.65 us
  transfers between devices with their start and end apart: 12, of which 4 were waited for; matrix products, arithmetic and copies ran while one was open for 46% of the time, Pallas kernels for 24%

profile of v4, /device:TPU:0, one launch (start us, length us, event | category | flops | bytes accessed | tf_op | source)
XLA Modules:
  0.0 215.4 jit_solution(11032582016485379989)
XLA Ops:
  9.1 2.5 %collective-permute-start = (f32[1152]{0:T(1024)S(1)}, f32[1152]{0:T(1024)S(1)}, u32[]{:S(2)}, u32[]{:S(2)}) collective-permute-start(f32[1152]{0:T(1024)S(1)} %pad_maximum_fusion.4), channel_id=1, source_target_pairs={{0,2},{1,3},{2,0},{3,1},{4,6},{5,7},{6,4},{7,5},{8,10},{9,11},{10,... | collective-permute-start | bytes 13832 | tf_op jit(solution)/shard_map/ppermute | solution.py:183
  18.2 1.0 fusion.100
  19.2 1.9 convolution_bitcast_fusion
  21.1 1.9 convolution_bitcast_fusion.1
  23.0 1.9 convolution_bitcast_fusion.2
  25.9 4.8 %slice_bitcast_fusion = (bf16[512,2048]{1,0:T(8,128)(2,1)}, bf16[512,2048]{1,0:T(8,128)(2,1)}) fusion(bf16[1,1024,2048]{2,1,0:T(8,128)(2,1)} %param.9), kind=kLoop, calls=%fused_computation.1 | loop fusion | bytes 8388608 | tf_op jit(solution)/shard_map/slice | solution.py:187
  31.0 1.7 collective-permute-start.2
  34.7 1.0 copy.66.w_ref
  35.8 10.8 %shard_map.77.rest_0_ = f32[512,2048]{1,0:T(8,128)} custom-call(s32[4]{0:T(128)} %and_select_fusion.src_left, s32[16]{0:T(128)} %copy-done, s32[4]{0:T(128)} %copy-done.3, s32[128]{0:T(128)} %copy-done.5, s32[1]{0:T(128)} %constant.81.clone.1.flag_ref, bf16[1024,2048]{1,0:T(8,128)(2,1)} %bitcast.181, f32[1024,1]{1,0:T(8,128)} %copy.66.w_ref, f32[16,128]{1,0:T(8,128)} %bitcast.187), custom_call_target="tpu_custom_call" | custom-call | tf_op jit(solution)/shard_map/pallas_call | solution.py:77
  47.9 1.1 copy.67.w_ref
  49.8 0.9 copy.69.w_ref
  50.6 8.3 %all-reduce.2.cloned.1.call-done = f32[3,128,128]{1,2,0:T(8,128)} async-done(((f32[3,128,128]{1,2,0:T(8,128)}), f32[3,128,128]{1,2,0:T(8,128)}) %all-reduce.2.cloned.1.call-update) | async-done | bytes 196624 | tf_op jit(solution)/shard_map/psum | solution.py:145
  59.0 1.0 slice_bitcast_fusion.9
  60.2 3.6 %collective-permute-start.8 = (f32[3,128,128]{2,1,0:T(8,128)S(1)}, f32[3,128,128]{2,1,0:T(8,128)S(1)}, u32[]{:S(2)}, u32[]{:S(2)}) collective-permute-start(f32[3,128,128]{2,1,0:T(8,128)S(1)} %copy.75), channel_id=1, source_target_pairs={{0,4},{4,8},{8,12},{12,16},{16,20},{20,24},{24,28},{1,5},{5,9},{9,... | collective-permute-start | bytes 589832 | tf_op jit(solution)/shard_map/ppermute | solution.py:159
  63.8 0.9 copy.70.w_ref
  64.6 0.9 copy.71.w_ref
  65.7 1.0 collective-permute-done.8
  67.1 11.7 %cholesky.59 = f32[128,128]{1,0:T(8,128)S(1)} custom-call(f32[128,128]{1,0:T(8,128)S(1)} %copy.80), custom_call_target="Cholesky" | custom-call | tf_op jit(solution)/shard_map/jit(cholesky)/cholesky | solution.py:94
  80.1 9.8 %custom-call.9 = f32[1,128,128]{1,2,0:T(8,128)S(1)} custom-call(f32[1,128,128]{2,1,0:T(8,128)S(1)} %fusion.33), custom_call_target="InvertDiagBlocksLowerTriangular" | custom-call | tf_op jit(solution)/shard_map/jit(_cho_solve)/triangular_solve | solution.py:96
  91.4 5.5 %collective-permute-start.9 = (f32[3,128,128]{2,1,0:T(8,128)S(1)}, f32[3,128,128]{2,1,0:T(8,128)S(1)}, u32[]{:S(2)}, u32[]{:S(2)}) collective-permute-start(f32[3,128,128]{2,1,0:T(8,128)S(1)} %pad_maximum_fusion.2), channel_id=1, source_target_pairs={{0,8},{4,12},{8,16},{12,20},{16,24},{20,28},{1,9},{5,13},{9,17},{1... | collective-permute-start | bytes 589832 | tf_op jit(solution)/shard_map/ppermute | solution.py:159
  97.0 2.9 %collective-permute-done.9 = f32[3,128,128]{2,1,0:T(8,128)S(1)} collective-permute-done((f32[3,128,128]{2,1,0:T(8,128)S(1)}, f32[3,128,128]{2,1,0:T(8,128)S(1)}, u32[]{:S(2)}, u32[]{:S(2)}) %collective-permute-start.9) | collective-permute-done | bytes 196640 | tf_op jit(solution)/shard_map/ppermute | solution.py:159
  100.1 11.7 %cholesky.70 = f32[128,128]{1,0:T(8,128)S(1)} custom-call(f32[128,128]{1,0:T(8,128)S(1)} %fusion.65), custom_call_target="Cholesky" | custom-call | tf_op jit(solution)/shard_map/jit(cholesky)/cholesky | solution.py:94
  113.2 9.8 %custom-call.10 = f32[1,128,128]{1,2,0:T(8,128)S(1)} custom-call(f32[1,128,128]{2,1,0:T(8,128)S(1)} %fusion.34), custom_call_target="InvertDiagBlocksLowerTriangular" | custom-call | tf_op jit(solution)/shard_map/jit(_cho_solve)/triangular_solve | solution.py:96
  124.4 5.6 %collective-permute-start.10 = (f32[3,128,128]{2,1,0:T(8,128)S(1)}, f32[3,128,128]{2,1,0:T(8,128)S(1)}, u32[]{:S(2)}, u32[]{:S(2)}) collective-permute-start(f32[3,128,128]{2,1,0:T(8,128)S(1)} %pad_maximum_fusion.3), channel_id=1, source_target_pairs={{0,16},{4,20},{8,24},{12,28},{1,17},{5,21},{9,25},{13,29},{2,18},{... | collective-permute-start | bytes 589832 | tf_op jit(solution)/shard_map/ppermute | solution.py:159
  130.7 2.3 %collective-permute-done.10 = f32[3,128,128]{2,1,0:T(8,128)S(1)} collective-permute-done((f32[3,128,128]{2,1,0:T(8,128)S(1)}, f32[3,128,128]{2,1,0:T(8,128)S(1)}, u32[]{:S(2)}, u32[]{:S(2)}) %collective-permute-start.10) | collective-permute-done | bytes 196640 | tf_op jit(solution)/shard_map/ppermute | solution.py:159
  133.9 11.7 %cholesky.81 = f32[128,128]{1,0:T(8,128)S(1)} custom-call(f32[128,128]{1,0:T(8,128)S(1)} %fusion.55), custom_call_target="Cholesky" | custom-call | tf_op jit(solution)/shard_map/jit(cholesky)/cholesky | solution.py:94
  147.0 9.8 %custom-call.11 = f32[1,128,128]{1,2,0:T(8,128)S(1)} custom-call(f32[1,128,128]{2,1,0:T(8,128)S(1)} %fusion.35), custom_call_target="InvertDiagBlocksLowerTriangular" | custom-call | tf_op jit(solution)/shard_map/jit(_cho_solve)/triangular_solve | solution.py:96
  158.9 11.8 %shard_map.78.rest_0_ = f32[512,2048]{1,0:T(8,128)} custom-call(s32[4]{0:T(128)} %and_select_fusion.src_left, s32[16]{0:T(128)} %copy-done, s32[4]{0:T(128)} %copy-done.3, s32[128]{0:T(128)} %slice_convert_fusion.mask_ref, s32[1]{0:T(128)} %constant.81.clone.1.flag_ref, ...), custom_call_target="tpu_custom_call", output_to_operand_aliasing={{}: (8, {})} | custom-call | tf_op jit(solution)/shard_map/pallas_call | solution.py:77
  170.7 9.5 %shard_map.79.rest_0_ = f32[512,2048]{1,0:T(8,128)} custom-call(s32[4]{0:T(128)} %and_select_fusion.src_left, s32[16]{0:T(128)} %copy-done, s32[4]{0:T(128)} %copy-done.3, s32[64]{0:T(128)} %get-tuple-element.24.mask_ref, s32[1]{0:T(128)} %constant.81.clone.1.flag_ref, ...), custom_call_target="tpu_custom_call", output_to_operand_aliasing={{}: (8, {})} | custom-call | tf_op jit(solution)/shard_map/pallas_call | solution.py:77
  180.2 9.4 %shard_map.80.rest_0_ = f32[512,2048]{1,0:T(8,128)} custom-call(s32[4]{0:T(128)} %and_select_fusion.src_left, s32[16]{0:T(128)} %copy-done, s32[4]{0:T(128)} %copy-done.3, s32[64]{0:T(128)} %get-tuple-element.25.mask_ref, s32[1]{0:T(128)} %constant.81.clone.1.flag_ref, bf16[512,2048]{1,0:T(8,128)(2,1)} %copy-done.1, ...), custom_call_target="tpu_custom_call", output_to_operand_aliasing={{}: (8, {})} | custom-call | tf_op jit(solution)/shard_map/pallas_call | solution.py:77
  189.6 9.5 %shard_map.81.rest_0_ = f32[512,2048]{1,0:T(8,128)} custom-call(s32[4]{0:T(128)} %and_select_fusion.src_left, s32[16]{0:T(128)} %copy-done, s32[4]{0:T(128)} %copy-done.3, s32[64]{0:T(128)} %get-tuple-element.26.mask_ref, s32[1]{0:T(128)} %constant.81.clone.1.flag_ref, ...), custom_call_target="tpu_custom_call", output_to_operand_aliasing={{}: (8, {})} | custom-call | tf_op jit(solution)/shard_map/pallas_call | solution.py:77
  199.1 9.5 %shard_map.82 = f32[512,2048]{1,0:T(8,128)} custom-call(s32[4]{0:T(128)} %and_select_fusion.src_left, s32[16]{0:T(128)} %copy-done, s32[4]{0:T(128)} %copy-done.3, s32[64]{0:T(128)} %get-tuple-element.27.mask_ref, s32[1]{0:T(128)} %constant.81.clone.1.flag_ref, bf16[512,2048]{1,0:T(8,128)(2,1)} %collective-permute-done.3.g_ref, ...), custom_call_target="tpu_custom_call", output_to_operand_aliasing={{}: (8, {})} | custom-call | tf_op jit(solution)/shard_map/pallas_call | solution.py:77
  (106 shorter events, 19.9 us)
Async XLA Ops:
  7.2 51.8 %all-reduce.2.cloned.1.call-start = ((), (), s32[]{:S(2)}) async-start(), calls=%async_computation | async-start | bytes 393216 | tf_op jit(solution)/shard_map/psum | solution.py:145
  8.0 22.8 %copy-start.5 = (s32[128]{0:T(128)}, s32[128]{0:T(128)S(1)}, u32[]{:S(2)}) copy-start(s32[128]{0:T(128)S(1)} %reshape_squeeze.6.mask_ref) | copy-start | bytes 1540
  8.7 37.9 %collective-permute-start.6 = (f32[1152]{0:T(1024)S(1)}, f32[1152]{0:T(1024)S(1)}, u32[]{:S(2)}, u32[]{:S(2)}) collective-permute-start(f32[1152]{0:T(1024)S(1)} %pad_maximum_fusion.4), channel_id=1, source_target_pairs={{0,1},{1,0},{2,3},{3,2},{4,5},{5,4},{6,7},{7,6},{8,9},{9,8},{10,11... | collective-permute-start | bytes 13832 | tf_op jit(solution)/shard_map/ppermute | solution.py:183
  9.1 37.5 %collective-permute-start = (f32[1152]{0:T(1024)S(1)}, f32[1152]{0:T(1024)S(1)}, u32[]{:S(2)}, u32[]{:S(2)}) collective-permute-start(f32[1152]{0:T(1024)S(1)} %pad_maximum_fusion.4), channel_id=1, source_target_pairs={{0,2},{1,3},{2,0},{3,1},{4,6},{5,7},{6,4},{7,5},{8,10},{9,11},{10,... | collective-permute-start | bytes 13832 | tf_op jit(solution)/shard_map/ppermute | solution.py:183
  12.4 21.1 %copy-start = (s32[16]{0:T(128)}, s32[16]{0:T(128)S(1)}, u32[]{:S(2)}) copy-start(s32[16]{0:T(128)S(1)} %select_reduce_fusion.3.src_right) | copy-start | bytes 196
  25.6 7.8 %copy-start.6 = (s32[16]{0:T(128)S(1)}, s32[16]{0:T(128)}, u32[]{:S(2)}) copy-start(s32[16]{0:T(128)} %param.13) | copy-start | bytes 196
  25.6 9.1 %copy-start.4 = (f32[1,1024]{1,0:T(1,128)S(1)}, f32[1,1024]{1,0:T(1,128)}, u32[]{:S(2)}) copy-start(f32[1,1024]{1,0:T(1,128)} %param.10) | copy-start | bytes 12292
  25.7 133.3 %collective-permute-start.7 = (bf16[1024,2048]{1,0:T(8,128)(2,1)}, bf16[1024,2048]{1,0:T(8,128)(2,1)}, u32[]{:S(2)}, u32[]{:S(2)}) collective-permute-start(bf16[1024,2048]{1,0:T(8,128)(2,1)} %bitcast.180), channel_id=1, source_target_pairs={{0,1},{1,0},{2,3},{3,2},{4,5},{5,4},{6,7},{7,6},{8,9},{9,8},{10,11... | collective-permute-start | bytes 12582920 | tf_op jit(solution)/shard_map/ppermute | solution.py:183
  30.7 102.3 %collective-permute-start.4 = (bf16[512,2048]{1,0:T(8,128)(2,1)}, bf16[512,2048]{1,0:T(8,128)(2,1)}, u32[]{:S(2)}, u32[]{:S(2)}) collective-permute-start(bf16[512,2048]{1,0:T(8,128)(2,1)} %get-tuple-element.8), channel_id=1, source_target_pairs={{0,2},{1,3},{2,0},{3,1},{4,6},{5,7},{6,4},{7,5},{8,10},{9,11},{10,... | collective-permute-start | bytes 6291464 | tf_op jit(solution)/shard_map/ppermute | solution.py:183
  31.0 102.2 %collective-permute-start.2 = (bf16[512,2048]{1,0:T(8,128)(2,1)}, bf16[512,2048]{1,0:T(8,128)(2,1)S(1)}, u32[]{:S(2)}, u32[]{:S(2)}) collective-permute-start(bf16[512,2048]{1,0:T(8,128)(2,1)} %get-tuple-element.9), channel_id=1, source_target_pairs={{0,2},{1,3},{2,0},{3,1},{4,6},{5,7},{6,4},{7,5},{8,10},{9,11},{10,... | collective-permute-start | bytes 6291464 | tf_op jit(solution)/shard_map/ppermute | solution.py:183
  33.5 2.3 %copy-start.3 = (s32[4]{0:T(128)}, s32[4]{0:T(128)S(1)}, u32[]{:S(2)}) copy-start(s32[4]{0:T(128)S(1)} %get-tuple-element.7.tile_ref) | copy-start | bytes 52
  50.6 13.1 %collective-permute-start.1 = (f32[1152]{0:T(1024)S(1)}, f32[1152]{0:T(1024)S(1)}, u32[]{:S(2)}, u32[]{:S(2)}) collective-permute-start(f32[1152]{0:T(1024)S(1)} %collective-permute-done), channel_id=1, source_target_pairs={{0,1},{1,0},{2,3},{3,2},{4,5},{5,4},{6,7},{7,6},{8,9},{9,8},{10,11... | collective-permute-start | bytes 13832 | tf_op jit(solution)/shard_map/ppermute | solution.py:183
  59.0 31.6 %copy-start.2 = (f32[3,128,128]{1,2,0:T(8,128)S(1)}, f32[3,128,128]{1,2,0:T(8,128)}, u32[]{:S(2)}) copy-start(f32[3,128,128]{1,2,0:T(8,128)} %all-reduce.2.cloned.1.call-done) | copy-start | bytes 589828
  60.2 6.6 %collective-permute-start.8 = (f32[3,128,128]{2,1,0:T(8,128)S(1)}, f32[3,128,128]{2,1,0:T(8,128)S(1)}, u32[]{:S(2)}, u32[]{:S(2)}) collective-permute-start(f32[3,128,128]{2,1,0:T(8,128)S(1)} %copy.75), channel_id=1, source_target_pairs={{0,4},{4,8},{8,12},{12,16},{16,20},{20,24},{24,28},{1,5},{5,9},{9,... | collective-permute-start | bytes 589832 | tf_op jit(solution)/shard_map/ppermute | solution.py:159
  91.4 8.5 %collective-permute-start.9 = (f32[3,128,128]{2,1,0:T(8,128)S(1)}, f32[3,128,128]{2,1,0:T(8,128)S(1)}, u32[]{:S(2)}, u32[]{:S(2)}) collective-permute-start(f32[3,128,128]{2,1,0:T(8,128)S(1)} %pad_maximum_fusion.2), channel_id=1, source_target_pairs={{0,8},{4,12},{8,16},{12,20},{16,24},{20,28},{1,9},{5,13},{9,17},{1... | collective-permute-start | bytes 589832 | tf_op jit(solution)/shard_map/ppermute | solution.py:159
  124.4 8.5 %collective-permute-start.10 = (f32[3,128,128]{2,1,0:T(8,128)S(1)}, f32[3,128,128]{2,1,0:T(8,128)S(1)}, u32[]{:S(2)}, u32[]{:S(2)}) collective-permute-start(f32[3,128,128]{2,1,0:T(8,128)S(1)} %pad_maximum_fusion.3), channel_id=1, source_target_pairs={{0,16},{4,20},{8,24},{12,28},{1,17},{5,21},{9,25},{13,29},{2,18},{... | collective-permute-start | bytes 589832 | tf_op jit(solution)/shard_map/ppermute | solution.py:159
  133.1 56.5 %collective-permute-start.5 = (bf16[512,2048]{1,0:T(8,128)(2,1)}, bf16[512,2048]{1,0:T(8,128)(2,1)}, u32[]{:S(2)}, u32[]{:S(2)}) collective-permute-start(bf16[512,2048]{1,0:T(8,128)(2,1)} %collective-permute-done.4.g_ref), channel_id=1, source_target_pairs={{0,1},{1,0},{2,3},{3,2},{4,5},{5,4},{6,7},{7,6},{8,9},{9,8},{10,11... | collective-permute-start | bytes 6291464 | tf_op jit(solution)/shard_map/ppermute | solution.py:183
  133.2 37.5 %copy-start.1 = (bf16[512,2048]{1,0:T(8,128)(2,1)}, bf16[512,2048]{1,0:T(8,128)(2,1)S(1)}, u32[]{:S(2)}) copy-start(bf16[512,2048]{1,0:T(8,128)(2,1)S(1)} %collective-permute-done.2.g_ref) | copy-start | bytes 6291460
  133.2 65.9 %collective-permute-start.3 = (bf16[512,2048]{1,0:T(8,128)(2,1)S(1)}, bf16[512,2048]{1,0:T(8,128)(2,1)}, u32[]{:S(2)}, u32[]{:S(2)}) collective-permute-start(bf16[512,2048]{1,0:T(8,128)(2,1)S(1)} %collective-permute-done.2.g_ref), channel_id=1, source_target_pairs={{0,1},{1,0},{2,3},{3,2},{4,5},{5,4},{6,7},{7,6},{8,9},{9,8},{10,11... | collective-permute-start | bytes 6291464 | tf_op jit(solution)/shard_map/ppermute | solution.py:183
Sparse Core Ops, SparseCore 0:
  25.7 33.1 all-reduce.1

commit v5 on v2

--- a/solution.py
+++ b/solution.py
@@ -44,7 +44,7 @@
     out_ref[:, pl.ds(e0, BLK)] += jnp.where(rows == cols, dvals, 0.0)
 
 
-def gram_rows(slab, weights, live_blocks, src_left, src_right, tile_order, diagonal, flag):
+def gram_rows(slab, weights, live_blocks, src_left, src_right, tile_order, diagonal, flag, group):
     height = slab.shape[0]
     col_blocks = L // BLK
     grid_spec = pltpu.PrefetchScalarGridSpec(
@@ -55,13 +55,13 @@
             pl.BlockSpec((height, 1), lambda k, *_: (0, 0)),
             pl.BlockSpec((col_blocks, BLK), lambda k, *_: (0, 0)),
         ],
-        out_specs=pl.BlockSpec((BLK, L), lambda k, *_: (k, 0)),
+        out_specs=pl.BlockSpec((None, BLK, L), lambda k, *_: (k // group, k % group, 0)),
         scratch_shapes=[pltpu.VMEM((height, L), jnp.bfloat16), pltpu.VMEM((BLK, height), jnp.bfloat16)],
     )
     return pl.pallas_call(
         gram_kernel,
         grid_spec=grid_spec,
-        out_shape=jax.ShapeDtypeStruct((L, L), jnp.float32),
+        out_shape=jax.ShapeDtypeStruct((col_blocks // group, group * BLK, L), jnp.float32),
         compiler_params=pltpu.CompilerParams(vmem_limit_bytes=56 * 1024 * 1024),
     )(src_left, src_right, tile_order, live_blocks.reshape(-1), flag.reshape(1),
       slab, weights.reshape(height, 1), diagonal.reshape(col_blocks, BLK))
@@ -77,14 +77,14 @@
     middle = 0.5 * (middle + middle.T)
     factor = jnp.linalg.cholesky(middle)
     half_width = top_one.shape[0]
-    solved = jax.scipy.linalg.cho_solve(
-        (factor, True), jnp.concatenate([cross_one.T, cross_two], axis=1)
+    solved = lax.linalg.triangular_solve(
+        factor, jnp.concatenate([cross_one.T, cross_two], axis=1), left_side=True, lower=True
     )
     solve_one = solved[:, :half_width]
     solve_two = solved[:, half_width:]
-    top_new = top_one - jnp.dot(cross_one, solve_one, precision=HIGHEST)
-    cross_new = -jnp.dot(cross_one, solve_two, precision=HIGHEST)
-    bottom_new = bottom_two - jnp.dot(cross_two.T, solve_two, precision=HIGHEST)
+    top_new = top_one - jnp.dot(solve_one.T, solve_one, precision=HIGHEST)
+    cross_new = -jnp.dot(solve_one.T, solve_two, precision=HIGHEST)
+    bottom_new = bottom_two - jnp.dot(solve_two.T, solve_two, precision=HIGHEST)
     return (top_new, cross_new, bottom_new)
 
 
@@ -149,11 +149,30 @@
     chain_out = jnp.stack(running)[None]
 
     flag = (my_index == 0).astype(jnp.int32)
+    owners = lax.axis_size("row")
+    own_blocks = block_count // owners
+    if owners == 4:
+        order = jnp.concatenate(
+            [lax.dynamic_slice_in_dim(tile_order, (my_index ^ q) * own_blocks, own_blocks) for q in range(owners)]
+        )
+    else:
+        order = tile_order
     partial = gram_rows(
-        local_slab, row_weights, live_blocks, jnp.take(source, tile_order), source,
-        tile_order, diagonal, flag,
+        local_slab, row_weights, live_blocks, jnp.take(source, order), source,
+        order, diagonal, flag, own_blocks,
     )
-    owned = lax.psum_scatter(partial, "row", scatter_dimension=0, tiled=True)
+    if owners == 4:
+        def exchange(value, step):
+            return lax.ppermute(value, "row", [(src, src ^ step) for src in range(owners)])
+
+        from_partner = exchange(partial[1], 1)
+        for_across = exchange(partial[3], 1)
+        from_across = exchange(partial[2] + for_across, 2)
+        owned = partial[0] + from_partner + from_across
+    else:
+        owned = lax.psum_scatter(
+            partial.reshape(L, L), "row", scatter_dimension=0, tiled=True
+        )
     return (owned[None], chain_out)
 
 

time: 193 us -> 256 us (1.33)
  waiting for transfers between devices: 46 us -> 85.8 us
  other arithmetic: 74.1 us -> 87.7 us
  local copies, waits for them, and re-layouts: 4.98 us -> 15.2 us
    ppermute x0 -> x3, waiting for transfers between devices: none -> 43.4 us  [exchange(): lax.ppermute(value, 'row', [(src, src ^ step) for src in range(owners)])]
    reduce_scatter x1 -> x0, waiting for transfers between devices: 28.7 us -> none  [local(): owned = lax.psum_scatter(partial, 'row', scatter_dimension=0, tiled=True)]
    psum x1, waiting for transfers between devices: 8.45 us -> 33.6 us  [local(): summed = lax.psum(part_pieces, 'row')]
    broadcast_in_dim x0 -> x1, other arithmetic: none -> 8.39 us  [local(): return (owned[None], chain_out)]
    squeeze x0 -> x1, local copies, waits for them, and re-layouts: none -> 7.94 us  [local(): from_partner = exchange(partial[1], 1)]
    add x0 -> x1, other arithmetic: none -> 6.52 us  [local(): from_across = exchange(partial[2] + for_across, 2)]
  transfers between devices with their start and end apart: 5 -> 7, of which waited for: 5 -> 5; matrix products, arithmetic and copies ran while one was open for 42% -> 35% of each run, Pallas kernels for 11% -> 0%
where the time goes in v5:
time: 256 us
  other arithmetic  87.7 us (34%)
  waiting for transfers between devices  85.8 us (34%)
  Pallas kernels  21.8 us (9%)
  between operations  19.6 us (8%)
  starting transfers between devices  15.7 us (6%)
  local copies, waits for them, and re-layouts  15.2 us (6%)
  matrix products  10.1 us (4%)
    ppermute x3, waiting for transfers between devices, exchange(): lax.ppermute(value, 'row', [(src, src ^ step) for src in range(owners)])  43.4 us
    another operation x9, other arithmetic, join_segments(): factor = jnp.linalg.cholesky(middle)  37.2 us
    psum x1, waiting for transfers between devices, local(): summed = lax.psum(part_pieces, 'row')  33.6 us
    another operation x6, other arithmetic, join_segments(): lax.linalg.triangular_solve(factor, jnp.concatenate([cross_one.T, cross_t...  31.4 us
    pallas_call x1, Pallas kernels, gram_rows(): pl.pallas_call(gram_kernel, grid_spec=grid_spec, out_shape=jax.ShapeDtype...  21.8 us
    ppermute x3, starting transfers between devices, local(): moved = lax.ppermute(jnp.stack(running), 'tm', pairs)  14.4 us
    ppermute x3, waiting for transfers between devices, local(): moved = lax.ppermute(jnp.stack(running), 'tm', pairs)  8.82 us
    broadcast_in_dim x1, other arithmetic, local(): return (owned[None], chain_out)  8.39 us
  transfers between devices with their start and end apart: 7, of which 5 were waited for; matrix products, arithmetic and copies ran while one was open for 35% of the time, Pallas kernels for 0%

profile of v5, /device:TPU:0, one launch (start us, length us, event | category | flops | bytes accessed | tf_op | source)
XLA Modules:
  0.0 255.9 jit_solution(5399410404324957416)
XLA Ops:
  7.2 0.8 select_reduce_fusion.3.src_right
  8.0 0.9 fusion.93
  10.3 1.4 reshape_squeeze.9.mask_ref
  11.6 1.7 copy.56.w_ref
  13.3 21.8 %shard_map.80 = f32[4,512,2048]{2,1,0:T(8,128)} custom-call(s32[16]{0:T(128)} %get-tuple-element.6.src_left, s32[16]{0:T(128)} %copy-done, s32[16]{0:T(128)} %get-tuple-element.7.tile_ref, s32[128]{0:T(128)} %reshape_squeeze.9.mask_ref, s32[1]{0:T(128)} %bitcast.6.flag_ref, bf16[1024,2048]{1,0:T(8,128)(2,1)} %bitcast.163, f32[1024,1]{1,0:T(8,128)} %copy.56.w_ref, ...), custom_call_target="tpu_custom_call" | custom-call | tf_op jit(solution)/shard_map/pallas_call | solution.py:61
  35.2 7.9 %slice_bitcast_fusion.2 = (f32[512,2048]{1,0:T(8,128)}, f32[512,2048]{1,0:T(8,128)}) fusion(f32[4,512,2048]{2,1,0:T(8,128)} %shard_map.80), kind=kLoop, calls=%fused_computation.4 | loop fusion | bytes 16777216 | tf_op jit(solution)/shard_map/squeeze | solution.py:168
  49.5 2.0 convolution_bitcast_fusion
  51.5 1.9 convolution_bitcast_fusion.1
  53.4 1.9 convolution_bitcast_fusion.2
  55.2 0.7 pad_maximum_fusion
  55.9 0.7 slice_bitcast_fusion.16
  56.6 33.6 %all-reduce.2.cloned.1.call-done = f32[3,128,128]{1,2,0:T(8,128)} async-done(((f32[3,128,128]{1,2,0:T(8,128)}), f32[3,128,128]{1,2,0:T(8,128)}) %all-reduce.2.cloned.1.call-update) | async-done | bytes 196624 | tf_op jit(solution)/shard_map/psum | solution.py:129
  90.2 1.0 slice_bitcast_fusion.14
  91.4 3.4 %collective-permute-start.3 = (f32[3,128,128]{2,1,0:T(8,128)S(1)}, f32[3,128,128]{2,1,0:T(8,128)S(1)}, u32[]{:S(2)}, u32[]{:S(2)}) collective-permute-start(f32[3,128,128]{2,1,0:T(8,128)S(1)} %copy.60), channel_id=1, source_target_pairs={{0,4},{4,8},{8,12},{12,16},{16,20},{20,24},{24,28},{1,5},{5,9},{9,... | collective-permute-start | bytes 589832 | tf_op jit(solution)/shard_map/ppermute | solution.py:143
  95.0 3.0 %collective-permute-done.3 = f32[3,128,128]{2,1,0:T(8,128)S(1)} collective-permute-done((f32[3,128,128]{2,1,0:T(8,128)S(1)}, f32[3,128,128]{2,1,0:T(8,128)S(1)}, u32[]{:S(2)}, u32[]{:S(2)}) %collective-permute-start.3) | collective-permute-done | bytes 196640 | tf_op jit(solution)/shard_map/ppermute | solution.py:143
  98.3 11.7 %cholesky.59 = f32[128,128]{1,0:T(8,128)S(1)} custom-call(f32[128,128]{1,0:T(8,128)S(1)} %copy.65), custom_call_target="Cholesky" | custom-call | tf_op jit(solution)/shard_map/jit(cholesky)/cholesky | solution.py:78
  110.7 0.7 fusion.37
  111.3 9.8 %custom-call.7 = f32[1,128,128]{1,2,0:T(8,128)S(1)} custom-call(f32[1,128,128]{2,1,0:T(8,128)S(1)} %fusion.37), custom_call_target="InvertDiagBlocksLowerTriangular" | custom-call | tf_op jit(solution)/shard_map/triangular_solve/custom-call.0 | solution.py:80
  121.5 1.1 fusion.11
  123.3 5.5 %collective-permute-start.4 = (f32[3,128,128]{2,1,0:T(8,128)S(1)}, f32[3,128,128]{2,1,0:T(8,128)S(1)}, u32[]{:S(2)}, u32[]{:S(2)}) collective-permute-start(f32[3,128,128]{2,1,0:T(8,128)S(1)} %pad_maximum_fusion.2), channel_id=1, source_target_pairs={{0,8},{4,12},{8,16},{12,20},{16,24},{20,28},{1,9},{5,13},{9,17},{1... | collective-permute-start | bytes 589832 | tf_op jit(solution)/shard_map/ppermute | solution.py:143
  128.9 2.9 %collective-permute-done.4 = f32[3,128,128]{2,1,0:T(8,128)S(1)} collective-permute-done((f32[3,128,128]{2,1,0:T(8,128)S(1)}, f32[3,128,128]{2,1,0:T(8,128)S(1)}, u32[]{:S(2)}, u32[]{:S(2)}) %collective-permute-start.4) | collective-permute-done | bytes 196640 | tf_op jit(solution)/shard_map/ppermute | solution.py:143
  132.0 11.7 %cholesky.70 = f32[128,128]{1,0:T(8,128)S(1)} custom-call(f32[128,128]{1,0:T(8,128)S(1)} %fusion.53), custom_call_target="Cholesky" | custom-call | tf_op jit(solution)/shard_map/jit(cholesky)/cholesky | solution.py:78
  143.8 6.5 %fusion = f32[512,2048]{1,0:T(8,128)} fusion(f32[512,2048]{1,0:T(8,128)} %collective-permute-done.1, f32[4,512,2048]{2,1,0:T(8,128)} %shard_map.80), kind=kLoop, calls=%fused_computation.3 | loop fusion | flops 1048576 | bytes 12582912 | tf_op jit(solution)/shard_map/add | solution.py:170
  150.3 0.7 collective-permute-start.2
  152.4 9.8 %custom-call.8 = f32[1,128,128]{1,2,0:T(8,128)S(1)} custom-call(f32[1,128,128]{2,1,0:T(8,128)S(1)} %fusion.38), custom_call_target="InvertDiagBlocksLowerTriangular" | custom-call | tf_op jit(solution)/shard_map/triangular_solve/custom-call.0 | solution.py:80
  163.5 5.5 %collective-permute-start.5 = (f32[3,128,128]{2,1,0:T(8,128)S(1)}, f32[3,128,128]{2,1,0:T(8,128)S(1)}, u32[]{:S(2)}, u32[]{:S(2)}) collective-permute-start(f32[3,128,128]{2,1,0:T(8,128)S(1)} %pad_maximum_fusion.3), channel_id=1, source_target_pairs={{0,16},{4,20},{8,24},{12,28},{1,17},{5,21},{9,25},{13,29},{2,18},{... | collective-permute-start | bytes 589832 | tf_op jit(solution)/shard_map/ppermute | solution.py:143
  169.1 3.0 %collective-permute-done.5 = f32[3,128,128]{2,1,0:T(8,128)S(1)} collective-permute-done((f32[3,128,128]{2,1,0:T(8,128)S(1)}, f32[3,128,128]{2,1,0:T(8,128)S(1)}, u32[]{:S(2)}, u32[]{:S(2)}) %collective-permute-start.5) | collective-permute-done | bytes 196640 | tf_op jit(solution)/shard_map/ppermute | solution.py:143
  172.4 11.7 %cholesky.81 = f32[128,128]{1,0:T(8,128)S(1)} custom-call(f32[128,128]{1,0:T(8,128)S(1)} %fusion.51), custom_call_target="Cholesky" | custom-call | tf_op jit(solution)/shard_map/jit(cholesky)/cholesky | solution.py:78
  185.4 9.8 %custom-call.9 = f32[1,128,128]{1,2,0:T(8,128)S(1)} custom-call(f32[1,128,128]{2,1,0:T(8,128)S(1)} %fusion.39), custom_call_target="InvertDiagBlocksLowerTriangular" | custom-call | tf_op jit(solution)/shard_map/triangular_solve/custom-call.0 | solution.py:80
  196.6 0.7 maximum_bitcast_fusion
  197.3 43.4 %collective-permute-done.2 = f32[512,2048]{1,0:T(8,128)} collective-permute-done((f32[512,2048]{1,0:T(8,128)}, f32[512,2048]{1,0:T(8,128)}, u32[]{:S(2)}, u32[]{:S(2)}) %collective-permute-start.2) | collective-permute-done | bytes 4194336 | tf_op jit(solution)/shard_map/ppermute | solution.py:166
  240.7 8.4 %fusion.3 = f32[1,512,2048]{2,1,0:T(8,128)} fusion(f32[512,2048]{1,0:T(8,128)} %collective-permute-done.2, f32[512,2048]{1,0:T(8,128)} %collective-permute-done, f32[4,512,2048]{2,1,0:T(8,128)} %shard_map.80), kind=kLoop, calls=%fused_computation.8 | loop fusion | flops 2097152 | bytes 16777216 | tf_op jit(solution)/shard_map/broadcast_in_dim | solution.py:176
  (70 shorter events, 10.8 us)
Async XLA Ops:
  7.2 83.0 %all-reduce.2.cloned.1.call-start = ((), (), s32[]{:S(2)}) async-start(), calls=%async_computation | async-start | bytes 393216 | tf_op jit(solution)/shard_map/psum | solution.py:129
  8.0 5.3 %copy-start = (s32[16]{0:T(128)}, s32[16]{0:T(128)S(1)}, u32[]{:S(2)}) copy-start(s32[16]{0:T(128)S(1)} %select_reduce_fusion.3.src_right) | copy-start | bytes 196
  35.2 8.4 %copy-start.1 = (s32[16]{0:T(128)S(1)}, s32[16]{0:T(128)}, u32[]{:S(2)}) copy-start(s32[16]{0:T(128)} %copy-done) | copy-start | bytes 196
  35.2 14.1 %copy-start.2 = (s32[1,8,16]{2,1,0:T(8,128)S(1)}, s32[1,8,16]{2,1,0:T(8,128)}, u32[]{:S(2)}) copy-start(s32[1,8,16]{2,1,0:T(8,128)} %param.11) | copy-start | bytes 1540
  35.2 14.4 %copy-start.3 = (f32[1,1024]{1,0:T(1,128)S(1)}, f32[1,1024]{1,0:T(1,128)}, u32[]{:S(2)}) copy-start(f32[1,1024]{1,0:T(1,128)} %param.10) | copy-start | bytes 12292
  43.1 100.6 %collective-permute-start.1 = (f32[512,2048]{1,0:T(8,128)}, f32[512,2048]{1,0:T(8,128)}, u32[]{:S(2)}, u32[]{:S(2)}) collective-permute-start(f32[512,2048]{1,0:T(8,128)} %get-tuple-element.9), channel_id=1, source_target_pairs={{0,1},{1,0},{2,3},{3,2},{4,5},{5,4},{6,7},{7,6},{8,9},{9,8},{10,11... | collective-permute-start | bytes 12582920 | tf_op jit(solution)/shard_map/ppermute | solution.py:166
  91.4 6.6 %collective-permute-start.3 = (f32[3,128,128]{2,1,0:T(8,128)S(1)}, f32[3,128,128]{2,1,0:T(8,128)S(1)}, u32[]{:S(2)}, u32[]{:S(2)}) collective-permute-start(f32[3,128,128]{2,1,0:T(8,128)S(1)} %copy.60), channel_id=1, source_target_pairs={{0,4},{4,8},{8,12},{12,16},{16,20},{20,24},{24,28},{1,5},{5,9},{9,... | collective-permute-start | bytes 589832 | tf_op jit(solution)/shard_map/ppermute | solution.py:143
  123.3 8.5 %collective-permute-start.4 = (f32[3,128,128]{2,1,0:T(8,128)S(1)}, f32[3,128,128]{2,1,0:T(8,128)S(1)}, u32[]{:S(2)}, u32[]{:S(2)}) collective-permute-start(f32[3,128,128]{2,1,0:T(8,128)S(1)} %pad_maximum_fusion.2), channel_id=1, source_target_pairs={{0,8},{4,12},{8,16},{12,20},{16,24},{20,28},{1,9},{5,13},{9,17},{1... | collective-permute-start | bytes 589832 | tf_op jit(solution)/shard_map/ppermute | solution.py:143
  128.8 68.5 %collective-permute-start = (f32[512,2048]{1,0:T(8,128)}, f32[512,2048]{1,0:T(8,128)}, u32[]{:S(2)}, u32[]{:S(2)}) collective-permute-start(f32[512,2048]{1,0:T(8,128)} %get-tuple-element.8), channel_id=1, source_target_pairs={{0,1},{1,0},{2,3},{3,2},{4,5},{5,4},{6,7},{7,6},{8,9},{9,8},{10,11... | collective-permute-start | bytes 12582920 | tf_op jit(solution)/shard_map/ppermute | solution.py:166
  150.3 90.4 %collective-permute-start.2 = (f32[512,2048]{1,0:T(8,128)}, f32[512,2048]{1,0:T(8,128)}, u32[]{:S(2)}, u32[]{:S(2)}) collective-permute-start(f32[512,2048]{1,0:T(8,128)} %fusion), channel_id=1, source_target_pairs={{0,2},{1,3},{2,0},{3,1},{4,6},{5,7},{6,4},{7,5},{8,10},{9,11},{10,... | collective-permute-start | bytes 12582920 | tf_op jit(solution)/shard_map/ppermute | solution.py:166
  163.5 8.5 %collective-permute-start.5 = (f32[3,128,128]{2,1,0:T(8,128)S(1)}, f32[3,128,128]{2,1,0:T(8,128)S(1)}, u32[]{:S(2)}, u32[]{:S(2)}) collective-permute-start(f32[3,128,128]{2,1,0:T(8,128)S(1)} %pad_maximum_fusion.3), channel_id=1, source_target_pairs={{0,16},{4,20},{8,24},{12,28},{1,17},{5,21},{9,25},{13,29},{2,18},{... | collective-permute-start | bytes 589832 | tf_op jit(solution)/shard_map/ppermute | solution.py:143
Sparse Core Ops, SparseCore 0:
  56.1 34.0 all-reduce.1

commit v6 on v5

--- a/solution.py
+++ b/solution.py
@@ -126,17 +126,53 @@
             contract_rows(final_cols, final_scaled),
         ]
     )
-    summed = lax.psum(part_pieces, "row")
+    owners = lax.axis_size("row")
+    own_blocks = block_count // owners
+
+    def exchange(value, step):
+        return lax.ppermute(value, "row", [(src, src ^ step) for src in range(owners)])
+
+    kernel_slab, part_pieces = lax.optimization_barrier((local_slab, part_pieces))
+    if owners & (owners - 1) == 0:
+        summed = part_pieces
+        step = 1
+        while step < owners:
+            summed = summed + exchange(summed, step)
+            step *= 2
+    else:
+        summed = lax.psum(part_pieces, "row")
     eye = jnp.eye(BLK, dtype=jnp.float32)
-    segment = (
+    segment = jnp.stack([
         summed[0] + eye * diagonal[:BLK][None, :],
         summed[1],
         summed[2] + eye * diagonal[L - BLK :][None, :],
-    )
+    ])
+
+    flag = (my_index == 0).astype(jnp.int32)
+    if owners == 4:
+        order = jnp.concatenate(
+            [lax.dynamic_slice_in_dim(tile_order, (my_index ^ q) * own_blocks, own_blocks) for q in range(owners)]
+        )
+    else:
+        order = tile_order
+    partial = gram_rows(
+        kernel_slab, row_weights, live_blocks, jnp.take(source, order), source,
+        order, diagonal, flag, own_blocks,
+    )
+    if owners == 4:
+        for_across = exchange(partial[3], 1)
+        to_across = partial[2] + for_across
+        to_across, segment = lax.optimization_barrier((to_across, segment))
+        from_across = exchange(to_across, 2)
+        from_partner = exchange(partial[1], 1)
+    else:
+        owned = lax.psum_scatter(
+            partial.reshape(L, L), "row", scatter_dimension=0, tiled=True
+        )
 
     times = lax.axis_size("tm")
     position = lax.axis_index("tm")
-    running = segment
+    running = (segment[0], segment[1], segment[2])
     shift = 1
     while shift < times:
         pairs = [(src, src + shift) for src in range(times - shift)]
@@ -147,32 +183,8 @@
         running = tuple(jnp.where(take, new, old) for new, old in zip(joined, running))
         shift *= 2
     chain_out = jnp.stack(running)[None]
-
-    flag = (my_index == 0).astype(jnp.int32)
-    owners = lax.axis_size("row")
-    own_blocks = block_count // owners
     if owners == 4:
-        order = jnp.concatenate(
-            [lax.dynamic_slice_in_dim(tile_order, (my_index ^ q) * own_blocks, own_blocks) for q in range(owners)]
-        )
-    else:
-        order = tile_order
-    partial = gram_rows(
-        local_slab, row_weights, live_blocks, jnp.take(source, order), source,
-        order, diagonal, flag, own_blocks,
-    )
-    if owners == 4:
-        def exchange(value, step):
-            return lax.ppermute(value, "row", [(src, src ^ step) for src in range(owners)])
-
-        from_partner = exchange(partial[1], 1)
-        for_across = exchange(partial[3], 1)
-        from_across = exchange(partial[2] + for_across, 2)
         owned = partial[0] + from_partner + from_across
-    else:
-        owned = lax.psum_scatter(
-            partial.reshape(L, L), "row", scatter_dimension=0, tiled=True
-        )
     return (owned[None], chain_out)
 
 

time: 256 us -> 210 us (0.82)
  waiting for transfers between devices: 85.8 us -> 50.5 us
  between operations: 19.6 us -> 6.33 us
  starting transfers between devices: 15.7 us -> 20.3 us
    psum x1 -> x0, waiting for transfers between devices: 33.6 us -> none  [local(): summed = lax.psum(part_pieces, 'row')]
    ppermute x3 -> x5, starting transfers between devices: 1.22 us -> 5.16 us  [exchange(): lax.ppermute(value, 'row', [(src, src ^ step) for src in range(owners)])]
    ppermute x3 -> x5, waiting for transfers between devices: 43.4 us -> 42.8 us  [exchange(): lax.ppermute(value, 'row', [(src, src ^ step) for src in range(owners)])]
    add x1 -> x4, other arithmetic: 6.52 us -> 6.54 us  [the longest x1 6.48 us: local(): to_across = partial[2] + for_across]
  transfers between devices with their start and end apart: 7 -> 8, of which waited for: 5 -> 6; matrix products, arithmetic and copies ran while one was open for 35% -> 24% of each run, Pallas kernels for 0% -> 0%
where the time goes in v6:
time: 210 us
  other arithmetic  86.8 us (41%)
  waiting for transfers between devices  50.5 us (24%)
  Pallas kernels  21.8 us (10%)
  starting transfers between devices  20.3 us (10%)
  local copies, waits for them, and re-layouts  15.1 us (7%)
  matrix products  8.86 us (4%)
  between operations  6.33 us (3%)
    ppermute x5, waiting for transfers between devices, exchange(): lax.ppermute(value, 'row', [(src, src ^ step) for src in range(owners)])  42.8 us
    another operation x9, other arithmetic, join_segments(): factor = jnp.linalg.cholesky(middle)  37.2 us
    another operation x6, other arithmetic, join_segments(): lax.linalg.triangular_solve(factor, jnp.concatenate([cross_one.T, cross_t...  31.4 us
    pallas_call x1, Pallas kernels, gram_rows(): pl.pallas_call(gram_kernel, grid_spec=grid_spec, out_shape=jax.ShapeDtype...  21.8 us
    ppermute x3, starting transfers between devices, local(): moved = lax.ppermute(jnp.stack(running), 'tm', pairs)  15.1 us
    broadcast_in_dim x1, other arithmetic, local(): return (owned[None], chain_out)  8.39 us
    squeeze x1, local copies, waits for them, and re-layouts, local(): from_partner = exchange(partial[1], 1)  7.88 us
    ppermute x3, waiting for transfers between devices, local(): moved = lax.ppermute(jnp.stack(running), 'tm', pairs)  7.69 us
  transfers between devices with their start and end apart: 8, of which 6 were waited for; matrix products, arithmetic and copies ran while one was open for 24% of the time, Pallas kernels for 0%

profile of v6, /device:TPU:0, one launch (start us, length us, event | category | flops | bytes accessed | tf_op | source)
XLA Modules:
  0.0 209.7 jit_solution(3906033491326596761)
XLA Ops:
  0.6 0.8 select_reduce_fusion.3.src_right
  7.2 1.0 fusion.78
  8.2 1.8 convolution_bitcast_fusion.2
  10.0 1.8 convolution_bitcast_fusion.1
  11.8 1.8 convolution_bitcast_fusion
  13.6 1.3 reshape_squeeze.7.mask_ref
  14.9 0.9 fusion.88
  17.2 1.7 copy.52.w_ref
  18.9 21.8 %shard_map.80 = f32[4,512,2048]{2,1,0:T(8,128)} custom-call(s32[16]{0:T(128)} %get-tuple-element.14.src_left, s32[16]{0:T(128)} %copy-done, s32[16]{0:T(128)} %get-tuple-element.15.tile_ref, s32[128]{0:T(128)} %reshape_squeeze.7.mask_ref, s32[1]{0:T(128)} %bitcast.6.flag_ref, bf16[1024,2048]{1,0:T(8,128)(2,1)} %bitcast.162, f32[1024,1]{1,0:T(8,128)} %copy.52.w_ref, ...), custom_call_target="tpu_custom_call" | custom-call | tf_op jit(solution)/shard_map/pallas_call | solution.py:61
  40.7 7.9 %slice_bitcast_fusion.2 = (f32[512,2048]{1,0:T(8,128)}, f32[512,2048]{1,0:T(8,128)}) fusion(f32[4,512,2048]{2,1,0:T(8,128)} %shard_map.80), kind=kLoop, calls=%fused_computation.4 | loop fusion | bytes 16777216 | tf_op jit(solution)/shard_map/squeeze | solution.py:167
  49.1 6.0 %collective-permute-done.2 = f32[3,128,128]{2,1,0:T(8,128)S(1)} collective-permute-done((f32[3,128,128]{2,1,0:T(8,128)S(1)}, f32[3,128,128]{2,1,0:T(8,128)S(1)}, u32[]{:S(2)}, u32[]{:S(2)}) %collective-permute-start.2) | collective-permute-done | bytes 196640 | tf_op jit(solution)/shard_map/ppermute | solution.py:133
  55.1 3.0 %collective-permute-start.3 = (f32[3,128,128]{2,1,0:T(8,128)S(1)}, f32[3,128,128]{2,1,0:T(8,128)S(1)}, u32[]{:S(2)}, u32[]{:S(2)}) collective-permute-start(f32[3,128,128]{2,1,0:T(8,128)S(1)} %add.101), channel_id=1, source_target_pairs={{0,2},{1,3},{2,0},{3,1},{4,6},{5,7},{6,4},{7,5},{8,10},{9,11},{10,... | collective-permute-start | bytes 589832 | tf_op jit(solution)/shard_map/ppermute | solution.py:133
  58.1 0.7 slice_bitcast_fusion.16
  58.8 4.8 %collective-permute-done.3 = f32[3,128,128]{2,1,0:T(8,128)S(1)} collective-permute-done((f32[3,128,128]{2,1,0:T(8,128)S(1)}, f32[3,128,128]{2,1,0:T(8,128)S(1)}, u32[]{:S(2)}, u32[]{:S(2)}) %collective-permute-start.3) | collective-permute-done | bytes 196640 | tf_op jit(solution)/shard_map/ppermute | solution.py:133
  63.6 6.5 %fusion = f32[512,2048]{1,0:T(8,128)} fusion(f32[512,2048]{1,0:T(8,128)} %collective-permute-done.1, f32[4,512,2048]{2,1,0:T(8,128)} %shard_map.80), kind=kLoop, calls=%fused_computation.3 | loop fusion | flops 1048576 | bytes 12582912 | tf_op jit(solution)/shard_map/add | solution.py:164
  70.2 3.8 %collective-permute-start.5 = (f32[3,128,128]{1,2,0:T(8,128)S(1)}, f32[3,128,128]{1,2,0:T(8,128)S(1)}, u32[]{:S(2)}, u32[]{:S(2)}) collective-permute-start(f32[3,128,128]{1,2,0:T(8,128)S(1)} %copy.53), channel_id=1, source_target_pairs={{0,4},{4,8},{8,12},{12,16},{16,20},{20,24},{24,28},{1,5},{5,9},{9,... | collective-permute-start | bytes 589832 | tf_op jit(solution)/shard_map/ppermute | solution.py:179
  74.3 3.5 %collective-permute-done.5 = f32[3,128,128]{1,2,0:T(8,128)S(1)} collective-permute-done((f32[3,128,128]{1,2,0:T(8,128)S(1)}, f32[3,128,128]{1,2,0:T(8,128)S(1)}, u32[]{:S(2)}, u32[]{:S(2)}) %collective-permute-start.5) | collective-permute-done | bytes 196640 | tf_op jit(solution)/shard_map/ppermute | solution.py:179
  78.0 11.7 %cholesky.59 = f32[128,128]{1,0:T(8,128)S(1)} custom-call(f32[128,128]{1,0:T(8,128)S(1)} %fusion.55), custom_call_target="Cholesky" | custom-call | tf_op jit(solution)/shard_map/jit(cholesky)/cholesky | solution.py:78
  90.4 0.7 fusion.37
  91.0 9.8 %custom-call.7 = f32[1,128,128]{1,2,0:T(8,128)S(1)} custom-call(f32[1,128,128]{2,1,0:T(8,128)S(1)} %fusion.37), custom_call_target="InvertDiagBlocksLowerTriangular" | custom-call | tf_op jit(solution)/shard_map/triangular_solve/custom-call.0 | solution.py:80
  102.3 5.6 %collective-permute-start.6 = (f32[3,128,128]{2,1,0:T(8,128)S(1)}, f32[3,128,128]{2,1,0:T(8,128)S(1)}, u32[]{:S(2)}, u32[]{:S(2)}) collective-permute-start(f32[3,128,128]{2,1,0:T(8,128)S(1)} %pad_maximum_fusion.2), channel_id=1, source_target_pairs={{0,8},{4,12},{8,16},{12,20},{16,24},{20,28},{1,9},{5,13},{9,17},{1... | collective-permute-start | bytes 589832 | tf_op jit(solution)/shard_map/ppermute | solution.py:179
  108.0 1.6 collective-permute-start.4
  109.5 1.3 collective-permute-done.6
  111.1 11.7 %cholesky.70 = f32[128,128]{1,0:T(8,128)S(1)} custom-call(f32[128,128]{1,0:T(8,128)S(1)} %fusion.52), custom_call_target="Cholesky" | custom-call | tf_op jit(solution)/shard_map/jit(cholesky)/cholesky | solution.py:78
  124.1 9.8 %custom-call.8 = f32[1,128,128]{1,2,0:T(8,128)S(1)} custom-call(f32[1,128,128]{2,1,0:T(8,128)S(1)} %fusion.38), custom_call_target="InvertDiagBlocksLowerTriangular" | custom-call | tf_op jit(solution)/shard_map/triangular_solve/custom-call.0 | solution.py:80
  135.3 5.7 %collective-permute-start.7 = (f32[3,128,128]{2,1,0:T(8,128)S(1)}, f32[3,128,128]{2,1,0:T(8,128)S(1)}, u32[]{:S(2)}, u32[]{:S(2)}) collective-permute-start(f32[3,128,128]{2,1,0:T(8,128)S(1)} %pad_maximum_fusion.3), channel_id=1, source_target_pairs={{0,16},{4,20},{8,24},{12,28},{1,17},{5,21},{9,25},{13,29},{2,18},{... | collective-permute-start | bytes 589832 | tf_op jit(solution)/shard_map/ppermute | solution.py:179
  141.0 2.9 %collective-permute-done.7 = f32[3,128,128]{2,1,0:T(8,128)S(1)} collective-permute-done((f32[3,128,128]{2,1,0:T(8,128)S(1)}, f32[3,128,128]{2,1,0:T(8,128)S(1)}, u32[]{:S(2)}, u32[]{:S(2)}) %collective-permute-start.7) | collective-permute-done | bytes 196640 | tf_op jit(solution)/shard_map/ppermute | solution.py:179
  144.3 11.7 %cholesky.81 = f32[128,128]{1,0:T(8,128)S(1)} custom-call(f32[128,128]{1,0:T(8,128)S(1)} %fusion.50), custom_call_target="Cholesky" | custom-call | tf_op jit(solution)/shard_map/jit(cholesky)/cholesky | solution.py:78
  157.3 9.8 %custom-call.9 = f32[1,128,128]{1,2,0:T(8,128)S(1)} custom-call(f32[1,128,128]{2,1,0:T(8,128)S(1)} %fusion.39), custom_call_target="InvertDiagBlocksLowerTriangular" | custom-call | tf_op jit(solution)/shard_map/triangular_solve/custom-call.0 | solution.py:80
  168.5 0.7 maximum_bitcast_fusion
  169.2 32.1 %collective-permute-done.4 = f32[512,2048]{1,0:T(8,128)} collective-permute-done((f32[512,2048]{1,0:T(8,128)}, f32[512,2048]{1,0:T(8,128)}, u32[]{:S(2)}, u32[]{:S(2)}) %collective-permute-start.4) | collective-permute-done | bytes 4194336 | tf_op jit(solution)/shard_map/ppermute | solution.py:133
  201.3 8.4 %fusion.3 = f32[1,512,2048]{2,1,0:T(8,128)} fusion(f32[512,2048]{1,0:T(8,128)} %collective-permute-done.4, f32[512,2048]{1,0:T(8,128)} %collective-permute-done, f32[4,512,2048]{2,1,0:T(8,128)} %shard_map.80), kind=kLoop, calls=%fused_computation.8 | loop fusion | flops 2097152 | bytes 16777216 | tf_op jit(solution)/shard_map/broadcast_in_dim | solution.py:188
  (70 shorter events, 11.0 us)
Async XLA Ops:
  1.4 17.5 %copy-start = (s32[16]{0:T(128)}, s32[16]{0:T(128)S(1)}, u32[]{:S(2)}) copy-start(s32[16]{0:T(128)S(1)} %select_reduce_fusion.3.src_right) | copy-start | bytes 196
  48.6 15.0 %collective-permute-start.1 = (f32[512,2048]{1,0:T(8,128)}, f32[512,2048]{1,0:T(8,128)}, u32[]{:S(2)}, u32[]{:S(2)}) collective-permute-start(f32[512,2048]{1,0:T(8,128)} %get-tuple-element.17), channel_id=1, source_target_pairs={{0,1},{1,0},{2,3},{3,2},{4,5},{5,4},{6,7},{7,6},{8,9},{9,8},{10,11... | collective-permute-start | bytes 12582920 | tf_op jit(solution)/shard_map/ppermute | solution.py:133
  49.0 6.0 %collective-permute-start.2 = (f32[3,128,128]{2,1,0:T(8,128)S(1)}, f32[3,128,128]{2,1,0:T(8,128)S(1)}, u32[]{:S(2)}, u32[]{:S(2)}) collective-permute-start(f32[3,128,128]{2,1,0:T(8,128)S(1)} %pad_maximum_fusion), channel_id=1, source_target_pairs={{0,1},{1,0},{2,3},{3,2},{4,5},{5,4},{6,7},{7,6},{8,9},{9,8},{10,11... | collective-permute-start | bytes 589832 | tf_op jit(solution)/shard_map/ppermute | solution.py:133
  55.1 8.4 %collective-permute-start.3 = (f32[3,128,128]{2,1,0:T(8,128)S(1)}, f32[3,128,128]{2,1,0:T(8,128)S(1)}, u32[]{:S(2)}, u32[]{:S(2)}) collective-permute-start(f32[3,128,128]{2,1,0:T(8,128)S(1)} %add.101), channel_id=1, source_target_pairs={{0,2},{1,3},{2,0},{3,1},{4,6},{5,7},{6,4},{7,5},{8,10},{9,11},{10,... | collective-permute-start | bytes 589832 | tf_op jit(solution)/shard_map/ppermute | solution.py:133
  70.2 7.5 %collective-permute-start.5 = (f32[3,128,128]{1,2,0:T(8,128)S(1)}, f32[3,128,128]{1,2,0:T(8,128)S(1)}, u32[]{:S(2)}, u32[]{:S(2)}) collective-permute-start(f32[3,128,128]{1,2,0:T(8,128)S(1)} %copy.53), channel_id=1, source_target_pairs={{0,4},{4,8},{8,12},{12,16},{16,20},{20,24},{24,28},{1,5},{5,9},{9,... | collective-permute-start | bytes 589832 | tf_op jit(solution)/shard_map/ppermute | solution.py:179
  102.3 8.5 %collective-permute-start.6 = (f32[3,128,128]{2,1,0:T(8,128)S(1)}, f32[3,128,128]{2,1,0:T(8,128)S(1)}, u32[]{:S(2)}, u32[]{:S(2)}) collective-permute-start(f32[3,128,128]{2,1,0:T(8,128)S(1)} %pad_maximum_fusion.2), channel_id=1, source_target_pairs={{0,8},{4,12},{8,16},{12,20},{16,24},{20,28},{1,9},{5,13},{9,17},{1... | collective-permute-start | bytes 589832 | tf_op jit(solution)/shard_map/ppermute | solution.py:179
  107.9 61.2 %collective-permute-start = (f32[512,2048]{1,0:T(8,128)}, f32[512,2048]{1,0:T(8,128)}, u32[]{:S(2)}, u32[]{:S(2)}) collective-permute-start(f32[512,2048]{1,0:T(8,128)} %get-tuple-element.16), channel_id=1, source_target_pairs={{0,1},{1,0},{2,3},{3,2},{4,5},{5,4},{6,7},{7,6},{8,9},{9,8},{10,11... | collective-permute-start | bytes 12582920 | tf_op jit(solution)/shard_map/ppermute | solution.py:133
  108.0 93.3 %collective-permute-start.4 = (f32[512,2048]{1,0:T(8,128)}, f32[512,2048]{1,0:T(8,128)}, u32[]{:S(2)}, u32[]{:S(2)}) collective-permute-start(f32[512,2048]{1,0:T(8,128)} %fusion), channel_id=1, source_target_pairs={{0,2},{1,3},{2,0},{3,1},{4,6},{5,7},{6,4},{7,5},{8,10},{9,11},{10,... | collective-permute-start | bytes 12582920 | tf_op jit(solution)/shard_map/ppermute | solution.py:133
  135.3 8.6 %collective-permute-start.7 = (f32[3,128,128]{2,1,0:T(8,128)S(1)}, f32[3,128,128]{2,1,0:T(8,128)S(1)}, u32[]{:S(2)}, u32[]{:S(2)}) collective-permute-start(f32[3,128,128]{2,1,0:T(8,128)S(1)} %pad_maximum_fusion.3), channel_id=1, source_target_pairs={{0,16},{4,20},{8,24},{12,28},{1,17},{5,21},{9,25},{13,29},{2,18},{... | collective-permute-start | bytes 589832 | tf_op jit(solution)/shard_map/ppermute | solution.py:179

commit v7 on v6

--- a/solution.py
+++ b/solution.py
@@ -9,8 +9,12 @@
 BLK = 128
 
 
-def gram_kernel(src_left, src_right, tile_ref, mask_ref, flag_ref, g_ref, w_ref, diag_ref,
-                out_ref, s_ref, lt_ref):
+def gram_kernel(src_left, src_right, tile_ref, mask_ref, flag_ref, g_ref, w_ref, diag_ref, *rest):
+    if len(rest) == 4:
+        acc_ref, out_ref, s_ref, lt_ref = rest
+    else:
+        acc_ref = None
+        out_ref, s_ref, lt_ref = rest
     k = pl.program_id(0)
     row_blocks = g_ref.shape[0] // BLK
     col_blocks = g_ref.shape[1] // BLK
@@ -35,36 +39,49 @@
         live = mask_ref[rb * col_blocks + src].astype(jnp.float32)
         vals = g_ref[rb * BLK:(rb + 1) * BLK, pl.ds(c0, BLK)].astype(jnp.float32) * live
         lt_ref[:, rb * BLK:(rb + 1) * BLK] = vals.T.astype(jnp.bfloat16)
-    out_ref[...] = jnp.dot(lt_ref[...], s_ref[...], preferred_element_type=jnp.float32)
-    blk = tile_ref[k]
-    e0 = pl.multiple_of(blk * BLK, BLK)
-    rows = lax.broadcasted_iota(jnp.int32, (BLK, BLK), 0)
-    cols = lax.broadcasted_iota(jnp.int32, (BLK, BLK), 1)
-    dvals = diag_ref[pl.ds(blk, 1), :] * flag_ref[0].astype(jnp.float32)
-    out_ref[:, pl.ds(e0, BLK)] += jnp.where(rows == cols, dvals, 0.0)
-
-
-def gram_rows(slab, weights, live_blocks, src_left, src_right, tile_order, diagonal, flag, group):
+    term = jnp.dot(lt_ref[...], s_ref[...], preferred_element_type=jnp.float32)
+    if acc_ref is None:
+        out_ref[...] = term
+        blk = tile_ref[k]
+        e0 = pl.multiple_of(blk * BLK, BLK)
+        rows = lax.broadcasted_iota(jnp.int32, (BLK, BLK), 0)
+        cols = lax.broadcasted_iota(jnp.int32, (BLK, BLK), 1)
+        dvals = diag_ref[pl.ds(blk, 1), :] * flag_ref[k].astype(jnp.float32)
+        out_ref[:, pl.ds(e0, BLK)] += jnp.where(rows == cols, dvals, 0.0)
+    else:
+        out_ref[...] = acc_ref[...] + term
+
+
+def gram_rows(slab, weights, live_blocks, src_left, src_right, out_tiles, diagonal, flags, group, acc=None):
     height = slab.shape[0]
     col_blocks = L // BLK
+    out_blocks = src_left.shape[0]
+    in_specs = [
+        pl.BlockSpec((height, L), lambda k, *_: (0, 0)),
+        pl.BlockSpec((height, 1), lambda k, *_: (0, 0)),
+        pl.BlockSpec((col_blocks, BLK), lambda k, *_: (0, 0)),
+    ]
+    operands = [slab, weights.reshape(height, 1), diagonal.reshape(col_blocks, BLK)]
+    aliases = {}
+    out_spec = pl.BlockSpec((None, BLK, L), lambda k, *_: (k // group, k % group, 0))
+    if acc is not None:
+        in_specs.append(out_spec)
+        operands.append(acc)
+        aliases = {8: 0}
     grid_spec = pltpu.PrefetchScalarGridSpec(
         num_scalar_prefetch=5,
-        grid=(col_blocks,),
-        in_specs=[
-            pl.BlockSpec((height, L), lambda k, *_: (0, 0)),
-            pl.BlockSpec((height, 1), lambda k, *_: (0, 0)),
-            pl.BlockSpec((col_blocks, BLK), lambda k, *_: (0, 0)),
-        ],
-        out_specs=pl.BlockSpec((None, BLK, L), lambda k, *_: (k // group, k % group, 0)),
+        grid=(out_blocks,),
+        in_specs=in_specs,
+        out_specs=out_spec,
         scratch_shapes=[pltpu.VMEM((height, L), jnp.bfloat16), pltpu.VMEM((BLK, height), jnp.bfloat16)],
     )
     return pl.pallas_call(
         gram_kernel,
         grid_spec=grid_spec,
-        out_shape=jax.ShapeDtypeStruct((col_blocks // group, group * BLK, L), jnp.float32),
+        out_shape=jax.ShapeDtypeStruct((out_blocks // group, group * BLK, L), jnp.float32),
+        input_output_aliases=aliases,
         compiler_params=pltpu.CompilerParams(vmem_limit_bytes=56 * 1024 * 1024),
-    )(src_left, src_right, tile_order, live_blocks.reshape(-1), flag.reshape(1),
-      slab, weights.reshape(height, 1), diagonal.reshape(col_blocks, BLK))
+    )(src_left, src_right, out_tiles, live_blocks.reshape(-1), flags, *operands)
 
 
 HIGHEST = lax.Precision.HIGHEST
@@ -148,24 +165,31 @@
         summed[2] + eye * diagonal[L - BLK :][None, :],
     ])
 
-    flag = (my_index == 0).astype(jnp.int32)
     if owners == 4:
+        packed_side = jnp.concatenate([row_weights, live_blocks.reshape(-1).astype(jnp.float32)])
+        across_slab = exchange(local_slab, 2)
+        across_side = exchange(packed_side, 2)
+        across_weights = across_side[:slab_height]
+        across_live = across_side[slab_height:].reshape(live_blocks.shape).astype(jnp.int32)
         order = jnp.concatenate(
-            [lax.dynamic_slice_in_dim(tile_order, (my_index ^ q) * own_blocks, own_blocks) for q in range(owners)]
-        )
-    else:
-        order = tile_order
-    partial = gram_rows(
-        kernel_slab, row_weights, live_blocks, jnp.take(source, order), source,
-        order, diagonal, flag, own_blocks,
-    )
-    if owners == 4:
-        for_across = exchange(partial[3], 1)
-        to_across = partial[2] + for_across
-        to_across, segment = lax.optimization_barrier((to_across, segment))
-        from_across = exchange(to_across, 2)
-        from_partner = exchange(partial[1], 1)
-    else:
+            [lax.dynamic_slice_in_dim(tile_order, (my_index ^ q) * own_blocks, own_blocks) for q in range(2)]
+        )
+        flags = (jnp.arange(2 * own_blocks) < own_blocks).astype(jnp.int32)
+        left_src = jnp.take(source, order)
+        partial = gram_rows(
+            kernel_slab, row_weights, live_blocks, left_src, source, order, diagonal, flags, own_blocks,
+        )
+        partial = gram_rows(
+            across_slab, across_weights, across_live, left_src, source, order, diagonal, flags,
+            own_blocks, partial,
+        )
+        owned = partial[0] + exchange(partial[1], 1)
+    else:
+        flags = jnp.full((block_count,), (my_index == 0).astype(jnp.int32))
+        partial = gram_rows(
+            kernel_slab, row_weights, live_blocks, jnp.take(source, tile_order), source,
+            tile_order, diagonal, flags, own_blocks,
+        )
         owned = lax.psum_scatter(
             partial.reshape(L, L), "row", scatter_dimension=0, tiled=True
         )
@@ -183,8 +207,6 @@
         running = tuple(jnp.where(take, new, old) for new, old in zip(joined, running))
         shift *= 2
     chain_out = jnp.stack(running)[None]
-    if owners == 4:
-        owned = partial[0] + from_partner + from_across
     return (owned[None], chain_out)
 
 

time: 210 us -> 247 us (1.18); the launches traced: 210 us -> 243 us
  waiting for transfers between devices: 50.5 us -> 85.8 us
  Pallas kernels: 21.8 us -> 31.4 us
  other arithmetic: 86.8 us -> 80.6 us
  local copies, waits for them, and re-layouts: 15.1 us -> 11.6 us
  starting transfers between devices: 20.3 us -> 17.8 us
    ppermute x5, waiting for transfers between devices: 42.8 us -> 78.8 us  [exchange(): lax.ppermute(value, 'row', [(src, src ^ step) for src in range(owners)])]
    pallas_call x1 -> x2, Pallas kernels: 21.8 us -> 31.4 us  [gram_rows(): pl.pallas_call(gram_kernel, grid_spec=grid_spec, out_shape=jax.ShapeDtype...]
    add x2 -> x0, other arithmetic: 6.5 us -> none  [the longest x1 6.48 us: local(): to_across = partial[2] + for_across]
    squeeze x5 -> x3, local copies, waits for them, and re-layouts: 8.07 us -> 4.88 us  [the longest x1 4.7 us: local(): owned = partial[0] + exchange(partial[1], 1)]
  transfers between devices with their start and end apart: 8 -> 8, of which waited for: 6 -> 3; matrix products, arithmetic and copies ran while one was open for 24% -> 36% of each run, Pallas kernels for 0% -> 6%
where the time goes in v7:
time: 247 us; the launch traced here: 243 us
  waiting for transfers between devices  85.8 us (35%)
  other arithmetic  80.6 us (33%)
  Pallas kernels  31.4 us (13%)
  starting transfers between devices  17.8 us (7%)
  local copies, waits for them, and re-layouts  11.6 us (5%)
  matrix products  9.14 us (4%)
  between operations  6.31 us (3%)
    ppermute x5, waiting for transfers between devices, exchange(): lax.ppermute(value, 'row', [(src, src ^ step) for src in range(owners)])  78.8 us
    another operation x9, other arithmetic, join_segments(): factor = jnp.linalg.cholesky(middle)  37.2 us
    pallas_call x2, Pallas kernels, gram_rows(): pl.pallas_call(gram_kernel, grid_spec=grid_spec, out_shape=jax.ShapeDtype...  31.4 us
    another operation x6, other arithmetic, join_segments(): lax.linalg.triangular_solve(factor, jnp.concatenate([cross_one.T, cross_t...  31.4 us
    ppermute x3, starting transfers between devices, local(): moved = lax.ppermute(jnp.stack(running), 'tm', pairs)  12.7 us
    ppermute x3, waiting for transfers between devices, local(): moved = lax.ppermute(jnp.stack(running), 'tm', pairs)  7.01 us
    broadcast_in_dim x1, other arithmetic, local(): return (owned[None], chain_out)  6.57 us
    dot_general x3, matrix products, contract_rows(): lax.dot_general(left_cols, right_cols, (((0,), (0,)), ((), ())), preferre...  5.61 us
  transfers between devices with their start and end apart: 8, of which 3 were waited for; matrix products, arithmetic and copies ran while one was open for 36% of the time, Pallas kernels for 6%

profile of v7, /device:TPU:0, one launch (start us, length us, event | category | flops | bytes accessed | tf_op | source)
XLA Modules:
  0.0 242.7 jit_solution(12873312927415003187)
XLA Ops:
  0.6 0.8 reshape_squeeze.4.mask_ref
  1.4 0.7 pad_maximum_fusion.4
  2.1 3.0 %collective-permute-start = (f32[1152]{0:T(1024)S(1)}, f32[1152]{0:T(1024)S(1)}, u32[]{:S(2)}, u32[]{:S(2)}) collective-permute-start(f32[1152]{0:T(1024)S(1)} %pad_maximum_fusion.4), channel_id=1, source_target_pairs={{0,2},{1,3},{2,0},{3,1},{4,6},{5,7},{6,4},{7,5},{8,10},{9,11},{10,... | collective-permute-start | bytes 13832 | tf_op jit(solution)/shard_map/ppermute | solution.py:150
  5.1 0.8 select_reduce_fusion.3.src_right
  11.7 1.0 fusion.81
  12.7 1.9 convolution_bitcast_fusion
  14.6 1.9 convolution_bitcast_fusion.1
  16.5 1.9 convolution_bitcast_fusion.2
  18.5 0.8 fusion.91
  20.0 2.1 collective-permute-start.4
  22.1 0.7 slice_bitcast_fusion.14
  22.8 78.8 %collective-permute-done.4 = f32[3,128,128]{1,2,0:T(8,128)S(1)} collective-permute-done((f32[3,128,128]{1,2,0:T(8,128)S(1)}, f32[3,128,128]{1,2,0:T(8,128)S(1)}, u32[]{:S(2)}, u32[]{:S(2)}) %collective-permute-start.4) | collective-permute-done | bytes 196640 | tf_op jit(solution)/shard_map/ppermute | solution.py:150
  101.8 3.4 %collective-permute-start.5 = (f32[3,128,128]{2,1,0:T(8,128)S(1)}, f32[3,128,128]{2,1,0:T(8,128)S(1)}, u32[]{:S(2)}, u32[]{:S(2)}) collective-permute-start(f32[3,128,128]{2,1,0:T(8,128)S(1)} %copy.63), channel_id=1, source_target_pairs={{0,4},{4,8},{8,12},{12,16},{16,20},{20,24},{24,28},{1,5},{5,9},{9,... | collective-permute-start | bytes 589832 | tf_op jit(solution)/shard_map/ppermute | solution.py:203
  106.4 1.0 copy.61.w_ref
  107.5 14.5 %shard_map.77.rest_0_ = f32[2,512,2048]{2,1,0:T(8,128)} custom-call(s32[8]{0:T(128)} %get-tuple-element.10.src_left, s32[16]{0:T(128)} %copy-done, s32[8]{0:T(128)} %get-tuple-element.11.tile_ref, s32[128]{0:T(128)} %copy-done.2, s32[8]{0:T(128)} %compare_convert_fusion.flag_ref, bf16[1024,2048]{1,0:T(8,128)(2,1)} %bitcast.154, f32[1024,1]{1,0:T(8,128)} %copy.61.w_ref, ...), custom_call_target="tpu_custom_call" | custom-call | tf_op jit(solution)/shard_map/pallas_call | solution.py:78
  122.0 1.0 copy.62.w_ref
  123.6 11.7 %cholesky.59 = f32[128,128]{1,0:T(8,128)S(1)} custom-call(f32[128,128]{1,0:T(8,128)S(1)} %copy.68), custom_call_target="Cholesky" | custom-call | tf_op jit(solution)/shard_map/jit(cholesky)/cholesky | solution.py:95
  135.4 0.7 compare_reduce_fusion.2
  136.1 0.7 fusion.35
  136.8 9.8 %custom-call.7 = f32[1,128,128]{1,2,0:T(8,128)S(1)} custom-call(f32[1,128,128]{2,1,0:T(8,128)S(1)} %fusion.35), custom_call_target="InvertDiagBlocksLowerTriangular" | custom-call | tf_op jit(solution)/shard_map/triangular_solve/custom-call.0 | solution.py:97
  147.9 3.6 %collective-permute-start.6 = (f32[3,128,128]{2,1,0:T(8,128)S(1)}, f32[3,128,128]{2,1,0:T(8,128)S(1)}, u32[]{:S(2)}, u32[]{:S(2)}) collective-permute-start(f32[3,128,128]{2,1,0:T(8,128)S(1)} %pad_maximum_fusion.2), channel_id=1, source_target_pairs={{0,8},{4,12},{8,16},{12,20},{16,24},{20,28},{1,9},{5,13},{9,17},{1... | collective-permute-start | bytes 589832 | tf_op jit(solution)/shard_map/ppermute | solution.py:203
  152.2 2.4 collective-permute-done.6
  154.8 11.7 %cholesky.70 = f32[128,128]{1,0:T(8,128)S(1)} custom-call(f32[128,128]{1,0:T(8,128)S(1)} %fusion.51), custom_call_target="Cholesky" | custom-call | tf_op jit(solution)/shard_map/jit(cholesky)/cholesky | solution.py:95
  166.5 16.9 %shard_map.78 = f32[2,512,2048]{2,1,0:T(8,128)} custom-call(s32[8]{0:T(128)} %get-tuple-element.10.src_left, s32[16]{0:T(128)} %copy-done, s32[8]{0:T(128)} %get-tuple-element.11.tile_ref, s32[128]{0:T(128)} %slice_convert_fusion.mask_ref, s32[8]{0:T(128)} %compare_convert_fusion.flag_ref, ...), custom_call_target="tpu_custom_call", output_to_operand_aliasing={{}: (8, {})} | custom-call | tf_op jit(solution)/shard_map/pallas_call | solution.py:78
  183.4 4.7 %slice_bitcast_fusion = f32[512,2048]{1,0:T(8,128)} fusion(f32[2,512,2048]{2,1,0:T(8,128)} %shard_map.78), kind=kLoop, calls=%fused_computation.1 | loop fusion | bytes 8388608 | tf_op jit(solution)/shard_map/squeeze | solution.py:186
  189.4 9.8 %custom-call.8 = f32[1,128,128]{1,2,0:T(8,128)S(1)} custom-call(f32[1,128,128]{2,1,0:T(8,128)S(1)} %fusion.36), custom_call_target="InvertDiagBlocksLowerTriangular" | custom-call | tf_op jit(solution)/shard_map/triangular_solve/custom-call.0 | solution.py:97
  200.6 5.6 %collective-permute-start.7 = (f32[3,128,128]{2,1,0:T(8,128)S(1)}, f32[3,128,128]{2,1,0:T(8,128)S(1)}, u32[]{:S(2)}, u32[]{:S(2)}) collective-permute-start(f32[3,128,128]{2,1,0:T(8,128)S(1)} %pad_maximum_fusion.3), channel_id=1, source_target_pairs={{0,16},{4,20},{8,24},{12,28},{1,17},{5,21},{9,25},{13,29},{2,18},{... | collective-permute-start | bytes 589832 | tf_op jit(solution)/shard_map/ppermute | solution.py:203
  206.3 4.6 %collective-permute-done.7 = f32[3,128,128]{2,1,0:T(8,128)S(1)} collective-permute-done((f32[3,128,128]{2,1,0:T(8,128)S(1)}, f32[3,128,128]{2,1,0:T(8,128)S(1)}, u32[]{:S(2)}, u32[]{:S(2)}) %collective-permute-start.7) | collective-permute-done | bytes 196640 | tf_op jit(solution)/shard_map/ppermute | solution.py:203
  211.2 11.7 %cholesky.81 = f32[128,128]{1,0:T(8,128)S(1)} custom-call(f32[128,128]{1,0:T(8,128)S(1)} %fusion.49), custom_call_target="Cholesky" | custom-call | tf_op jit(solution)/shard_map/jit(cholesky)/cholesky | solution.py:95
  224.3 9.8 %custom-call.9 = f32[1,128,128]{1,2,0:T(8,128)S(1)} custom-call(f32[1,128,128]{2,1,0:T(8,128)S(1)} %fusion.37), custom_call_target="InvertDiagBlocksLowerTriangular" | custom-call | tf_op jit(solution)/shard_map/triangular_solve/custom-call.0 | solution.py:97
  235.4 0.7 maximum_bitcast_fusion
  236.1 6.6 %fusion.1 = f32[1,512,2048]{2,1,0:T(8,128)} fusion(f32[512,2048]{1,0:T(8,128)} %collective-permute-done.2, f32[2,512,2048]{2,1,0:T(8,128)} %shard_map.78), kind=kLoop, calls=%fused_computation.4 | loop fusion | flops 1048576 | bytes 12582912 | tf_op jit(solution)/shard_map/broadcast_in_dim | solution.py:210
  (77 shorter events, 11.2 us)
Async XLA Ops:
  0.6 105.8 %copy-start.1 = (f32[1,1024]{1,0:T(1,128)S(1)}, f32[1,1024]{1,0:T(1,128)}, u32[]{:S(2)}) copy-start(f32[1,1024]{1,0:T(1,128)} %param.10) | copy-start | bytes 12292
  1.4 106.0 %copy-start.2 = (s32[128]{0:T(128)}, s32[128]{0:T(128)S(1)}, u32[]{:S(2)}) copy-start(s32[128]{0:T(128)S(1)} %reshape_squeeze.4.mask_ref) | copy-start | bytes 1540
  2.1 119.9 %collective-permute-start = (f32[1152]{0:T(1024)S(1)}, f32[1152]{0:T(1024)S(1)}, u32[]{:S(2)}, u32[]{:S(2)}) collective-permute-start(f32[1152]{0:T(1024)S(1)} %pad_maximum_fusion.4), channel_id=1, source_target_pairs={{0,2},{1,3},{2,0},{3,1},{4,6},{5,7},{6,4},{7,5},{8,10},{9,11},{10,... | collective-permute-start | bytes 13832 | tf_op jit(solution)/shard_map/ppermute | solution.py:150
  5.1 161.4 %collective-permute-start.1 = (bf16[1024,2048]{1,0:T(8,128)(2,1)}, bf16[1024,2048]{1,0:T(8,128)(2,1)}, u32[]{:S(2)}, u32[]{:S(2)}) collective-permute-start(bf16[1024,2048]{1,0:T(8,128)(2,1)} %bitcast.153), channel_id=1, source_target_pairs={{0,2},{1,3},{2,0},{3,1},{4,6},{5,7},{6,4},{7,5},{8,10},{9,11},{10,... | collective-permute-start | bytes 12582920 | tf_op jit(solution)/shard_map/ppermute | solution.py:150
  5.9 101.6 %copy-start = (s32[16]{0:T(128)}, s32[16]{0:T(128)S(1)}, u32[]{:S(2)}) copy-start(s32[16]{0:T(128)S(1)} %select_reduce_fusion.3.src_right) | copy-start | bytes 196
  18.4 1.6 collective-permute-start.3
  20.0 81.5 %collective-permute-start.4 = (f32[3,128,128]{1,2,0:T(8,128)S(1)}, f32[3,128,128]{1,2,0:T(8,128)S(1)}, u32[]{:S(2)}, u32[]{:S(2)}) collective-permute-start(f32[3,128,128]{1,2,0:T(8,128)S(1)} %add.90), channel_id=1, source_target_pairs={{0,2},{1,3},{2,0},{3,1},{4,6},{5,7},{6,4},{7,5},{8,10},{9,11},{10,... | collective-permute-start | bytes 589832 | tf_op jit(solution)/shard_map/ppermute | solution.py:150
  101.8 21.4 %collective-permute-start.5 = (f32[3,128,128]{2,1,0:T(8,128)S(1)}, f32[3,128,128]{2,1,0:T(8,128)S(1)}, u32[]{:S(2)}, u32[]{:S(2)}) collective-permute-start(f32[3,128,128]{2,1,0:T(8,128)S(1)} %copy.63), channel_id=1, source_target_pairs={{0,4},{4,8},{8,12},{12,16},{16,20},{20,24},{24,28},{1,5},{5,9},{9,... | collective-permute-start | bytes 589832 | tf_op jit(solution)/shard_map/ppermute | solution.py:203
  147.9 6.6 %collective-permute-start.6 = (f32[3,128,128]{2,1,0:T(8,128)S(1)}, f32[3,128,128]{2,1,0:T(8,128)S(1)}, u32[]{:S(2)}, u32[]{:S(2)}) collective-permute-start(f32[3,128,128]{2,1,0:T(8,128)S(1)} %pad_maximum_fusion.2), channel_id=1, source_target_pairs={{0,8},{4,12},{8,16},{12,20},{16,24},{20,28},{1,9},{5,13},{9,17},{1... | collective-permute-start | bytes 589832 | tf_op jit(solution)/shard_map/ppermute | solution.py:203
  188.1 48.0 %collective-permute-start.2 = (f32[512,2048]{1,0:T(8,128)}, f32[512,2048]{1,0:T(8,128)}, u32[]{:S(2)}, u32[]{:S(2)}) collective-permute-start(f32[512,2048]{1,0:T(8,128)} %slice_bitcast_fusion), channel_id=1, source_target_pairs={{0,1},{1,0},{2,3},{3,2},{4,5},{5,4},{6,7},{7,6},{8,9},{9,8},{10,11... | collective-permute-start | bytes 12582920 | tf_op jit(solution)/shard_map/ppermute | solution.py:150
  200.6 10.3 %collective-permute-start.7 = (f32[3,128,128]{2,1,0:T(8,128)S(1)}, f32[3,128,128]{2,1,0:T(8,128)S(1)}, u32[]{:S(2)}, u32[]{:S(2)}) collective-permute-start(f32[3,128,128]{2,1,0:T(8,128)S(1)} %pad_maximum_fusion.3), channel_id=1, source_target_pairs={{0,16},{4,20},{8,24},{12,28},{1,17},{5,21},{9,25},{13,29},{2,18},{... | collective-permute-start | bytes 589832 | tf_op jit(solution)/shard_map/ppermute | solution.py:203

commit v8 on v7

--- a/solution.py
+++ b/solution.py
@@ -150,14 +150,7 @@
         return lax.ppermute(value, "row", [(src, src ^ step) for src in range(owners)])
 
     kernel_slab, part_pieces = lax.optimization_barrier((local_slab, part_pieces))
-    if owners & (owners - 1) == 0:
-        summed = part_pieces
-        step = 1
-        while step < owners:
-            summed = summed + exchange(summed, step)
-            step *= 2
-    else:
-        summed = lax.psum(part_pieces, "row")
+    summed = lax.psum(part_pieces, "row")
     eye = jnp.eye(BLK, dtype=jnp.float32)
     segment = jnp.stack([
         summed[0] + eye * diagonal[:BLK][None, :],
@@ -179,6 +172,7 @@
         partial = gram_rows(
             kernel_slab, row_weights, live_blocks, left_src, source, order, diagonal, flags, own_blocks,
         )
+        partial, segment = lax.optimization_barrier((partial, segment))
         partial = gram_rows(
             across_slab, across_weights, across_live, left_src, source, order, diagonal, flags,
             own_blocks, partial,

time: 247 us -> 246 us (level)
  waiting for transfers between devices: 85.8 us -> 69.6 us
  between operations: 6.31 us -> 19.7 us
    ppermute x5 -> x3, waiting for transfers between devices: 78.8 us -> 59.3 us  [exchange(): lax.ppermute(value, 'row', [(src, src ^ step) for src in range(owners)])]
    ppermute x3, waiting for transfers between devices: 7.01 us -> 10.2 us  [local(): moved = lax.ppermute(jnp.stack(running), 'tm', pairs)]
    ppermute x5 -> x3, starting transfers between devices: 5.13 us -> 3.05 us  [exchange(): lax.ppermute(value, 'row', [(src, src ^ step) for src in range(owners)])]
  transfers between devices with their start and end apart: 8 -> 7, of which waited for: 3 -> 4; matrix products, arithmetic and copies ran while one was open for 36% -> 38% of each run, Pallas kernels for 6% -> 6%
where the time goes in v8:
time: 246 us; the launch traced here: 241 us
  other arithmetic  81.8 us (33%)
  waiting for transfers between devices  69.6 us (28%)
  Pallas kernels  31.3 us (13%)
  between operations  19.7 us (8%)
  starting transfers between devices  17.9 us (7%)
  local copies, waits for them, and re-layouts  12.3 us (5%)
  matrix products  8.93 us (4%)
    ppermute x3, waiting for transfers between devices, exchange(): lax.ppermute(value, 'row', [(src, src ^ step) for src in range(owners)])  59.3 us
    another operation x9, other arithmetic, join_segments(): factor = jnp.linalg.cholesky(middle)  37.2 us
    another operation x6, other arithmetic, join_segments(): lax.linalg.triangular_solve(factor, jnp.concatenate([cross_one.T, cross_t...  31.4 us
    pallas_call x2, Pallas kernels, gram_rows(): pl.pallas_call(gram_kernel, grid_spec=grid_spec, out_shape=jax.ShapeDtype...  31.3 us
    ppermute x3, starting transfers between devices, local(): moved = lax.ppermute(jnp.stack(running), 'tm', pairs)  14.8 us
    ppermute x3, waiting for transfers between devices, local(): moved = lax.ppermute(jnp.stack(running), 'tm', pairs)  10.2 us
    broadcast_in_dim x1, other arithmetic, local(): return (owned[None], chain_out)  6.57 us
    dot_general x3, matrix products, contract_rows(): lax.dot_general(left_cols, right_cols, (((0,), (0,)), ((), ())), preferre...  5.4 us
  transfers between devices with their start and end apart: 7, of which 4 were waited for; matrix products, arithmetic and copies ran while one was open for 38% of the time, Pallas kernels for 6%

profile of v8, /device:TPU:0, one launch (start us, length us, event | category | flops | bytes accessed | tf_op | source)
XLA Modules:
  0.0 241.5 jit_solution(16742276285501012518)
XLA Ops:
  7.2 3.0 %collective-permute-start.1 = (bf16[1024,2048]{1,0:T(8,128)(2,1)}, bf16[1024,2048]{1,0:T(8,128)(2,1)}, u32[]{:S(2)}, u32[]{:S(2)}) collective-permute-start(bf16[1024,2048]{1,0:T(8,128)(2,1)} %bitcast.152), channel_id=1, source_target_pairs={{0,2},{1,3},{2,0},{3,1},{4,6},{5,7},{6,4},{7,5},{8,10},{9,11},{10,... | collective-permute-start | bytes 12582920 | tf_op jit(solution)/shard_map/ppermute | solution.py:150
  10.2 0.8 select_reduce_fusion.3.src_right
  16.8 1.0 fusion.76
  17.8 1.8 convolution_bitcast_fusion
  19.7 1.8 convolution_bitcast_fusion.1
  21.4 1.8 convolution_bitcast_fusion.2
  23.2 0.7 pad_maximum_fusion
  24.0 0.8 reshape_squeeze.4.mask_ref
  24.7 0.7 pad_maximum_fusion.4
  25.5 0.8 fusion.86
  27.6 0.7 slice_bitcast_fusion.14
  28.8 1.7 copy.54.w_ref
  30.5 14.5 %shard_map.77.rest_0_ = f32[2,512,2048]{2,1,0:T(8,128)} custom-call(s32[8]{0:T(128)} %get-tuple-element.14.src_left, s32[16]{0:T(128)} %copy-done, s32[8]{0:T(128)} %get-tuple-element.15.tile_ref, s32[128]{0:T(128)} %copy-done.1, s32[8]{0:T(128)} %compare_convert_fusion.flag_ref, bf16[1024,2048]{1,0:T(8,128)(2,1)} %bitcast.153, f32[1024,1]{1,0:T(8,128)} %copy.54.w_ref, ...), custom_call_target="tpu_custom_call" | custom-call | tf_op jit(solution)/shard_map/pallas_call | solution.py:78
  45.0 59.3 %collective-permute-done = f32[1152]{0:T(1024)S(1)} collective-permute-done((f32[1152]{0:T(1024)S(1)}, f32[1152]{0:T(1024)S(1)}, u32[]{:S(2)}, u32[]{:S(2)}) %collective-permute-start) | collective-permute-done | bytes 4640 | tf_op jit(solution)/shard_map/ppermute | solution.py:150
  104.4 1.0 copy.55.w_ref
  105.4 0.9 slice_add_fusion.1
  106.5 3.6 %collective-permute-start.3 = (f32[3,128,128]{1,2,0:T(8,128)S(1)}, f32[3,128,128]{1,2,0:T(8,128)S(1)}, u32[]{:S(2)}, u32[]{:S(2)}) collective-permute-start(f32[3,128,128]{1,2,0:T(8,128)S(1)} %copy.56), channel_id=1, source_target_pairs={{0,4},{4,8},{8,12},{12,16},{16,20},{20,24},{24,28},{1,5},{5,9},{9,... | collective-permute-start | bytes 589832 | tf_op jit(solution)/shard_map/ppermute | solution.py:197
  110.3 3.1 %collective-permute-done.3 = f32[3,128,128]{1,2,0:T(8,128)S(1)} collective-permute-done((f32[3,128,128]{1,2,0:T(8,128)S(1)}, f32[3,128,128]{1,2,0:T(8,128)S(1)}, u32[]{:S(2)}, u32[]{:S(2)}) %collective-permute-start.3) | collective-permute-done | bytes 196640 | tf_op jit(solution)/shard_map/ppermute | solution.py:197
  113.7 11.7 %cholesky.59 = f32[128,128]{1,0:T(8,128)S(1)} custom-call(f32[128,128]{1,0:T(8,128)S(1)} %fusion.53), custom_call_target="Cholesky" | custom-call | tf_op jit(solution)/shard_map/jit(cholesky)/cholesky | solution.py:95
  126.8 9.8 %custom-call.7 = f32[1,128,128]{1,2,0:T(8,128)S(1)} custom-call(f32[1,128,128]{2,1,0:T(8,128)S(1)} %fusion.35), custom_call_target="InvertDiagBlocksLowerTriangular" | custom-call | tf_op jit(solution)/shard_map/triangular_solve/custom-call.0 | solution.py:97
  138.0 5.6 %collective-permute-start.4 = (f32[3,128,128]{2,1,0:T(8,128)S(1)}, f32[3,128,128]{2,1,0:T(8,128)S(1)}, u32[]{:S(2)}, u32[]{:S(2)}) collective-permute-start(f32[3,128,128]{2,1,0:T(8,128)S(1)} %pad_maximum_fusion.2), channel_id=1, source_target_pairs={{0,8},{4,12},{8,16},{12,20},{16,24},{20,28},{1,9},{5,13},{9,17},{1... | collective-permute-start | bytes 589832 | tf_op jit(solution)/shard_map/ppermute | solution.py:197
  144.1 2.5 %collective-permute-done.4 = f32[3,128,128]{2,1,0:T(8,128)S(1)} collective-permute-done((f32[3,128,128]{2,1,0:T(8,128)S(1)}, f32[3,128,128]{2,1,0:T(8,128)S(1)}, u32[]{:S(2)}, u32[]{:S(2)}) %collective-permute-start.4) | collective-permute-done | bytes 196640 | tf_op jit(solution)/shard_map/ppermute | solution.py:197
  146.8 11.7 %cholesky.70 = f32[128,128]{1,0:T(8,128)S(1)} custom-call(f32[128,128]{1,0:T(8,128)S(1)} %fusion.50), custom_call_target="Cholesky" | custom-call | tf_op jit(solution)/shard_map/jit(cholesky)/cholesky | solution.py:95
  158.6 16.8 %shard_map.78 = f32[2,512,2048]{2,1,0:T(8,128)} custom-call(s32[8]{0:T(128)} %get-tuple-element.14.src_left, s32[16]{0:T(128)} %copy-done, s32[8]{0:T(128)} %get-tuple-element.15.tile_ref, s32[128]{0:T(128)} %slice_convert_fusion.mask_ref, s32[8]{0:T(128)} %compare_convert_fusion.flag_ref, ...), custom_call_target="tpu_custom_call", output_to_operand_aliasing={{}: (8, {})} | custom-call | tf_op jit(solution)/shard_map/pallas_call | solution.py:78
  175.4 4.7 %slice_bitcast_fusion = f32[512,2048]{1,0:T(8,128)} fusion(f32[2,512,2048]{2,1,0:T(8,128)} %shard_map.78), kind=kLoop, calls=%fused_computation.1 | loop fusion | bytes 8388608 | tf_op jit(solution)/shard_map/squeeze | solution.py:180
  181.4 9.8 %custom-call.8 = f32[1,128,128]{1,2,0:T(8,128)S(1)} custom-call(f32[1,128,128]{2,1,0:T(8,128)S(1)} %fusion.36), custom_call_target="InvertDiagBlocksLowerTriangular" | custom-call | tf_op jit(solution)/shard_map/triangular_solve/custom-call.0 | solution.py:97
  192.6 5.6 %collective-permute-start.5 = (f32[3,128,128]{2,1,0:T(8,128)S(1)}, f32[3,128,128]{2,1,0:T(8,128)S(1)}, u32[]{:S(2)}, u32[]{:S(2)}) collective-permute-start(f32[3,128,128]{2,1,0:T(8,128)S(1)} %pad_maximum_fusion.3), channel_id=1, source_target_pairs={{0,16},{4,20},{8,24},{12,28},{1,17},{5,21},{9,25},{13,29},{2,18},{... | collective-permute-start | bytes 589832 | tf_op jit(solution)/shard_map/ppermute | solution.py:197
  198.2 4.6 %collective-permute-done.5 = f32[3,128,128]{2,1,0:T(8,128)S(1)} collective-permute-done((f32[3,128,128]{2,1,0:T(8,128)S(1)}, f32[3,128,128]{2,1,0:T(8,128)S(1)}, u32[]{:S(2)}, u32[]{:S(2)}) %collective-permute-start.5) | collective-permute-done | bytes 196640 | tf_op jit(solution)/shard_map/ppermute | solution.py:197
  203.2 11.7 %cholesky.81 = f32[128,128]{1,0:T(8,128)S(1)} custom-call(f32[128,128]{1,0:T(8,128)S(1)} %fusion.48), custom_call_target="Cholesky" | custom-call | tf_op jit(solution)/shard_map/jit(cholesky)/cholesky | solution.py:95
  216.2 9.8 %custom-call.9 = f32[1,128,128]{1,2,0:T(8,128)S(1)} custom-call(f32[1,128,128]{2,1,0:T(8,128)S(1)} %fusion.37), custom_call_target="InvertDiagBlocksLowerTriangular" | custom-call | tf_op jit(solution)/shard_map/triangular_solve/custom-call.0 | solution.py:97
  227.4 0.7 maximum_bitcast_fusion
  228.1 6.6 %fusion.1 = f32[1,512,2048]{2,1,0:T(8,128)} fusion(f32[512,2048]{1,0:T(8,128)} %collective-permute-done.2, f32[2,512,2048]{2,1,0:T(8,128)} %shard_map.78), kind=kLoop, calls=%fused_computation.4 | loop fusion | flops 1048576 | bytes 12582912 | tf_op jit(solution)/shard_map/broadcast_in_dim | solution.py:204
  (75 shorter events, 12.2 us)
Async XLA Ops:
  7.2 98.2 %all-reduce.2.cloned.1.call-start = ((), (), s32[]{:S(2)}) async-start(), calls=%async_computation | async-start | bytes 393216 | tf_op jit(solution)/shard_map/psum | solution.py:153
  7.2 151.3 %collective-permute-start.1 = (bf16[1024,2048]{1,0:T(8,128)(2,1)}, bf16[1024,2048]{1,0:T(8,128)(2,1)}, u32[]{:S(2)}, u32[]{:S(2)}) collective-permute-start(bf16[1024,2048]{1,0:T(8,128)(2,1)} %bitcast.152), channel_id=1, source_target_pairs={{0,2},{1,3},{2,0},{3,1},{4,6},{5,7},{6,4},{7,5},{8,10},{9,11},{10,... | collective-permute-start | bytes 12582920 | tf_op jit(solution)/shard_map/ppermute | solution.py:150
  11.0 19.5 %copy-start = (s32[16]{0:T(128)}, s32[16]{0:T(128)S(1)}, u32[]{:S(2)}) copy-start(s32[16]{0:T(128)S(1)} %select_reduce_fusion.3.src_right) | copy-start | bytes 196
  24.7 5.8 %copy-start.1 = (s32[128]{0:T(128)}, s32[128]{0:T(128)S(1)}, u32[]{:S(2)}) copy-start(s32[128]{0:T(128)S(1)} %reshape_squeeze.4.mask_ref) | copy-start | bytes 1540
  25.4 78.9 %collective-permute-start = (f32[1152]{0:T(1024)S(1)}, f32[1152]{0:T(1024)S(1)}, u32[]{:S(2)}, u32[]{:S(2)}) collective-permute-start(f32[1152]{0:T(1024)S(1)} %pad_maximum_fusion.4), channel_id=1, source_target_pairs={{0,2},{1,3},{2,0},{3,1},{4,6},{5,7},{6,4},{7,5},{8,10},{9,11},{10,... | collective-permute-start | bytes 13832 | tf_op jit(solution)/shard_map/ppermute | solution.py:150
  106.5 7.0 %collective-permute-start.3 = (f32[3,128,128]{1,2,0:T(8,128)S(1)}, f32[3,128,128]{1,2,0:T(8,128)S(1)}, u32[]{:S(2)}, u32[]{:S(2)}) collective-permute-start(f32[3,128,128]{1,2,0:T(8,128)S(1)} %copy.56), channel_id=1, source_target_pairs={{0,4},{4,8},{8,12},{12,16},{16,20},{20,24},{24,28},{1,5},{5,9},{9,... | collective-permute-start | bytes 589832 | tf_op jit(solution)/shard_map/ppermute | solution.py:197
  138.0 8.5 %collective-permute-start.4 = (f32[3,128,128]{2,1,0:T(8,128)S(1)}, f32[3,128,128]{2,1,0:T(8,128)S(1)}, u32[]{:S(2)}, u32[]{:S(2)}) collective-permute-start(f32[3,128,128]{2,1,0:T(8,128)S(1)} %pad_maximum_fusion.2), channel_id=1, source_target_pairs={{0,8},{4,12},{8,16},{12,20},{16,24},{20,28},{1,9},{5,13},{9,17},{1... | collective-permute-start | bytes 589832 | tf_op jit(solution)/shard_map/ppermute | solution.py:197
  180.1 48.0 %collective-permute-start.2 = (f32[512,2048]{1,0:T(8,128)}, f32[512,2048]{1,0:T(8,128)}, u32[]{:S(2)}, u32[]{:S(2)}) collective-permute-start(f32[512,2048]{1,0:T(8,128)} %slice_bitcast_fusion), channel_id=1, source_target_pairs={{0,1},{1,0},{2,3},{3,2},{4,5},{5,4},{6,7},{7,6},{8,9},{9,8},{10,11... | collective-permute-start | bytes 12582920 | tf_op jit(solution)/shard_map/ppermute | solution.py:150
  192.6 10.2 %collective-permute-start.5 = (f32[3,128,128]{2,1,0:T(8,128)S(1)}, f32[3,128,128]{2,1,0:T(8,128)S(1)}, u32[]{:S(2)}, u32[]{:S(2)}) collective-permute-start(f32[3,128,128]{2,1,0:T(8,128)S(1)} %pad_maximum_fusion.3), channel_id=1, source_target_pairs={{0,16},{4,20},{8,24},{12,28},{1,17},{5,21},{9,25},{13,29},{2,18},{... | collective-permute-start | bytes 589832 | tf_op jit(solution)/shard_map/ppermute | solution.py:197
Sparse Core Ops, SparseCore 0:
  24.1 33.2 all-reduce.1

commit v9 on v8

--- a/solution.py
+++ b/solution.py
@@ -150,7 +150,13 @@
         return lax.ppermute(value, "row", [(src, src ^ step) for src in range(owners)])
 
     kernel_slab, part_pieces = lax.optimization_barrier((local_slab, part_pieces))
-    summed = lax.psum(part_pieces, "row")
+    packed_side = jnp.concatenate([row_weights, live_blocks.reshape(-1).astype(jnp.float32)])
+    side_slots = jnp.zeros((owners, packed_side.shape[0]), jnp.float32)
+    side_slots = lax.dynamic_update_index_in_dim(side_slots, packed_side, my_index, 0)
+    piece_count = part_pieces.size
+    summed_all = lax.psum(jnp.concatenate([part_pieces.reshape(-1), side_slots.reshape(-1)]), "row")
+    summed = summed_all[:piece_count].reshape(part_pieces.shape)
+    every_side = summed_all[piece_count:].reshape(side_slots.shape)
     eye = jnp.eye(BLK, dtype=jnp.float32)
     segment = jnp.stack([
         summed[0] + eye * diagonal[:BLK][None, :],
@@ -159,9 +165,8 @@
     ])
 
     if owners == 4:
-        packed_side = jnp.concatenate([row_weights, live_blocks.reshape(-1).astype(jnp.float32)])
         across_slab = exchange(local_slab, 2)
-        across_side = exchange(packed_side, 2)
+        across_side = lax.dynamic_index_in_dim(every_side, my_index ^ 2, 0, False)
         across_weights = across_side[:slab_height]
         across_live = across_side[slab_height:].reshape(live_blocks.shape).astype(jnp.int32)
         order = jnp.concatenate(

time: 246 us -> 200 us (0.81)
  the two profiles are of different devices: /device:TPU:0 before, /device:TPU:25 now
where the time goes in v9:
time: 200 us; the launch traced here: 199 us
  other arithmetic  81.9 us (41%)
  waiting for transfers between devices  33.4 us (17%)
  Pallas kernels  31.4 us (16%)
  between operations  19.7 us (10%)
  local copies, waits for them, and re-layouts  13.3 us (7%)
  starting transfers between devices  10.5 us (5%)
  matrix products  8.88 us (4%)
    another operation x9, other arithmetic, join_segments(): factor = jnp.linalg.cholesky(middle)  37.2 us
    pallas_call x2, Pallas kernels, gram_rows(): pl.pallas_call(gram_kernel, grid_spec=grid_spec, out_shape=jax.ShapeDtype...  31.4 us
    another operation x6, other arithmetic, join_segments(): lax.linalg.triangular_solve(factor, jnp.concatenate([cross_one.T, cross_t...  31.4 us
    ppermute x3, waiting for transfers between devices, local(): moved = lax.ppermute(jnp.stack(running), 'tm', pairs)  19.7 us
    psum x1, waiting for transfers between devices, local(): lax.psum(jnp.concatenate([part_pieces.reshape(-1), side_slots.reshape(-1)...  13.7 us
    broadcast_in_dim x1, other arithmetic, local(): return (owned[None], chain_out)  6.57 us
    ppermute x3, starting transfers between devices, local(): moved = lax.ppermute(jnp.stack(running), 'tm', pairs)  6.08 us
    dot_general x3, matrix products, contract_rows(): lax.dot_general(left_cols, right_cols, (((0,), (0,)), ((), ())), preferre...  5.35 us
  transfers between devices with their start and end apart: 6, of which 4 were waited for; matrix products, arithmetic and copies ran while one was open for 47% of the time, Pallas kernels for 7%

profile of v9, /device:TPU:25, one launch (start us, length us, event | category | flops | bytes accessed | tf_op | source)
XLA Modules:
  0.0 199.2 jit_solution(10752940199878476700)
XLA Ops:
  7.2 1.3 collective-permute-start
  8.5 0.8 select_reduce_fusion.3.src_right
  15.1 1.0 fusion.80
  16.1 1.8 convolution_bitcast_fusion
  17.9 1.8 convolution_bitcast_fusion.1
  19.7 1.8 convolution_bitcast_fusion.2
  21.5 0.8 reshape_squeeze.4.mask_ref
  23.1 0.7 pad_maximum_fusion
  23.8 0.8 fusion.91
  26.1 1.0 copy.54.w_ref
  28.3 14.6 %shard_map.80.rest_0_ = f32[2,512,2048]{2,1,0:T(8,128)} custom-call(s32[8]{0:T(128)} %get-tuple-element.14.src_left, s32[16]{0:T(128)} %copy-done, s32[8]{0:T(128)} %get-tuple-element.15.tile_ref, s32[128]{0:T(128)} %copy-done.2, s32[8]{0:T(128)} %compare_convert_fusion.flag_ref, bf16[1024,2048]{1,0:T(8,128)(2,1)} %bitcast.175, f32[1024,1]{1,0:T(8,128)} %copy.54.w_ref, ...), custom_call_target="tpu_custom_call" | custom-call | tf_op jit(solution)/shard_map/pallas_call | solution.py:78
  42.8 13.7 %all-reduce.2.cloned.1.call-done = f32[53760]{0:T(1024)} async-done(((f32[53760]{0:T(1024)}), f32[53760]{0:T(1024)}) %all-reduce.2.cloned.1.call-update) | async-done | bytes 215056 | tf_op jit(solution)/shard_map/psum | solution.py:157
  56.5 0.9 fusion.50
  57.4 0.8 slice_bitcast_fusion.13
  58.4 3.1 %collective-permute-start.2 = (f32[3,128,128]{1,2,0:T(8,128)S(1)}, f32[3,128,128]{1,2,0:T(8,128)S(1)}, u32[]{:S(2)}, u32[]{:S(2)}) collective-permute-start(f32[3,128,128]{1,2,0:T(8,128)S(1)} %copy.56), channel_id=1, source_target_pairs={{0,4},{4,8},{8,12},{12,16},{16,20},{20,24},{24,28},{1,5},{5,9},{9,... | collective-permute-start | bytes 589832 | tf_op jit(solution)/shard_map/ppermute | solution.py:202
  61.7 0.7 slice.171
  62.5 3.7 %collective-permute-done.2 = f32[3,128,128]{1,2,0:T(8,128)S(1)} collective-permute-done((f32[3,128,128]{1,2,0:T(8,128)S(1)}, f32[3,128,128]{1,2,0:T(8,128)S(1)}, u32[]{:S(2)}, u32[]{:S(2)}) %collective-permute-start.2) | collective-permute-done | bytes 196640 | tf_op jit(solution)/shard_map/ppermute | solution.py:202
  66.4 11.7 %cholesky.59 = f32[128,128]{1,0:T(8,128)S(1)} custom-call(f32[128,128]{1,0:T(8,128)S(1)} %fusion.57), custom_call_target="Cholesky" | custom-call | tf_op jit(solution)/shard_map/jit(cholesky)/cholesky | solution.py:95
  79.5 9.8 %custom-call.7 = f32[1,128,128]{1,2,0:T(8,128)S(1)} custom-call(f32[1,128,128]{2,1,0:T(8,128)S(1)} %fusion.35), custom_call_target="InvertDiagBlocksLowerTriangular" | custom-call | tf_op jit(solution)/shard_map/triangular_solve/custom-call.0 | solution.py:97
  90.7 1.5 collective-permute-start.3
  92.2 1.0 copy.55.w_ref
  93.9 3.7 %collective-permute-done.3 = f32[3,128,128]{2,1,0:T(8,128)S(1)} collective-permute-done((f32[3,128,128]{2,1,0:T(8,128)S(1)}, f32[3,128,128]{2,1,0:T(8,128)S(1)}, u32[]{:S(2)}, u32[]{:S(2)}) %collective-permute-start.3) | collective-permute-done | bytes 196640 | tf_op jit(solution)/shard_map/ppermute | solution.py:202
  97.8 11.7 %cholesky.70 = f32[128,128]{1,0:T(8,128)S(1)} custom-call(f32[128,128]{1,0:T(8,128)S(1)} %fusion.54), custom_call_target="Cholesky" | custom-call | tf_op jit(solution)/shard_map/jit(cholesky)/cholesky | solution.py:95
  109.5 16.9 %shard_map.81 = f32[2,512,2048]{2,1,0:T(8,128)} custom-call(s32[8]{0:T(128)} %get-tuple-element.14.src_left, s32[16]{0:T(128)} %copy-done, s32[8]{0:T(128)} %get-tuple-element.15.tile_ref, s32[128]{0:T(128)} %fusion.86.mask_ref, s32[8]{0:T(128)} %compare_convert_fusion.flag_ref, ...), custom_call_target="tpu_custom_call", output_to_operand_aliasing={{}: (8, {})} | custom-call | tf_op jit(solution)/shard_map/pallas_call | solution.py:78
  126.4 4.7 %slice_bitcast_fusion = f32[512,2048]{1,0:T(8,128)} fusion(f32[2,512,2048]{2,1,0:T(8,128)} %shard_map.81), kind=kLoop, calls=%fused_computation.1 | loop fusion | bytes 8388608 | tf_op jit(solution)/shard_map/squeeze | solution.py:185
  131.1 3.1 %collective-permute-start.1 = (f32[512,2048]{1,0:T(8,128)}, f32[512,2048]{1,0:T(8,128)}, u32[]{:S(2)}, u32[]{:S(2)}) collective-permute-start(f32[512,2048]{1,0:T(8,128)} %slice_bitcast_fusion), channel_id=1, source_target_pairs={{0,1},{1,0},{2,3},{3,2},{4,5},{5,4},{6,7},{7,6},{8,9},{9,8},{10,11... | collective-permute-start | bytes 12582920 | tf_op jit(solution)/shard_map/ppermute | solution.py:150
  135.5 9.8 %custom-call.8 = f32[1,128,128]{1,2,0:T(8,128)S(1)} custom-call(f32[1,128,128]{2,1,0:T(8,128)S(1)} %fusion.36), custom_call_target="InvertDiagBlocksLowerTriangular" | custom-call | tf_op jit(solution)/shard_map/triangular_solve/custom-call.0 | solution.py:97
  146.7 1.5 collective-permute-start.4
  148.2 12.4 %collective-permute-done.4 = f32[3,128,128]{2,1,0:T(8,128)S(1)} collective-permute-done((f32[3,128,128]{2,1,0:T(8,128)S(1)}, f32[3,128,128]{2,1,0:T(8,128)S(1)}, u32[]{:S(2)}, u32[]{:S(2)}) %collective-permute-start.4) | collective-permute-done | bytes 196640 | tf_op jit(solution)/shard_map/ppermute | solution.py:202
  160.9 11.7 %cholesky.81 = f32[128,128]{1,0:T(8,128)S(1)} custom-call(f32[128,128]{1,0:T(8,128)S(1)} %fusion.52), custom_call_target="Cholesky" | custom-call | tf_op jit(solution)/shard_map/jit(cholesky)/cholesky | solution.py:95
  173.9 9.8 %custom-call.9 = f32[1,128,128]{1,2,0:T(8,128)S(1)} custom-call(f32[1,128,128]{2,1,0:T(8,128)S(1)} %fusion.37), custom_call_target="InvertDiagBlocksLowerTriangular" | custom-call | tf_op jit(solution)/shard_map/triangular_solve/custom-call.0 | solution.py:97
  185.8 6.6 %fusion.1 = f32[1,512,2048]{2,1,0:T(8,128)} fusion(f32[512,2048]{1,0:T(8,128)} %collective-permute-done.1, f32[2,512,2048]{2,1,0:T(8,128)} %shard_map.81), kind=kLoop, calls=%fused_computation.4 | loop fusion | flops 1048576 | bytes 12582912 | tf_op jit(solution)/shard_map/broadcast_in_dim | solution.py:209
  (83 shorter events, 14.4 us)
Async XLA Ops:
  7.2 18.9 %copy-start.1 = (f32[1,1024]{1,0:T(1,128)S(1)}, f32[1,1024]{1,0:T(1,128)}, u32[]{:S(2)}) copy-start(f32[1,1024]{1,0:T(1,128)} %param.10) | copy-start | bytes 12292
  7.2 49.3 %all-reduce.2.cloned.1.call-start = ((), (), s32[]{:S(2)}) async-start(), calls=%async_computation | async-start | bytes 434176 | tf_op jit(solution)/shard_map/psum | solution.py:157
  7.2 102.3 %collective-permute-start = (bf16[1024,2048]{1,0:T(8,128)(2,1)}, bf16[1024,2048]{1,0:T(8,128)(2,1)}, u32[]{:S(2)}, u32[]{:S(2)}) collective-permute-start(bf16[1024,2048]{1,0:T(8,128)(2,1)} %bitcast.174), channel_id=1, source_target_pairs={{0,2},{1,3},{2,0},{3,1},{4,6},{5,7},{6,4},{7,5},{8,10},{9,11},{10,... | collective-permute-start | bytes 12582920 | tf_op jit(solution)/shard_map/ppermute | solution.py:150
  9.3 19.0 %copy-start = (s32[16]{0:T(128)}, s32[16]{0:T(128)S(1)}, u32[]{:S(2)}) copy-start(s32[16]{0:T(128)S(1)} %select_reduce_fusion.3.src_right) | copy-start | bytes 196
  22.3 6.0 %copy-start.2 = (s32[128]{0:T(128)}, s32[128]{0:T(128)S(1)}, u32[]{:S(2)}) copy-start(s32[128]{0:T(128)S(1)} %reshape_squeeze.4.mask_ref) | copy-start | bytes 1540
  58.4 7.8 %collective-permute-start.2 = (f32[3,128,128]{1,2,0:T(8,128)S(1)}, f32[3,128,128]{1,2,0:T(8,128)S(1)}, u32[]{:S(2)}, u32[]{:S(2)}) collective-permute-start(f32[3,128,128]{1,2,0:T(8,128)S(1)} %copy.56), channel_id=1, source_target_pairs={{0,4},{4,8},{8,12},{12,16},{16,20},{20,24},{24,28},{1,5},{5,9},{9,... | collective-permute-start | bytes 589832 | tf_op jit(solution)/shard_map/ppermute | solution.py:202
  90.7 6.8 %collective-permute-start.3 = (f32[3,128,128]{2,1,0:T(8,128)S(1)}, f32[3,128,128]{2,1,0:T(8,128)S(1)}, u32[]{:S(2)}, u32[]{:S(2)}) collective-permute-start(f32[3,128,128]{2,1,0:T(8,128)S(1)} %pad_maximum_fusion.3), channel_id=1, source_target_pairs={{0,8},{4,12},{8,16},{12,20},{16,24},{20,28},{1,9},{5,13},{9,17},{1... | collective-permute-start | bytes 589832 | tf_op jit(solution)/shard_map/ppermute | solution.py:202
  131.1 54.7 %collective-permute-start.1 = (f32[512,2048]{1,0:T(8,128)}, f32[512,2048]{1,0:T(8,128)}, u32[]{:S(2)}, u32[]{:S(2)}) collective-permute-start(f32[512,2048]{1,0:T(8,128)} %slice_bitcast_fusion), channel_id=1, source_target_pairs={{0,1},{1,0},{2,3},{3,2},{4,5},{5,4},{6,7},{7,6},{8,9},{9,8},{10,11... | collective-permute-start | bytes 12582920 | tf_op jit(solution)/shard_map/ppermute | solution.py:150
  146.7 13.9 %collective-permute-start.4 = (f32[3,128,128]{2,1,0:T(8,128)S(1)}, f32[3,128,128]{2,1,0:T(8,128)S(1)}, u32[]{:S(2)}, u32[]{:S(2)}) collective-permute-start(f32[3,128,128]{2,1,0:T(8,128)S(1)} %pad_maximum_fusion.4), channel_id=1, source_target_pairs={{0,16},{4,20},{8,24},{12,28},{1,17},{5,21},{9,25},{13,29},{2,18},{... | collective-permute-start | bytes 589832 | tf_op jit(solution)/shard_map/ppermute | solution.py:202
Sparse Core Ops, SparseCore 0:
  23.9 32.5 all-reduce.1

commit v10 on v9

--- a/solution.py
+++ b/solution.py
@@ -154,7 +154,12 @@
     side_slots = jnp.zeros((owners, packed_side.shape[0]), jnp.float32)
     side_slots = lax.dynamic_update_index_in_dim(side_slots, packed_side, my_index, 0)
     piece_count = part_pieces.size
-    summed_all = lax.psum(jnp.concatenate([part_pieces.reshape(-1), side_slots.reshape(-1)]), "row")
+    summed_all = jnp.concatenate([part_pieces.reshape(-1), side_slots.reshape(-1)])
+    if owners == 4:
+        summed_all = summed_all + exchange(summed_all, 1)
+        summed_all = summed_all + exchange(summed_all, 2)
+    else:
+        summed_all = lax.psum(summed_all, "row")
     summed = summed_all[:piece_count].reshape(part_pieces.shape)
     every_side = summed_all[piece_count:].reshape(side_slots.shape)
     eye = jnp.eye(BLK, dtype=jnp.float32)
@@ -165,7 +170,8 @@
     ])
 
     if owners == 4:
-        across_slab = exchange(local_slab, 2)
+        send_slab, summed_all = lax.optimization_barrier((local_slab, summed_all))
+        across_slab = exchange(send_slab, 2)
         across_side = lax.dynamic_index_in_dim(every_side, my_index ^ 2, 0, False)
         across_weights = across_side[:slab_height]
         across_live = across_side[slab_height:].reshape(live_blocks.shape).astype(jnp.int32)

time: 200 us -> 215 us (1.075)
  the two profiles are of different devices: /device:TPU:25 before, /device:TPU:31 now
where the time goes in v10:
time: 215 us; the launch traced here: 214 us
  other arithmetic  80.5 us (37%)
  waiting for transfers between devices  68.3 us (32%)
  Pallas kernels  31.4 us (15%)
  local copies, waits for them, and re-layouts  11.7 us (5%)
  matrix products  8.87 us (4%)
  starting transfers between devices  7.29 us (3%)
  between operations  6.35 us (3%)
    ppermute x4, waiting for transfers between devices, exchange(): lax.ppermute(value, 'row', [(src, src ^ step) for src in range(owners)])  46.6 us
    another operation x9, other arithmetic, join_segments(): factor = jnp.linalg.cholesky(middle)  37.2 us
    another operation x6, other arithmetic, join_segments(): lax.linalg.triangular_solve(factor, jnp.concatenate([cross_one.T, cross_t...  31.4 us
    pallas_call x2, Pallas kernels, gram_rows(): pl.pallas_call(gram_kernel, grid_spec=grid_spec, out_shape=jax.ShapeDtype...  31.4 us
    ppermute x3, waiting for transfers between devices, local(): moved = lax.ppermute(jnp.stack(running), 'tm', pairs)  21.7 us
    broadcast_in_dim x1, other arithmetic, local(): return (owned[None], chain_out)  6.57 us
    dot_general x3, matrix products, contract_rows(): lax.dot_general(left_cols, right_cols, (((0,), (0,)), ((), ())), preferre...  5.33 us
    squeeze x1, local copies, waits for them, and re-layouts, local(): owned = partial[0] + exchange(partial[1], 1)  4.7 us
  transfers between devices with their start and end apart: 7, of which 5 were waited for; matrix products, arithmetic and copies ran while one was open for 38% of the time, Pallas kernels for 7%

profile of v10, /device:TPU:31, one launch (start us, length us, event | category | flops | bytes accessed | tf_op | source)
XLA Modules:
  0.0 214.5 jit_solution(2554843259106720606)
XLA Ops:
  0.6 0.8 select_reduce_fusion.3.src_right
  7.2 1.0 fusion.80
  8.2 1.8 convolution_bitcast_fusion
  10.0 1.8 convolution_bitcast_fusion.1
  11.8 1.8 convolution_bitcast_fusion.2
  13.6 0.8 reshape_squeeze.4.mask_ref
  14.4 0.7 pad_maximum_fusion.5
  15.2 0.7 collective-permute-start
  16.5 0.8 fusion.92
  18.1 1.0 copy.54.w_ref
  19.8 14.5 %shard_map.80.rest_0_ = f32[2,512,2048]{2,1,0:T(8,128)} custom-call(s32[8]{0:T(128)} %get-tuple-element.16.src_left, s32[16]{0:T(128)} %copy-done, s32[8]{0:T(128)} %get-tuple-element.17.tile_ref, s32[128]{0:T(128)} %copy-done.2, s32[8]{0:T(128)} %compare_convert_fusion.flag_ref, bf16[1024,2048]{1,0:T(8,128)(2,1)} %bitcast.4.g_ref, f32[1024,1]{1,0:T(8,128)} %copy.54.w_ref, ...), custom_call_target="tpu_custom_call" | custom-call | tf_op jit(solution)/shard_map/pallas_call | solution.py:78
  34.6 0.7 slice_bitcast_fusion.17
  35.3 6.0 %collective-permute-done.1 = f32[53760]{0:T(1024)S(1)} collective-permute-done((f32[53760]{0:T(1024)S(1)}, f32[53760]{0:T(1024)S(1)}, u32[]{:S(2)}, u32[]{:S(2)}) %collective-permute-start.1) | collective-permute-done | bytes 215072 | tf_op jit(solution)/shard_map/ppermute | solution.py:150
  41.8 1.3 collective-permute-start.4
  43.4 5.7 %collective-permute-done.4 = f32[3,128,128]{1,2,0:T(8,128)S(1)} collective-permute-done((f32[3,128,128]{1,2,0:T(8,128)S(1)}, f32[3,128,128]{1,2,0:T(8,128)S(1)}, u32[]{:S(2)}, u32[]{:S(2)}) %collective-permute-start.4) | collective-permute-done | bytes 196640 | tf_op jit(solution)/shard_map/ppermute | solution.py:208
  49.3 11.7 %cholesky.59 = f32[128,128]{1,0:T(8,128)S(1)} custom-call(f32[128,128]{1,0:T(8,128)S(1)} %fusion.57), custom_call_target="Cholesky" | custom-call | tf_op jit(solution)/shard_map/jit(cholesky)/cholesky | solution.py:95
  62.4 9.8 %custom-call.7 = f32[1,128,128]{1,2,0:T(8,128)S(1)} custom-call(f32[1,128,128]{2,1,0:T(8,128)S(1)} %fusion.35), custom_call_target="InvertDiagBlocksLowerTriangular" | custom-call | tf_op jit(solution)/shard_map/triangular_solve/custom-call.0 | solution.py:97
  73.7 1.5 collective-permute-start.5
  75.2 1.0 copy.55.w_ref
  76.8 3.6 %collective-permute-done.5 = f32[3,128,128]{2,1,0:T(8,128)S(1)} collective-permute-done((f32[3,128,128]{2,1,0:T(8,128)S(1)}, f32[3,128,128]{2,1,0:T(8,128)S(1)}, u32[]{:S(2)}, u32[]{:S(2)}) %collective-permute-start.5) | collective-permute-done | bytes 196640 | tf_op jit(solution)/shard_map/ppermute | solution.py:208
  80.7 11.7 %cholesky.70 = f32[128,128]{1,0:T(8,128)S(1)} custom-call(f32[128,128]{1,0:T(8,128)S(1)} %fusion.54), custom_call_target="Cholesky" | custom-call | tf_op jit(solution)/shard_map/jit(cholesky)/cholesky | solution.py:95
  92.4 40.6 %collective-permute-done.2.g_ref = bf16[1024,2048]{1,0:T(8,128)(2,1)} collective-permute-done((bf16[1024,2048]{1,0:T(8,128)(2,1)}, bf16[1024,2048]{1,0:T(8,128)(2,1)}, u32[]{:S(2)}, u32[]{:S(2)}) %collective-permute-start.2) | collective-permute-done | bytes 4194336 | tf_op jit(solution)/shard_map/ppermute | solution.py:150
  133.0 16.9 %shard_map.81 = f32[2,512,2048]{2,1,0:T(8,128)} custom-call(s32[8]{0:T(128)} %get-tuple-element.16.src_left, s32[16]{0:T(128)} %copy-done, s32[8]{0:T(128)} %get-tuple-element.17.tile_ref, s32[128]{0:T(128)} %fusion.86.mask_ref, s32[8]{0:T(128)} %compare_convert_fusion.flag_ref, ...), custom_call_target="tpu_custom_call", output_to_operand_aliasing={{}: (8, {})} | custom-call | tf_op jit(solution)/shard_map/pallas_call | solution.py:78
  149.9 4.7 %slice_bitcast_fusion = f32[512,2048]{1,0:T(8,128)} fusion(f32[2,512,2048]{2,1,0:T(8,128)} %shard_map.81), kind=kLoop, calls=%fused_computation.1 | loop fusion | bytes 8388608 | tf_op jit(solution)/shard_map/squeeze | solution.py:191
  154.6 1.7 collective-permute-start.3
  157.6 9.8 %custom-call.8 = f32[1,128,128]{1,2,0:T(8,128)S(1)} custom-call(f32[1,128,128]{2,1,0:T(8,128)S(1)} %fusion.36), custom_call_target="InvertDiagBlocksLowerTriangular" | custom-call | tf_op jit(solution)/shard_map/triangular_solve/custom-call.0 | solution.py:97
  168.8 1.5 collective-permute-start.6
  170.3 12.3 %collective-permute-done.6 = f32[3,128,128]{2,1,0:T(8,128)S(1)} collective-permute-done((f32[3,128,128]{2,1,0:T(8,128)S(1)}, f32[3,128,128]{2,1,0:T(8,128)S(1)}, u32[]{:S(2)}, u32[]{:S(2)}) %collective-permute-start.6) | collective-permute-done | bytes 196640 | tf_op jit(solution)/shard_map/ppermute | solution.py:208
  183.0 11.7 %cholesky.81 = f32[128,128]{1,0:T(8,128)S(1)} custom-call(f32[128,128]{1,0:T(8,128)S(1)} %fusion.52), custom_call_target="Cholesky" | custom-call | tf_op jit(solution)/shard_map/jit(cholesky)/cholesky | solution.py:95
  196.1 9.8 %custom-call.9 = f32[1,128,128]{1,2,0:T(8,128)S(1)} custom-call(f32[1,128,128]{2,1,0:T(8,128)S(1)} %fusion.37), custom_call_target="InvertDiagBlocksLowerTriangular" | custom-call | tf_op jit(solution)/shard_map/triangular_solve/custom-call.0 | solution.py:97
  207.2 0.7 maximum_bitcast_fusion
  207.9 6.6 %fusion.1 = f32[1,512,2048]{2,1,0:T(8,128)} fusion(f32[512,2048]{1,0:T(8,128)} %collective-permute-done.3, f32[2,512,2048]{2,1,0:T(8,128)} %shard_map.81), kind=kLoop, calls=%fused_computation.4 | loop fusion | flops 1048576 | bytes 12582912 | tf_op jit(solution)/shard_map/broadcast_in_dim | solution.py:215
  (86 shorter events, 13.1 us)
Async XLA Ops:
  0.6 17.5 %copy-start.1 = (f32[1,1024]{1,0:T(1,128)S(1)}, f32[1,1024]{1,0:T(1,128)}, u32[]{:S(2)}) copy-start(f32[1,1024]{1,0:T(1,128)} %param.10) | copy-start | bytes 12292
  1.4 18.4 %copy-start = (s32[16]{0:T(128)}, s32[16]{0:T(128)S(1)}, u32[]{:S(2)}) copy-start(s32[16]{0:T(128)S(1)} %select_reduce_fusion.3.src_right) | copy-start | bytes 196
  14.4 5.4 %copy-start.2 = (s32[128]{0:T(128)}, s32[128]{0:T(128)S(1)}, u32[]{:S(2)}) copy-start(s32[128]{0:T(128)S(1)} %reshape_squeeze.4.mask_ref) | copy-start | bytes 1540
  15.2 19.1 %collective-permute-start = (f32[53760]{0:T(1024)S(1)}, f32[53760]{0:T(1024)S(1)}, u32[]{:S(2)}, u32[]{:S(2)}) collective-permute-start(f32[53760]{0:T(1024)S(1)} %pad_maximum_fusion), channel_id=1, source_target_pairs={{0,1},{1,0},{2,3},{3,2},{4,5},{5,4},{6,7},{7,6},{8,9},{9,8},{10,11... | collective-permute-start | bytes 645128 | tf_op jit(solution)/shard_map/ppermute | solution.py:150
  34.3 7.0 %collective-permute-start.1 = (f32[53760]{0:T(1024)S(1)}, f32[53760]{0:T(1024)S(1)}, u32[]{:S(2)}, u32[]{:S(2)}) collective-permute-start(f32[53760]{0:T(1024)S(1)} %fusion.90), channel_id=1, source_target_pairs={{0,2},{1,3},{2,0},{3,1},{4,6},{5,7},{6,4},{7,5},{8,10},{9,11},{10,... | collective-permute-start | bytes 645128 | tf_op jit(solution)/shard_map/ppermute | solution.py:150
  41.4 91.7 %collective-permute-start.2 = (bf16[1024,2048]{1,0:T(8,128)(2,1)}, bf16[1024,2048]{1,0:T(8,128)(2,1)}, u32[]{:S(2)}, u32[]{:S(2)}) collective-permute-start(bf16[1024,2048]{1,0:T(8,128)(2,1)} %bitcast.4.g_ref), channel_id=1, source_target_pairs={{0,2},{1,3},{2,0},{3,1},{4,6},{5,7},{6,4},{7,5},{8,10},{9,11},{10,... | collective-permute-start | bytes 12582920 | tf_op jit(solution)/shard_map/ppermute | solution.py:150
  41.8 7.3 %collective-permute-start.4 = (f32[3,128,128]{1,2,0:T(8,128)S(1)}, f32[3,128,128]{1,2,0:T(8,128)S(1)}, u32[]{:S(2)}, u32[]{:S(2)}) collective-permute-start(f32[3,128,128]{1,2,0:T(8,128)S(1)} %copy.56), channel_id=1, source_target_pairs={{0,4},{4,8},{8,12},{12,16},{16,20},{20,24},{24,28},{1,5},{5,9},{9,... | collective-permute-start | bytes 589832 | tf_op jit(solution)/shard_map/ppermute | solution.py:208
  73.7 6.8 %collective-permute-start.5 = (f32[3,128,128]{2,1,0:T(8,128)S(1)}, f32[3,128,128]{2,1,0:T(8,128)S(1)}, u32[]{:S(2)}, u32[]{:S(2)}) collective-permute-start(f32[3,128,128]{2,1,0:T(8,128)S(1)} %pad_maximum_fusion.3), channel_id=1, source_target_pairs={{0,8},{4,12},{8,16},{12,20},{16,24},{20,28},{1,9},{5,13},{9,17},{1... | collective-permute-start | bytes 589832 | tf_op jit(solution)/shard_map/ppermute | solution.py:208
  154.6 53.3 %collective-permute-start.3 = (f32[512,2048]{1,0:T(8,128)}, f32[512,2048]{1,0:T(8,128)}, u32[]{:S(2)}, u32[]{:S(2)}) collective-permute-start(f32[512,2048]{1,0:T(8,128)} %slice_bitcast_fusion), channel_id=1, source_target_pairs={{0,1},{1,0},{2,3},{3,2},{4,5},{5,4},{6,7},{7,6},{8,9},{9,8},{10,11... | collective-permute-start | bytes 12582920 | tf_op jit(solution)/shard_map/ppermute | solution.py:150
  168.8 13.9 %collective-permute-start.6 = (f32[3,128,128]{2,1,0:T(8,128)S(1)}, f32[3,128,128]{2,1,0:T(8,128)S(1)}, u32[]{:S(2)}, u32[]{:S(2)}) collective-permute-start(f32[3,128,128]{2,1,0:T(8,128)S(1)} %pad_maximum_fusion.4), channel_id=1, source_target_pairs={{0,16},{4,20},{8,24},{12,28},{1,17},{5,21},{9,25},{13,29},{2,18},{... | collective-permute-start | bytes 589832 | tf_op jit(solution)/shard_map/ppermute | solution.py:208

commit v11 on v10

--- a/solution.py
+++ b/solution.py
@@ -149,7 +149,6 @@
     def exchange(value, step):
         return lax.ppermute(value, "row", [(src, src ^ step) for src in range(owners)])
 
-    kernel_slab, part_pieces = lax.optimization_barrier((local_slab, part_pieces))
     packed_side = jnp.concatenate([row_weights, live_blocks.reshape(-1).astype(jnp.float32)])
     side_slots = jnp.zeros((owners, packed_side.shape[0]), jnp.float32)
     side_slots = lax.dynamic_update_index_in_dim(side_slots, packed_side, my_index, 0)
@@ -160,6 +159,7 @@
         summed_all = summed_all + exchange(summed_all, 2)
     else:
         summed_all = lax.psum(summed_all, "row")
+    kernel_slab, summed_all = lax.optimization_barrier((local_slab, summed_all))
     summed = summed_all[:piece_count].reshape(part_pieces.shape)
     every_side = summed_all[piece_count:].reshape(side_slots.shape)
     eye = jnp.eye(BLK, dtype=jnp.float32)
@@ -170,8 +170,7 @@
     ])
 
     if owners == 4:
-        send_slab, summed_all = lax.optimization_barrier((local_slab, summed_all))
-        across_slab = exchange(send_slab, 2)
+        across_slab = exchange(kernel_slab, 2)
         across_side = lax.dynamic_index_in_dim(every_side, my_index ^ 2, 0, False)
         across_weights = across_side[:slab_height]
         across_live = across_side[slab_height:].reshape(live_blocks.shape).astype(jnp.int32)

time: 215 us -> 201 us (0.935)
  the two profiles are of different devices: /device:TPU:31 before, /device:TPU:25 now
where the time goes in v11:
time: 201 us; the launch traced here: 200 us
  other arithmetic  80.5 us (40%)
  waiting for transfers between devices  49.8 us (25%)
  Pallas kernels  31.4 us (16%)
  local copies, waits for them, and re-layouts  11.7 us (6%)
  starting transfers between devices  11.1 us (6%)
  matrix products  8.87 us (4%)
  between operations  6.35 us (3%)
    another operation x9, other arithmetic, join_segments(): factor = jnp.linalg.cholesky(middle)  37.2 us
    pallas_call x2, Pallas kernels, gram_rows(): pl.pallas_call(gram_kernel, grid_spec=grid_spec, out_shape=jax.ShapeDtype...  31.4 us
    another operation x6, other arithmetic, join_segments(): lax.linalg.triangular_solve(factor, jnp.concatenate([cross_one.T, cross_t...  31.4 us
    ppermute x4, waiting for transfers between devices, exchange(): lax.ppermute(value, 'row', [(src, src ^ step) for src in range(owners)])  29.2 us
    ppermute x3, waiting for transfers between devices, local(): moved = lax.ppermute(jnp.stack(running), 'tm', pairs)  20.6 us
    broadcast_in_dim x1, other arithmetic, local(): return (owned[None], chain_out)  6.57 us
    ppermute x3, starting transfers between devices, local(): moved = lax.ppermute(jnp.stack(running), 'tm', pairs)  6.07 us
    dot_general x3, matrix products, contract_rows(): lax.dot_general(left_cols, right_cols, (((0,), (0,)), ((), ())), preferre...  5.34 us
  transfers between devices with their start and end apart: 7, of which 5 were waited for; matrix products, arithmetic and copies ran while one was open for 40% of the time, Pallas kernels for 7%

profile of v11, /device:TPU:25, one launch (start us, length us, event | category | flops | bytes accessed | tf_op | source)
XLA Modules:
  0.0 199.8 jit_solution(15344294055930048391)
XLA Ops:
  0.6 0.8 select_reduce_fusion.3.src_right
  7.2 1.0 fusion.78
  8.2 1.8 convolution_bitcast_fusion
  10.0 1.8 convolution_bitcast_fusion.1
  11.8 1.8 convolution_bitcast_fusion.2
  13.6 0.8 reshape_squeeze.4.mask_ref
  14.4 0.7 pad_maximum_fusion.5
  15.2 0.7 collective-permute-start
  16.5 0.8 fusion.90
  18.1 1.0 copy.54.w_ref
  19.8 1.3 collective-permute-start.1
  21.8 5.0 %collective-permute-done.1 = f32[53760]{0:T(1024)S(1)} collective-permute-done((f32[53760]{0:T(1024)S(1)}, f32[53760]{0:T(1024)S(1)}, u32[]{:S(2)}, u32[]{:S(2)}) %collective-permute-start.1) | collective-permute-done | bytes 215072 | tf_op jit(solution)/shard_map/ppermute | solution.py:150
  26.8 1.3 collective-permute-start.2
  28.2 14.5 %shard_map.80.rest_0_ = f32[2,512,2048]{2,1,0:T(8,128)} custom-call(s32[8]{0:T(128)} %get-tuple-element.14.src_left, s32[16]{0:T(128)} %copy-done, s32[8]{0:T(128)} %get-tuple-element.15.tile_ref, s32[128]{0:T(128)} %copy-done.2, s32[8]{0:T(128)} %compare_convert_fusion.flag_ref, bf16[1024,2048]{1,0:T(8,128)(2,1)} %bitcast.171, f32[1024,1]{1,0:T(8,128)} %copy.54.w_ref, ...), custom_call_target="tpu_custom_call" | custom-call | tf_op jit(solution)/shard_map/pallas_call | solution.py:78
  42.9 3.1 %collective-permute-start.4 = (f32[3,128,128]{1,2,0:T(8,128)S(1)}, f32[3,128,128]{1,2,0:T(8,128)S(1)}, u32[]{:S(2)}, u32[]{:S(2)}) collective-permute-start(f32[3,128,128]{1,2,0:T(8,128)S(1)} %copy.56), channel_id=1, source_target_pairs={{0,4},{4,8},{8,12},{12,16},{16,20},{20,24},{24,28},{1,5},{5,9},{9,... | collective-permute-start | bytes 589832 | tf_op jit(solution)/shard_map/ppermute | solution.py:207
  46.2 4.8 %collective-permute-done.4 = f32[3,128,128]{1,2,0:T(8,128)S(1)} collective-permute-done((f32[3,128,128]{1,2,0:T(8,128)S(1)}, f32[3,128,128]{1,2,0:T(8,128)S(1)}, u32[]{:S(2)}, u32[]{:S(2)}) %collective-permute-start.4) | collective-permute-done | bytes 196640 | tf_op jit(solution)/shard_map/ppermute | solution.py:207
  51.3 11.7 %cholesky.59 = f32[128,128]{1,0:T(8,128)S(1)} custom-call(f32[128,128]{1,0:T(8,128)S(1)} %fusion.53), custom_call_target="Cholesky" | custom-call | tf_op jit(solution)/shard_map/jit(cholesky)/cholesky | solution.py:95
  64.3 9.8 %custom-call.7 = f32[1,128,128]{1,2,0:T(8,128)S(1)} custom-call(f32[1,128,128]{2,1,0:T(8,128)S(1)} %fusion.35), custom_call_target="InvertDiagBlocksLowerTriangular" | custom-call | tf_op jit(solution)/shard_map/triangular_solve/custom-call.0 | solution.py:97
  75.6 1.5 collective-permute-start.5
  77.1 1.0 copy.55.w_ref
  78.8 3.6 %collective-permute-done.5 = f32[3,128,128]{2,1,0:T(8,128)S(1)} collective-permute-done((f32[3,128,128]{2,1,0:T(8,128)S(1)}, f32[3,128,128]{2,1,0:T(8,128)S(1)}, u32[]{:S(2)}, u32[]{:S(2)}) %collective-permute-start.5) | collective-permute-done | bytes 196640 | tf_op jit(solution)/shard_map/ppermute | solution.py:207
  82.7 11.7 %cholesky.70 = f32[128,128]{1,0:T(8,128)S(1)} custom-call(f32[128,128]{1,0:T(8,128)S(1)} %fusion.50), custom_call_target="Cholesky" | custom-call | tf_op jit(solution)/shard_map/jit(cholesky)/cholesky | solution.py:95
  94.4 24.2 %collective-permute-done.2.g_ref = bf16[1024,2048]{1,0:T(8,128)(2,1)} collective-permute-done((bf16[1024,2048]{1,0:T(8,128)(2,1)}, bf16[1024,2048]{1,0:T(8,128)(2,1)}, u32[]{:S(2)}, u32[]{:S(2)}) %collective-permute-start.2) | collective-permute-done | bytes 4194336 | tf_op jit(solution)/shard_map/ppermute | solution.py:150
  118.5 16.9 %shard_map.81 = f32[2,512,2048]{2,1,0:T(8,128)} custom-call(s32[8]{0:T(128)} %get-tuple-element.14.src_left, s32[16]{0:T(128)} %copy-done, s32[8]{0:T(128)} %get-tuple-element.15.tile_ref, s32[128]{0:T(128)} %fusion.84.mask_ref, s32[8]{0:T(128)} %compare_convert_fusion.flag_ref, ...), custom_call_target="tpu_custom_call", output_to_operand_aliasing={{}: (8, {})} | custom-call | tf_op jit(solution)/shard_map/pallas_call | solution.py:78
  135.4 4.7 %slice_bitcast_fusion = f32[512,2048]{1,0:T(8,128)} fusion(f32[2,512,2048]{2,1,0:T(8,128)} %shard_map.81), kind=kLoop, calls=%fused_computation.1 | loop fusion | bytes 8388608 | tf_op jit(solution)/shard_map/squeeze | solution.py:190
  140.1 1.7 collective-permute-start.3
  143.1 9.8 %custom-call.8 = f32[1,128,128]{1,2,0:T(8,128)S(1)} custom-call(f32[1,128,128]{2,1,0:T(8,128)S(1)} %fusion.36), custom_call_target="InvertDiagBlocksLowerTriangular" | custom-call | tf_op jit(solution)/shard_map/triangular_solve/custom-call.0 | solution.py:97
  154.3 1.5 collective-permute-start.6
  155.8 12.2 %collective-permute-done.6 = f32[3,128,128]{2,1,0:T(8,128)S(1)} collective-permute-done((f32[3,128,128]{2,1,0:T(8,128)S(1)}, f32[3,128,128]{2,1,0:T(8,128)S(1)}, u32[]{:S(2)}, u32[]{:S(2)}) %collective-permute-start.6) | collective-permute-done | bytes 196640 | tf_op jit(solution)/shard_map/ppermute | solution.py:207
  168.4 11.7 %cholesky.81 = f32[128,128]{1,0:T(8,128)S(1)} custom-call(f32[128,128]{1,0:T(8,128)S(1)} %fusion.48), custom_call_target="Cholesky" | custom-call | tf_op jit(solution)/shard_map/jit(cholesky)/cholesky | solution.py:95
  181.4 9.8 %custom-call.9 = f32[1,128,128]{1,2,0:T(8,128)S(1)} custom-call(f32[1,128,128]{2,1,0:T(8,128)S(1)} %fusion.37), custom_call_target="InvertDiagBlocksLowerTriangular" | custom-call | tf_op jit(solution)/shard_map/triangular_solve/custom-call.0 | solution.py:97
  193.3 6.6 %fusion.1 = f32[1,512,2048]{2,1,0:T(8,128)} fusion(f32[512,2048]{1,0:T(8,128)} %collective-permute-done.3, f32[2,512,2048]{2,1,0:T(8,128)} %shard_map.81), kind=kLoop, calls=%fused_computation.4 | loop fusion | flops 1048576 | bytes 12582912 | tf_op jit(solution)/shard_map/broadcast_in_dim | solution.py:214
  (86 shorter events, 13.9 us)
Async XLA Ops:
  0.6 17.5 %copy-start.1 = (f32[1,1024]{1,0:T(1,128)S(1)}, f32[1,1024]{1,0:T(1,128)}, u32[]{:S(2)}) copy-start(f32[1,1024]{1,0:T(1,128)} %param.10) | copy-start | bytes 12292
  1.4 26.8 %copy-start = (s32[16]{0:T(128)}, s32[16]{0:T(128)S(1)}, u32[]{:S(2)}) copy-start(s32[16]{0:T(128)S(1)} %select_reduce_fusion.3.src_right) | copy-start | bytes 196
  14.4 13.8 %copy-start.2 = (s32[128]{0:T(128)}, s32[128]{0:T(128)S(1)}, u32[]{:S(2)}) copy-start(s32[128]{0:T(128)S(1)} %reshape_squeeze.4.mask_ref) | copy-start | bytes 1540
  15.2 4.5 %collective-permute-start = (f32[53760]{0:T(1024)S(1)}, f32[53760]{0:T(1024)S(1)}, u32[]{:S(2)}, u32[]{:S(2)}) collective-permute-start(f32[53760]{0:T(1024)S(1)} %pad_maximum_fusion), channel_id=1, source_target_pairs={{0,1},{1,0},{2,3},{3,2},{4,5},{5,4},{6,7},{7,6},{8,9},{9,8},{10,11... | collective-permute-start | bytes 645128 | tf_op jit(solution)/shard_map/ppermute | solution.py:150
  19.8 7.0 %collective-permute-start.1 = (f32[53760]{0:T(1024)S(1)}, f32[53760]{0:T(1024)S(1)}, u32[]{:S(2)}, u32[]{:S(2)}) collective-permute-start(f32[53760]{0:T(1024)S(1)} %fusion.88), channel_id=1, source_target_pairs={{0,2},{1,3},{2,0},{3,1},{4,6},{5,7},{6,4},{7,5},{8,10},{9,11},{10,... | collective-permute-start | bytes 645128 | tf_op jit(solution)/shard_map/ppermute | solution.py:150
  26.8 91.7 %collective-permute-start.2 = (bf16[1024,2048]{1,0:T(8,128)(2,1)}, bf16[1024,2048]{1,0:T(8,128)(2,1)}, u32[]{:S(2)}, u32[]{:S(2)}) collective-permute-start(bf16[1024,2048]{1,0:T(8,128)(2,1)} %bitcast.170), channel_id=1, source_target_pairs={{0,2},{1,3},{2,0},{3,1},{4,6},{5,7},{6,4},{7,5},{8,10},{9,11},{10,... | collective-permute-start | bytes 12582920 | tf_op jit(solution)/shard_map/ppermute | solution.py:150
  42.9 8.1 %collective-permute-start.4 = (f32[3,128,128]{1,2,0:T(8,128)S(1)}, f32[3,128,128]{1,2,0:T(8,128)S(1)}, u32[]{:S(2)}, u32[]{:S(2)}) collective-permute-start(f32[3,128,128]{1,2,0:T(8,128)S(1)} %copy.56), channel_id=1, source_target_pairs={{0,4},{4,8},{8,12},{12,16},{16,20},{20,24},{24,28},{1,5},{5,9},{9,... | collective-permute-start | bytes 589832 | tf_op jit(solution)/shard_map/ppermute | solution.py:207
  75.6 6.8 %collective-permute-start.5 = (f32[3,128,128]{2,1,0:T(8,128)S(1)}, f32[3,128,128]{2,1,0:T(8,128)S(1)}, u32[]{:S(2)}, u32[]{:S(2)}) collective-permute-start(f32[3,128,128]{2,1,0:T(8,128)S(1)} %pad_maximum_fusion.3), channel_id=1, source_target_pairs={{0,8},{4,12},{8,16},{12,20},{16,24},{20,28},{1,9},{5,13},{9,17},{1... | collective-permute-start | bytes 589832 | tf_op jit(solution)/shard_map/ppermute | solution.py:207
  140.1 53.2 %collective-permute-start.3 = (f32[512,2048]{1,0:T(8,128)}, f32[512,2048]{1,0:T(8,128)}, u32[]{:S(2)}, u32[]{:S(2)}) collective-permute-start(f32[512,2048]{1,0:T(8,128)} %slice_bitcast_fusion), channel_id=1, source_target_pairs={{0,1},{1,0},{2,3},{3,2},{4,5},{5,4},{6,7},{7,6},{8,9},{9,8},{10,11... | collective-permute-start | bytes 12582920 | tf_op jit(solution)/shard_map/ppermute | solution.py:150
  154.3 13.8 %collective-permute-start.6 = (f32[3,128,128]{2,1,0:T(8,128)S(1)}, f32[3,128,128]{2,1,0:T(8,128)S(1)}, u32[]{:S(2)}, u32[]{:S(2)}) collective-permute-start(f32[3,128,128]{2,1,0:T(8,128)S(1)} %pad_maximum_fusion.4), channel_id=1, source_target_pairs={{0,16},{4,20},{8,24},{12,28},{1,17},{5,21},{9,25},{13,29},{2,18},{... | collective-permute-start | bytes 589832 | tf_op jit(solution)/shard_map/ppermute | solution.py:207

commit v12 on v2

--- a/solution.py
+++ b/solution.py
@@ -49,7 +49,7 @@
     col_blocks = L // BLK
     grid_spec = pltpu.PrefetchScalarGridSpec(
         num_scalar_prefetch=5,
-        grid=(col_blocks,),
+        grid=(src_left.shape[0],),
         in_specs=[
             pl.BlockSpec((height, L), lambda k, *_: (0, 0)),
             pl.BlockSpec((height, 1), lambda k, *_: (0, 0)),
@@ -61,7 +61,7 @@
     return pl.pallas_call(
         gram_kernel,
         grid_spec=grid_spec,
-        out_shape=jax.ShapeDtypeStruct((L, L), jnp.float32),
+        out_shape=jax.ShapeDtypeStruct((src_left.shape[0] * BLK, L), jnp.float32),
         compiler_params=pltpu.CompilerParams(vmem_limit_bytes=56 * 1024 * 1024),
     )(src_left, src_right, tile_order, live_blocks.reshape(-1), flag.reshape(1),
       slab, weights.reshape(height, 1), diagonal.reshape(col_blocks, BLK))
@@ -149,11 +149,21 @@
     chain_out = jnp.stack(running)[None]
 
     flag = (my_index == 0).astype(jnp.int32)
-    partial = gram_rows(
-        local_slab, row_weights, live_blocks, jnp.take(source, tile_order), source,
-        tile_order, diagonal, flag,
-    )
-    owned = lax.psum_scatter(partial, "row", scatter_dimension=0, tiled=True)
+    owners = lax.axis_size("row")
+    own_blocks = block_count // owners
+    half = max(own_blocks // 2, 1)
+    by_owner = tile_order.reshape(owners, own_blocks)
+    pieces = []
+    for lo, hi in ((0, half), (half, own_blocks)):
+        if lo == hi:
+            continue
+        order = by_owner[:, lo:hi].reshape(-1)
+        partial = gram_rows(
+            local_slab, row_weights, live_blocks, jnp.take(source, order), source,
+            order, diagonal, flag,
+        )
+        pieces.append(lax.psum_scatter(partial, "row", scatter_dimension=0, tiled=True))
+    owned = jnp.concatenate(pieces, axis=0) if len(pieces) > 1 else pieces[0]
     return (owned[None], chain_out)
 
 

time: 193 us -> 217 us (1.12)
  waiting for transfers between devices: 46 us -> 54.7 us
  Pallas kernels: 21.8 us -> 29.1 us
  other arithmetic: 74.1 us -> 78.7 us
    reduce_scatter x1 -> x2, waiting for transfers between devices: 28.7 us -> 44.8 us  [local(): lax.psum_scatter(partial, 'row', scatter_dimension=0, tiled=True)]
    psum x1, waiting for transfers between devices: 8.45 us -> 0.01 us  [local(): summed = lax.psum(part_pieces, 'row')]
    pallas_call x1 -> x2, Pallas kernels: 21.8 us -> 29.1 us  [gram_rows(): pl.pallas_call(gram_kernel, grid_spec=grid_spec, out_shape=jax.ShapeDtype...]
    broadcast_in_dim x0 -> x1, other arithmetic: none -> 4.73 us  [local(): return (owned[None], chain_out)]
  transfers between devices with their start and end apart: 5 -> 6, of which waited for: 5 -> 4; matrix products, arithmetic and copies ran while one was open for 42% -> 38% of each run, Pallas kernels for 11% -> 13%
where the time goes in v12:
time: 217 us; the launch traced here: 216 us
  other arithmetic  78.7 us (36%)
  waiting for transfers between devices  54.7 us (25%)
  Pallas kernels  29.1 us (13%)
  between operations  19.4 us (9%)
  starting transfers between devices  16.2 us (7%)
  matrix products  11.1 us (5%)
  local copies, waits for them, and re-layouts  7.06 us (3%)
    reduce_scatter x2, waiting for transfers between devices, local(): lax.psum_scatter(partial, 'row', scatter_dimension=0, tiled=True)  44.8 us
    another operation x9, other arithmetic, join_segments(): factor = jnp.linalg.cholesky(middle)  37.2 us
    another operation x6, other arithmetic, join_segments(): jax.scipy.linalg.cho_solve((factor, True), jnp.concatenate([cross_one.T,...  31.4 us
    pallas_call x2, Pallas kernels, gram_rows(): pl.pallas_call(gram_kernel, grid_spec=grid_spec, out_shape=jax.ShapeDtype...  29.1 us
    ppermute x3, starting transfers between devices, local(): moved = lax.ppermute(jnp.stack(running), 'tm', pairs)  16.1 us
    ppermute x3, waiting for transfers between devices, local(): moved = lax.ppermute(jnp.stack(running), 'tm', pairs)  9.92 us
    dot_general x3, matrix products, contract_rows(): lax.dot_general(left_cols, right_cols, (((0,), (0,)), ((), ())), preferre...  5.6 us
    broadcast_in_dim x1, other arithmetic, local(): return (owned[None], chain_out)  4.73 us
  transfers between devices with their start and end apart: 6, of which 4 were waited for; matrix products, arithmetic and copies ran while one was open for 38% of the time, Pallas kernels for 13%

profile of v12, /device:TPU:0, one launch (start us, length us, event | category | flops | bytes accessed | tf_op | source)
XLA Modules:
  0.0 216.3 jit_solution(16451217544184071634)
XLA Ops:
  7.2 0.8 select_reduce_fusion.3.src_right
  13.8 1.0 fusion.100
  14.8 1.9 convolution_bitcast_fusion
  16.7 1.9 convolution_bitcast_fusion.1
  18.6 1.9 convolution_bitcast_fusion.2
  20.5 0.7 pad_maximum_fusion
  21.2 0.7 reshape.200
  24.0 1.0 copy.57.w_ref
  25.0 14.5 %shard_map.81 = f32[1024,2048]{1,0:T(8,128)} custom-call(s32[8]{0:T(128)} %and_select_fusion.src_left, s32[16]{0:T(128)} %copy-done, s32[8]{0:T(128)} %copy-done.4, s32[128]{0:T(128)} %reshape_squeeze.12.mask_ref, s32[1]{0:T(128)} %bitcast.1.flag_ref, bf16[1024,2048]{1,0:T(8,128)(2,1)} %bitcast.172, f32[1024,1]{1,0:T(8,128)} %copy.57.w_ref, f32[16,128]{1,0:T(8,128)} %bitcast.180), custom_call_target="tpu_custom_call" | custom-call | tf_op jit(solution)/shard_map/pallas_call | solution.py:61
  41.3 14.6 %shard_map.80 = f32[1024,2048]{1,0:T(8,128)} custom-call(s32[8]{0:T(128)} %and_select_fusion.1.src_left, s32[16]{0:T(128)} %copy-done, s32[8]{0:T(128)} %copy-done.3, s32[128]{0:T(128)} %reshape_squeeze.12.mask_ref, s32[1]{0:T(128)} %bitcast.1.flag_ref, bf16[1024,2048]{1,0:T(8,128)(2,1)} %bitcast.173, f32[1024,1]{1,0:T(8,128)} %copy.57.w_ref, ...), custom_call_target="tpu_custom_call" | custom-call | tf_op jit(solution)/shard_map/pallas_call | solution.py:61
  55.9 0.7 slice_bitcast_fusion.12
  56.6 1.0 slice_bitcast_fusion.7
  57.8 4.9 %collective-permute-start = (f32[3,128,128]{2,1,0:T(8,128)S(1)}, f32[3,128,128]{2,1,0:T(8,128)S(1)}, u32[]{:S(2)}, u32[]{:S(2)}) collective-permute-start(f32[3,128,128]{2,1,0:T(8,128)S(1)} %copy.62), channel_id=1, source_target_pairs={{0,4},{4,8},{8,12},{12,16},{16,20},{20,24},{24,28},{1,5},{5,9},{9,... | collective-permute-start | bytes 589832 | tf_op jit(solution)/shard_map/ppermute | solution.py:143
  62.9 3.9 %collective-permute-done = f32[3,128,128]{2,1,0:T(8,128)S(1)} collective-permute-done((f32[3,128,128]{2,1,0:T(8,128)S(1)}, f32[3,128,128]{2,1,0:T(8,128)S(1)}, u32[]{:S(2)}, u32[]{:S(2)}) %collective-permute-start) | collective-permute-done | bytes 196640 | tf_op jit(solution)/shard_map/ppermute | solution.py:143
  67.1 11.7 %cholesky.59 = f32[128,128]{1,0:T(8,128)S(1)} custom-call(f32[128,128]{1,0:T(8,128)S(1)} %copy.67), custom_call_target="Cholesky" | custom-call | tf_op jit(solution)/shard_map/jit(cholesky)/cholesky | solution.py:78
  79.5 0.7 fusion.33
  80.2 9.8 %custom-call.9 = f32[1,128,128]{1,2,0:T(8,128)S(1)} custom-call(f32[1,128,128]{2,1,0:T(8,128)S(1)} %fusion.33), custom_call_target="InvertDiagBlocksLowerTriangular" | custom-call | tf_op jit(solution)/shard_map/jit(_cho_solve)/triangular_solve | solution.py:80
  90.6 1.1 fusion.7
  92.1 1.0 fusion.6
  93.1 5.5 %collective-permute-start.1 = (f32[3,128,128]{2,1,0:T(8,128)S(1)}, f32[3,128,128]{2,1,0:T(8,128)S(1)}, u32[]{:S(2)}, u32[]{:S(2)}) collective-permute-start(f32[3,128,128]{2,1,0:T(8,128)S(1)} %pad_maximum_fusion.2), channel_id=1, source_target_pairs={{0,8},{4,12},{8,16},{12,20},{16,24},{20,28},{1,9},{5,13},{9,17},{1... | collective-permute-start | bytes 589832 | tf_op jit(solution)/shard_map/ppermute | solution.py:143
  98.7 3.0 %collective-permute-done.1 = f32[3,128,128]{2,1,0:T(8,128)S(1)} collective-permute-done((f32[3,128,128]{2,1,0:T(8,128)S(1)}, f32[3,128,128]{2,1,0:T(8,128)S(1)}, u32[]{:S(2)}, u32[]{:S(2)}) %collective-permute-start.1) | collective-permute-done | bytes 196640 | tf_op jit(solution)/shard_map/ppermute | solution.py:143
  102.0 11.7 %cholesky.70 = f32[128,128]{1,0:T(8,128)S(1)} custom-call(f32[128,128]{1,0:T(8,128)S(1)} %fusion.65), custom_call_target="Cholesky" | custom-call | tf_op jit(solution)/shard_map/jit(cholesky)/cholesky | solution.py:78
  114.4 0.7 fusion.34
  115.0 9.8 %custom-call.10 = f32[1,128,128]{1,2,0:T(8,128)S(1)} custom-call(f32[1,128,128]{2,1,0:T(8,128)S(1)} %fusion.34), custom_call_target="InvertDiagBlocksLowerTriangular" | custom-call | tf_op jit(solution)/shard_map/jit(_cho_solve)/triangular_solve | solution.py:80
  126.3 5.6 %collective-permute-start.2 = (f32[3,128,128]{2,1,0:T(8,128)S(1)}, f32[3,128,128]{2,1,0:T(8,128)S(1)}, u32[]{:S(2)}, u32[]{:S(2)}) collective-permute-start(f32[3,128,128]{2,1,0:T(8,128)S(1)} %pad_maximum_fusion.3), channel_id=1, source_target_pairs={{0,16},{4,20},{8,24},{12,28},{1,17},{5,21},{9,25},{13,29},{2,18},{... | collective-permute-start | bytes 589832 | tf_op jit(solution)/shard_map/ppermute | solution.py:143
  132.0 3.0 %collective-permute-done.2 = f32[3,128,128]{2,1,0:T(8,128)S(1)} collective-permute-done((f32[3,128,128]{2,1,0:T(8,128)S(1)}, f32[3,128,128]{2,1,0:T(8,128)S(1)}, u32[]{:S(2)}, u32[]{:S(2)}) %collective-permute-start.2) | collective-permute-done | bytes 196640 | tf_op jit(solution)/shard_map/ppermute | solution.py:143
  135.3 11.7 %cholesky.81 = f32[128,128]{1,0:T(8,128)S(1)} custom-call(f32[128,128]{1,0:T(8,128)S(1)} %fusion.55), custom_call_target="Cholesky" | custom-call | tf_op jit(solution)/shard_map/jit(cholesky)/cholesky | solution.py:78
  147.7 0.7 fusion.35
  148.3 9.8 %custom-call.11 = f32[1,128,128]{1,2,0:T(8,128)S(1)} custom-call(f32[1,128,128]{2,1,0:T(8,128)S(1)} %fusion.35), custom_call_target="InvertDiagBlocksLowerTriangular" | custom-call | tf_op jit(solution)/shard_map/jit(_cho_solve)/triangular_solve | solution.py:80
  159.6 0.7 maximum_bitcast_fusion.1
  160.3 44.8 %reduce-scatter.3.cloned.1.call-done = f32[256,2048]{1,0:T(8,128)} async-done(((f32[1024,2048]{1,0:T(8,128)}), f32[256,2048]{1,0:T(8,128)}) %reduce-scatter.3.cloned.1.call-update) | async-done | bytes 2097168 | tf_op jit(solution)/shard_map/reduce_scatter | solution.py:165
  205.0 4.7 %maximum_bitcast_fusion = f32[1,512,2048]{2,1,0:T(8,128)} fusion(f32[256,2048]{1,0:T(8,128)} %reduce-scatter.5.cloned.1.call-done, f32[256,2048]{1,0:T(8,128)} %reduce-scatter.3.cloned.1.call-done), kind=kLoop, calls=%fused_computation.2 | loop fusion | flops 1048576 | bytes 8388608 | tf_op jit(solution)/shard_map/broadcast_in_dim | solution.py:167
  (82 shorter events, 11.4 us)
Async XLA Ops:
  7.2 16.3 %copy-start.2 = (s32[1,8,16]{2,1,0:T(8,128)S(1)}, s32[1,8,16]{2,1,0:T(8,128)}, u32[]{:S(2)}) copy-start(s32[1,8,16]{2,1,0:T(8,128)} %param.13) | copy-start | bytes 1540
  7.2 16.8 %copy-start.5 = (f32[1,1024]{1,0:T(1,128)S(1)}, f32[1,1024]{1,0:T(1,128)}, u32[]{:S(2)}) copy-start(f32[1,1024]{1,0:T(1,128)} %param.12) | copy-start | bytes 12292
  7.2 49.4 %all-reduce.2.cloned.1.call-start = ((), (), s32[]{:S(2)}) async-start(), calls=%async_computation.4 | async-start | bytes 393216 | tf_op jit(solution)/shard_map/psum | solution.py:129
  8.0 17.0 %copy-start = (s32[16]{0:T(128)}, s32[16]{0:T(128)S(1)}, u32[]{:S(2)}) copy-start(s32[16]{0:T(128)S(1)} %select_reduce_fusion.3.src_right) | copy-start | bytes 196
  21.2 139.1 %reduce-scatter.5.cloned.1.call-start = ((), (), s32[]{:S(2)}) async-start(), calls=%async_computation.3 | async-start | bytes 10485760 | tf_op jit(solution)/shard_map/reduce_scatter | solution.py:165
  22.1 2.9 %copy-start.4 = (s32[8]{0:T(128)}, s32[8]{0:T(128)S(1)}, u32[]{:S(2)}) copy-start(s32[8]{0:T(128)S(1)} %reshape.204.tile_ref) | copy-start | bytes 100
  22.2 18.6 %copy-start.3 = (s32[8]{0:T(128)}, s32[8]{0:T(128)S(1)}, u32[]{:S(2)}) copy-start(s32[8]{0:T(128)S(1)} %reshape.201.tile_ref) | copy-start | bytes 100
  39.5 0.6 copy-start.1
  39.6 165.5 %reduce-scatter.3.cloned.1.call-start = ((), (), s32[]{:S(2)}) async-start(), calls=%async_computation.2 | async-start | bytes 10485760 | tf_op jit(solution)/shard_map/reduce_scatter | solution.py:165
  57.8 9.0 %collective-permute-start = (f32[3,128,128]{2,1,0:T(8,128)S(1)}, f32[3,128,128]{2,1,0:T(8,128)S(1)}, u32[]{:S(2)}, u32[]{:S(2)}) collective-permute-start(f32[3,128,128]{2,1,0:T(8,128)S(1)} %copy.62), channel_id=1, source_target_pairs={{0,4},{4,8},{8,12},{12,16},{16,20},{20,24},{24,28},{1,5},{5,9},{9,... | collective-permute-start | bytes 589832 | tf_op jit(solution)/shard_map/ppermute | solution.py:143
  93.1 8.6 %collective-permute-start.1 = (f32[3,128,128]{2,1,0:T(8,128)S(1)}, f32[3,128,128]{2,1,0:T(8,128)S(1)}, u32[]{:S(2)}, u32[]{:S(2)}) collective-permute-start(f32[3,128,128]{2,1,0:T(8,128)S(1)} %pad_maximum_fusion.2), channel_id=1, source_target_pairs={{0,8},{4,12},{8,16},{12,20},{16,24},{20,28},{1,9},{5,13},{9,17},{1... | collective-permute-start | bytes 589832 | tf_op jit(solution)/shard_map/ppermute | solution.py:143
  126.3 8.6 %collective-permute-start.2 = (f32[3,128,128]{2,1,0:T(8,128)S(1)}, f32[3,128,128]{2,1,0:T(8,128)S(1)}, u32[]{:S(2)}, u32[]{:S(2)}) collective-permute-start(f32[3,128,128]{2,1,0:T(8,128)S(1)} %pad_maximum_fusion.3), channel_id=1, source_target_pairs={{0,16},{4,20},{8,24},{12,28},{1,17},{5,21},{9,25},{13,29},{2,18},{... | collective-permute-start | bytes 589832 | tf_op jit(solution)/shard_map/ppermute | solution.py:143
Sparse Core Ops, SparseCore 0:
  21.3 34.5 all-reduce.1
  58.6 71.9 reduce-scatter.4
  133.1 71.8 reduce-scatter.2

commit v13 on v11

--- a/solution.py
+++ b/solution.py
@@ -179,16 +179,22 @@
         )
         flags = (jnp.arange(2 * own_blocks) < own_blocks).astype(jnp.int32)
         left_src = jnp.take(source, order)
-        partial = gram_rows(
-            kernel_slab, row_weights, live_blocks, left_src, source, order, diagonal, flags, own_blocks,
-        )
-        partial, segment = lax.optimization_barrier((partial, segment))
-        partial = gram_rows(
-            across_slab, across_weights, across_live, left_src, source, order, diagonal, flags,
-            own_blocks, partial,
-        )
-        owned = partial[0] + exchange(partial[1], 1)
-    else:
+
+        def own_part(slab_in):
+            return gram_rows(
+                slab_in, row_weights, live_blocks, left_src, source, order, diagonal, flags, own_blocks,
+            )
+
+        def across_part(slab_in, partial):
+            total = gram_rows(
+                slab_in, across_weights, across_live, left_src, source, order, diagonal, flags,
+                own_blocks, partial,
+            )
+            return total[0] + exchange(total[1], 1)
+
+        hooks = {1: ("own", kernel_slab), 2: ("across", across_slab)}
+    else:
+        hooks = {}
         flags = jnp.full((block_count,), (my_index == 0).astype(jnp.int32))
         partial = gram_rows(
             kernel_slab, row_weights, live_blocks, jnp.take(source, tile_order), source,
@@ -202,7 +208,21 @@
     position = lax.axis_index("tm")
     running = (segment[0], segment[1], segment[2])
     shift = 1
+    round_index = 0
+    state = {}
+
+    def run_hook(kind, slab_in, running):
+        slab_in, running = lax.optimization_barrier((slab_in, running))
+        if kind == "own":
+            state["partial"] = own_part(slab_in)
+        else:
+            state["owned"] = across_part(slab_in, state["partial"])
+        return running
+
     while shift < times:
+        if round_index in hooks:
+            running = run_hook(*hooks.pop(round_index), running)
+        round_index += 1
         pairs = [(src, src + shift) for src in range(times - shift)]
         moved = lax.ppermute(jnp.stack(running), "tm", pairs)
         earlier = (moved[0], moved[1], moved[2])
@@ -210,6 +230,10 @@
         take = position >= shift
         running = tuple(jnp.where(take, new, old) for new, old in zip(joined, running))
         shift *= 2
+    for key in sorted(hooks):
+        running = run_hook(*hooks[key], running)
+    if "owned" in state:
+        owned = state["owned"]
     chain_out = jnp.stack(running)[None]
     return (owned[None], chain_out)
 

time: 201 us -> 191 us (0.950)
  waiting for transfers between devices: 49.8 us -> 40.8 us
    ppermute x3, waiting for transfers between devices: 20.6 us -> 15.5 us  [local(): moved = lax.ppermute(jnp.stack(running), 'tm', pairs)]
    ppermute x4, waiting for transfers between devices: 29.2 us -> 25.3 us  [exchange(): lax.ppermute(value, 'row', [(src, src ^ step) for src in range(owners)])]
    squeeze x5 -> x1, local copies, waits for them, and re-layouts: 4.89 us -> 4.7 us  [across_part(): return total[0] + exchange(total[1], 1)]
  transfers between devices with their start and end apart: 7 -> 7, of which waited for: 5 -> 4; matrix products, arithmetic and copies ran while one was open for 40% -> 42% of each run, Pallas kernels for 7% -> 8%
where the time goes in v13:
time: 191 us
  other arithmetic  80.4 us (42%)
  waiting for transfers between devices  40.8 us (21%)
  Pallas kernels  31.3 us (16%)
  local copies, waits for them, and re-layouts  11.6 us (6%)
  starting transfers between devices  11.5 us (6%)
  matrix products  8.88 us (5%)
  between operations  6.34 us (3%)
    another operation x9, other arithmetic, join_segments(): factor = jnp.linalg.cholesky(middle)  37.2 us
    another operation x6, other arithmetic, join_segments(): lax.linalg.triangular_solve(factor, jnp.concatenate([cross_one.T, cross_t...  31.4 us
    pallas_call x2, Pallas kernels, gram_rows(): pl.pallas_call(gram_kernel, grid_spec=grid_spec, out_shape=jax.ShapeDtype...  31.3 us
    ppermute x4, waiting for transfers between devices, exchange(): lax.ppermute(value, 'row', [(src, src ^ step) for src in range(owners)])  25.3 us
    ppermute x3, waiting for transfers between devices, local(): moved = lax.ppermute(jnp.stack(running), 'tm', pairs)  15.5 us
    broadcast_in_dim x1, other arithmetic, local(): return (owned[None], chain_out)  6.57 us
    ppermute x3, starting transfers between devices, local(): moved = lax.ppermute(jnp.stack(running), 'tm', pairs)  6.11 us
    ppermute x4, starting transfers between devices, exchange(): lax.ppermute(value, 'row', [(src, src ^ step) for src in range(owners)])  5.4 us
  transfers between devices with their start and end apart: 7, of which 4 were waited for; matrix products, arithmetic and copies ran while one was open for 42% of the time, Pallas kernels for 8%

profile of v13, /device:TPU:25, one launch (start us, length us, event | category | flops | bytes accessed | tf_op | source)
XLA Modules:
  0.0 190.7 jit_solution(10631752146248573663)
XLA Ops:
  0.6 0.8 select_reduce_fusion.3.src_right
  5.9 0.8 reshape_squeeze.4.mask_ref
  8.0 1.0 fusion.79
  9.0 1.8 convolution_bitcast_fusion
  10.8 1.8 convolution_bitcast_fusion.1
  12.6 1.8 convolution_bitcast_fusion.2
  14.4 0.7 pad_maximum_fusion.5
  15.3 0.7 collective-permute-start
  16.0 0.8 fusion.91
  17.6 1.1 copy.66.w_ref
  19.2 1.3 collective-permute-start.1
  21.2 5.0 %collective-permute-done.1 = f32[53760]{0:T(1024)S(1)} collective-permute-done((f32[53760]{0:T(1024)S(1)}, f32[53760]{0:T(1024)S(1)}, u32[]{:S(2)}, u32[]{:S(2)}) %collective-permute-start.1) | collective-permute-done | bytes 215072 | tf_op jit(solution)/shard_map/ppermute | solution.py:150
  26.3 3.1 %collective-permute-start.3 = (f32[3,128,128]{2,1,0:T(8,128)S(1)}, f32[3,128,128]{2,1,0:T(8,128)S(1)}, u32[]{:S(2)}, u32[]{:S(2)}) collective-permute-start(f32[3,128,128]{2,1,0:T(8,128)S(1)} %pad_maximum_fusion.2), channel_id=1, source_target_pairs={{0,4},{4,8},{8,12},{12,16},{16,20},{20,24},{24,28},{1,5},{5,9},{9,... | collective-permute-start | bytes 589832 | tf_op jit(solution)/shard_map/ppermute | solution.py:227
  30.1 1.3 collective-permute-start.2
  31.4 3.2 %collective-permute-done.3 = f32[3,128,128]{2,1,0:T(8,128)S(1)} collective-permute-done((f32[3,128,128]{2,1,0:T(8,128)S(1)}, f32[3,128,128]{2,1,0:T(8,128)S(1)}, u32[]{:S(2)}, u32[]{:S(2)}) %collective-permute-start.3) | collective-permute-done | bytes 196640 | tf_op jit(solution)/shard_map/ppermute | solution.py:227
  35.1 11.7 %cholesky.59 = f32[128,128]{1,0:T(8,128)S(1)} custom-call(f32[128,128]{1,0:T(8,128)S(1)} %copy.55), custom_call_target="Cholesky" | custom-call | tf_op jit(solution)/shard_map/jit(cholesky)/cholesky | solution.py:95
  48.1 9.8 %custom-call.7 = f32[1,128,128]{1,2,0:T(8,128)S(1)} custom-call(f32[1,128,128]{2,1,0:T(8,128)S(1)} %fusion.35), custom_call_target="InvertDiagBlocksLowerTriangular" | custom-call | tf_op jit(solution)/shard_map/triangular_solve/custom-call.0 | solution.py:97
  59.3 1.5 collective-permute-start.4
  60.8 1.0 copy.67.w_ref
  62.4 14.5 %shard_map.80.rest_0_ = f32[2,512,2048]{2,1,0:T(8,128)} custom-call(s32[8]{0:T(128)} %get-tuple-element.26.src_left, s32[16]{0:T(128)} %copy-done, s32[8]{0:T(128)} %get-tuple-element.27.tile_ref, s32[128]{0:T(128)} %copy-done.2, s32[8]{0:T(128)} %compare_convert_fusion.flag_ref, bf16[1024,2048]{1,0:T(8,128)(2,1)} %bitcast.177, f32[1024,1]{1,0:T(8,128)} %copy.66.w_ref, ...), custom_call_target="tpu_custom_call" | custom-call | tf_op jit(solution)/shard_map/pallas_call | solution.py:78
  77.1 11.7 %cholesky.70 = f32[128,128]{1,0:T(8,128)S(1)} custom-call(f32[128,128]{1,0:T(8,128)S(1)} %fusion.51), custom_call_target="Cholesky" | custom-call | tf_op jit(solution)/shard_map/jit(cholesky)/cholesky | solution.py:95
  90.2 9.8 %custom-call.8 = f32[1,128,128]{1,2,0:T(8,128)S(1)} custom-call(f32[1,128,128]{2,1,0:T(8,128)S(1)} %fusion.36), custom_call_target="InvertDiagBlocksLowerTriangular" | custom-call | tf_op jit(solution)/shard_map/triangular_solve/custom-call.0 | solution.py:97
  101.2 20.3 %collective-permute-done.2.g_ref = bf16[1024,2048]{1,0:T(8,128)(2,1)} collective-permute-done((bf16[1024,2048]{1,0:T(8,128)(2,1)}, bf16[1024,2048]{1,0:T(8,128)(2,1)}, u32[]{:S(2)}, u32[]{:S(2)}) %collective-permute-start.2) | collective-permute-done | bytes 4194336 | tf_op jit(solution)/shard_map/ppermute | solution.py:150
  121.5 16.8 %shard_map.81 = f32[2,512,2048]{2,1,0:T(8,128)} custom-call(s32[8]{0:T(128)} %get-tuple-element.26.src_left, s32[16]{0:T(128)} %copy-done, s32[8]{0:T(128)} %get-tuple-element.27.tile_ref, s32[128]{0:T(128)} %fusion.85.mask_ref, s32[8]{0:T(128)} %compare_convert_fusion.flag_ref, ...), custom_call_target="tpu_custom_call", output_to_operand_aliasing={{}: (8, {})} | custom-call | tf_op jit(solution)/shard_map/pallas_call | solution.py:78
  138.3 4.7 %slice_bitcast_fusion = f32[512,2048]{1,0:T(8,128)} fusion(f32[2,512,2048]{2,1,0:T(8,128)} %shard_map.81), kind=kLoop, calls=%fused_computation.1 | loop fusion | bytes 8388608 | tf_op jit(solution)/shard_map/squeeze | solution.py:193
  143.0 2.0 %collective-permute-start.5 = (f32[512,2048]{1,0:T(8,128)}, f32[512,2048]{1,0:T(8,128)}, u32[]{:S(2)}, u32[]{:S(2)}) collective-permute-start(f32[512,2048]{1,0:T(8,128)} %slice_bitcast_fusion), channel_id=1, source_target_pairs={{0,1},{1,0},{2,3},{3,2},{4,5},{5,4},{6,7},{7,6},{8,9},{9,8},{10,11... | collective-permute-start | bytes 12582920 | tf_op jit(solution)/shard_map/ppermute | solution.py:150
  145.2 1.5 collective-permute-start.6
  146.7 12.2 %collective-permute-done.6 = f32[3,128,128]{2,1,0:T(8,128)S(1)} collective-permute-done((f32[3,128,128]{2,1,0:T(8,128)S(1)}, f32[3,128,128]{2,1,0:T(8,128)S(1)}, u32[]{:S(2)}, u32[]{:S(2)}) %collective-permute-start.6) | collective-permute-done | bytes 196640 | tf_op jit(solution)/shard_map/ppermute | solution.py:227
  159.3 11.7 %cholesky.81 = f32[128,128]{1,0:T(8,128)S(1)} custom-call(f32[128,128]{1,0:T(8,128)S(1)} %fusion.49), custom_call_target="Cholesky" | custom-call | tf_op jit(solution)/shard_map/jit(cholesky)/cholesky | solution.py:95
  172.3 9.8 %custom-call.9 = f32[1,128,128]{1,2,0:T(8,128)S(1)} custom-call(f32[1,128,128]{2,1,0:T(8,128)S(1)} %fusion.37), custom_call_target="InvertDiagBlocksLowerTriangular" | custom-call | tf_op jit(solution)/shard_map/triangular_solve/custom-call.0 | solution.py:97
  183.5 0.7 maximum_bitcast_fusion
  184.2 6.6 %fusion.1 = f32[1,512,2048]{2,1,0:T(8,128)} fusion(f32[512,2048]{1,0:T(8,128)} %collective-permute-done.5, f32[2,512,2048]{2,1,0:T(8,128)} %shard_map.81), kind=kLoop, calls=%fused_computation.4 | loop fusion | flops 1048576 | bytes 12582912 | tf_op jit(solution)/shard_map/broadcast_in_dim | solution.py:238
  (81 shorter events, 12.8 us)
Async XLA Ops:
  0.6 16.9 %copy-start.1 = (f32[1,1024]{1,0:T(1,128)S(1)}, f32[1,1024]{1,0:T(1,128)}, u32[]{:S(2)}) copy-start(f32[1,1024]{1,0:T(1,128)} %param.10) | copy-start | bytes 12292
  1.4 33.6 %copy-start = (s32[16]{0:T(128)}, s32[16]{0:T(128)S(1)}, u32[]{:S(2)}) copy-start(s32[16]{0:T(128)S(1)} %select_reduce_fusion.3.src_right) | copy-start | bytes 196
  6.7 28.4 %copy-start.2 = (s32[128]{0:T(128)}, s32[128]{0:T(128)S(1)}, u32[]{:S(2)}) copy-start(s32[128]{0:T(128)S(1)} %reshape_squeeze.4.mask_ref) | copy-start | bytes 1540
  15.3 3.9 %collective-permute-start = (f32[53760]{0:T(1024)S(1)}, f32[53760]{0:T(1024)S(1)}, u32[]{:S(2)}, u32[]{:S(2)}) collective-permute-start(f32[53760]{0:T(1024)S(1)} %pad_maximum_fusion), channel_id=1, source_target_pairs={{0,1},{1,0},{2,3},{3,2},{4,5},{5,4},{6,7},{7,6},{8,9},{9,8},{10,11... | collective-permute-start | bytes 645128 | tf_op jit(solution)/shard_map/ppermute | solution.py:150
  19.2 7.0 %collective-permute-start.1 = (f32[53760]{0:T(1024)S(1)}, f32[53760]{0:T(1024)S(1)}, u32[]{:S(2)}, u32[]{:S(2)}) collective-permute-start(f32[53760]{0:T(1024)S(1)} %fusion.89), channel_id=1, source_target_pairs={{0,2},{1,3},{2,0},{3,1},{4,6},{5,7},{6,4},{7,5},{8,10},{9,11},{10,... | collective-permute-start | bytes 645128 | tf_op jit(solution)/shard_map/ppermute | solution.py:150
  26.3 8.4 %collective-permute-start.3 = (f32[3,128,128]{2,1,0:T(8,128)S(1)}, f32[3,128,128]{2,1,0:T(8,128)S(1)}, u32[]{:S(2)}, u32[]{:S(2)}) collective-permute-start(f32[3,128,128]{2,1,0:T(8,128)S(1)} %pad_maximum_fusion.2), channel_id=1, source_target_pairs={{0,4},{4,8},{8,12},{12,16},{16,20},{20,24},{24,28},{1,5},{5,9},{9,... | collective-permute-start | bytes 589832 | tf_op jit(solution)/shard_map/ppermute | solution.py:227
  30.1 91.3 %collective-permute-start.2 = (bf16[1024,2048]{1,0:T(8,128)(2,1)}, bf16[1024,2048]{1,0:T(8,128)(2,1)}, u32[]{:S(2)}, u32[]{:S(2)}) collective-permute-start(bf16[1024,2048]{1,0:T(8,128)(2,1)} %bitcast.176), channel_id=1, source_target_pairs={{0,2},{1,3},{2,0},{3,1},{4,6},{5,7},{6,4},{7,5},{8,10},{9,11},{10,... | collective-permute-start | bytes 12582920 | tf_op jit(solution)/shard_map/ppermute | solution.py:150
  59.3 17.6 %collective-permute-start.4 = (f32[3,128,128]{2,1,0:T(8,128)S(1)}, f32[3,128,128]{2,1,0:T(8,128)S(1)}, u32[]{:S(2)}, u32[]{:S(2)}) collective-permute-start(f32[3,128,128]{2,1,0:T(8,128)S(1)} %pad_maximum_fusion.3), channel_id=1, source_target_pairs={{0,8},{4,12},{8,16},{12,20},{16,24},{20,28},{1,9},{5,13},{9,17},{1... | collective-permute-start | bytes 589832 | tf_op jit(solution)/shard_map/ppermute | solution.py:227
  143.0 41.2 %collective-permute-start.5 = (f32[512,2048]{1,0:T(8,128)}, f32[512,2048]{1,0:T(8,128)}, u32[]{:S(2)}, u32[]{:S(2)}) collective-permute-start(f32[512,2048]{1,0:T(8,128)} %slice_bitcast_fusion), channel_id=1, source_target_pairs={{0,1},{1,0},{2,3},{3,2},{4,5},{5,4},{6,7},{7,6},{8,9},{9,8},{10,11... | collective-permute-start | bytes 12582920 | tf_op jit(solution)/shard_map/ppermute | solution.py:150
  145.2 13.8 %collective-permute-start.6 = (f32[3,128,128]{2,1,0:T(8,128)S(1)}, f32[3,128,128]{2,1,0:T(8,128)S(1)}, u32[]{:S(2)}, u32[]{:S(2)}) collective-permute-start(f32[3,128,128]{2,1,0:T(8,128)S(1)} %pad_maximum_fusion.4), channel_id=1, source_target_pairs={{0,16},{4,20},{8,24},{12,28},{1,17},{5,21},{9,25},{13,29},{2,18},{... | collective-permute-start | bytes 589832 | tf_op jit(solution)/shard_map/ppermute | solution.py:227

commit v14 on v13

--- a/solution.py
+++ b/solution.py
@@ -1,3 +1,5 @@
+import functools
+
 import jax
 import jax.numpy as jnp
 from jax import lax
@@ -84,6 +86,94 @@
     )(src_left, src_right, out_tiles, live_blocks.reshape(-1), flags, *operands)
 
 
+def split_kernel(src_left, src_right, tile_ref, mask_ref, flag_ref, g_ref, w_ref, diag_ref, *rest,
+                 group, accumulate):
+    if accumulate:
+        acc_first, acc_second, out_first, out_second, s_ref, lt_ref = rest
+    else:
+        acc_first = acc_second = None
+        out_first, out_second, s_ref, lt_ref = rest
+    k = pl.program_id(0)
+    row_blocks = g_ref.shape[0] // BLK
+    col_blocks = g_ref.shape[1] // BLK
+
+    @pl.when(k == 0)
+    def _():
+        def fill(j, carry):
+            src = src_right[j]
+            c0 = pl.multiple_of(src * BLK, BLK)
+            d0 = pl.multiple_of(j * BLK, BLK)
+            for rb in range(row_blocks):
+                live = mask_ref[rb * col_blocks + src].astype(jnp.float32)
+                vals = g_ref[rb * BLK:(rb + 1) * BLK, pl.ds(c0, BLK)].astype(jnp.float32)
+                wts = w_ref[rb * BLK:(rb + 1) * BLK, :]
+                s_ref[rb * BLK:(rb + 1) * BLK, pl.ds(d0, BLK)] = (wts * (vals * live)).astype(jnp.bfloat16)
+            return carry
+        lax.fori_loop(0, col_blocks, fill, 0)
+
+    src = src_left[k]
+    c0 = pl.multiple_of(src * BLK, BLK)
+    for rb in range(row_blocks):
+        live = mask_ref[rb * col_blocks + src].astype(jnp.float32)
+        vals = g_ref[rb * BLK:(rb + 1) * BLK, pl.ds(c0, BLK)].astype(jnp.float32) * live
+        lt_ref[:, rb * BLK:(rb + 1) * BLK] = vals.T.astype(jnp.bfloat16)
+    term = jnp.dot(lt_ref[...], s_ref[...], preferred_element_type=jnp.float32)
+
+    def store(out_ref, acc_ref):
+        if acc_ref is None:
+            out_ref[...] = term
+            blk = tile_ref[k]
+            e0 = pl.multiple_of(blk * BLK, BLK)
+            rows = lax.broadcasted_iota(jnp.int32, (BLK, BLK), 0)
+            cols = lax.broadcasted_iota(jnp.int32, (BLK, BLK), 1)
+            dvals = diag_ref[pl.ds(blk, 1), :] * flag_ref[k].astype(jnp.float32)
+            out_ref[:, pl.ds(e0, BLK)] += jnp.where(rows == cols, dvals, 0.0)
+        else:
+            out_ref[...] = acc_ref[...] + term
+
+    @pl.when(k < group)
+    def _():
+        store(out_first, acc_first)
+
+    @pl.when(k >= group)
+    def _():
+        store(out_second, acc_second)
+
+
+def split_rows(slab, weights, live_blocks, src_left, src_right, out_tiles, diagonal, flags, group,
+               acc=None):
+    height = slab.shape[0]
+    col_blocks = L // BLK
+    in_specs = [
+        pl.BlockSpec((height, L), lambda k, *_: (0, 0)),
+        pl.BlockSpec((height, 1), lambda k, *_: (0, 0)),
+        pl.BlockSpec((col_blocks, BLK), lambda k, *_: (0, 0)),
+    ]
+    operands = [slab, weights.reshape(height, 1), diagonal.reshape(col_blocks, BLK)]
+    first_spec = pl.BlockSpec((BLK, L), lambda k, *_: (jnp.minimum(k, group - 1), 0))
+    second_spec = pl.BlockSpec((BLK, L), lambda k, *_: (jnp.maximum(k - group, 0), 0))
+    aliases = {}
+    if acc is not None:
+        in_specs += [first_spec, second_spec]
+        operands += list(acc)
+        aliases = {8: 0, 9: 1}
+    grid_spec = pltpu.PrefetchScalarGridSpec(
+        num_scalar_prefetch=5,
+        grid=(2 * group,),
+        in_specs=in_specs,
+        out_specs=[first_spec, second_spec],
+        scratch_shapes=[pltpu.VMEM((height, L), jnp.bfloat16), pltpu.VMEM((BLK, height), jnp.bfloat16)],
+    )
+    shape = jax.ShapeDtypeStruct((group * BLK, L), jnp.float32)
+    return pl.pallas_call(
+        functools.partial(split_kernel, group=group, accumulate=acc is not None),
+        grid_spec=grid_spec,
+        out_shape=(shape, shape),
+        input_output_aliases=aliases,
+        compiler_params=pltpu.CompilerParams(vmem_limit_bytes=56 * 1024 * 1024),
+    )(src_left, src_right, out_tiles, live_blocks.reshape(-1), flags, *operands)
+
+
 HIGHEST = lax.Precision.HIGHEST
 
 
@@ -181,16 +271,16 @@
         left_src = jnp.take(source, order)
 
         def own_part(slab_in):
-            return gram_rows(
+            return split_rows(
                 slab_in, row_weights, live_blocks, left_src, source, order, diagonal, flags, own_blocks,
             )
 
         def across_part(slab_in, partial):
-            total = gram_rows(
+            mine, partners = split_rows(
                 slab_in, across_weights, across_live, left_src, source, order, diagonal, flags,
                 own_blocks, partial,
             )
-            return total[0] + exchange(total[1], 1)
+            return mine + exchange(partners, 1)
 
         hooks = {1: ("own", kernel_slab), 2: ("across", across_slab)}
     else:

time: 191 us -> 188 us (0.984)
  the two profiles are of different devices: /device:TPU:25 before, /device:TPU:29 now
where the time goes in v14:
time: 188 us; the launch traced here: 187 us
  other arithmetic  80.6 us (43%)
  waiting for transfers between devices  42 us (22%)
  Pallas kernels  32.7 us (17%)
  starting transfers between devices  9.54 us (5%)
  matrix products  8.84 us (5%)
  local copies, waits for them, and re-layouts  6.95 us (4%)
  between operations  6.34 us (3%)
    another operation x9, other arithmetic, join_segments(): factor = jnp.linalg.cholesky(middle)  37.2 us
    pallas_call x2, Pallas kernels, split_rows(): pl.pallas_call(functools.partial(split_kernel, group=group, accumulate=ac...  32.7 us
    another operation x6, other arithmetic, join_segments(): lax.linalg.triangular_solve(factor, jnp.concatenate([cross_one.T, cross_t...  31.4 us
    ppermute x4, waiting for transfers between devices, exchange(): lax.ppermute(value, 'row', [(src, src ^ step) for src in range(owners)])  25.6 us
    ppermute x3, waiting for transfers between devices, local(): moved = lax.ppermute(jnp.stack(running), 'tm', pairs)  16.4 us
    broadcast_in_dim x1, other arithmetic, local(): return (owned[None], chain_out)  6.57 us
    ppermute x3, starting transfers between devices, local(): moved = lax.ppermute(jnp.stack(running), 'tm', pairs)  6.14 us
    dot_general x3, matrix products, contract_rows(): lax.dot_general(left_cols, right_cols, (((0,), (0,)), ((), ())), preferre...  5.32 us
  transfers between devices with their start and end apart: 7, of which 4 were waited for; matrix products, arithmetic and copies ran while one was open for 43% of the time, Pallas kernels for 8%

profile of v14, /device:TPU:29, one launch (start us, length us, event | category | flops | bytes accessed | tf_op | source)
XLA Modules:
  0.0 186.9 jit_solution(10445720151455538580)
XLA Ops:
  0.6 0.8 select_reduce_fusion.3.src_right
  5.9 0.8 reshape_squeeze.4.mask_ref
  8.0 1.0 fusion.77
  9.0 1.8 convolution_bitcast_fusion
  10.8 1.8 convolution_bitcast_fusion.1
  12.6 1.8 convolution_bitcast_fusion.2
  14.4 0.7 pad_maximum_fusion.5
  15.2 0.7 collective-permute-start
  16.0 0.8 fusion.89
  17.5 1.1 copy.67.w_ref
  19.5 0.7 slice_bitcast_fusion.12
  20.2 6.0 %collective-permute-done.1 = f32[53760]{0:T(1024)S(1)} collective-permute-done((f32[53760]{0:T(1024)S(1)}, f32[53760]{0:T(1024)S(1)}, u32[]{:S(2)}, u32[]{:S(2)}) %collective-permute-start.1) | collective-permute-done | bytes 215072 | tf_op jit(solution)/shard_map/ppermute | solution.py:240
  26.3 3.2 %collective-permute-start.3 = (f32[3,128,128]{2,1,0:T(8,128)S(1)}, f32[3,128,128]{2,1,0:T(8,128)S(1)}, u32[]{:S(2)}, u32[]{:S(2)}) collective-permute-start(f32[3,128,128]{2,1,0:T(8,128)S(1)} %pad_maximum_fusion.2), channel_id=1, source_target_pairs={{0,4},{4,8},{8,12},{12,16},{16,20},{20,24},{24,28},{1,5},{5,9},{9,... | collective-permute-start | bytes 589832 | tf_op jit(solution)/shard_map/ppermute | solution.py:317
  29.5 0.7 and_select_fusion
  30.6 4.2 %collective-permute-done.3 = f32[3,128,128]{2,1,0:T(8,128)S(1)} collective-permute-done((f32[3,128,128]{2,1,0:T(8,128)S(1)}, f32[3,128,128]{2,1,0:T(8,128)S(1)}, u32[]{:S(2)}, u32[]{:S(2)}) %collective-permute-start.3) | collective-permute-done | bytes 196640 | tf_op jit(solution)/shard_map/ppermute | solution.py:317
  35.1 11.7 %cholesky.59 = f32[128,128]{1,0:T(8,128)S(1)} custom-call(f32[128,128]{1,0:T(8,128)S(1)} %copy.56), custom_call_target="Cholesky" | custom-call | tf_op jit(solution)/shard_map/jit(cholesky)/cholesky | solution.py:185
  48.2 9.8 %custom-call.7 = f32[1,128,128]{1,2,0:T(8,128)S(1)} custom-call(f32[1,128,128]{2,1,0:T(8,128)S(1)} %fusion.33), custom_call_target="InvertDiagBlocksLowerTriangular" | custom-call | tf_op jit(solution)/shard_map/triangular_solve/custom-call.0 | solution.py:187
  59.3 1.5 collective-permute-start.4
  60.8 1.1 copy.68.w_ref
  62.5 15.1 %shard_map.80 = (f32[512,2048]{1,0:T(8,128)}, f32[512,2048]{1,0:T(8,128)}) custom-call(s32[8]{0:T(128)} %get-tuple-element.34.src_left, s32[16]{0:T(128)} %copy-done, s32[8]{0:T(128)} %get-tuple-element.35.tile_ref, s32[128]{0:T(128)} %copy-done.2, s32[8]{0:T(128)} %compare_convert_fusion.flag_ref, bf16[1024,2048]{1,0:T(8,128)(2,1)} %bitcast.169, ...), custom_call_target="tpu_custom_call" | custom-call | tf_op jit(solution)/shard_map/pallas_call | solution.py:168
  77.9 11.7 %cholesky.70 = f32[128,128]{1,0:T(8,128)S(1)} custom-call(f32[128,128]{1,0:T(8,128)S(1)} %fusion.49), custom_call_target="Cholesky" | custom-call | tf_op jit(solution)/shard_map/jit(cholesky)/cholesky | solution.py:185
  89.7 0.7 compare_reduce_fusion.1
  91.0 9.8 %custom-call.8 = f32[1,128,128]{1,2,0:T(8,128)S(1)} custom-call(f32[1,128,128]{2,1,0:T(8,128)S(1)} %fusion.34), custom_call_target="InvertDiagBlocksLowerTriangular" | custom-call | tf_op jit(solution)/shard_map/triangular_solve/custom-call.0 | solution.py:187
  102.0 19.6 %collective-permute-done.2.g_ref = bf16[1024,2048]{1,0:T(8,128)(2,1)} collective-permute-done((bf16[1024,2048]{1,0:T(8,128)(2,1)}, bf16[1024,2048]{1,0:T(8,128)(2,1)}, u32[]{:S(2)}, u32[]{:S(2)}) %collective-permute-start.2) | collective-permute-done | bytes 4194336 | tf_op jit(solution)/shard_map/ppermute | solution.py:240
  121.6 17.6 %shard_map.81 = (f32[512,2048]{1,0:T(8,128)}, f32[512,2048]{1,0:T(8,128)}) custom-call(s32[8]{0:T(128)} %get-tuple-element.34.src_left, s32[16]{0:T(128)} %copy-done, s32[8]{0:T(128)} %get-tuple-element.35.tile_ref, s32[128]{0:T(128)} %fusion.83.mask_ref, s32[8]{0:T(128)} %compare_convert_fusion.flag_ref, ...), custom_call_target="tpu_custom_call", output_to_operand_aliasing={{0}: (8, {}), {1}: (9, {})} | custom-call | tf_op jit(solution)/shard_map/pallas_call | solution.py:168
  139.2 2.1 %collective-permute-start.5 = (f32[512,2048]{1,0:T(8,128)}, f32[512,2048]{1,0:T(8,128)}, u32[]{:S(2)}, u32[]{:S(2)}) collective-permute-start(f32[512,2048]{1,0:T(8,128)} %get-tuple-element.28), channel_id=1, source_target_pairs={{0,1},{1,0},{2,3},{3,2},{4,5},{5,4},{6,7},{7,6},{8,9},{9,8},{10,11... | collective-permute-start | bytes 12582920 | tf_op jit(solution)/shard_map/ppermute | solution.py:240
  141.4 1.5 collective-permute-start.6
  142.9 12.2 %collective-permute-done.6 = f32[3,128,128]{2,1,0:T(8,128)S(1)} collective-permute-done((f32[3,128,128]{2,1,0:T(8,128)S(1)}, f32[3,128,128]{2,1,0:T(8,128)S(1)}, u32[]{:S(2)}, u32[]{:S(2)}) %collective-permute-start.6) | collective-permute-done | bytes 196640 | tf_op jit(solution)/shard_map/ppermute | solution.py:317
  155.5 11.7 %cholesky.81 = f32[128,128]{1,0:T(8,128)S(1)} custom-call(f32[128,128]{1,0:T(8,128)S(1)} %fusion.47), custom_call_target="Cholesky" | custom-call | tf_op jit(solution)/shard_map/jit(cholesky)/cholesky | solution.py:185
  168.5 9.8 %custom-call.9 = f32[1,128,128]{1,2,0:T(8,128)S(1)} custom-call(f32[1,128,128]{2,1,0:T(8,128)S(1)} %fusion.35), custom_call_target="InvertDiagBlocksLowerTriangular" | custom-call | tf_op jit(solution)/shard_map/triangular_solve/custom-call.0 | solution.py:187
  179.6 0.7 maximum_bitcast_fusion
  180.3 6.6 %add_bitcast_fusion = f32[1,512,2048]{2,1,0:T(8,128)} fusion(f32[512,2048]{1,0:T(8,128)} %get-tuple-element.27, f32[512,2048]{1,0:T(8,128)} %collective-permute-done.5), kind=kLoop, calls=%fused_computation.1 | loop fusion | flops 1048576 | bytes 12582912 | tf_op jit(solution)/shard_map/broadcast_in_dim | solution.py:328
  (80 shorter events, 11.6 us)
Async XLA Ops:
  0.6 16.9 %copy-start.1 = (f32[1,1024]{1,0:T(1,128)S(1)}, f32[1,1024]{1,0:T(1,128)}, u32[]{:S(2)}) copy-start(f32[1,1024]{1,0:T(1,128)} %param.10) | copy-start | bytes 12292
  1.4 33.7 %copy-start = (s32[16]{0:T(128)}, s32[16]{0:T(128)S(1)}, u32[]{:S(2)}) copy-start(s32[16]{0:T(128)S(1)} %select_reduce_fusion.3.src_right) | copy-start | bytes 196
  6.7 28.4 %copy-start.2 = (s32[128]{0:T(128)}, s32[128]{0:T(128)S(1)}, u32[]{:S(2)}) copy-start(s32[128]{0:T(128)S(1)} %reshape_squeeze.4.mask_ref) | copy-start | bytes 1540
  15.2 4.0 %collective-permute-start = (f32[53760]{0:T(1024)S(1)}, f32[53760]{0:T(1024)S(1)}, u32[]{:S(2)}, u32[]{:S(2)}) collective-permute-start(f32[53760]{0:T(1024)S(1)} %pad_maximum_fusion), channel_id=1, source_target_pairs={{0,1},{1,0},{2,3},{3,2},{4,5},{5,4},{6,7},{7,6},{8,9},{9,8},{10,11... | collective-permute-start | bytes 645128 | tf_op jit(solution)/shard_map/ppermute | solution.py:240
  19.2 7.0 %collective-permute-start.1 = (f32[53760]{0:T(1024)S(1)}, f32[53760]{0:T(1024)S(1)}, u32[]{:S(2)}, u32[]{:S(2)}) collective-permute-start(f32[53760]{0:T(1024)S(1)} %fusion.87), channel_id=1, source_target_pairs={{0,2},{1,3},{2,0},{3,1},{4,6},{5,7},{6,4},{7,5},{8,10},{9,11},{10,... | collective-permute-start | bytes 645128 | tf_op jit(solution)/shard_map/ppermute | solution.py:240
  26.3 8.4 %collective-permute-start.3 = (f32[3,128,128]{2,1,0:T(8,128)S(1)}, f32[3,128,128]{2,1,0:T(8,128)S(1)}, u32[]{:S(2)}, u32[]{:S(2)}) collective-permute-start(f32[3,128,128]{2,1,0:T(8,128)S(1)} %pad_maximum_fusion.2), channel_id=1, source_target_pairs={{0,4},{4,8},{8,12},{12,16},{16,20},{20,24},{24,28},{1,5},{5,9},{9,... | collective-permute-start | bytes 589832 | tf_op jit(solution)/shard_map/ppermute | solution.py:317
  30.3 91.3 %collective-permute-start.2 = (bf16[1024,2048]{1,0:T(8,128)(2,1)}, bf16[1024,2048]{1,0:T(8,128)(2,1)}, u32[]{:S(2)}, u32[]{:S(2)}) collective-permute-start(bf16[1024,2048]{1,0:T(8,128)(2,1)} %bitcast.168), channel_id=1, source_target_pairs={{0,2},{1,3},{2,0},{3,1},{4,6},{5,7},{6,4},{7,5},{8,10},{9,11},{10,... | collective-permute-start | bytes 12582920 | tf_op jit(solution)/shard_map/ppermute | solution.py:240
  59.3 18.4 %collective-permute-start.4 = (f32[3,128,128]{2,1,0:T(8,128)S(1)}, f32[3,128,128]{2,1,0:T(8,128)S(1)}, u32[]{:S(2)}, u32[]{:S(2)}) collective-permute-start(f32[3,128,128]{2,1,0:T(8,128)S(1)} %pad_maximum_fusion.3), channel_id=1, source_target_pairs={{0,8},{4,12},{8,16},{12,20},{16,24},{20,28},{1,9},{5,13},{9,17},{1... | collective-permute-start | bytes 589832 | tf_op jit(solution)/shard_map/ppermute | solution.py:317
  139.2 41.2 %collective-permute-start.5 = (f32[512,2048]{1,0:T(8,128)}, f32[512,2048]{1,0:T(8,128)}, u32[]{:S(2)}, u32[]{:S(2)}) collective-permute-start(f32[512,2048]{1,0:T(8,128)} %get-tuple-element.28), channel_id=1, source_target_pairs={{0,1},{1,0},{2,3},{3,2},{4,5},{5,4},{6,7},{7,6},{8,9},{9,8},{10,11... | collective-permute-start | bytes 12582920 | tf_op jit(solution)/shard_map/ppermute | solution.py:240
  141.4 13.7 %collective-permute-start.6 = (f32[3,128,128]{2,1,0:T(8,128)S(1)}, f32[3,128,128]{2,1,0:T(8,128)S(1)}, u32[]{:S(2)}, u32[]{:S(2)}) collective-permute-start(f32[3,128,128]{2,1,0:T(8,128)S(1)} %pad_maximum_fusion.4), channel_id=1, source_target_pairs={{0,16},{4,20},{8,24},{12,28},{1,17},{5,21},{9,25},{13,29},{2,18},{... | collective-permute-start | bytes 589832 | tf_op jit(solution)/shard_map/ppermute | solution.py:317

commit v15 on v14

--- a/solution.py
+++ b/solution.py
@@ -282,7 +282,7 @@
             )
             return mine + exchange(partners, 1)
 
-        hooks = {1: ("own", kernel_slab), 2: ("across", across_slab)}
+        hooks = {1: ("own", kernel_slab), 3: ("across", across_slab)}
     else:
         hooks = {}
         flags = jnp.full((block_count,), (my_index == 0).astype(jnp.int32))

time: 188 us -> 187 us (level)
  the two profiles are of different devices: /device:TPU:29 before, /device:TPU:0 now
where the time goes in v15:
time: 187 us; the launch traced here: 186 us
  other arithmetic  80.5 us (43%)
  Pallas kernels  32.8 us (18%)
  waiting for transfers between devices  30.9 us (17%)
  starting transfers between devices  19.8 us (11%)
  matrix products  8.87 us (5%)
  local copies, waits for them, and re-layouts  6.95 us (4%)
  between operations  6.34 us (3%)
    another operation x9, other arithmetic, join_segments(): factor = jnp.linalg.cholesky(middle)  37.2 us
    pallas_call x2, Pallas kernels, split_rows(): pl.pallas_call(functools.partial(split_kernel, group=group, accumulate=ac...  32.8 us
    another operation x6, other arithmetic, join_segments(): lax.linalg.triangular_solve(factor, jnp.concatenate([cross_one.T, cross_t...  31.4 us
    ppermute x4, waiting for transfers between devices, exchange(): lax.ppermute(value, 'row', [(src, src ^ step) for src in range(owners)])  29 us
    ppermute x3, starting transfers between devices, local(): moved = lax.ppermute(jnp.stack(running), 'tm', pairs)  14.8 us
    broadcast_in_dim x1, other arithmetic, local(): return (owned[None], chain_out)  6.57 us
    dot_general x3, matrix products, contract_rows(): lax.dot_general(left_cols, right_cols, (((0,), (0,)), ((), ())), preferre...  5.35 us
    ppermute x4, starting transfers between devices, exchange(): lax.ppermute(value, 'row', [(src, src ^ step) for src in range(owners)])  4.99 us
  transfers between devices with their start and end apart: 7, of which 6 were waited for; matrix products, arithmetic and copies ran while one was open for 30% of the time, Pallas kernels for 8%

profile of v15, /device:TPU:0, one launch (start us, length us, event | category | flops | bytes accessed | tf_op | source)
XLA Modules:
  0.0 186.2 jit_solution(2514242057638202225)
XLA Ops:
  0.6 0.8 select_reduce_fusion.3.src_right
  5.9 0.8 reshape_squeeze.4.mask_ref
  8.0 1.0 fusion.74
  9.0 1.8 convolution_bitcast_fusion
  10.8 1.8 convolution_bitcast_fusion.1
  12.6 1.8 convolution_bitcast_fusion.2
  14.4 0.7 pad_maximum_fusion.5
  15.8 0.8 fusion.86
  16.9 3.0 %collective-permute-start.1 = (f32[53760]{0:T(1024)S(1)}, f32[53760]{0:T(1024)S(1)}, u32[]{:S(2)}, u32[]{:S(2)}) collective-permute-start(f32[53760]{0:T(1024)S(1)} %fusion.84), channel_id=1, source_target_pairs={{0,2},{1,3},{2,0},{3,1},{4,6},{5,7},{6,4},{7,5},{8,10},{9,11},{10,... | collective-permute-start | bytes 645128 | tf_op jit(solution)/shard_map/ppermute | solution.py:240
  19.9 0.7 slice_bitcast_fusion.12
  20.5 5.0 %collective-permute-done.1 = f32[53760]{0:T(1024)S(1)} collective-permute-done((f32[53760]{0:T(1024)S(1)}, f32[53760]{0:T(1024)S(1)}, u32[]{:S(2)}, u32[]{:S(2)}) %collective-permute-start.1) | collective-permute-done | bytes 215072 | tf_op jit(solution)/shard_map/ppermute | solution.py:240
  25.6 3.6 %collective-permute-start.3 = (f32[3,128,128]{2,1,0:T(8,128)S(1)}, f32[3,128,128]{2,1,0:T(8,128)S(1)}, u32[]{:S(2)}, u32[]{:S(2)}) collective-permute-start(f32[3,128,128]{2,1,0:T(8,128)S(1)} %pad_maximum_fusion.2), channel_id=1, source_target_pairs={{0,4},{4,8},{8,12},{12,16},{16,20},{20,24},{24,28},{1,5},{5,9},{9,... | collective-permute-start | bytes 589832 | tf_op jit(solution)/shard_map/ppermute | solution.py:317
  29.9 1.1 copy.71.w_ref
  31.7 1.2 collective-permute-done.3
  33.2 11.7 %cholesky.59 = f32[128,128]{1,0:T(8,128)S(1)} custom-call(f32[128,128]{1,0:T(8,128)S(1)} %copy.54), custom_call_target="Cholesky" | custom-call | tf_op jit(solution)/shard_map/jit(cholesky)/cholesky | solution.py:185
  46.3 9.8 %custom-call.7 = f32[1,128,128]{1,2,0:T(8,128)S(1)} custom-call(f32[1,128,128]{2,1,0:T(8,128)S(1)} %fusion.31), custom_call_target="InvertDiagBlocksLowerTriangular" | custom-call | tf_op jit(solution)/shard_map/triangular_solve/custom-call.0 | solution.py:187
  57.4 5.5 %collective-permute-start.4 = (f32[3,128,128]{2,1,0:T(8,128)S(1)}, f32[3,128,128]{2,1,0:T(8,128)S(1)}, u32[]{:S(2)}, u32[]{:S(2)}) collective-permute-start(f32[3,128,128]{2,1,0:T(8,128)S(1)} %pad_maximum_fusion.3), channel_id=1, source_target_pairs={{0,8},{4,12},{8,16},{12,20},{16,24},{20,28},{1,9},{5,13},{9,17},{1... | collective-permute-start | bytes 589832 | tf_op jit(solution)/shard_map/ppermute | solution.py:317
  63.6 1.5 collective-permute-start.2
  65.2 0.8 collective-permute-done.4
  66.2 11.7 %cholesky.70 = f32[128,128]{1,0:T(8,128)S(1)} custom-call(f32[128,128]{1,0:T(8,128)S(1)} %fusion.46), custom_call_target="Cholesky" | custom-call | tf_op jit(solution)/shard_map/jit(cholesky)/cholesky | solution.py:185
  79.3 9.8 %custom-call.8 = f32[1,128,128]{1,2,0:T(8,128)S(1)} custom-call(f32[1,128,128]{2,1,0:T(8,128)S(1)} %fusion.32), custom_call_target="InvertDiagBlocksLowerTriangular" | custom-call | tf_op jit(solution)/shard_map/triangular_solve/custom-call.0 | solution.py:187
  90.4 5.6 %collective-permute-start.5 = (f32[3,128,128]{2,1,0:T(8,128)S(1)}, f32[3,128,128]{2,1,0:T(8,128)S(1)}, u32[]{:S(2)}, u32[]{:S(2)}) collective-permute-start(f32[3,128,128]{2,1,0:T(8,128)S(1)} %pad_maximum_fusion.4), channel_id=1, source_target_pairs={{0,16},{4,20},{8,24},{12,28},{1,17},{5,21},{9,25},{13,29},{2,18},{... | collective-permute-start | bytes 589832 | tf_op jit(solution)/shard_map/ppermute | solution.py:317
  96.1 1.1 copy.72.w_ref
  97.8 15.2 %shard_map.80 = (f32[512,2048]{1,0:T(8,128)}, f32[512,2048]{1,0:T(8,128)}) custom-call(s32[8]{0:T(128)} %get-tuple-element.34.src_left, s32[16]{0:T(128)} %copy-done, s32[8]{0:T(128)} %get-tuple-element.35.tile_ref, s32[128]{0:T(128)} %copy-done.2, s32[8]{0:T(128)} %compare_convert_fusion.flag_ref, bf16[1024,2048]{1,0:T(8,128)(2,1)} %bitcast.164, ...), custom_call_target="tpu_custom_call" | custom-call | tf_op jit(solution)/shard_map/pallas_call | solution.py:168
  113.3 11.7 %cholesky.81 = f32[128,128]{1,0:T(8,128)S(1)} custom-call(f32[128,128]{1,0:T(8,128)S(1)} %fusion.44), custom_call_target="Cholesky" | custom-call | tf_op jit(solution)/shard_map/jit(cholesky)/cholesky | solution.py:185
  125.1 0.7 compare_reduce_fusion
  126.4 9.8 %custom-call.9 = f32[1,128,128]{1,2,0:T(8,128)S(1)} custom-call(f32[1,128,128]{2,1,0:T(8,128)S(1)} %fusion.33), custom_call_target="InvertDiagBlocksLowerTriangular" | custom-call | tf_op jit(solution)/shard_map/triangular_solve/custom-call.0 | solution.py:187
  137.4 17.1 %collective-permute-done.2.g_ref = bf16[1024,2048]{1,0:T(8,128)(2,1)} collective-permute-done((bf16[1024,2048]{1,0:T(8,128)(2,1)}, bf16[1024,2048]{1,0:T(8,128)(2,1)}, u32[]{:S(2)}, u32[]{:S(2)}) %collective-permute-start.2) | collective-permute-done | bytes 4194336 | tf_op jit(solution)/shard_map/ppermute | solution.py:240
  154.5 17.6 %shard_map.81 = (f32[512,2048]{1,0:T(8,128)}, f32[512,2048]{1,0:T(8,128)}) custom-call(s32[8]{0:T(128)} %get-tuple-element.34.src_left, s32[16]{0:T(128)} %copy-done, s32[8]{0:T(128)} %get-tuple-element.35.tile_ref, s32[128]{0:T(128)} %fusion.80.mask_ref, s32[8]{0:T(128)} %compare_convert_fusion.flag_ref, ...), custom_call_target="tpu_custom_call", output_to_operand_aliasing={{0}: (8, {}), {1}: (9, {})} | custom-call | tf_op jit(solution)/shard_map/pallas_call | solution.py:168
  172.2 0.7 maximum_bitcast_fusion
  172.9 6.7 %collective-permute-done.6 = f32[512,2048]{1,0:T(8,128)} collective-permute-done((f32[512,2048]{1,0:T(8,128)}, f32[512,2048]{1,0:T(8,128)}, u32[]{:S(2)}, u32[]{:S(2)}) %collective-permute-start.6) | collective-permute-done | bytes 4194336 | tf_op jit(solution)/shard_map/ppermute | solution.py:240
  179.6 6.6 %add_bitcast_fusion = f32[1,512,2048]{2,1,0:T(8,128)} fusion(f32[512,2048]{1,0:T(8,128)} %get-tuple-element.27, f32[512,2048]{1,0:T(8,128)} %collective-permute-done.6), kind=kLoop, calls=%fused_computation.1 | loop fusion | flops 1048576 | bytes 12582912 | tf_op jit(solution)/shard_map/broadcast_in_dim | solution.py:328
  (80 shorter events, 12.4 us)
Async XLA Ops:
  0.6 29.3 %copy-start.1 = (f32[1,1024]{1,0:T(1,128)S(1)}, f32[1,1024]{1,0:T(1,128)}, u32[]{:S(2)}) copy-start(f32[1,1024]{1,0:T(1,128)} %param.10) | copy-start | bytes 12292
  1.4 43.5 %copy-start = (s32[16]{0:T(128)}, s32[16]{0:T(128)S(1)}, u32[]{:S(2)}) copy-start(s32[16]{0:T(128)S(1)} %select_reduce_fusion.3.src_right) | copy-start | bytes 196
  6.7 38.3 %copy-start.2 = (s32[128]{0:T(128)}, s32[128]{0:T(128)S(1)}, u32[]{:S(2)}) copy-start(s32[128]{0:T(128)S(1)} %reshape_squeeze.4.mask_ref) | copy-start | bytes 1540
  15.3 1.6 collective-permute-start
  16.9 8.6 %collective-permute-start.1 = (f32[53760]{0:T(1024)S(1)}, f32[53760]{0:T(1024)S(1)}, u32[]{:S(2)}, u32[]{:S(2)}) collective-permute-start(f32[53760]{0:T(1024)S(1)} %fusion.84), channel_id=1, source_target_pairs={{0,2},{1,3},{2,0},{3,1},{4,6},{5,7},{6,4},{7,5},{8,10},{9,11},{10,... | collective-permute-start | bytes 645128 | tf_op jit(solution)/shard_map/ppermute | solution.py:240
  25.6 7.2 %collective-permute-start.3 = (f32[3,128,128]{2,1,0:T(8,128)S(1)}, f32[3,128,128]{2,1,0:T(8,128)S(1)}, u32[]{:S(2)}, u32[]{:S(2)}) collective-permute-start(f32[3,128,128]{2,1,0:T(8,128)S(1)} %pad_maximum_fusion.2), channel_id=1, source_target_pairs={{0,4},{4,8},{8,12},{12,16},{16,20},{20,24},{24,28},{1,5},{5,9},{9,... | collective-permute-start | bytes 589832 | tf_op jit(solution)/shard_map/ppermute | solution.py:317
  57.4 8.5 %collective-permute-start.4 = (f32[3,128,128]{2,1,0:T(8,128)S(1)}, f32[3,128,128]{2,1,0:T(8,128)S(1)}, u32[]{:S(2)}, u32[]{:S(2)}) collective-permute-start(f32[3,128,128]{2,1,0:T(8,128)S(1)} %pad_maximum_fusion.3), channel_id=1, source_target_pairs={{0,8},{4,12},{8,16},{12,20},{16,24},{20,28},{1,9},{5,13},{9,17},{1... | collective-permute-start | bytes 589832 | tf_op jit(solution)/shard_map/ppermute | solution.py:317
  63.6 90.9 %collective-permute-start.2 = (bf16[1024,2048]{1,0:T(8,128)(2,1)}, bf16[1024,2048]{1,0:T(8,128)(2,1)}, u32[]{:S(2)}, u32[]{:S(2)}) collective-permute-start(bf16[1024,2048]{1,0:T(8,128)(2,1)} %bitcast.163), channel_id=1, source_target_pairs={{0,2},{1,3},{2,0},{3,1},{4,6},{5,7},{6,4},{7,5},{8,10},{9,11},{10,... | collective-permute-start | bytes 12582920 | tf_op jit(solution)/shard_map/ppermute | solution.py:240
  90.4 22.6 %collective-permute-start.5 = (f32[3,128,128]{2,1,0:T(8,128)S(1)}, f32[3,128,128]{2,1,0:T(8,128)S(1)}, u32[]{:S(2)}, u32[]{:S(2)}) collective-permute-start(f32[3,128,128]{2,1,0:T(8,128)S(1)} %pad_maximum_fusion.4), channel_id=1, source_target_pairs={{0,16},{4,20},{8,24},{12,28},{1,17},{5,21},{9,25},{13,29},{2,18},{... | collective-permute-start | bytes 589832 | tf_op jit(solution)/shard_map/ppermute | solution.py:317
  172.1 7.5 %collective-permute-start.6 = (f32[512,2048]{1,0:T(8,128)}, f32[512,2048]{1,0:T(8,128)}, u32[]{:S(2)}, u32[]{:S(2)}) collective-permute-start(f32[512,2048]{1,0:T(8,128)} %get-tuple-element.28), channel_id=1, source_target_pairs={{0,1},{1,0},{2,3},{3,2},{4,5},{5,4},{6,7},{7,6},{8,9},{9,8},{10,11... | collective-permute-start | bytes 12582920 | tf_op jit(solution)/shard_map/ppermute | solution.py:240

commit v16 on v15

--- a/solution.py
+++ b/solution.py
@@ -260,7 +260,12 @@
     ])
 
     if owners == 4:
-        across_slab = exchange(kernel_slab, 2)
+        halves = 2
+        half_rows = slab_height // halves
+        across_halves = [
+            exchange(lax.slice_in_dim(kernel_slab, h * half_rows, (h + 1) * half_rows), 2)
+            for h in range(halves)
+        ]
         across_side = lax.dynamic_index_in_dim(every_side, my_index ^ 2, 0, False)
         across_weights = across_side[:slab_height]
         across_live = across_side[slab_height:].reshape(live_blocks.shape).astype(jnp.int32)
@@ -275,14 +280,16 @@
                 slab_in, row_weights, live_blocks, left_src, source, order, diagonal, flags, own_blocks,
             )
 
-        def across_part(slab_in, partial):
-            mine, partners = split_rows(
-                slab_in, across_weights, across_live, left_src, source, order, diagonal, flags,
-                own_blocks, partial,
+        def across_part(slab_in, partial, half):
+            rows = lax.slice_in_dim(across_weights, half * half_rows, (half + 1) * half_rows)
+            live = lax.slice_in_dim(
+                across_live, half * (half_rows // BLK), (half + 1) * (half_rows // BLK)
             )
-            return mine + exchange(partners, 1)
-
-        hooks = {1: ("own", kernel_slab), 3: ("across", across_slab)}
+            return split_rows(
+                slab_in, rows, live, left_src, source, order, diagonal, flags, own_blocks, partial,
+            )
+
+        hooks = {1: ("own", kernel_slab), 2: ("across", across_halves[0]), 3: ("last", across_halves[1])}
     else:
         hooks = {}
         flags = jnp.full((block_count,), (my_index == 0).astype(jnp.int32))
@@ -305,8 +312,11 @@
         slab_in, running = lax.optimization_barrier((slab_in, running))
         if kind == "own":
             state["partial"] = own_part(slab_in)
+        elif kind == "across":
+            state["partial"] = across_part(slab_in, state["partial"], 0)
         else:
-            state["owned"] = across_part(slab_in, state["partial"])
+            mine, partners = across_part(slab_in, state["partial"], 1)
+            state["owned"] = mine + exchange(partners, 1)
         return running
 
     while shift < times:

time: 187 us -> 184 us (0.984)
  waiting for transfers between devices: 30.9 us -> 12.1 us
  Pallas kernels: 32.8 us -> 44.4 us
  local copies, waits for them, and re-layouts: 6.95 us -> 12.3 us
    ppermute x4 -> x5, waiting for transfers between devices: 29 us -> 12.1 us  [exchange(): lax.ppermute(value, 'row', [(src, src ^ step) for src in range(owners)])]
    pallas_call x2 -> x3, Pallas kernels: 32.8 us -> 44.4 us  [split_rows(): pl.pallas_call(functools.partial(split_kernel, group=group, accumulate=ac...]
    slice x0 -> x1, local copies, waits for them, and re-layouts: none -> 3.98 us  [local(): lax.slice_in_dim(kernel_slab, h * half_rows, (h + 1) * half_rows)]
    ppermute x3, starting transfers between devices: 14.8 us -> 12.7 us  [local(): moved = lax.ppermute(jnp.stack(running), 'tm', pairs)]
    ppermute x3, waiting for transfers between devices: 1.94 us -> 0.01 us  [local(): moved = lax.ppermute(jnp.stack(running), 'tm', pairs)]
    ppermute x4 -> x5, starting transfers between devices: 4.99 us -> 6.23 us  [exchange(): lax.ppermute(value, 'row', [(src, src ^ step) for src in range(owners)])]
  transfers between devices with their start and end apart: 7 -> 8, of which waited for: 6 -> 2; matrix products, arithmetic and copies ran while one was open for 30% -> 47% of each run, Pallas kernels for 8% -> 16%
where the time goes in v16:
time: 184 us; the launch traced here: 183 us
  other arithmetic  80.1 us (44%)
  Pallas kernels  44.4 us (24%)
  starting transfers between devices  19 us (10%)
  local copies, waits for them, and re-layouts  12.3 us (7%)
  waiting for transfers between devices  12.1 us (7%)
  matrix products  8.85 us (5%)
  between operations  6.3 us (3%)
    pallas_call x3, Pallas kernels, split_rows(): pl.pallas_call(functools.partial(split_kernel, group=group, accumulate=ac...  44.4 us
    another operation x9, other arithmetic, join_segments(): factor = jnp.linalg.cholesky(middle)  37.3 us
    another operation x6, other arithmetic, join_segments(): lax.linalg.triangular_solve(factor, jnp.concatenate([cross_one.T, cross_t...  31.4 us
    ppermute x3, starting transfers between devices, local(): moved = lax.ppermute(jnp.stack(running), 'tm', pairs)  12.7 us
    ppermute x5, waiting for transfers between devices, exchange(): lax.ppermute(value, 'row', [(src, src ^ step) for src in range(owners)])  12.1 us
    broadcast_in_dim x1, other arithmetic, local(): return (owned[None], chain_out)  6.57 us
    ppermute x5, starting transfers between devices, exchange(): lax.ppermute(value, 'row', [(src, src ^ step) for src in range(owners)])  6.23 us
    dot_general x3, matrix products, contract_rows(): lax.dot_general(left_cols, right_cols, (((0,), (0,)), ((), ())), preferre...  5.33 us
  transfers between devices with their start and end apart: 8, of which 2 were waited for; matrix products, arithmetic and copies ran while one was open for 47% of the time, Pallas kernels for 16%

profile of v16, /device:TPU:0, one launch (start us, length us, event | category | flops | bytes accessed | tf_op | source)
XLA Modules:
  0.0 183.0 jit_solution(7716506657248698443)
XLA Ops:
  0.6 0.8 select_reduce_fusion.3.src_right
  7.2 1.0 fusion.74
  8.2 1.8 convolution_bitcast_fusion
  10.0 1.8 convolution_bitcast_fusion.1
  11.8 1.8 convolution_bitcast_fusion.2
  13.6 0.8 reshape_squeeze.4.mask_ref
  16.3 0.8 fusion.86
  17.9 1.1 copy.77.w_ref
  19.7 2.6 %collective-permute-start.1 = (f32[53760]{0:T(1024)S(1)}, f32[53760]{0:T(1024)S(1)}, u32[]{:S(2)}, u32[]{:S(2)}) collective-permute-start(f32[53760]{0:T(1024)S(1)} %fusion.83), channel_id=1, source_target_pairs={{0,2},{1,3},{2,0},{3,1},{4,6},{5,7},{6,4},{7,5},{8,10},{9,11},{10,... | collective-permute-start | bytes 645128 | tf_op jit(solution)/shard_map/ppermute | solution.py:240
  22.9 5.3 %collective-permute-done.1 = f32[53760]{0:T(1024)S(1)} collective-permute-done((f32[53760]{0:T(1024)S(1)}, f32[53760]{0:T(1024)S(1)}, u32[]{:S(2)}, u32[]{:S(2)}) %collective-permute-start.1) | collective-permute-done | bytes 215072 | tf_op jit(solution)/shard_map/ppermute | solution.py:240
  28.4 3.7 %collective-permute-start.4 = (f32[3,128,128]{2,1,0:T(8,128)S(1)}, f32[3,128,128]{2,1,0:T(8,128)S(1)}, u32[]{:S(2)}, u32[]{:S(2)}) collective-permute-start(f32[3,128,128]{2,1,0:T(8,128)S(1)} %pad_maximum_fusion.2), channel_id=1, source_target_pairs={{0,4},{4,8},{8,12},{12,16},{16,20},{20,24},{24,28},{1,5},{5,9},{9,... | collective-permute-start | bytes 589832 | tf_op jit(solution)/shard_map/ppermute | solution.py:327
  32.0 4.0 %fusion.84 = (bf16[512,2048]{1,0:T(8,128)(2,1)}, bf16[512,2048]{1,0:T(8,128)(2,1)S(1)}) fusion(bf16[1024,2048]{1,0:T(8,128)(2,1)} %bitcast.167), kind=kLoop, calls=%fused_computation.147 | loop fusion | bytes 8388608 | tf_op jit(solution)/shard_map/slice | solution.py:266
  36.1 1.6 collective-permute-start.3
  38.1 11.7 %cholesky.59 = f32[128,128]{1,0:T(8,128)S(1)} custom-call(f32[128,128]{1,0:T(8,128)S(1)} %copy.59), custom_call_target="Cholesky" | custom-call | tf_op jit(solution)/shard_map/jit(cholesky)/cholesky | solution.py:185
  49.8 0.7 compare_reduce_fusion.2
  51.2 9.8 %custom-call.7 = f32[1,128,128]{1,2,0:T(8,128)S(1)} custom-call(f32[1,128,128]{2,1,0:T(8,128)S(1)} %fusion.31), custom_call_target="InvertDiagBlocksLowerTriangular" | custom-call | tf_op jit(solution)/shard_map/triangular_solve/custom-call.0 | solution.py:187
  62.4 3.9 %collective-permute-start.5 = (f32[3,128,128]{2,1,0:T(8,128)S(1)}, f32[3,128,128]{2,1,0:T(8,128)S(1)}, u32[]{:S(2)}, u32[]{:S(2)}) collective-permute-start(f32[3,128,128]{2,1,0:T(8,128)S(1)} %pad_maximum_fusion.3), channel_id=1, source_target_pairs={{0,8},{4,12},{8,16},{12,20},{16,24},{20,28},{1,9},{5,13},{9,17},{1... | collective-permute-start | bytes 589832 | tf_op jit(solution)/shard_map/ppermute | solution.py:327
  66.3 0.9 copy.78.w_ref
  67.2 1.5 collective-permute-start.2
  68.7 0.9 copy.79.w_ref
  69.9 11.7 %cholesky.70 = f32[128,128]{1,0:T(8,128)S(1)} custom-call(f32[128,128]{1,0:T(8,128)S(1)} %fusion.46), custom_call_target="Cholesky" | custom-call | tf_op jit(solution)/shard_map/jit(cholesky)/cholesky | solution.py:185
  81.7 0.7 compare_reduce_fusion.1
  83.1 9.8 %custom-call.8 = f32[1,128,128]{1,2,0:T(8,128)S(1)} custom-call(f32[1,128,128]{2,1,0:T(8,128)S(1)} %fusion.32), custom_call_target="InvertDiagBlocksLowerTriangular" | custom-call | tf_op jit(solution)/shard_map/triangular_solve/custom-call.0 | solution.py:187
  94.3 5.2 %collective-permute-start.6 = (f32[3,128,128]{2,1,0:T(8,128)S(1)}, f32[3,128,128]{2,1,0:T(8,128)S(1)}, u32[]{:S(2)}, u32[]{:S(2)}) collective-permute-start(f32[3,128,128]{2,1,0:T(8,128)S(1)} %pad_maximum_fusion.4), channel_id=1, source_target_pairs={{0,16},{4,20},{8,24},{12,28},{1,17},{5,21},{9,25},{13,29},{2,18},{... | collective-permute-start | bytes 589832 | tf_op jit(solution)/shard_map/ppermute | solution.py:327
  100.2 15.2 %shard_map.80 = (f32[512,2048]{1,0:T(8,128)}, f32[512,2048]{1,0:T(8,128)}) custom-call(s32[8]{0:T(128)} %get-tuple-element.46.src_left, s32[16]{0:T(128)} %copy-done, s32[8]{0:T(128)} %get-tuple-element.47.tile_ref, s32[128]{0:T(128)} %copy-done.2, s32[8]{0:T(128)} %compare_convert_fusion.flag_ref, bf16[1024,2048]{1,0:T(8,128)(2,1)} %bitcast.168, ...), custom_call_target="tpu_custom_call" | custom-call | tf_op jit(solution)/shard_map/pallas_call | solution.py:168
  115.3 14.6 %shard_map.81 = (f32[512,2048]{1,0:T(8,128)}, f32[512,2048]{1,0:T(8,128)}) custom-call(s32[8]{0:T(128)} %get-tuple-element.46.src_left, s32[16]{0:T(128)} %copy-done, s32[8]{0:T(128)} %get-tuple-element.47.tile_ref, s32[64]{0:T(128)} %get-tuple-element.58.mask_ref, s32[8]{0:T(128)} %compare_convert_fusion.flag_ref, ...), custom_call_target="tpu_custom_call", output_to_operand_aliasing={{0}: (8, {}), {1}: (9, {})} | custom-call | tf_op jit(solution)/shard_map/pallas_call | solution.py:168
  130.3 11.7 %cholesky.81 = f32[128,128]{1,0:T(8,128)S(1)} custom-call(f32[128,128]{1,0:T(8,128)S(1)} %fusion.44), custom_call_target="Cholesky" | custom-call | tf_op jit(solution)/shard_map/jit(cholesky)/cholesky | solution.py:185
  143.3 9.8 %custom-call.9 = f32[1,128,128]{1,2,0:T(8,128)S(1)} custom-call(f32[1,128,128]{2,1,0:T(8,128)S(1)} %fusion.33), custom_call_target="InvertDiagBlocksLowerTriangular" | custom-call | tf_op jit(solution)/shard_map/triangular_solve/custom-call.0 | solution.py:187
  154.3 14.6 %shard_map.82 = (f32[512,2048]{1,0:T(8,128)}, f32[512,2048]{1,0:T(8,128)}) custom-call(s32[8]{0:T(128)} %get-tuple-element.46.src_left, s32[16]{0:T(128)} %copy-done, s32[8]{0:T(128)} %get-tuple-element.47.tile_ref, s32[64]{0:T(128)} %get-tuple-element.59.mask_ref, s32[8]{0:T(128)} %compare_convert_fusion.flag_ref, ...), custom_call_target="tpu_custom_call", output_to_operand_aliasing={{0}: (8, {}), {1}: (9, {})} | custom-call | tf_op jit(solution)/shard_map/pallas_call | solution.py:168
  169.0 0.7 maximum_bitcast_fusion
  169.7 6.7 %collective-permute-done.7 = f32[512,2048]{1,0:T(8,128)} collective-permute-done((f32[512,2048]{1,0:T(8,128)}, f32[512,2048]{1,0:T(8,128)}, u32[]{:S(2)}, u32[]{:S(2)}) %collective-permute-start.7) | collective-permute-done | bytes 4194336 | tf_op jit(solution)/shard_map/ppermute | solution.py:240
  176.4 6.6 %add_bitcast_fusion = f32[1,512,2048]{2,1,0:T(8,128)} fusion(f32[512,2048]{1,0:T(8,128)} %get-tuple-element.39, f32[512,2048]{1,0:T(8,128)} %collective-permute-done.7), kind=kLoop, calls=%fused_computation.1 | loop fusion | flops 1048576 | bytes 12582912 | tf_op jit(solution)/shard_map/broadcast_in_dim | solution.py:338
  (86 shorter events, 13.1 us)
Async XLA Ops:
  0.6 17.2 %copy-start.1 = (f32[1,1024]{1,0:T(1,128)S(1)}, f32[1,1024]{1,0:T(1,128)}, u32[]{:S(2)}) copy-start(f32[1,1024]{1,0:T(1,128)} %param.10) | copy-start | bytes 12292
  1.4 34.6 %copy-start = (s32[16]{0:T(128)}, s32[16]{0:T(128)S(1)}, u32[]{:S(2)}) copy-start(s32[16]{0:T(128)S(1)} %select_reduce_fusion.3.src_right) | copy-start | bytes 196
  14.4 21.6 %copy-start.2 = (s32[128]{0:T(128)}, s32[128]{0:T(128)S(1)}, u32[]{:S(2)}) copy-start(s32[128]{0:T(128)S(1)} %reshape_squeeze.4.mask_ref) | copy-start | bytes 1540
  15.2 4.4 %collective-permute-start = (f32[53760]{0:T(1024)S(1)}, f32[53760]{0:T(1024)S(1)}, u32[]{:S(2)}, u32[]{:S(2)}) collective-permute-start(f32[53760]{0:T(1024)S(1)} %pad_maximum_fusion), channel_id=1, source_target_pairs={{0,1},{1,0},{2,3},{3,2},{4,5},{5,4},{6,7},{7,6},{8,9},{9,8},{10,11... | collective-permute-start | bytes 645128 | tf_op jit(solution)/shard_map/ppermute | solution.py:240
  19.7 8.6 %collective-permute-start.1 = (f32[53760]{0:T(1024)S(1)}, f32[53760]{0:T(1024)S(1)}, u32[]{:S(2)}, u32[]{:S(2)}) collective-permute-start(f32[53760]{0:T(1024)S(1)} %fusion.83), channel_id=1, source_target_pairs={{0,2},{1,3},{2,0},{3,1},{4,6},{5,7},{6,4},{7,5},{8,10},{9,11},{10,... | collective-permute-start | bytes 645128 | tf_op jit(solution)/shard_map/ppermute | solution.py:240
  28.4 9.4 %collective-permute-start.4 = (f32[3,128,128]{2,1,0:T(8,128)S(1)}, f32[3,128,128]{2,1,0:T(8,128)S(1)}, u32[]{:S(2)}, u32[]{:S(2)}) collective-permute-start(f32[3,128,128]{2,1,0:T(8,128)S(1)} %pad_maximum_fusion.2), channel_id=1, source_target_pairs={{0,4},{4,8},{8,12},{12,16},{16,20},{20,24},{24,28},{1,5},{5,9},{9,... | collective-permute-start | bytes 589832 | tf_op jit(solution)/shard_map/ppermute | solution.py:327
  36.1 58.0 %collective-permute-start.3 = (bf16[512,2048]{1,0:T(8,128)(2,1)}, bf16[512,2048]{1,0:T(8,128)(2,1)}, u32[]{:S(2)}, u32[]{:S(2)}) collective-permute-start(bf16[512,2048]{1,0:T(8,128)(2,1)} %get-tuple-element.48), channel_id=1, source_target_pairs={{0,2},{1,3},{2,0},{3,1},{4,6},{5,7},{6,4},{7,5},{8,10},{9,11},{10,... | collective-permute-start | bytes 6291464 | tf_op jit(solution)/shard_map/ppermute | solution.py:240
  62.4 7.3 %collective-permute-start.5 = (f32[3,128,128]{2,1,0:T(8,128)S(1)}, f32[3,128,128]{2,1,0:T(8,128)S(1)}, u32[]{:S(2)}, u32[]{:S(2)}) collective-permute-start(f32[3,128,128]{2,1,0:T(8,128)S(1)} %pad_maximum_fusion.3), channel_id=1, source_target_pairs={{0,8},{4,12},{8,16},{12,20},{16,24},{20,28},{1,9},{5,13},{9,17},{1... | collective-permute-start | bytes 589832 | tf_op jit(solution)/shard_map/ppermute | solution.py:327
  67.2 87.1 %collective-permute-start.2 = (bf16[512,2048]{1,0:T(8,128)(2,1)S(1)}, bf16[512,2048]{1,0:T(8,128)(2,1)}, u32[]{:S(2)}, u32[]{:S(2)}) collective-permute-start(bf16[512,2048]{1,0:T(8,128)(2,1)S(1)} %get-tuple-element.49), channel_id=1, source_target_pairs={{0,2},{1,3},{2,0},{3,1},{4,6},{5,7},{6,4},{7,5},{8,10},{9,11},{10,... | collective-permute-start | bytes 6291464 | tf_op jit(solution)/shard_map/ppermute | solution.py:240
  94.3 35.7 %collective-permute-start.6 = (f32[3,128,128]{2,1,0:T(8,128)S(1)}, f32[3,128,128]{2,1,0:T(8,128)S(1)}, u32[]{:S(2)}, u32[]{:S(2)}) collective-permute-start(f32[3,128,128]{2,1,0:T(8,128)S(1)} %pad_maximum_fusion.4), channel_id=1, source_target_pairs={{0,16},{4,20},{8,24},{12,28},{1,17},{5,21},{9,25},{13,29},{2,18},{... | collective-permute-start | bytes 589832 | tf_op jit(solution)/shard_map/ppermute | solution.py:327
  168.9 7.5 %collective-permute-start.7 = (f32[512,2048]{1,0:T(8,128)}, f32[512,2048]{1,0:T(8,128)}, u32[]{:S(2)}, u32[]{:S(2)}) collective-permute-start(f32[512,2048]{1,0:T(8,128)} %get-tuple-element.40), channel_id=1, source_target_pairs={{0,1},{1,0},{2,3},{3,2},{4,5},{5,4},{6,7},{7,6},{8,9},{9,8},{10,11... | collective-permute-start | bytes 12582920 | tf_op jit(solution)/shard_map/ppermute | solution.py:240

commit v17 on v16

--- a/solution.py
+++ b/solution.py
@@ -12,7 +12,10 @@
 
 
 def gram_kernel(src_left, src_right, tile_ref, mask_ref, flag_ref, g_ref, w_ref, diag_ref, *rest):
-    if len(rest) == 4:
+    extra_ref = None
+    if len(rest) == 5:
+        acc_ref, extra_ref, out_ref, s_ref, lt_ref = rest
+    elif len(rest) == 4:
         acc_ref, out_ref, s_ref, lt_ref = rest
     else:
         acc_ref = None
@@ -50,11 +53,14 @@
         cols = lax.broadcasted_iota(jnp.int32, (BLK, BLK), 1)
         dvals = diag_ref[pl.ds(blk, 1), :] * flag_ref[k].astype(jnp.float32)
         out_ref[:, pl.ds(e0, BLK)] += jnp.where(rows == cols, dvals, 0.0)
-    else:
+    elif extra_ref is None:
         out_ref[...] = acc_ref[...] + term
-
-
-def gram_rows(slab, weights, live_blocks, src_left, src_right, out_tiles, diagonal, flags, group, acc=None):
+    else:
+        out_ref[...] = (acc_ref[...] + extra_ref[...]) + term
+
+
+def gram_rows(slab, weights, live_blocks, src_left, src_right, out_tiles, diagonal, flags, group, acc=None,
+              extra=None):
     height = slab.shape[0]
     col_blocks = L // BLK
     out_blocks = src_left.shape[0]
@@ -70,6 +76,9 @@
         in_specs.append(out_spec)
         operands.append(acc)
         aliases = {8: 0}
+    if extra is not None:
+        in_specs.append(out_spec)
+        operands.append(extra)
     grid_spec = pltpu.PrefetchScalarGridSpec(
         num_scalar_prefetch=5,
         grid=(out_blocks,),
@@ -289,6 +298,26 @@
                 slab_in, rows, live, left_src, source, order, diagonal, flags, own_blocks, partial,
             )
 
+        partner_side = lax.dynamic_index_in_dim(every_side, my_index ^ 3, 0, False)
+        partner_weights = partner_side[:slab_height]
+        partner_live = partner_side[slab_height:].reshape(live_blocks.shape).astype(jnp.int32)
+        last_weights = jnp.concatenate([
+            lax.slice_in_dim(across_weights, half_rows, slab_height),
+            lax.slice_in_dim(partner_weights, half_rows, slab_height),
+        ])
+        last_live = jnp.concatenate([
+            lax.slice_in_dim(across_live, half_rows // BLK, slab_height // BLK),
+            lax.slice_in_dim(partner_live, half_rows // BLK, slab_height // BLK),
+        ])
+        mine_order = order[:own_blocks]
+
+        def last_part(slab_in, mine, received):
+            total = gram_rows(
+                slab_in, last_weights, last_live, jnp.take(source, mine_order), source, mine_order,
+                diagonal, flags[:own_blocks], own_blocks, mine[None], received[None],
+            )
+            return total[0]
+
         hooks = {1: ("own", kernel_slab), 2: ("across", across_halves[0]), 3: ("last", across_halves[1])}
     else:
         hooks = {}
@@ -313,10 +342,12 @@
         if kind == "own":
             state["partial"] = own_part(slab_in)
         elif kind == "across":
-            state["partial"] = across_part(slab_in, state["partial"], 0)
+            mine, partners = across_part(slab_in, state["partial"], 0)
+            state["mine"] = mine
+            state["received"] = exchange(partners, 1)
         else:
-            mine, partners = across_part(slab_in, state["partial"], 1)
-            state["owned"] = mine + exchange(partners, 1)
+            both = jnp.concatenate([slab_in, exchange(slab_in, 1)], axis=0)
+            state["owned"] = last_part(both, state["mine"], state["received"])
         return running
 
     while shift < times:

time: 184 us -> 176 us (0.957)
  waiting for transfers between devices: 12.1 us -> 5.95 us
    pallas_call x3 -> x2, Pallas kernels: 44.4 us -> 29.9 us  [split_rows(): pl.pallas_call(functools.partial(split_kernel, group=group, accumulate=ac...]
    pallas_call x0 -> x1, Pallas kernels: none -> 12.8 us  [gram_rows(): pl.pallas_call(gram_kernel, grid_spec=grid_spec, out_shape=jax.ShapeDtype...]
    ppermute x5 -> x6, waiting for transfers between devices: 12.1 us -> 5.42 us  [exchange(): lax.ppermute(value, 'row', [(src, src ^ step) for src in range(owners)])]
    broadcast_in_dim x1 -> x0, other arithmetic: 6.57 us -> none  [local(): return (owned[None], chain_out)]
    concatenate x0 -> x3, other arithmetic: none -> 4.1 us  [the longest x1 4.08 us: run_hook(): both = jnp.concatenate([slab_in, exchange(slab_in, 1)], axis=0)]
    ppermute x5 -> x6, starting transfers between devices: 6.23 us -> 6.79 us  [exchange(): lax.ppermute(value, 'row', [(src, src ^ step) for src in range(owners)])]
  transfers between devices with their start and end apart: 8 -> 9, of which waited for: 2 -> 3; matrix products, arithmetic and copies ran while one was open for 47% -> 52% of each run, Pallas kernels for 16% -> 17%
where the time goes in v17:
time: 176 us
  other arithmetic  78.8 us (45%)
  Pallas kernels  42.7 us (24%)
  starting transfers between devices  19.8 us (11%)
  local copies, waits for them, and re-layouts  13 us (7%)
  matrix products  8.97 us (5%)
  between operations  6.31 us (4%)
  waiting for transfers between devices  5.95 us (3%)
    another operation x9, other arithmetic, join_segments(): factor = jnp.linalg.cholesky(middle)  37.2 us
    another operation x6, other arithmetic, join_segments(): lax.linalg.triangular_solve(factor, jnp.concatenate([cross_one.T, cross_t...  31.4 us
    pallas_call x2, Pallas kernels, split_rows(): pl.pallas_call(functools.partial(split_kernel, group=group, accumulate=ac...  29.9 us
    ppermute x3, starting transfers between devices, local(): moved = lax.ppermute(jnp.stack(running), 'tm', pairs)  13 us
    pallas_call x1, Pallas kernels, gram_rows(): pl.pallas_call(gram_kernel, grid_spec=grid_spec, out_shape=jax.ShapeDtype...  12.8 us
    ppermute x6, starting transfers between devices, exchange(): lax.ppermute(value, 'row', [(src, src ^ step) for src in range(owners)])  6.79 us
    dot_general x3, matrix products, contract_rows(): lax.dot_general(left_cols, right_cols, (((0,), (0,)), ((), ())), preferre...  5.46 us
    ppermute x6, waiting for transfers between devices, exchange(): lax.ppermute(value, 'row', [(src, src ^ step) for src in range(owners)])  5.42 us
  transfers between devices with their start and end apart: 9, of which 3 were waited for; matrix products, arithmetic and copies ran while one was open for 52% of the time, Pallas kernels for 17%

profile of v17, /device:TPU:0, one launch (start us, length us, event | category | flops | bytes accessed | tf_op | source)
XLA Modules:
  0.0 175.5 jit_solution(13492820911315696697)
XLA Ops:
  0.6 0.8 select_reduce_fusion.3.src_right
  7.2 1.0 fusion.74
  8.2 1.9 %convolution_bitcast_fusion = f32[1,128,128]{2,1,0:T(8,128)S(1)} fusion(f32[1024]{0:T(1024)} %bitcast.184, bf16[1,1024,2048]{2,1,0:T(8,128)(2,1)} %param.9, s32[]{:T(128)S(6)} %select_n.111, bf16[1024]{0:T(1024)(128)(2,1)S(1)} %get-tuple-element.64), kind=kOutput, calls=%fused_computation.15 | convolution fusion | flops 34865152 | bytes 599040 | tf_op jit(solution)/shard_map/dot_general | solution.py:208
  10.1 1.8 %convolution_bitcast_fusion.1 = f32[1,128,128]{2,1,0:T(8,128)S(1)} fusion(f32[1024]{0:T(1024)} %bitcast.185, bf16[1,1024,2048]{2,1,0:T(8,128)(2,1)} %param.9, s32[]{:T(128)S(6)} %select_n.109, s32[]{:T(128)S(6)} %select_n.111, bf16[1024]{0:T(1024)(128)(2,1)S(1)} %get-tuple-element.64, bf16[1024]{0:T(1024)(128)(2,1)S(1)} %get-tuple-element.65), kind=kOutput, calls=%fused_computation.16 | convolution fusion | flops 34865152 | bytes 598024 | tf_op jit(solution)/shard_map/dot_general | solution.py:208
  11.9 1.8 %convolution_bitcast_fusion.2 = f32[1,128,128]{2,1,0:T(8,128)S(1)} fusion(f32[1024]{0:T(1024)} %bitcast.186, bf16[1,1024,2048]{2,1,0:T(8,128)(2,1)} %param.9, s32[]{:T(128)S(6)} %select_n.109, bf16[1024]{0:T(1024)(128)(2,1)S(1)} %get-tuple-element.65), kind=kOutput, calls=%fused_computation.17 | convolution fusion | flops 34865152 | bytes 599040 | tf_op jit(solution)/shard_map/dot_general | solution.py:208
  13.7 0.8 reshape_squeeze.4.mask_ref
  14.5 0.7 pad_maximum_fusion.6
  16.4 0.8 compare_select_fusion.2
  17.9 1.0 copy.76.w_ref
  19.0 0.7 slice_bitcast_fusion.13
  19.7 2.6 %collective-permute-start.1 = (f32[53760]{0:T(1024)S(1)}, f32[53760]{0:T(1024)S(1)}, u32[]{:S(2)}, u32[]{:S(2)}) collective-permute-start(f32[53760]{0:T(1024)S(1)} %fusion.83), channel_id=1, source_target_pairs={{0,2},{1,3},{2,0},{3,1},{4,6},{5,7},{6,4},{7,5},{8,10},{9,11},{10,... | collective-permute-start | bytes 645128 | tf_op jit(solution)/shard_map/ppermute | solution.py:249
  22.3 0.7 and_select_fusion
  23.0 5.3 %collective-permute-done.1 = f32[53760]{0:T(1024)S(1)} collective-permute-done((f32[53760]{0:T(1024)S(1)}, f32[53760]{0:T(1024)S(1)}, u32[]{:S(2)}, u32[]{:S(2)}) %collective-permute-start.1) | collective-permute-done | bytes 215072 | tf_op jit(solution)/shard_map/ppermute | solution.py:249
  28.4 3.5 %collective-permute-start.4 = (f32[3,128,128]{2,1,0:T(8,128)S(1)}, f32[3,128,128]{2,1,0:T(8,128)S(1)}, u32[]{:S(2)}, u32[]{:S(2)}) collective-permute-start(f32[3,128,128]{2,1,0:T(8,128)S(1)} %pad_maximum_fusion.3), channel_id=1, source_target_pairs={{0,4},{4,8},{8,12},{12,16},{16,20},{20,24},{24,28},{1,5},{5,9},{9,... | collective-permute-start | bytes 589832 | tf_op jit(solution)/shard_map/ppermute | solution.py:358
  31.9 4.0 %fusion.84 = (bf16[512,2048]{1,0:T(8,128)(2,1)}, bf16[512,2048]{1,0:T(8,128)(2,1)S(1)}) fusion(bf16[1024,2048]{1,0:T(8,128)(2,1)} %bitcast.168), kind=kLoop, calls=%fused_computation.154 | loop fusion | bytes 8388608 | tf_op jit(solution)/shard_map/slice | solution.py:275
  36.0 1.6 collective-permute-start.3
  38.0 11.7 %cholesky.59 = f32[128,128]{1,0:T(8,128)S(1)} custom-call(f32[128,128]{1,0:T(8,128)S(1)} %copy.58), custom_call_target="Cholesky" | custom-call | tf_op jit(solution)/shard_map/jit(cholesky)/cholesky | solution.py:194
  51.0 9.8 %custom-call.7 = f32[1,128,128]{1,2,0:T(8,128)S(1)} custom-call(f32[1,128,128]{2,1,0:T(8,128)S(1)} %fusion.31), custom_call_target="InvertDiagBlocksLowerTriangular" | custom-call | tf_op jit(solution)/shard_map/triangular_solve/custom-call.0 | solution.py:196
  62.2 3.8 %collective-permute-start.5 = (f32[3,128,128]{2,1,0:T(8,128)S(1)}, f32[3,128,128]{2,1,0:T(8,128)S(1)}, u32[]{:S(2)}, u32[]{:S(2)}) collective-permute-start(f32[3,128,128]{2,1,0:T(8,128)S(1)} %pad_maximum_fusion.4), channel_id=1, source_target_pairs={{0,8},{4,12},{8,16},{12,20},{16,24},{20,28},{1,9},{5,13},{9,17},{1... | collective-permute-start | bytes 589832 | tf_op jit(solution)/shard_map/ppermute | solution.py:358
  66.1 0.9 copy.77.w_ref
  67.0 1.5 collective-permute-start.2
  69.3 11.7 %cholesky.70 = f32[128,128]{1,0:T(8,128)S(1)} custom-call(f32[128,128]{1,0:T(8,128)S(1)} %fusion.46), custom_call_target="Cholesky" | custom-call | tf_op jit(solution)/shard_map/jit(cholesky)/cholesky | solution.py:194
  82.4 9.8 %custom-call.8 = f32[1,128,128]{1,2,0:T(8,128)S(1)} custom-call(f32[1,128,128]{2,1,0:T(8,128)S(1)} %fusion.32), custom_call_target="InvertDiagBlocksLowerTriangular" | custom-call | tf_op jit(solution)/shard_map/triangular_solve/custom-call.0 | solution.py:196
  93.6 5.6 %collective-permute-start.6 = (f32[3,128,128]{2,1,0:T(8,128)S(1)}, f32[3,128,128]{2,1,0:T(8,128)S(1)}, u32[]{:S(2)}, u32[]{:S(2)}) collective-permute-start(f32[3,128,128]{2,1,0:T(8,128)S(1)} %pad_maximum_fusion.5), channel_id=1, source_target_pairs={{0,16},{4,20},{8,24},{12,28},{1,17},{5,21},{9,25},{13,29},{2,18},{... | collective-permute-start | bytes 589832 | tf_op jit(solution)/shard_map/ppermute | solution.py:358
  99.7 15.2 %shard_map.80 = (f32[512,2048]{1,0:T(8,128)}, f32[512,2048]{1,0:T(8,128)}) custom-call(s32[8]{0:T(128)} %get-tuple-element.42.src_left, s32[16]{0:T(128)} %copy-done, s32[8]{0:T(128)} %get-tuple-element.43.tile_ref, s32[128]{0:T(128)} %copy-done.4, s32[8]{0:T(128)} %compare_convert_fusion.flag_ref, bf16[1024,2048]{1,0:T(8,128)(2,1)} %bitcast.169, ...), custom_call_target="tpu_custom_call" | custom-call | tf_op jit(solution)/shard_map/pallas_call | solution.py:177
  114.9 14.7 %shard_map.81 = (f32[512,2048]{1,0:T(8,128)}, f32[512,2048]{1,0:T(8,128)}) custom-call(s32[8]{0:T(128)} %get-tuple-element.42.src_left, s32[16]{0:T(128)} %copy-done, s32[8]{0:T(128)} %get-tuple-element.43.tile_ref, s32[64]{0:T(128)} %get-tuple-element.59.mask_ref, s32[8]{0:T(128)} %compare_convert_fusion.flag_ref, ...), custom_call_target="tpu_custom_call", output_to_operand_aliasing={{0}: (8, {}), {1}: (9, {})} | custom-call | tf_op jit(solution)/shard_map/pallas_call | solution.py:177
  130.0 11.7 %cholesky.81 = f32[128,128]{1,0:T(8,128)S(1)} custom-call(f32[128,128]{1,0:T(8,128)S(1)} %fusion.44), custom_call_target="Cholesky" | custom-call | tf_op jit(solution)/shard_map/jit(cholesky)/cholesky | solution.py:194
  143.0 9.8 %custom-call.9 = f32[1,128,128]{1,2,0:T(8,128)S(1)} custom-call(f32[1,128,128]{2,1,0:T(8,128)S(1)} %fusion.33), custom_call_target="InvertDiagBlocksLowerTriangular" | custom-call | tf_op jit(solution)/shard_map/triangular_solve/custom-call.0 | solution.py:196
  155.8 1.1 copy.78.w_ref
  157.9 0.7 maximum_bitcast_fusion
  158.6 4.1 %pad_maximum_fusion.g_ref = bf16[1024,2048]{1,0:T(8,128)(2,1)} fusion(bf16[512,2048]{1,0:T(8,128)(2,1)S(1)} %collective-permute-done.7, bf16[512,2048]{1,0:T(8,128)(2,1)} %collective-permute-done.2), kind=kLoop, calls=%fused_computation.2 | loop fusion | flops 8388608 | bytes 8388608 | tf_op jit(solution)/shard_map/concatenate | solution.py:349
  162.7 12.8 %shard_map.82 = f32[1,512,2048]{2,1,0:T(8,128)} custom-call(s32[4]{0:T(128)} %and_select_fusion.1.src_left, s32[16]{0:T(128)} %copy-done, s32[4]{0:T(128)} %copy-done.3, s32[128]{0:T(128)} %reshape.289.mask_ref, s32[4]{0:T(128)} %bitcast.193, bf16[1024,2048]{1,0:T(8,128)(2,1)} %pad_maximum_fusion.g_ref, ...), custom_call_target="tpu_custom_call", output_to_operand_aliasing={{}: (8, {})} | custom-call | tf_op jit(solution)/shard_map/pallas_call | solution.py:89
  (101 shorter events, 15.4 us)
Async XLA Ops:
  0.6 17.3 %copy-start.2 = (f32[1,1024]{1,0:T(1,128)S(1)}, f32[1,1024]{1,0:T(1,128)}, u32[]{:S(2)}) copy-start(f32[1,1024]{1,0:T(1,128)} %param.10) | copy-start | bytes 12292
  1.4 34.5 %copy-start = (s32[16]{0:T(128)}, s32[16]{0:T(128)S(1)}, u32[]{:S(2)}) copy-start(s32[16]{0:T(128)S(1)} %select_reduce_fusion.3.src_right) | copy-start | bytes 196
  14.5 21.4 %copy-start.4 = (s32[128]{0:T(128)}, s32[128]{0:T(128)S(1)}, u32[]{:S(2)}) copy-start(s32[128]{0:T(128)S(1)} %reshape_squeeze.4.mask_ref) | copy-start | bytes 1540
  15.3 4.3 %collective-permute-start = (f32[53760]{0:T(1024)S(1)}, f32[53760]{0:T(1024)S(1)}, u32[]{:S(2)}, u32[]{:S(2)}) collective-permute-start(f32[53760]{0:T(1024)S(1)} %pad_maximum_fusion.1), channel_id=1, source_target_pairs={{0,1},{1,0},{2,3},{3,2},{4,5},{5,4},{6,7},{7,6},{8,9},{9,8},{10,11... | collective-permute-start | bytes 645128 | tf_op jit(solution)/shard_map/ppermute | solution.py:249
  17.2 138.1 %copy-start.3 = (s32[4]{0:T(128)}, s32[4]{0:T(128)S(1)}, u32[]{:S(2)}) copy-start(s32[4]{0:T(128)S(1)} %get-tuple-element.45.tile_ref) | copy-start | bytes 52
  19.7 8.6 %collective-permute-start.1 = (f32[53760]{0:T(1024)S(1)}, f32[53760]{0:T(1024)S(1)}, u32[]{:S(2)}, u32[]{:S(2)}) collective-permute-start(f32[53760]{0:T(1024)S(1)} %fusion.83), channel_id=1, source_target_pairs={{0,2},{1,3},{2,0},{3,1},{4,6},{5,7},{6,4},{7,5},{8,10},{9,11},{10,... | collective-permute-start | bytes 645128 | tf_op jit(solution)/shard_map/ppermute | solution.py:249
  28.4 9.2 %collective-permute-start.4 = (f32[3,128,128]{2,1,0:T(8,128)S(1)}, f32[3,128,128]{2,1,0:T(8,128)S(1)}, u32[]{:S(2)}, u32[]{:S(2)}) collective-permute-start(f32[3,128,128]{2,1,0:T(8,128)S(1)} %pad_maximum_fusion.3), channel_id=1, source_target_pairs={{0,4},{4,8},{8,12},{12,16},{16,20},{20,24},{24,28},{1,5},{5,9},{9,... | collective-permute-start | bytes 589832 | tf_op jit(solution)/shard_map/ppermute | solution.py:358
  36.0 57.4 %collective-permute-start.3 = (bf16[512,2048]{1,0:T(8,128)(2,1)}, bf16[512,2048]{1,0:T(8,128)(2,1)}, u32[]{:S(2)}, u32[]{:S(2)}) collective-permute-start(bf16[512,2048]{1,0:T(8,128)(2,1)} %get-tuple-element.46), channel_id=1, source_target_pairs={{0,2},{1,3},{2,0},{3,1},{4,6},{5,7},{6,4},{7,5},{8,10},{9,11},{10,... | collective-permute-start | bytes 6291464 | tf_op jit(solution)/shard_map/ppermute | solution.py:249
  62.2 6.9 %collective-permute-start.5 = (f32[3,128,128]{2,1,0:T(8,128)S(1)}, f32[3,128,128]{2,1,0:T(8,128)S(1)}, u32[]{:S(2)}, u32[]{:S(2)}) collective-permute-start(f32[3,128,128]{2,1,0:T(8,128)S(1)} %pad_maximum_fusion.4), channel_id=1, source_target_pairs={{0,8},{4,12},{8,16},{12,20},{16,24},{20,28},{1,9},{5,13},{9,17},{1... | collective-permute-start | bytes 589832 | tf_op jit(solution)/shard_map/ppermute | solution.py:358
  67.0 87.1 %collective-permute-start.2 = (bf16[512,2048]{1,0:T(8,128)(2,1)S(1)}, bf16[512,2048]{1,0:T(8,128)(2,1)}, u32[]{:S(2)}, u32[]{:S(2)}) collective-permute-start(bf16[512,2048]{1,0:T(8,128)(2,1)S(1)} %get-tuple-element.47), channel_id=1, source_target_pairs={{0,2},{1,3},{2,0},{3,1},{4,6},{5,7},{6,4},{7,5},{8,10},{9,11},{10,... | collective-permute-start | bytes 6291464 | tf_op jit(solution)/shard_map/ppermute | solution.py:249
  93.6 36.1 %collective-permute-start.6 = (f32[3,128,128]{2,1,0:T(8,128)S(1)}, f32[3,128,128]{2,1,0:T(8,128)S(1)}, u32[]{:S(2)}, u32[]{:S(2)}) collective-permute-start(f32[3,128,128]{2,1,0:T(8,128)S(1)} %pad_maximum_fusion.5), channel_id=1, source_target_pairs={{0,16},{4,20},{8,24},{12,28},{1,17},{5,21},{9,25},{13,29},{2,18},{... | collective-permute-start | bytes 589832 | tf_op jit(solution)/shard_map/ppermute | solution.py:358
  114.9 39.7 %copy-start.1 = (s32[16]{0:T(128)S(1)}, s32[16]{0:T(128)}, u32[]{:S(2)}) copy-start(s32[16]{0:T(128)} %copy-done) | copy-start | bytes 196
  129.6 33.1 %collective-permute-start.8 = (f32[512,2048]{1,0:T(8,128)}, f32[512,2048]{1,0:T(8,128)}, u32[]{:S(2)}, u32[]{:S(2)}) collective-permute-start(f32[512,2048]{1,0:T(8,128)} %get-tuple-element.36), channel_id=1, source_target_pairs={{0,1},{1,0},{2,3},{3,2},{4,5},{5,4},{6,7},{7,6},{8,9},{9,8},{10,11... | collective-permute-start | bytes 12582920 | tf_op jit(solution)/shard_map/ppermute | solution.py:249
  154.1 4.6 %collective-permute-start.7 = (bf16[512,2048]{1,0:T(8,128)(2,1)}, bf16[512,2048]{1,0:T(8,128)(2,1)S(1)}, u32[]{:S(2)}, u32[]{:S(2)}) collective-permute-start(bf16[512,2048]{1,0:T(8,128)(2,1)} %collective-permute-done.2), channel_id=1, source_target_pairs={{0,1},{1,0},{2,3},{3,2},{4,5},{5,4},{6,7},{7,6},{8,9},{9,8},{10,11... | collective-permute-start | bytes 6291464 | tf_op jit(solution)/shard_map/ppermute | solution.py:249

commit v18 on v17

--- a/solution.py
+++ b/solution.py
@@ -235,12 +235,12 @@
 
     first_cols, first_scaled = edge_cols(0)
     final_cols, final_scaled = edge_cols(block_count - 1)
+    edge_gram = contract_rows(
+        jnp.concatenate([first_cols, final_cols], axis=1),
+        jnp.concatenate([first_scaled, final_scaled], axis=1),
+    )
     part_pieces = jnp.stack(
-        [
-            contract_rows(first_cols, first_scaled),
-            contract_rows(first_cols, final_scaled),
-            contract_rows(final_cols, final_scaled),
-        ]
+        [edge_gram[:BLK, :BLK], edge_gram[:BLK, BLK:], edge_gram[BLK:, BLK:]]
     )
     owners = lax.axis_size("row")
     own_blocks = block_count // owners

time: 176 us -> 171 us (0.972)
  matrix products: 8.97 us -> 3.86 us
    dot_general x3 -> x1, matrix products: 5.46 us -> 0.35 us  [contract_rows(): lax.dot_general(left_cols, right_cols, (((0,), (0,)), ((), ())), preferre...]
  transfers between devices with their start and end apart: 9 -> 9, of which waited for: 3 -> 3; matrix products, arithmetic and copies ran while one was open for 52% -> 53% of each run, Pallas kernels for 17% -> 18%
where the time goes in v18:
time: 171 us
  other arithmetic  78.9 us (46%)
  Pallas kernels  42.7 us (25%)
  starting transfers between devices  19.9 us (12%)
  local copies, waits for them, and re-layouts  13.1 us (8%)
  between operations  6.4 us (4%)
  waiting for transfers between devices  5.94 us (3%)
  matrix products  3.86 us (2%)
    another operation x9, other arithmetic, join_segments(): factor = jnp.linalg.cholesky(middle)  37.2 us
    another operation x6, other arithmetic, join_segments(): lax.linalg.triangular_solve(factor, jnp.concatenate([cross_one.T, cross_t...  31.4 us
    pallas_call x2, Pallas kernels, split_rows(): pl.pallas_call(functools.partial(split_kernel, group=group, accumulate=ac...  29.9 us
    ppermute x3, starting transfers between devices, local(): moved = lax.ppermute(jnp.stack(running), 'tm', pairs)  13.1 us
    pallas_call x1, Pallas kernels, gram_rows(): pl.pallas_call(gram_kernel, grid_spec=grid_spec, out_shape=jax.ShapeDtype...  12.8 us
    ppermute x6, starting transfers between devices, exchange(): lax.ppermute(value, 'row', [(src, src ^ step) for src in range(owners)])  6.79 us
    ppermute x6, waiting for transfers between devices, exchange(): lax.ppermute(value, 'row', [(src, src ^ step) for src in range(owners)])  5.41 us
    concatenate x1, other arithmetic, run_hook(): both = jnp.concatenate([slab_in, exchange(slab_in, 1)], axis=0)  4.05 us
  transfers between devices with their start and end apart: 9, of which 3 were waited for; matrix products, arithmetic and copies ran while one was open for 53% of the time, Pallas kernels for 18%

profile of v18, /device:TPU:0, one launch (start us, length us, event | category | flops | bytes accessed | tf_op | source)
XLA Modules:
  0.0 170.8 jit_solution(9927040191108388089)
XLA Ops:
  0.7 0.8 select_reduce_fusion.3.src_right
  5.9 0.8 reshape_squeeze.4.mask_ref
  8.0 1.0 fusion.68
  9.0 1.5 multiply_convert_fusion.1
  13.0 1.0 copy.76.w_ref
  14.1 0.7 slice_bitcast_fusion.16
  14.8 2.6 %collective-permute-start.1 = (f32[53760]{0:T(1024)S(1)}, f32[53760]{0:T(1024)S(1)}, u32[]{:S(2)}, u32[]{:S(2)}) collective-permute-start(f32[53760]{0:T(1024)S(1)} %fusion.75), channel_id=1, source_target_pairs={{0,2},{1,3},{2,0},{3,1},{4,6},{5,7},{6,4},{7,5},{8,10},{9,11},{10,... | collective-permute-start | bytes 645128 | tf_op jit(solution)/shard_map/ppermute | solution.py:249
  17.4 0.7 and_select_fusion
  18.1 5.3 %collective-permute-done.1 = f32[53760]{0:T(1024)S(1)} collective-permute-done((f32[53760]{0:T(1024)S(1)}, f32[53760]{0:T(1024)S(1)}, u32[]{:S(2)}, u32[]{:S(2)}) %collective-permute-start.1) | collective-permute-done | bytes 215072 | tf_op jit(solution)/shard_map/ppermute | solution.py:249
  23.5 3.6 %collective-permute-start.4 = (f32[3,128,128]{2,1,0:T(8,128)S(1)}, f32[3,128,128]{2,1,0:T(8,128)S(1)}, u32[]{:S(2)}, u32[]{:S(2)}) collective-permute-start(f32[3,128,128]{2,1,0:T(8,128)S(1)} %pad_maximum_fusion.3), channel_id=1, source_target_pairs={{0,4},{4,8},{8,12},{12,16},{16,20},{20,24},{24,28},{1,5},{5,9},{9,... | collective-permute-start | bytes 589832 | tf_op jit(solution)/shard_map/ppermute | solution.py:358
  27.1 4.0 %fusion.76 = (bf16[512,2048]{1,0:T(8,128)(2,1)}, bf16[512,2048]{1,0:T(8,128)(2,1)S(1)}) fusion(bf16[1024,2048]{1,0:T(8,128)(2,1)} %bitcast.158), kind=kLoop, calls=%fused_computation.149 | loop fusion | bytes 8388608 | tf_op jit(solution)/shard_map/slice | solution.py:275
  31.2 1.6 collective-permute-start.3
  33.2 11.7 %cholesky.59 = f32[128,128]{1,0:T(8,128)S(1)} custom-call(f32[128,128]{1,0:T(8,128)S(1)} %copy.58), custom_call_target="Cholesky" | custom-call | tf_op jit(solution)/shard_map/jit(cholesky)/cholesky | solution.py:194
  45.6 0.7 fusion.25
  46.3 9.8 %custom-call.7 = f32[1,128,128]{1,2,0:T(8,128)S(1)} custom-call(f32[1,128,128]{2,1,0:T(8,128)S(1)} %fusion.25), custom_call_target="InvertDiagBlocksLowerTriangular" | custom-call | tf_op jit(solution)/shard_map/triangular_solve/custom-call.0 | solution.py:196
  57.4 3.9 %collective-permute-start.5 = (f32[3,128,128]{2,1,0:T(8,128)S(1)}, f32[3,128,128]{2,1,0:T(8,128)S(1)}, u32[]{:S(2)}, u32[]{:S(2)}) collective-permute-start(f32[3,128,128]{2,1,0:T(8,128)S(1)} %pad_maximum_fusion.4), channel_id=1, source_target_pairs={{0,8},{4,12},{8,16},{12,20},{16,24},{20,28},{1,9},{5,13},{9,17},{1... | collective-permute-start | bytes 589832 | tf_op jit(solution)/shard_map/ppermute | solution.py:358
  61.4 0.9 copy.77.w_ref
  62.2 1.5 collective-permute-start.2
  64.6 11.7 %cholesky.70 = f32[128,128]{1,0:T(8,128)S(1)} custom-call(f32[128,128]{1,0:T(8,128)S(1)} %fusion.40), custom_call_target="Cholesky" | custom-call | tf_op jit(solution)/shard_map/jit(cholesky)/cholesky | solution.py:194
  77.0 0.7 fusion.26
  77.7 9.8 %custom-call.8 = f32[1,128,128]{1,2,0:T(8,128)S(1)} custom-call(f32[1,128,128]{2,1,0:T(8,128)S(1)} %fusion.26), custom_call_target="InvertDiagBlocksLowerTriangular" | custom-call | tf_op jit(solution)/shard_map/triangular_solve/custom-call.0 | solution.py:196
  88.8 5.6 %collective-permute-start.6 = (f32[3,128,128]{2,1,0:T(8,128)S(1)}, f32[3,128,128]{2,1,0:T(8,128)S(1)}, u32[]{:S(2)}, u32[]{:S(2)}) collective-permute-start(f32[3,128,128]{2,1,0:T(8,128)S(1)} %pad_maximum_fusion.5), channel_id=1, source_target_pairs={{0,16},{4,20},{8,24},{12,28},{1,17},{5,21},{9,25},{13,29},{2,18},{... | collective-permute-start | bytes 589832 | tf_op jit(solution)/shard_map/ppermute | solution.py:358
  95.0 15.2 %shard_map.77 = (f32[512,2048]{1,0:T(8,128)}, f32[512,2048]{1,0:T(8,128)}) custom-call(s32[8]{0:T(128)} %get-tuple-element.42.src_left, s32[16]{0:T(128)} %copy-done, s32[8]{0:T(128)} %get-tuple-element.43.tile_ref, s32[128]{0:T(128)} %copy-done.4, s32[8]{0:T(128)} %compare_convert_fusion.flag_ref, bf16[1024,2048]{1,0:T(8,128)(2,1)} %bitcast.159, ...), custom_call_target="tpu_custom_call" | custom-call | tf_op jit(solution)/shard_map/pallas_call | solution.py:177
  110.2 14.7 %shard_map.78 = (f32[512,2048]{1,0:T(8,128)}, f32[512,2048]{1,0:T(8,128)}) custom-call(s32[8]{0:T(128)} %get-tuple-element.42.src_left, s32[16]{0:T(128)} %copy-done, s32[8]{0:T(128)} %get-tuple-element.43.tile_ref, s32[64]{0:T(128)} %get-tuple-element.68.mask_ref, s32[8]{0:T(128)} %compare_convert_fusion.flag_ref, ...), custom_call_target="tpu_custom_call", output_to_operand_aliasing={{0}: (8, {}), {1}: (9, {})} | custom-call | tf_op jit(solution)/shard_map/pallas_call | solution.py:177
  125.3 11.7 %cholesky.81 = f32[128,128]{1,0:T(8,128)S(1)} custom-call(f32[128,128]{1,0:T(8,128)S(1)} %fusion.38), custom_call_target="Cholesky" | custom-call | tf_op jit(solution)/shard_map/jit(cholesky)/cholesky | solution.py:194
  137.6 0.7 fusion.27
  138.3 9.8 %custom-call.9 = f32[1,128,128]{1,2,0:T(8,128)S(1)} custom-call(f32[1,128,128]{2,1,0:T(8,128)S(1)} %fusion.27), custom_call_target="InvertDiagBlocksLowerTriangular" | custom-call | tf_op jit(solution)/shard_map/triangular_solve/custom-call.0 | solution.py:196
  151.1 1.1 copy.78.w_ref
  152.4 0.7 reshape.229.mask_ref
  153.1 0.7 maximum_bitcast_fusion
  153.9 4.0 %pad_maximum_fusion.g_ref = bf16[1024,2048]{1,0:T(8,128)(2,1)} fusion(bf16[512,2048]{1,0:T(8,128)(2,1)S(1)} %collective-permute-done.7, bf16[512,2048]{1,0:T(8,128)(2,1)} %collective-permute-done.2), kind=kLoop, calls=%fused_computation.2 | loop fusion | flops 8388608 | bytes 8388608 | tf_op jit(solution)/shard_map/concatenate | solution.py:349
  158.0 12.8 %shard_map.79 = f32[1,512,2048]{2,1,0:T(8,128)} custom-call(s32[4]{0:T(128)} %and_select_fusion.1.src_left, s32[16]{0:T(128)} %copy-done, s32[4]{0:T(128)} %copy-done.3, s32[128]{0:T(128)} %reshape.229.mask_ref, s32[4]{0:T(128)} %bitcast.182, bf16[1024,2048]{1,0:T(8,128)(2,1)} %pad_maximum_fusion.g_ref, ...), custom_call_target="tpu_custom_call", output_to_operand_aliasing={{}: (8, {})} | custom-call | tf_op jit(solution)/shard_map/pallas_call | solution.py:89
  (103 shorter events, 13.2 us)
Async XLA Ops:
  0.6 10.4 %copy-start.2 = (f32[1,1024]{1,0:T(1,128)S(1)}, f32[1,1024]{1,0:T(1,128)}, u32[]{:S(2)}) copy-start(f32[1,1024]{1,0:T(1,128)} %param.10) | copy-start | bytes 12292
  0.6 11.6 %copy-start.5 = (s32[16]{0:T(128)S(1)}, s32[16]{0:T(128)}, u32[]{:S(2)}) copy-start(s32[16]{0:T(128)} %param.13) | copy-start | bytes 196
  1.4 22.1 %copy-start = (s32[16]{0:T(128)}, s32[16]{0:T(128)S(1)}, u32[]{:S(2)}) copy-start(s32[16]{0:T(128)S(1)} %select_reduce_fusion.3.src_right) | copy-start | bytes 196
  6.7 16.8 %copy-start.4 = (s32[128]{0:T(128)}, s32[128]{0:T(128)S(1)}, u32[]{:S(2)}) copy-start(s32[128]{0:T(128)S(1)} %reshape_squeeze.4.mask_ref) | copy-start | bytes 1540
  11.2 3.6 %collective-permute-start = (f32[53760]{0:T(1024)S(1)}, f32[53760]{0:T(1024)S(1)}, u32[]{:S(2)}, u32[]{:S(2)}) collective-permute-start(f32[53760]{0:T(1024)S(1)} %pad_maximum_fusion.1), channel_id=1, source_target_pairs={{0,1},{1,0},{2,3},{3,2},{4,5},{5,4},{6,7},{7,6},{8,9},{9,8},{10,11... | collective-permute-start | bytes 645128 | tf_op jit(solution)/shard_map/ppermute | solution.py:249
  12.3 138.3 %copy-start.3 = (s32[4]{0:T(128)}, s32[4]{0:T(128)S(1)}, u32[]{:S(2)}) copy-start(s32[4]{0:T(128)S(1)} %get-tuple-element.49.tile_ref) | copy-start | bytes 52
  14.8 8.6 %collective-permute-start.1 = (f32[53760]{0:T(1024)S(1)}, f32[53760]{0:T(1024)S(1)}, u32[]{:S(2)}, u32[]{:S(2)}) collective-permute-start(f32[53760]{0:T(1024)S(1)} %fusion.75), channel_id=1, source_target_pairs={{0,2},{1,3},{2,0},{3,1},{4,6},{5,7},{6,4},{7,5},{8,10},{9,11},{10,... | collective-permute-start | bytes 645128 | tf_op jit(solution)/shard_map/ppermute | solution.py:249
  23.5 9.3 %collective-permute-start.4 = (f32[3,128,128]{2,1,0:T(8,128)S(1)}, f32[3,128,128]{2,1,0:T(8,128)S(1)}, u32[]{:S(2)}, u32[]{:S(2)}) collective-permute-start(f32[3,128,128]{2,1,0:T(8,128)S(1)} %pad_maximum_fusion.3), channel_id=1, source_target_pairs={{0,4},{4,8},{8,12},{12,16},{16,20},{20,24},{24,28},{1,5},{5,9},{9,... | collective-permute-start | bytes 589832 | tf_op jit(solution)/shard_map/ppermute | solution.py:358
  31.2 57.5 %collective-permute-start.3 = (bf16[512,2048]{1,0:T(8,128)(2,1)}, bf16[512,2048]{1,0:T(8,128)(2,1)}, u32[]{:S(2)}, u32[]{:S(2)}) collective-permute-start(bf16[512,2048]{1,0:T(8,128)(2,1)} %get-tuple-element.52), channel_id=1, source_target_pairs={{0,2},{1,3},{2,0},{3,1},{4,6},{5,7},{6,4},{7,5},{8,10},{9,11},{10,... | collective-permute-start | bytes 6291464 | tf_op jit(solution)/shard_map/ppermute | solution.py:249
  57.4 6.9 %collective-permute-start.5 = (f32[3,128,128]{2,1,0:T(8,128)S(1)}, f32[3,128,128]{2,1,0:T(8,128)S(1)}, u32[]{:S(2)}, u32[]{:S(2)}) collective-permute-start(f32[3,128,128]{2,1,0:T(8,128)S(1)} %pad_maximum_fusion.4), channel_id=1, source_target_pairs={{0,8},{4,12},{8,16},{12,20},{16,24},{20,28},{1,9},{5,13},{9,17},{1... | collective-permute-start | bytes 589832 | tf_op jit(solution)/shard_map/ppermute | solution.py:358
  62.2 87.1 %collective-permute-start.2 = (bf16[512,2048]{1,0:T(8,128)(2,1)S(1)}, bf16[512,2048]{1,0:T(8,128)(2,1)}, u32[]{:S(2)}, u32[]{:S(2)}) collective-permute-start(bf16[512,2048]{1,0:T(8,128)(2,1)S(1)} %get-tuple-element.53), channel_id=1, source_target_pairs={{0,2},{1,3},{2,0},{3,1},{4,6},{5,7},{6,4},{7,5},{8,10},{9,11},{10,... | collective-permute-start | bytes 6291464 | tf_op jit(solution)/shard_map/ppermute | solution.py:249
  88.8 36.1 %collective-permute-start.6 = (f32[3,128,128]{2,1,0:T(8,128)S(1)}, f32[3,128,128]{2,1,0:T(8,128)S(1)}, u32[]{:S(2)}, u32[]{:S(2)}) collective-permute-start(f32[3,128,128]{2,1,0:T(8,128)S(1)} %pad_maximum_fusion.5), channel_id=1, source_target_pairs={{0,16},{4,20},{8,24},{12,28},{1,17},{5,21},{9,25},{13,29},{2,18},{... | collective-permute-start | bytes 589832 | tf_op jit(solution)/shard_map/ppermute | solution.py:358
  110.2 39.8 %copy-start.1 = (s32[16]{0:T(128)S(1)}, s32[16]{0:T(128)}, u32[]{:S(2)}) copy-start(s32[16]{0:T(128)} %copy-done) | copy-start | bytes 196
  124.9 33.1 %collective-permute-start.8 = (f32[512,2048]{1,0:T(8,128)}, f32[512,2048]{1,0:T(8,128)}, u32[]{:S(2)}, u32[]{:S(2)}) collective-permute-start(f32[512,2048]{1,0:T(8,128)} %get-tuple-element.36), channel_id=1, source_target_pairs={{0,1},{1,0},{2,3},{3,2},{4,5},{5,4},{6,7},{7,6},{8,9},{9,8},{10,11... | collective-permute-start | bytes 12582920 | tf_op jit(solution)/shard_map/ppermute | solution.py:249
  149.4 4.6 %collective-permute-start.7 = (bf16[512,2048]{1,0:T(8,128)(2,1)}, bf16[512,2048]{1,0:T(8,128)(2,1)S(1)}, u32[]{:S(2)}, u32[]{:S(2)}) collective-permute-start(bf16[512,2048]{1,0:T(8,128)(2,1)} %collective-permute-done.2), channel_id=1, source_target_pairs={{0,1},{1,0},{2,3},{3,2},{4,5},{5,4},{6,7},{7,6},{8,9},{9,8},{10,11... | collective-permute-start | bytes 6291464 | tf_op jit(solution)/shard_map/ppermute | solution.py:249

commit v19 on v18

--- a/solution.py
+++ b/solution.py
@@ -66,10 +66,10 @@
     out_blocks = src_left.shape[0]
     in_specs = [
         pl.BlockSpec((height, L), lambda k, *_: (0, 0)),
-        pl.BlockSpec((height, 1), lambda k, *_: (0, 0)),
+        pl.BlockSpec((height, BLK), lambda k, *_: (0, 0)),
         pl.BlockSpec((col_blocks, BLK), lambda k, *_: (0, 0)),
     ]
-    operands = [slab, weights.reshape(height, 1), diagonal.reshape(col_blocks, BLK)]
+    operands = [slab, jnp.broadcast_to(weights.reshape(height, 1), (height, BLK)), diagonal.reshape(col_blocks, BLK)]
     aliases = {}
     out_spec = pl.BlockSpec((None, BLK, L), lambda k, *_: (k // group, k % group, 0))
     if acc is not None:
@@ -155,10 +155,10 @@
     col_blocks = L // BLK
     in_specs = [
         pl.BlockSpec((height, L), lambda k, *_: (0, 0)),
-        pl.BlockSpec((height, 1), lambda k, *_: (0, 0)),
+        pl.BlockSpec((height, BLK), lambda k, *_: (0, 0)),
         pl.BlockSpec((col_blocks, BLK), lambda k, *_: (0, 0)),
     ]
-    operands = [slab, weights.reshape(height, 1), diagonal.reshape(col_blocks, BLK)]
+    operands = [slab, jnp.broadcast_to(weights.reshape(height, 1), (height, BLK)), diagonal.reshape(col_blocks, BLK)]
     first_spec = pl.BlockSpec((BLK, L), lambda k, *_: (jnp.minimum(k, group - 1), 0))
     second_spec = pl.BlockSpec((BLK, L), lambda k, *_: (jnp.maximum(k - group, 0), 0))
     aliases = {}

time: 171 us -> 170 us (level)
  Pallas kernels: 42.7 us -> 38.2 us
  waiting for transfers between devices: 5.94 us -> 9.1 us
    pallas_call x2, Pallas kernels: 29.9 us -> 27 us  [split_rows(): pl.pallas_call(functools.partial(split_kernel, group=group, accumulate=ac...]
    ppermute x3, waiting for transfers between devices: 0.53 us -> 2.82 us  [local(): moved = lax.ppermute(jnp.stack(running), 'tm', pairs)]
    reshape x3 -> x0, local copies, waits for them, and re-layouts: 2 us -> none  [the longest x1 1.05 us: gram_rows(): weights.reshape(height, 1)]
    broadcast_in_dim x0 -> x2, local copies, waits for them, and re-layouts: none -> 1.87 us  [the longest x1 1.05 us: gram_rows(): jnp.broadcast_to(weights.reshape(height, 1), (height, BLK))]
  transfers between devices with their start and end apart: 9 -> 9, of which waited for: 3 -> 3; matrix products, arithmetic and copies ran while one was open for 53% -> 53% of each run, Pallas kernels for 18% -> 16%
where the time goes in v19:
time: 170 us; the launch traced here: 169 us
  other arithmetic  79 us (46%)
  Pallas kernels  38.2 us (22%)
  starting transfers between devices  18.8 us (11%)
  local copies, waits for them, and re-layouts  13.8 us (8%)
  waiting for transfers between devices  9.1 us (5%)
  between operations  6.39 us (4%)
  matrix products  3.86 us (2%)
    another operation x9, other arithmetic, join_segments(): factor = jnp.linalg.cholesky(middle)  37.2 us
    another operation x6, other arithmetic, join_segments(): lax.linalg.triangular_solve(factor, jnp.concatenate([cross_one.T, cross_t...  31.4 us
    pallas_call x2, Pallas kernels, split_rows(): pl.pallas_call(functools.partial(split_kernel, group=group, accumulate=ac...  27 us
    ppermute x3, starting transfers between devices, local(): moved = lax.ppermute(jnp.stack(running), 'tm', pairs)  12.9 us
    pallas_call x1, Pallas kernels, gram_rows(): pl.pallas_call(gram_kernel, grid_spec=grid_spec, out_shape=jax.ShapeDtype...  11.2 us
    ppermute x6, waiting for transfers between devices, exchange(): lax.ppermute(value, 'row', [(src, src ^ step) for src in range(owners)])  6.28 us
    ppermute x6, starting transfers between devices, exchange(): lax.ppermute(value, 'row', [(src, src ^ step) for src in range(owners)])  5.84 us
    slice x1, local copies, waits for them, and re-layouts, local(): lax.slice_in_dim(kernel_slab, h * half_rows, (h + 1) * half_rows)  4.83 us
  transfers between devices with their start and end apart: 9, of which 3 were waited for; matrix products, arithmetic and copies ran while one was open for 53% of the time, Pallas kernels for 16%

profile of v19, /device:TPU:0, one launch (start us, length us, event | category | flops | bytes accessed | tf_op | source)
XLA Modules:
  0.0 169.2 jit_solution(16957237983338085560)
XLA Ops:
  0.7 0.8 select_reduce_fusion.3.src_right
  5.9 0.8 reshape_squeeze.4.mask_ref
  8.0 1.0 fusion.68
  9.0 1.5 multiply_convert_fusion.1
  13.0 0.7 slice_bitcast_fusion.16
  13.7 2.6 %collective-permute-start.1 = (f32[53760]{0:T(1024)S(1)}, f32[53760]{0:T(1024)S(1)}, u32[]{:S(2)}, u32[]{:S(2)}) collective-permute-start(f32[53760]{0:T(1024)S(1)} %fusion.75), channel_id=1, source_target_pairs={{0,2},{1,3},{2,0},{3,1},{4,6},{5,7},{6,4},{7,5},{8,10},{9,11},{10,... | collective-permute-start | bytes 645128 | tf_op jit(solution)/shard_map/ppermute | solution.py:249
  17.0 5.3 %collective-permute-done.1 = f32[53760]{0:T(1024)S(1)} collective-permute-done((f32[53760]{0:T(1024)S(1)}, f32[53760]{0:T(1024)S(1)}, u32[]{:S(2)}, u32[]{:S(2)}) %collective-permute-start.1) | collective-permute-done | bytes 215072 | tf_op jit(solution)/shard_map/ppermute | solution.py:249
  22.4 3.6 %collective-permute-start.4 = (f32[3,128,128]{2,1,0:T(8,128)S(1)}, f32[3,128,128]{2,1,0:T(8,128)S(1)}, u32[]{:S(2)}, u32[]{:S(2)}) collective-permute-start(f32[3,128,128]{2,1,0:T(8,128)S(1)} %pad_maximum_fusion.3), channel_id=1, source_target_pairs={{0,4},{4,8},{8,12},{12,16},{16,20},{20,24},{24,28},{1,5},{5,9},{9,... | collective-permute-start | bytes 589832 | tf_op jit(solution)/shard_map/ppermute | solution.py:358
  26.1 4.8 %fusion.76 = (bf16[512,2048]{1,0:T(8,128)(2,1)}, bf16[512,2048]{1,0:T(8,128)(2,1)}) fusion(bf16[1024,2048]{1,0:T(8,128)(2,1)} %bitcast.155), kind=kLoop, calls=%fused_computation.149 | loop fusion | bytes 8388608 | tf_op jit(solution)/shard_map/slice | solution.py:275
  31.0 1.6 collective-permute-start.3
  33.5 11.7 %cholesky.59 = f32[128,128]{1,0:T(8,128)S(1)} custom-call(f32[128,128]{1,0:T(8,128)S(1)} %copy.55), custom_call_target="Cholesky" | custom-call | tf_op jit(solution)/shard_map/jit(cholesky)/cholesky | solution.py:194
  45.9 0.7 fusion.25
  46.6 9.8 %custom-call.7 = f32[1,128,128]{1,2,0:T(8,128)S(1)} custom-call(f32[1,128,128]{2,1,0:T(8,128)S(1)} %fusion.25), custom_call_target="InvertDiagBlocksLowerTriangular" | custom-call | tf_op jit(solution)/shard_map/triangular_solve/custom-call.0 | solution.py:196
  57.8 3.7 %collective-permute-start.5 = (f32[3,128,128]{2,1,0:T(8,128)S(1)}, f32[3,128,128]{2,1,0:T(8,128)S(1)}, u32[]{:S(2)}, u32[]{:S(2)}) collective-permute-start(f32[3,128,128]{2,1,0:T(8,128)S(1)} %pad_maximum_fusion.4), channel_id=1, source_target_pairs={{0,8},{4,12},{8,16},{12,20},{16,24},{20,28},{1,9},{5,13},{9,17},{1... | collective-permute-start | bytes 589832 | tf_op jit(solution)/shard_map/ppermute | solution.py:358
  61.6 2.8 %collective-permute-done.5 = f32[3,128,128]{2,1,0:T(8,128)S(1)} collective-permute-done((f32[3,128,128]{2,1,0:T(8,128)S(1)}, f32[3,128,128]{2,1,0:T(8,128)S(1)}, u32[]{:S(2)}, u32[]{:S(2)}) %collective-permute-start.5) | collective-permute-done | bytes 196640 | tf_op jit(solution)/shard_map/ppermute | solution.py:358
  64.7 11.7 %cholesky.70 = f32[128,128]{1,0:T(8,128)S(1)} custom-call(f32[128,128]{1,0:T(8,128)S(1)} %fusion.40), custom_call_target="Cholesky" | custom-call | tf_op jit(solution)/shard_map/jit(cholesky)/cholesky | solution.py:194
  77.1 0.7 fusion.26
  77.7 9.8 %custom-call.8 = f32[1,128,128]{1,2,0:T(8,128)S(1)} custom-call(f32[1,128,128]{2,1,0:T(8,128)S(1)} %fusion.26), custom_call_target="InvertDiagBlocksLowerTriangular" | custom-call | tf_op jit(solution)/shard_map/triangular_solve/custom-call.0 | solution.py:196
  88.9 5.6 %collective-permute-start.6 = (f32[3,128,128]{2,1,0:T(8,128)S(1)}, f32[3,128,128]{2,1,0:T(8,128)S(1)}, u32[]{:S(2)}, u32[]{:S(2)}) collective-permute-start(f32[3,128,128]{2,1,0:T(8,128)S(1)} %pad_maximum_fusion.5), channel_id=1, source_target_pairs={{0,16},{4,20},{8,24},{12,28},{1,17},{5,21},{9,25},{13,29},{2,18},{... | collective-permute-start | bytes 589832 | tf_op jit(solution)/shard_map/ppermute | solution.py:358
  95.0 1.0 mul.105.w_ref
  96.0 13.6 %shard_map.77 = (f32[512,2048]{1,0:T(8,128)}, f32[512,2048]{1,0:T(8,128)}) custom-call(s32[8]{0:T(128)} %get-tuple-element.42.src_left, s32[16]{0:T(128)} %copy-done, s32[8]{0:T(128)} %get-tuple-element.43.tile_ref, s32[128]{0:T(128)} %copy-done.4, s32[8]{0:T(128)} %compare_convert_fusion.flag_ref, bf16[1024,2048]{1,0:T(8,128)(2,1)} %bitcast.156, ...), custom_call_target="tpu_custom_call" | custom-call | tf_op jit(solution)/shard_map/pallas_call | solution.py:177
  109.6 0.8 broadcast_in_dim.49.w_ref
  110.4 13.4 %shard_map.78 = (f32[512,2048]{1,0:T(8,128)}, f32[512,2048]{1,0:T(8,128)}) custom-call(s32[8]{0:T(128)} %get-tuple-element.42.src_left, s32[16]{0:T(128)} %copy-done, s32[8]{0:T(128)} %get-tuple-element.43.tile_ref, s32[64]{0:T(128)} %get-tuple-element.68.mask_ref, s32[8]{0:T(128)} %compare_convert_fusion.flag_ref, ...), custom_call_target="tpu_custom_call", output_to_operand_aliasing={{0}: (8, {}), {1}: (9, {})} | custom-call | tf_op jit(solution)/shard_map/pallas_call | solution.py:177
  124.2 11.7 %cholesky.81 = f32[128,128]{1,0:T(8,128)S(1)} custom-call(f32[128,128]{1,0:T(8,128)S(1)} %fusion.38), custom_call_target="Cholesky" | custom-call | tf_op jit(solution)/shard_map/jit(cholesky)/cholesky | solution.py:194
  136.6 0.7 fusion.27
  137.3 9.8 %custom-call.9 = f32[1,128,128]{1,2,0:T(8,128)S(1)} custom-call(f32[1,128,128]{2,1,0:T(8,128)S(1)} %fusion.27), custom_call_target="InvertDiagBlocksLowerTriangular" | custom-call | tf_op jit(solution)/shard_map/triangular_solve/custom-call.0 | solution.py:196
  150.4 0.7 reshape.227.mask_ref
  151.2 0.7 maximum_bitcast_fusion
  151.9 0.9 collective-permute-done.7
  152.8 4.1 %pad_maximum_fusion.g_ref = bf16[1024,2048]{1,0:T(8,128)(2,1)} fusion(bf16[512,2048]{1,0:T(8,128)(2,1)} %collective-permute-done.7, bf16[512,2048]{1,0:T(8,128)(2,1)S(1)} %collective-permute-done.2), kind=kLoop, calls=%fused_computation.2 | loop fusion | flops 8388608 | bytes 8388608 | tf_op jit(solution)/shard_map/concatenate | solution.py:349
  156.9 1.0 broadcast_in_dim.47.w_ref
  157.9 11.2 %shard_map.79 = f32[1,512,2048]{2,1,0:T(8,128)} custom-call(s32[4]{0:T(128)} %and_select_fusion.1.src_left, s32[16]{0:T(128)} %copy-done, s32[4]{0:T(128)} %copy-done.3, s32[128]{0:T(128)} %reshape.227.mask_ref, s32[4]{0:T(128)} %bitcast.179, bf16[1024,2048]{1,0:T(8,128)(2,1)} %pad_maximum_fusion.g_ref, ...), custom_call_target="tpu_custom_call", output_to_operand_aliasing={{}: (8, {})} | custom-call | tf_op jit(solution)/shard_map/pallas_call | solution.py:89
  (103 shorter events, 13.9 us)
Async XLA Ops:
  0.6 10.4 %copy-start.2 = (f32[1,1024]{1,0:T(1,128)S(1)}, f32[1,1024]{1,0:T(1,128)}, u32[]{:S(2)}) copy-start(f32[1,1024]{1,0:T(1,128)} %param.10) | copy-start | bytes 12292
  0.6 11.6 %copy-start.5 = (s32[16]{0:T(128)S(1)}, s32[16]{0:T(128)}, u32[]{:S(2)}) copy-start(s32[16]{0:T(128)} %param.13) | copy-start | bytes 196
  1.4 29.5 %copy-start = (s32[16]{0:T(128)}, s32[16]{0:T(128)S(1)}, u32[]{:S(2)}) copy-start(s32[16]{0:T(128)S(1)} %select_reduce_fusion.3.src_right) | copy-start | bytes 196
  6.7 24.2 %copy-start.4 = (s32[128]{0:T(128)}, s32[128]{0:T(128)S(1)}, u32[]{:S(2)}) copy-start(s32[128]{0:T(128)S(1)} %reshape_squeeze.4.mask_ref) | copy-start | bytes 1540
  11.2 2.5 %collective-permute-start = (f32[53760]{0:T(1024)S(1)}, f32[53760]{0:T(1024)S(1)}, u32[]{:S(2)}, u32[]{:S(2)}) collective-permute-start(f32[53760]{0:T(1024)S(1)} %pad_maximum_fusion.1), channel_id=1, source_target_pairs={{0,1},{1,0},{2,3},{3,2},{4,5},{5,4},{6,7},{7,6},{8,9},{9,8},{10,11... | collective-permute-start | bytes 645128 | tf_op jit(solution)/shard_map/ppermute | solution.py:249
  12.3 137.2 %copy-start.3 = (s32[4]{0:T(128)}, s32[4]{0:T(128)S(1)}, u32[]{:S(2)}) copy-start(s32[4]{0:T(128)S(1)} %get-tuple-element.49.tile_ref) | copy-start | bytes 52
  13.7 8.6 %collective-permute-start.1 = (f32[53760]{0:T(1024)S(1)}, f32[53760]{0:T(1024)S(1)}, u32[]{:S(2)}, u32[]{:S(2)}) collective-permute-start(f32[53760]{0:T(1024)S(1)} %fusion.75), channel_id=1, source_target_pairs={{0,2},{1,3},{2,0},{3,1},{4,6},{5,7},{6,4},{7,5},{8,10},{9,11},{10,... | collective-permute-start | bytes 645128 | tf_op jit(solution)/shard_map/ppermute | solution.py:249
  22.4 10.7 %collective-permute-start.4 = (f32[3,128,128]{2,1,0:T(8,128)S(1)}, f32[3,128,128]{2,1,0:T(8,128)S(1)}, u32[]{:S(2)}, u32[]{:S(2)}) collective-permute-start(f32[3,128,128]{2,1,0:T(8,128)S(1)} %pad_maximum_fusion.3), channel_id=1, source_target_pairs={{0,4},{4,8},{8,12},{12,16},{16,20},{20,24},{24,28},{1,5},{5,9},{9,... | collective-permute-start | bytes 589832 | tf_op jit(solution)/shard_map/ppermute | solution.py:358
  31.0 57.7 %collective-permute-start.3 = (bf16[512,2048]{1,0:T(8,128)(2,1)}, bf16[512,2048]{1,0:T(8,128)(2,1)}, u32[]{:S(2)}, u32[]{:S(2)}) collective-permute-start(bf16[512,2048]{1,0:T(8,128)(2,1)} %get-tuple-element.52), channel_id=1, source_target_pairs={{0,2},{1,3},{2,0},{3,1},{4,6},{5,7},{6,4},{7,5},{8,10},{9,11},{10,... | collective-permute-start | bytes 6291464 | tf_op jit(solution)/shard_map/ppermute | solution.py:249
  32.6 115.7 %collective-permute-start.2 = (bf16[512,2048]{1,0:T(8,128)(2,1)}, bf16[512,2048]{1,0:T(8,128)(2,1)S(1)}, u32[]{:S(2)}, u32[]{:S(2)}) collective-permute-start(bf16[512,2048]{1,0:T(8,128)(2,1)} %get-tuple-element.53), channel_id=1, source_target_pairs={{0,2},{1,3},{2,0},{3,1},{4,6},{5,7},{6,4},{7,5},{8,10},{9,11},{10,... | collective-permute-start | bytes 6291464 | tf_op jit(solution)/shard_map/ppermute | solution.py:249
  57.8 6.7 %collective-permute-start.5 = (f32[3,128,128]{2,1,0:T(8,128)S(1)}, f32[3,128,128]{2,1,0:T(8,128)S(1)}, u32[]{:S(2)}, u32[]{:S(2)}) collective-permute-start(f32[3,128,128]{2,1,0:T(8,128)S(1)} %pad_maximum_fusion.4), channel_id=1, source_target_pairs={{0,8},{4,12},{8,16},{12,20},{16,24},{20,28},{1,9},{5,13},{9,17},{1... | collective-permute-start | bytes 589832 | tf_op jit(solution)/shard_map/ppermute | solution.py:358
  88.9 35.0 %collective-permute-start.6 = (f32[3,128,128]{2,1,0:T(8,128)S(1)}, f32[3,128,128]{2,1,0:T(8,128)S(1)}, u32[]{:S(2)}, u32[]{:S(2)}) collective-permute-start(f32[3,128,128]{2,1,0:T(8,128)S(1)} %pad_maximum_fusion.5), channel_id=1, source_target_pairs={{0,16},{4,20},{8,24},{12,28},{1,17},{5,21},{9,25},{13,29},{2,18},{... | collective-permute-start | bytes 589832 | tf_op jit(solution)/shard_map/ppermute | solution.py:358
  110.4 38.4 %copy-start.1 = (s32[16]{0:T(128)S(1)}, s32[16]{0:T(128)}, u32[]{:S(2)}) copy-start(s32[16]{0:T(128)} %copy-done) | copy-start | bytes 196
  123.8 33.1 %collective-permute-start.8 = (f32[512,2048]{1,0:T(8,128)}, f32[512,2048]{1,0:T(8,128)}, u32[]{:S(2)}, u32[]{:S(2)}) collective-permute-start(f32[512,2048]{1,0:T(8,128)} %get-tuple-element.36), channel_id=1, source_target_pairs={{0,1},{1,0},{2,3},{3,2},{4,5},{5,4},{6,7},{7,6},{8,9},{9,8},{10,11... | collective-permute-start | bytes 12582920 | tf_op jit(solution)/shard_map/ppermute | solution.py:249
  148.3 4.5 %collective-permute-start.7 = (bf16[512,2048]{1,0:T(8,128)(2,1)S(1)}, bf16[512,2048]{1,0:T(8,128)(2,1)}, u32[]{:S(2)}, u32[]{:S(2)}) collective-permute-start(bf16[512,2048]{1,0:T(8,128)(2,1)S(1)} %collective-permute-done.2), channel_id=1, source_target_pairs={{0,1},{1,0},{2,3},{3,2},{4,5},{5,4},{6,7},{7,6},{8,9},{9,8},{10,11... | collective-permute-start | bytes 6291464 | tf_op jit(solution)/shard_map/ppermute | solution.py:249

commit v20 on v19

--- a/solution.py
+++ b/solution.py
@@ -183,6 +183,73 @@
     )(src_left, src_right, out_tiles, live_blocks.reshape(-1), flags, *operands)
 
 
+def pair_kernel(src_left, src_right, tile_ref, mask_ref, flag_ref, g1_ref, g2_ref, w_ref, diag_ref,
+                acc_ref, extra_ref, out_ref, s_ref, lt_ref):
+    k = pl.program_id(0)
+    first_blocks = g1_ref.shape[0] // BLK
+    row_blocks = first_blocks + g2_ref.shape[0] // BLK
+    col_blocks = g1_ref.shape[1] // BLK
+
+    def rows_of(rb, cols):
+        if rb < first_blocks:
+            return g1_ref[rb * BLK:(rb + 1) * BLK, cols]
+        return g2_ref[(rb - first_blocks) * BLK:(rb - first_blocks + 1) * BLK, cols]
+
+    @pl.when(k == 0)
+    def _():
+        def fill(j, carry):
+            src = src_right[j]
+            c0 = pl.multiple_of(src * BLK, BLK)
+            d0 = pl.multiple_of(j * BLK, BLK)
+            for rb in range(row_blocks):
+                live = mask_ref[rb * col_blocks + src].astype(jnp.float32)
+                vals = rows_of(rb, pl.ds(c0, BLK)).astype(jnp.float32)
+                wts = w_ref[rb * BLK:(rb + 1) * BLK, :]
+                s_ref[rb * BLK:(rb + 1) * BLK, pl.ds(d0, BLK)] = (wts * (vals * live)).astype(jnp.bfloat16)
+            return carry
+        lax.fori_loop(0, col_blocks, fill, 0)
+
+    src = src_left[k]
+    c0 = pl.multiple_of(src * BLK, BLK)
+    for rb in range(row_blocks):
+        live = mask_ref[rb * col_blocks + src].astype(jnp.float32)
+        vals = rows_of(rb, pl.ds(c0, BLK)).astype(jnp.float32) * live
+        lt_ref[:, rb * BLK:(rb + 1) * BLK] = vals.T.astype(jnp.bfloat16)
+    term = jnp.dot(lt_ref[...], s_ref[...], preferred_element_type=jnp.float32)
+    out_ref[...] = (acc_ref[...] + extra_ref[...]) + term
+
+
+def pair_rows(slab_one, slab_two, weights, live_blocks, src_left, src_right, out_tiles, diagonal, flags,
+              group, acc, extra):
+    height = slab_one.shape[0] + slab_two.shape[0]
+    col_blocks = L // BLK
+    out_blocks = src_left.shape[0]
+    out_spec = pl.BlockSpec((None, BLK, L), lambda k, *_: (k // group, k % group, 0))
+    grid_spec = pltpu.PrefetchScalarGridSpec(
+        num_scalar_prefetch=5,
+        grid=(out_blocks,),
+        in_specs=[
+            pl.BlockSpec(slab_one.shape, lambda k, *_: (0, 0)),
+            pl.BlockSpec(slab_two.shape, lambda k, *_: (0, 0)),
+            pl.BlockSpec((height, BLK), lambda k, *_: (0, 0)),
+            pl.BlockSpec((col_blocks, BLK), lambda k, *_: (0, 0)),
+            out_spec,
+            out_spec,
+        ],
+        out_specs=out_spec,
+        scratch_shapes=[pltpu.VMEM((height, L), jnp.bfloat16), pltpu.VMEM((BLK, height), jnp.bfloat16)],
+    )
+    return pl.pallas_call(
+        pair_kernel,
+        grid_spec=grid_spec,
+        out_shape=jax.ShapeDtypeStruct((out_blocks // group, group * BLK, L), jnp.float32),
+        input_output_aliases={9: 0},
+        compiler_params=pltpu.CompilerParams(vmem_limit_bytes=56 * 1024 * 1024),
+    )(src_left, src_right, out_tiles, live_blocks.reshape(-1), flags, slab_one, slab_two,
+      jnp.broadcast_to(weights.reshape(height, 1), (height, BLK)), diagonal.reshape(col_blocks, BLK),
+      acc, extra)
+
+
 HIGHEST = lax.Precision.HIGHEST
 
 
@@ -311,10 +378,10 @@
         ])
         mine_order = order[:own_blocks]
 
-        def last_part(slab_in, mine, received):
-            total = gram_rows(
-                slab_in, last_weights, last_live, jnp.take(source, mine_order), source, mine_order,
-                diagonal, flags[:own_blocks], own_blocks, mine[None], received[None],
+        def last_part(slab_one, slab_two, mine, received):
+            total = pair_rows(
+                slab_one, slab_two, last_weights, last_live, jnp.take(source, mine_order), source,
+                mine_order, diagonal, flags[:own_blocks], own_blocks, mine[None], received[None],
             )
             return total[0]
 
@@ -346,8 +413,9 @@
             state["mine"] = mine
             state["received"] = exchange(partners, 1)
         else:
-            both = jnp.concatenate([slab_in, exchange(slab_in, 1)], axis=0)
-            state["owned"] = last_part(both, state["mine"], state["received"])
+            state["owned"] = last_part(
+                slab_in, exchange(slab_in, 1), state["mine"], state["received"]
+            )
         return running
 
     while shift < times:

time: 170 us -> 165 us (0.971)
  other arithmetic: 79 us -> 75 us
    concatenate x1 -> x0, other arithmetic: 4.11 us -> none  [run_hook(): both = jnp.concatenate([slab_in, exchange(slab_in, 1)], axis=0)]
  transfers between devices with their start and end apart: 9 -> 9, of which waited for: 3 -> 3; matrix products, arithmetic and copies ran while one was open for 53% -> 52% of each run, Pallas kernels for 16% -> 16%
where the time goes in v20:
time: 165 us
  other arithmetic  75 us (45%)
  Pallas kernels  37.8 us (23%)
  starting transfers between devices  18.7 us (11%)
  local copies, waits for them, and re-layouts  13.8 us (8%)
  waiting for transfers between devices  9.13 us (6%)
  between operations  6.4 us (4%)
  matrix products  3.87 us (2%)
    another operation x9, other arithmetic, join_segments(): factor = jnp.linalg.cholesky(middle)  37.2 us
    another operation x6, other arithmetic, join_segments(): lax.linalg.triangular_solve(factor, jnp.concatenate([cross_one.T, cross_t...  31.4 us
    pallas_call x2, Pallas kernels, split_rows(): pl.pallas_call(functools.partial(split_kernel, group=group, accumulate=ac...  26.8 us
    ppermute x3, starting transfers between devices, local(): moved = lax.ppermute(jnp.stack(running), 'tm', pairs)  12.9 us
    pallas_call x1, Pallas kernels, pair_rows(): pl.pallas_call(pair_kernel, grid_spec=grid_spec, out_shape=jax.ShapeDtype...  11 us
    ppermute x6, waiting for transfers between devices, exchange(): lax.ppermute(value, 'row', [(src, src ^ step) for src in range(owners)])  6.31 us
    ppermute x6, starting transfers between devices, exchange(): lax.ppermute(value, 'row', [(src, src ^ step) for src in range(owners)])  5.79 us
    slice x1, local copies, waits for them, and re-layouts, local(): lax.slice_in_dim(kernel_slab, h * half_rows, (h + 1) * half_rows)  4.89 us
  transfers between devices with their start and end apart: 9, of which 3 were waited for; matrix products, arithmetic and copies ran while one was open for 52% of the time, Pallas kernels for 16%

profile of v20, /device:TPU:0, one launch (start us, length us, event | category | flops | bytes accessed | tf_op | source)
XLA Modules:
  0.0 164.7 jit_solution(2080371264755780766)
XLA Ops:
  0.7 0.8 select_reduce_fusion.3.src_right
  5.9 0.8 reshape_squeeze.4.mask_ref
  8.0 1.0 fusion.68
  9.0 1.5 multiply_convert_fusion.1
  12.4 0.6 gather_fusion.1
  13.1 0.7 slice_bitcast_fusion.16
  13.8 2.6 %collective-permute-start.1 = (f32[53760]{0:T(1024)S(1)}, f32[53760]{0:T(1024)S(1)}, u32[]{:S(2)}, u32[]{:S(2)}) collective-permute-start(f32[53760]{0:T(1024)S(1)} %fusion.75), channel_id=1, source_target_pairs={{0,2},{1,3},{2,0},{3,1},{4,6},{5,7},{6,4},{7,5},{8,10},{9,11},{10,... | collective-permute-start | bytes 645128 | tf_op jit(solution)/shard_map/ppermute | solution.py:316
  16.4 0.7 and_select_fusion
  17.1 5.3 %collective-permute-done.1 = f32[53760]{0:T(1024)S(1)} collective-permute-done((f32[53760]{0:T(1024)S(1)}, f32[53760]{0:T(1024)S(1)}, u32[]{:S(2)}, u32[]{:S(2)}) %collective-permute-start.1) | collective-permute-done | bytes 215072 | tf_op jit(solution)/shard_map/ppermute | solution.py:316
  22.5 3.6 %collective-permute-start.4 = (f32[3,128,128]{2,1,0:T(8,128)S(1)}, f32[3,128,128]{2,1,0:T(8,128)S(1)}, u32[]{:S(2)}, u32[]{:S(2)}) collective-permute-start(f32[3,128,128]{2,1,0:T(8,128)S(1)} %pad_maximum_fusion.2), channel_id=1, source_target_pairs={{0,4},{4,8},{8,12},{12,16},{16,20},{20,24},{24,28},{1,5},{5,9},{9,... | collective-permute-start | bytes 589832 | tf_op jit(solution)/shard_map/ppermute | solution.py:426
  26.1 4.9 %fusion.76 = (bf16[512,2048]{1,0:T(8,128)(2,1)}, bf16[512,2048]{1,0:T(8,128)(2,1)}) fusion(bf16[1024,2048]{1,0:T(8,128)(2,1)} %bitcast.155), kind=kLoop, calls=%fused_computation.148 | loop fusion | bytes 8388608 | tf_op jit(solution)/shard_map/slice | solution.py:342
  31.1 1.6 collective-permute-start.3
  33.6 11.7 %cholesky.59 = f32[128,128]{1,0:T(8,128)S(1)} custom-call(f32[128,128]{1,0:T(8,128)S(1)} %copy.55), custom_call_target="Cholesky" | custom-call | tf_op jit(solution)/shard_map/jit(cholesky)/cholesky | solution.py:261
  46.0 0.7 fusion.25
  46.7 9.8 %custom-call.7 = f32[1,128,128]{1,2,0:T(8,128)S(1)} custom-call(f32[1,128,128]{2,1,0:T(8,128)S(1)} %fusion.25), custom_call_target="InvertDiagBlocksLowerTriangular" | custom-call | tf_op jit(solution)/shard_map/triangular_solve/custom-call.0 | solution.py:263
  57.8 3.7 %collective-permute-start.5 = (f32[3,128,128]{2,1,0:T(8,128)S(1)}, f32[3,128,128]{2,1,0:T(8,128)S(1)}, u32[]{:S(2)}, u32[]{:S(2)}) collective-permute-start(f32[3,128,128]{2,1,0:T(8,128)S(1)} %pad_maximum_fusion.3), channel_id=1, source_target_pairs={{0,8},{4,12},{8,16},{12,20},{16,24},{20,28},{1,9},{5,13},{9,17},{1... | collective-permute-start | bytes 589832 | tf_op jit(solution)/shard_map/ppermute | solution.py:426
  61.7 2.8 %collective-permute-done.5 = f32[3,128,128]{2,1,0:T(8,128)S(1)} collective-permute-done((f32[3,128,128]{2,1,0:T(8,128)S(1)}, f32[3,128,128]{2,1,0:T(8,128)S(1)}, u32[]{:S(2)}, u32[]{:S(2)}) %collective-permute-start.5) | collective-permute-done | bytes 196640 | tf_op jit(solution)/shard_map/ppermute | solution.py:426
  64.7 11.7 %cholesky.70 = f32[128,128]{1,0:T(8,128)S(1)} custom-call(f32[128,128]{1,0:T(8,128)S(1)} %fusion.40), custom_call_target="Cholesky" | custom-call | tf_op jit(solution)/shard_map/jit(cholesky)/cholesky | solution.py:261
  77.1 0.7 fusion.26
  77.8 9.8 %custom-call.8 = f32[1,128,128]{1,2,0:T(8,128)S(1)} custom-call(f32[1,128,128]{2,1,0:T(8,128)S(1)} %fusion.26), custom_call_target="InvertDiagBlocksLowerTriangular" | custom-call | tf_op jit(solution)/shard_map/triangular_solve/custom-call.0 | solution.py:263
  88.9 5.6 %collective-permute-start.6 = (f32[3,128,128]{2,1,0:T(8,128)S(1)}, f32[3,128,128]{2,1,0:T(8,128)S(1)}, u32[]{:S(2)}, u32[]{:S(2)}) collective-permute-start(f32[3,128,128]{2,1,0:T(8,128)S(1)} %pad_maximum_fusion.4), channel_id=1, source_target_pairs={{0,16},{4,20},{8,24},{12,28},{1,17},{5,21},{9,25},{13,29},{2,18},{... | collective-permute-start | bytes 589832 | tf_op jit(solution)/shard_map/ppermute | solution.py:426
  95.1 1.0 mul.105.w_ref
  96.1 13.5 %shard_map.77 = (f32[512,2048]{1,0:T(8,128)}, f32[512,2048]{1,0:T(8,128)}) custom-call(s32[8]{0:T(128)} %get-tuple-element.42.src_left, s32[16]{0:T(128)} %copy-done, s32[8]{0:T(128)} %get-tuple-element.43.tile_ref, s32[128]{0:T(128)} %copy-done.5, s32[8]{0:T(128)} %compare_convert_fusion.flag_ref, bf16[1024,2048]{1,0:T(8,128)(2,1)} %bitcast.156, ...), custom_call_target="tpu_custom_call" | custom-call | tf_op jit(solution)/shard_map/pallas_call | solution.py:177
  109.5 0.9 broadcast_in_dim.49.w_ref
  110.4 13.3 %shard_map.78 = (f32[512,2048]{1,0:T(8,128)}, f32[512,2048]{1,0:T(8,128)}) custom-call(s32[8]{0:T(128)} %get-tuple-element.42.src_left, s32[16]{0:T(128)} %copy-done, s32[8]{0:T(128)} %get-tuple-element.43.tile_ref, s32[64]{0:T(128)} %get-tuple-element.68.mask_ref, s32[8]{0:T(128)} %compare_convert_fusion.flag_ref, ...), custom_call_target="tpu_custom_call", output_to_operand_aliasing={{0}: (8, {}), {1}: (9, {})} | custom-call | tf_op jit(solution)/shard_map/pallas_call | solution.py:177
  124.1 11.7 %cholesky.81 = f32[128,128]{1,0:T(8,128)S(1)} custom-call(f32[128,128]{1,0:T(8,128)S(1)} %fusion.38), custom_call_target="Cholesky" | custom-call | tf_op jit(solution)/shard_map/jit(cholesky)/cholesky | solution.py:261
  136.5 0.7 fusion.27
  137.2 9.8 %custom-call.9 = f32[1,128,128]{1,2,0:T(8,128)S(1)} custom-call(f32[1,128,128]{2,1,0:T(8,128)S(1)} %fusion.27), custom_call_target="InvertDiagBlocksLowerTriangular" | custom-call | tf_op jit(solution)/shard_map/triangular_solve/custom-call.0 | solution.py:263
  151.0 0.7 maximum_bitcast_fusion
  151.7 1.0 collective-permute-done.7.g2_ref
  152.7 1.0 broadcast_in_dim.47.w_ref
  153.7 11.0 %shard_map.79 = f32[1,512,2048]{2,1,0:T(8,128)} custom-call(s32[4]{0:T(128)} %and_select_fusion.1.src_left, s32[16]{0:T(128)} %copy-done, s32[4]{0:T(128)} %copy-done.4, s32[128]{0:T(128)} %reshape.227.mask_ref, s32[4]{0:T(128)} %bitcast.179, bf16[512,2048]{1,0:T(8,128)(2,1)} %copy-done.2, ...), custom_call_target="tpu_custom_call", output_to_operand_aliasing={{}: (9, {})} | custom-call | tf_op jit(solution)/shard_map/pallas_call | solution.py:242
  (104 shorter events, 13.3 us)
Async XLA Ops:
  0.6 10.4 %copy-start.3 = (f32[1,1024]{1,0:T(1,128)S(1)}, f32[1,1024]{1,0:T(1,128)}, u32[]{:S(2)}) copy-start(f32[1,1024]{1,0:T(1,128)} %param.10) | copy-start | bytes 12292
  0.6 11.6 %copy-start.6 = (s32[16]{0:T(128)S(1)}, s32[16]{0:T(128)}, u32[]{:S(2)}) copy-start(s32[16]{0:T(128)} %param.13) | copy-start | bytes 196
  1.4 29.6 %copy-start = (s32[16]{0:T(128)}, s32[16]{0:T(128)S(1)}, u32[]{:S(2)}) copy-start(s32[16]{0:T(128)S(1)} %select_reduce_fusion.3.src_right) | copy-start | bytes 196
  6.7 24.3 %copy-start.5 = (s32[128]{0:T(128)}, s32[128]{0:T(128)S(1)}, u32[]{:S(2)}) copy-start(s32[128]{0:T(128)S(1)} %reshape_squeeze.4.mask_ref) | copy-start | bytes 1540
  11.2 2.6 %collective-permute-start = (f32[53760]{0:T(1024)S(1)}, f32[53760]{0:T(1024)S(1)}, u32[]{:S(2)}, u32[]{:S(2)}) collective-permute-start(f32[53760]{0:T(1024)S(1)} %pad_maximum_fusion), channel_id=1, source_target_pairs={{0,1},{1,0},{2,3},{3,2},{4,5},{5,4},{6,7},{7,6},{8,9},{9,8},{10,11... | collective-permute-start | bytes 645128 | tf_op jit(solution)/shard_map/ppermute | solution.py:316
  12.4 137.1 %copy-start.4 = (s32[4]{0:T(128)}, s32[4]{0:T(128)S(1)}, u32[]{:S(2)}) copy-start(s32[4]{0:T(128)S(1)} %get-tuple-element.49.tile_ref) | copy-start | bytes 52
  13.8 8.6 %collective-permute-start.1 = (f32[53760]{0:T(1024)S(1)}, f32[53760]{0:T(1024)S(1)}, u32[]{:S(2)}, u32[]{:S(2)}) collective-permute-start(f32[53760]{0:T(1024)S(1)} %fusion.75), channel_id=1, source_target_pairs={{0,2},{1,3},{2,0},{3,1},{4,6},{5,7},{6,4},{7,5},{8,10},{9,11},{10,... | collective-permute-start | bytes 645128 | tf_op jit(solution)/shard_map/ppermute | solution.py:316
  22.5 10.7 %collective-permute-start.4 = (f32[3,128,128]{2,1,0:T(8,128)S(1)}, f32[3,128,128]{2,1,0:T(8,128)S(1)}, u32[]{:S(2)}, u32[]{:S(2)}) collective-permute-start(f32[3,128,128]{2,1,0:T(8,128)S(1)} %pad_maximum_fusion.2), channel_id=1, source_target_pairs={{0,4},{4,8},{8,12},{12,16},{16,20},{20,24},{24,28},{1,5},{5,9},{9,... | collective-permute-start | bytes 589832 | tf_op jit(solution)/shard_map/ppermute | solution.py:426
  31.1 57.7 %collective-permute-start.3 = (bf16[512,2048]{1,0:T(8,128)(2,1)}, bf16[512,2048]{1,0:T(8,128)(2,1)}, u32[]{:S(2)}, u32[]{:S(2)}) collective-permute-start(bf16[512,2048]{1,0:T(8,128)(2,1)} %get-tuple-element.52), channel_id=1, source_target_pairs={{0,2},{1,3},{2,0},{3,1},{4,6},{5,7},{6,4},{7,5},{8,10},{9,11},{10,... | collective-permute-start | bytes 6291464 | tf_op jit(solution)/shard_map/ppermute | solution.py:316
  32.7 115.5 %collective-permute-start.2 = (bf16[512,2048]{1,0:T(8,128)(2,1)}, bf16[512,2048]{1,0:T(8,128)(2,1)S(1)}, u32[]{:S(2)}, u32[]{:S(2)}) collective-permute-start(bf16[512,2048]{1,0:T(8,128)(2,1)} %get-tuple-element.53), channel_id=1, source_target_pairs={{0,2},{1,3},{2,0},{3,1},{4,6},{5,7},{6,4},{7,5},{8,10},{9,11},{10,... | collective-permute-start | bytes 6291464 | tf_op jit(solution)/shard_map/ppermute | solution.py:316
  57.8 6.7 %collective-permute-start.5 = (f32[3,128,128]{2,1,0:T(8,128)S(1)}, f32[3,128,128]{2,1,0:T(8,128)S(1)}, u32[]{:S(2)}, u32[]{:S(2)}) collective-permute-start(f32[3,128,128]{2,1,0:T(8,128)S(1)} %pad_maximum_fusion.3), channel_id=1, source_target_pairs={{0,8},{4,12},{8,16},{12,20},{16,24},{20,28},{1,9},{5,13},{9,17},{1... | collective-permute-start | bytes 589832 | tf_op jit(solution)/shard_map/ppermute | solution.py:426
  88.9 34.8 %collective-permute-start.6 = (f32[3,128,128]{2,1,0:T(8,128)S(1)}, f32[3,128,128]{2,1,0:T(8,128)S(1)}, u32[]{:S(2)}, u32[]{:S(2)}) collective-permute-start(f32[3,128,128]{2,1,0:T(8,128)S(1)} %pad_maximum_fusion.4), channel_id=1, source_target_pairs={{0,16},{4,20},{8,24},{12,28},{1,17},{5,21},{9,25},{13,29},{2,18},{... | collective-permute-start | bytes 589832 | tf_op jit(solution)/shard_map/ppermute | solution.py:426
  110.4 38.4 %copy-start.1 = (s32[16]{0:T(128)S(1)}, s32[16]{0:T(128)}, u32[]{:S(2)}) copy-start(s32[16]{0:T(128)} %copy-done) | copy-start | bytes 196
  123.8 29.0 %collective-permute-start.8 = (f32[512,2048]{1,0:T(8,128)}, f32[512,2048]{1,0:T(8,128)}, u32[]{:S(2)}, u32[]{:S(2)}) collective-permute-start(f32[512,2048]{1,0:T(8,128)} %get-tuple-element.36), channel_id=1, source_target_pairs={{0,1},{1,0},{2,3},{3,2},{4,5},{5,4},{6,7},{7,6},{8,9},{9,8},{10,11... | collective-permute-start | bytes 12582920 | tf_op jit(solution)/shard_map/ppermute | solution.py:316
  148.2 5.5 %copy-start.2 = (bf16[512,2048]{1,0:T(8,128)(2,1)}, bf16[512,2048]{1,0:T(8,128)(2,1)S(1)}, u32[]{:S(2)}) copy-start(bf16[512,2048]{1,0:T(8,128)(2,1)S(1)} %collective-permute-done.2.g1_ref) | copy-start | bytes 6291460
  148.2 4.5 %collective-permute-start.7 = (bf16[512,2048]{1,0:T(8,128)(2,1)S(1)}, bf16[512,2048]{1,0:T(8,128)(2,1)}, u32[]{:S(2)}, u32[]{:S(2)}) collective-permute-start(bf16[512,2048]{1,0:T(8,128)(2,1)S(1)} %collective-permute-done.2.g1_ref), channel_id=1, source_target_pairs={{0,1},{1,0},{2,3},{3,2},{4,5},{5,4},{6,7},{7,6},{8,9},{9,8},{10,11... | collective-permute-start | bytes 6291464 | tf_op jit(solution)/shard_map/ppermute | solution.py:316

commit v21 on v20

--- a/solution.py
+++ b/solution.py
@@ -410,11 +410,13 @@
             state["partial"] = own_part(slab_in)
         elif kind == "across":
             mine, partners = across_part(slab_in, state["partial"], 0)
+            second, mine, partners = lax.optimization_barrier((across_halves[1], mine, partners))
+            state["second"] = (second, exchange(second, 1))
             state["mine"] = mine
             state["received"] = exchange(partners, 1)
         else:
             state["owned"] = last_part(
-                slab_in, exchange(slab_in, 1), state["mine"], state["received"]
+                *state["second"], state["mine"], state["received"]
             )
         return running
 

time: 165 us -> 188 us (1.14)
  the two profiles are of different devices: /device:TPU:0 before, /device:TPU:27 now
where the time goes in v21:
time: 188 us; the launch traced here: 187 us
  other arithmetic  75.6 us (40%)
  waiting for transfers between devices  39.5 us (21%)
  Pallas kernels  38.1 us (20%)
  local copies, waits for them, and re-layouts  13.9 us (7%)
  starting transfers between devices  9.61 us (5%)
  between operations  6.34 us (3%)
  matrix products  3.86 us (2%)
    another operation x9, other arithmetic, join_segments(): factor = jnp.linalg.cholesky(middle)  37.2 us
    another operation x6, other arithmetic, join_segments(): lax.linalg.triangular_solve(factor, jnp.concatenate([cross_one.T, cross_t...  31.4 us
    pallas_call x2, Pallas kernels, split_rows(): pl.pallas_call(functools.partial(split_kernel, group=group, accumulate=ac...  27 us
    ppermute x6, waiting for transfers between devices, exchange(): lax.ppermute(value, 'row', [(src, src ^ step) for src in range(owners)])  22.6 us
    ppermute x3, waiting for transfers between devices, local(): moved = lax.ppermute(jnp.stack(running), 'tm', pairs)  16.9 us
    pallas_call x1, Pallas kernels, pair_rows(): pl.pallas_call(pair_kernel, grid_spec=grid_spec, out_shape=jax.ShapeDtype...  11.1 us
    ppermute x6, starting transfers between devices, exchange(): lax.ppermute(value, 'row', [(src, src ^ step) for src in range(owners)])  5.34 us
    slice x1, local copies, waits for them, and re-layouts, local(): lax.slice_in_dim(kernel_slab, h * half_rows, (h + 1) * half_rows)  4.95 us
  transfers between devices with their start and end apart: 9, of which 4 were waited for; matrix products, arithmetic and copies ran while one was open for 44% of the time, Pallas kernels for 14%

profile of v21, /device:TPU:27, one launch (start us, length us, event | category | flops | bytes accessed | tf_op | source)
XLA Modules:
  0.0 187.0 jit_solution(4720783509464901742)
XLA Ops:
  0.6 0.8 select_reduce_fusion.3.src_right
  5.9 0.8 reshape_squeeze.4.mask_ref
  6.7 0.7 pad_maximum_fusion.5
  8.8 1.0 fusion.68
  9.8 1.5 multiply_convert_fusion.1
  11.8 0.7 collective-permute-start
  14.6 1.3 collective-permute-start.1
  16.5 5.0 %collective-permute-done.1 = f32[53760]{0:T(1024)S(1)} collective-permute-done((f32[53760]{0:T(1024)S(1)}, f32[53760]{0:T(1024)S(1)}, u32[]{:S(2)}, u32[]{:S(2)}) %collective-permute-start.1) | collective-permute-done | bytes 215072 | tf_op jit(solution)/shard_map/ppermute | solution.py:316
  21.7 5.0 %fusion.76 = (bf16[512,2048]{1,0:T(8,128)(2,1)}, bf16[512,2048]{1,0:T(8,128)(2,1)}) fusion(bf16[1024,2048]{1,0:T(8,128)(2,1)} %bitcast.155), kind=kLoop, calls=%fused_computation.148 | loop fusion | bytes 8388608 | tf_op jit(solution)/shard_map/slice | solution.py:342
  26.6 1.2 collective-permute-start.2
  28.1 1.3 collective-permute-start.4
  29.7 5.4 %collective-permute-done.4 = f32[3,128,128]{2,1,0:T(8,128)S(1)} collective-permute-done((f32[3,128,128]{2,1,0:T(8,128)S(1)}, f32[3,128,128]{2,1,0:T(8,128)S(1)}, u32[]{:S(2)}, u32[]{:S(2)}) %collective-permute-start.4) | collective-permute-done | bytes 196640 | tf_op jit(solution)/shard_map/ppermute | solution.py:428
  35.4 11.7 %cholesky.59 = f32[128,128]{1,0:T(8,128)S(1)} custom-call(f32[128,128]{1,0:T(8,128)S(1)} %copy.55), custom_call_target="Cholesky" | custom-call | tf_op jit(solution)/shard_map/jit(cholesky)/cholesky | solution.py:261
  48.5 9.8 %custom-call.7 = f32[1,128,128]{1,2,0:T(8,128)S(1)} custom-call(f32[1,128,128]{2,1,0:T(8,128)S(1)} %fusion.25), custom_call_target="InvertDiagBlocksLowerTriangular" | custom-call | tf_op jit(solution)/shard_map/triangular_solve/custom-call.0 | solution.py:263
  59.6 1.5 collective-permute-start.5
  61.6 1.0 mul.105.w_ref
  62.6 13.6 %shard_map.77 = (f32[512,2048]{1,0:T(8,128)}, f32[512,2048]{1,0:T(8,128)}) custom-call(s32[8]{0:T(128)} %get-tuple-element.46.src_left, s32[16]{0:T(128)} %copy-done, s32[8]{0:T(128)} %get-tuple-element.47.tile_ref, s32[128]{0:T(128)} %copy-done.5, s32[8]{0:T(128)} %compare_convert_fusion.flag_ref, bf16[1024,2048]{1,0:T(8,128)(2,1)} %bitcast.156, ...), custom_call_target="tpu_custom_call" | custom-call | tf_op jit(solution)/shard_map/pallas_call | solution.py:177
  76.5 11.7 %cholesky.70 = f32[128,128]{1,0:T(8,128)S(1)} custom-call(f32[128,128]{1,0:T(8,128)S(1)} %fusion.40), custom_call_target="Cholesky" | custom-call | tf_op jit(solution)/shard_map/jit(cholesky)/cholesky | solution.py:261
  88.2 0.7 compare_reduce_fusion.1
  88.9 0.7 fusion.26
  89.6 9.8 %custom-call.8 = f32[1,128,128]{1,2,0:T(8,128)S(1)} custom-call(f32[1,128,128]{2,1,0:T(8,128)S(1)} %fusion.26), custom_call_target="InvertDiagBlocksLowerTriangular" | custom-call | tf_op jit(solution)/shard_map/triangular_solve/custom-call.0 | solution.py:263
  100.6 17.6 %collective-permute-done.3.g_ref = bf16[512,2048]{1,0:T(8,128)(2,1)} collective-permute-done((bf16[512,2048]{1,0:T(8,128)(2,1)}, bf16[512,2048]{1,0:T(8,128)(2,1)}, u32[]{:S(2)}, u32[]{:S(2)}) %collective-permute-start.3) | collective-permute-done | bytes 2097184 | tf_op jit(solution)/shard_map/ppermute | solution.py:316
  118.2 0.8 broadcast_in_dim.48.w_ref
  119.0 13.4 %shard_map.78 = (f32[512,2048]{1,0:T(8,128)}, f32[512,2048]{1,0:T(8,128)}) custom-call(s32[8]{0:T(128)} %get-tuple-element.46.src_left, s32[16]{0:T(128)} %copy-done, s32[8]{0:T(128)} %get-tuple-element.47.tile_ref, s32[64]{0:T(128)} %get-tuple-element.72.mask_ref, s32[8]{0:T(128)} %compare_convert_fusion.flag_ref, ...), custom_call_target="tpu_custom_call", output_to_operand_aliasing={{0}: (8, {}), {1}: (9, {})} | custom-call | tf_op jit(solution)/shard_map/pallas_call | solution.py:177
  132.5 1.8 collective-permute-start.7
  135.9 1.5 collective-permute-start.8
  138.1 11.5 %collective-permute-done.8 = f32[3,128,128]{2,1,0:T(8,128)S(1)} collective-permute-done((f32[3,128,128]{2,1,0:T(8,128)S(1)}, f32[3,128,128]{2,1,0:T(8,128)S(1)}, u32[]{:S(2)}, u32[]{:S(2)}) %collective-permute-start.8) | collective-permute-done | bytes 196640 | tf_op jit(solution)/shard_map/ppermute | solution.py:428
  150.0 11.7 %cholesky.81 = f32[128,128]{1,0:T(8,128)S(1)} custom-call(f32[128,128]{1,0:T(8,128)S(1)} %fusion.38), custom_call_target="Cholesky" | custom-call | tf_op jit(solution)/shard_map/jit(cholesky)/cholesky | solution.py:261
  163.0 9.8 %custom-call.9 = f32[1,128,128]{1,2,0:T(8,128)S(1)} custom-call(f32[1,128,128]{2,1,0:T(8,128)S(1)} %fusion.27), custom_call_target="InvertDiagBlocksLowerTriangular" | custom-call | tf_op jit(solution)/shard_map/triangular_solve/custom-call.0 | solution.py:263
  174.1 0.7 maximum_bitcast_fusion
  174.9 1.0 broadcast_in_dim.49.w_ref
  175.8 11.1 %shard_map.79 = f32[1,512,2048]{2,1,0:T(8,128)} custom-call(s32[4]{0:T(128)} %and_select_fusion.1.src_left, s32[16]{0:T(128)} %copy-done, s32[4]{0:T(128)} %copy-done.4, s32[128]{0:T(128)} %reshape.227.mask_ref, s32[4]{0:T(128)} %bitcast.179, bf16[512,2048]{1,0:T(8,128)(2,1)} %copy-done.2, ...), custom_call_target="tpu_custom_call", output_to_operand_aliasing={{}: (9, {})} | custom-call | tf_op jit(solution)/shard_map/pallas_call | solution.py:242
  (104 shorter events, 14.5 us)
Async XLA Ops:
  0.6 12.5 %copy-start.6 = (s32[16]{0:T(128)S(1)}, s32[16]{0:T(128)}, u32[]{:S(2)}) copy-start(s32[16]{0:T(128)} %param.13) | copy-start | bytes 196
  1.4 25.2 %copy-start = (s32[16]{0:T(128)}, s32[16]{0:T(128)S(1)}, u32[]{:S(2)}) copy-start(s32[16]{0:T(128)S(1)} %select_reduce_fusion.3.src_right) | copy-start | bytes 196
  6.7 19.9 %copy-start.5 = (s32[128]{0:T(128)}, s32[128]{0:T(128)S(1)}, u32[]{:S(2)}) copy-start(s32[128]{0:T(128)S(1)} %reshape_squeeze.4.mask_ref) | copy-start | bytes 1540
  11.8 2.7 %collective-permute-start = (f32[53760]{0:T(1024)S(1)}, f32[53760]{0:T(1024)S(1)}, u32[]{:S(2)}, u32[]{:S(2)}) collective-permute-start(f32[53760]{0:T(1024)S(1)} %pad_maximum_fusion), channel_id=1, source_target_pairs={{0,1},{1,0},{2,3},{3,2},{4,5},{5,4},{6,7},{7,6},{8,9},{9,8},{10,11... | collective-permute-start | bytes 645128 | tf_op jit(solution)/shard_map/ppermute | solution.py:316
  13.2 121.7 %copy-start.4 = (s32[4]{0:T(128)}, s32[4]{0:T(128)S(1)}, u32[]{:S(2)}) copy-start(s32[4]{0:T(128)S(1)} %get-tuple-element.53.tile_ref) | copy-start | bytes 52
  14.6 7.0 %collective-permute-start.1 = (f32[53760]{0:T(1024)S(1)}, f32[53760]{0:T(1024)S(1)}, u32[]{:S(2)}, u32[]{:S(2)}) collective-permute-start(f32[53760]{0:T(1024)S(1)} %fusion.75), channel_id=1, source_target_pairs={{0,2},{1,3},{2,0},{3,1},{4,6},{5,7},{6,4},{7,5},{8,10},{9,11},{10,... | collective-permute-start | bytes 645128 | tf_op jit(solution)/shard_map/ppermute | solution.py:316
  21.6 40.0 %copy-start.3 = (f32[1,1024]{1,0:T(1,128)S(1)}, f32[1,1024]{1,0:T(1,128)}, u32[]{:S(2)}) copy-start(f32[1,1024]{1,0:T(1,128)} %param.10) | copy-start | bytes 12292
  26.6 105.8 %collective-permute-start.2 = (bf16[512,2048]{1,0:T(8,128)(2,1)}, bf16[512,2048]{1,0:T(8,128)(2,1)S(1)}, u32[]{:S(2)}, u32[]{:S(2)}) collective-permute-start(bf16[512,2048]{1,0:T(8,128)(2,1)} %get-tuple-element.57), channel_id=1, source_target_pairs={{0,2},{1,3},{2,0},{3,1},{4,6},{5,7},{6,4},{7,5},{8,10},{9,11},{10,... | collective-permute-start | bytes 6291464 | tf_op jit(solution)/shard_map/ppermute | solution.py:316
  27.9 90.4 %collective-permute-start.3 = (bf16[512,2048]{1,0:T(8,128)(2,1)}, bf16[512,2048]{1,0:T(8,128)(2,1)}, u32[]{:S(2)}, u32[]{:S(2)}) collective-permute-start(bf16[512,2048]{1,0:T(8,128)(2,1)} %get-tuple-element.56), channel_id=1, source_target_pairs={{0,2},{1,3},{2,0},{3,1},{4,6},{5,7},{6,4},{7,5},{8,10},{9,11},{10,... | collective-permute-start | bytes 6291464 | tf_op jit(solution)/shard_map/ppermute | solution.py:316
  28.1 6.9 %collective-permute-start.4 = (f32[3,128,128]{2,1,0:T(8,128)S(1)}, f32[3,128,128]{2,1,0:T(8,128)S(1)}, u32[]{:S(2)}, u32[]{:S(2)}) collective-permute-start(f32[3,128,128]{2,1,0:T(8,128)S(1)} %pad_maximum_fusion.2), channel_id=1, source_target_pairs={{0,4},{4,8},{8,12},{12,16},{16,20},{20,24},{24,28},{1,5},{5,9},{9,... | collective-permute-start | bytes 589832 | tf_op jit(solution)/shard_map/ppermute | solution.py:428
  59.6 16.6 %collective-permute-start.5 = (f32[3,128,128]{2,1,0:T(8,128)S(1)}, f32[3,128,128]{2,1,0:T(8,128)S(1)}, u32[]{:S(2)}, u32[]{:S(2)}) collective-permute-start(f32[3,128,128]{2,1,0:T(8,128)S(1)} %pad_maximum_fusion.3), channel_id=1, source_target_pairs={{0,8},{4,12},{8,16},{12,20},{16,24},{20,28},{1,9},{5,13},{9,17},{1... | collective-permute-start | bytes 589832 | tf_op jit(solution)/shard_map/ppermute | solution.py:428
  119.0 15.2 %copy-start.1 = (s32[16]{0:T(128)S(1)}, s32[16]{0:T(128)}, u32[]{:S(2)}) copy-start(s32[16]{0:T(128)} %copy-done) | copy-start | bytes 196
  132.5 43.4 %copy-start.2 = (bf16[512,2048]{1,0:T(8,128)(2,1)}, bf16[512,2048]{1,0:T(8,128)(2,1)S(1)}, u32[]{:S(2)}) copy-start(bf16[512,2048]{1,0:T(8,128)(2,1)S(1)} %collective-permute-done.2.g1_ref) | copy-start | bytes 6291460
  132.5 42.4 %collective-permute-start.7 = (f32[512,2048]{1,0:T(8,128)}, f32[512,2048]{1,0:T(8,128)}, u32[]{:S(2)}, u32[]{:S(2)}) collective-permute-start(f32[512,2048]{1,0:T(8,128)} %get-tuple-element.37), channel_id=1, source_target_pairs={{0,1},{1,0},{2,3},{3,2},{4,5},{5,4},{6,7},{7,6},{8,9},{9,8},{10,11... | collective-permute-start | bytes 12582920 | tf_op jit(solution)/shard_map/ppermute | solution.py:316
  135.9 13.7 %collective-permute-start.8 = (f32[3,128,128]{2,1,0:T(8,128)S(1)}, f32[3,128,128]{2,1,0:T(8,128)S(1)}, u32[]{:S(2)}, u32[]{:S(2)}) collective-permute-start(f32[3,128,128]{2,1,0:T(8,128)S(1)} %pad_maximum_fusion.4), channel_id=1, source_target_pairs={{0,16},{4,20},{8,24},{12,28},{1,17},{5,21},{9,25},{13,29},{2,18},{... | collective-permute-start | bytes 589832 | tf_op jit(solution)/shard_map/ppermute | solution.py:428
  138.0 36.8 %collective-permute-start.6 = (bf16[512,2048]{1,0:T(8,128)(2,1)S(1)}, bf16[512,2048]{1,0:T(8,128)(2,1)}, u32[]{:S(2)}, u32[]{:S(2)}) collective-permute-start(bf16[512,2048]{1,0:T(8,128)(2,1)S(1)} %collective-permute-done.2.g1_ref), channel_id=1, source_target_pairs={{0,1},{1,0},{2,3},{3,2},{4,5},{5,4},{6,7},{7,6},{8,9},{9,8},{10,11... | collective-permute-start | bytes 6291464 | tf_op jit(solution)/shard_map/ppermute | solution.py:316

commit v22 on v20

--- a/solution.py
+++ b/solution.py
@@ -385,7 +385,8 @@
             )
             return total[0]
 
-        hooks = {1: ("own", kernel_slab), 2: ("across", across_halves[0]), 3: ("last", across_halves[1])}
+        hooks = {2: ("across", across_halves[0]), 3: ("last", across_halves[1])}
+        early_partial = own_part(local_slab)
     else:
         hooks = {}
         flags = jnp.full((block_count,), (my_index == 0).astype(jnp.int32))
@@ -403,6 +404,8 @@
     shift = 1
     round_index = 0
     state = {}
+    if owners == 4:
+        state["partial"] = early_partial
 
     def run_hook(kind, slab_in, running):
         slab_in, running = lax.optimization_barrier((slab_in, running))

time: 165 us -> 164 us (level)
  local copies, waits for them, and re-layouts: 13.8 us -> 11.5 us
    slice x1, local copies, waits for them, and re-layouts: 4.89 us -> 2.62 us  [local(): lax.slice_in_dim(kernel_slab, h * half_rows, (h + 1) * half_rows)]
  transfers between devices with their start and end apart: 9 -> 9, of which waited for: 3 -> 3; matrix products, arithmetic and copies ran while one was open for 52% -> 51% of each run, Pallas kernels for 16% -> 16%
where the time goes in v22:
time: 164 us
  other arithmetic  74.9 us (46%)
  Pallas kernels  37.9 us (23%)
  starting transfers between devices  19.8 us (12%)
  local copies, waits for them, and re-layouts  11.5 us (7%)
  waiting for transfers between devices  9.15 us (6%)
  between operations  6.43 us (4%)
  matrix products  3.87 us (2%)
    another operation x9, other arithmetic, join_segments(): factor = jnp.linalg.cholesky(middle)  37.2 us
    another operation x6, other arithmetic, join_segments(): lax.linalg.triangular_solve(factor, jnp.concatenate([cross_one.T, cross_t...  31.4 us
    pallas_call x2, Pallas kernels, split_rows(): pl.pallas_call(functools.partial(split_kernel, group=group, accumulate=ac...  26.9 us
    ppermute x3, starting transfers between devices, local(): moved = lax.ppermute(jnp.stack(running), 'tm', pairs)  14 us
    pallas_call x1, Pallas kernels, pair_rows(): pl.pallas_call(pair_kernel, grid_spec=grid_spec, out_shape=jax.ShapeDtype...  11 us
    ppermute x6, waiting for transfers between devices, exchange(): lax.ppermute(value, 'row', [(src, src ^ step) for src in range(owners)])  6.33 us
    ppermute x6, starting transfers between devices, exchange(): lax.ppermute(value, 'row', [(src, src ^ step) for src in range(owners)])  5.8 us
  transfers between devices with their start and end apart: 9, of which 3 were waited for; matrix products, arithmetic and copies ran while one was open for 51% of the time, Pallas kernels for 16%

profile of v22, /device:TPU:0, one launch (start us, length us, event | category | flops | bytes accessed | tf_op | source)
XLA Modules:
  0.0 163.6 jit_solution(10711024647601504052)
XLA Ops:
  0.7 0.8 select_reduce_fusion.3.src_right
  5.9 0.8 reshape_squeeze.4.mask_ref
  8.0 1.0 fusion.68
  9.0 1.5 multiply_convert_fusion.1
  12.5 0.6 gather_fusion.1
  13.1 0.6 and_select_fusion
  13.8 1.0 mul.105.w_ref
  14.8 13.5 %shard_map.77 = (f32[512,2048]{1,0:T(8,128)}, f32[512,2048]{1,0:T(8,128)}) custom-call(s32[8]{0:T(128)} %get-tuple-element.34.src_left, s32[16]{0:T(128)} %copy-done, s32[8]{0:T(128)} %get-tuple-element.35.tile_ref, s32[128]{0:T(128)} %copy-done.6, s32[8]{0:T(128)} %compare_convert_fusion.flag_ref, bf16[1024,2048]{1,0:T(8,128)(2,1)} %bitcast.155, ...), custom_call_target="tpu_custom_call" | custom-call | tf_op jit(solution)/shard_map/pallas_call | solution.py:177
  28.3 2.6 %collective-permute-start.1 = (f32[53760]{0:T(1024)S(1)}, f32[53760]{0:T(1024)S(1)}, u32[]{:S(2)}, u32[]{:S(2)}) collective-permute-start(f32[53760]{0:T(1024)S(1)} %fusion.75), channel_id=1, source_target_pairs={{0,2},{1,3},{2,0},{3,1},{4,6},{5,7},{6,4},{7,5},{8,10},{9,11},{10,... | collective-permute-start | bytes 645128 | tf_op jit(solution)/shard_map/ppermute | solution.py:316
  30.9 0.7 slice_bitcast_fusion.16
  31.6 5.3 %collective-permute-done.1 = f32[53760]{0:T(1024)S(1)} collective-permute-done((f32[53760]{0:T(1024)S(1)}, f32[53760]{0:T(1024)S(1)}, u32[]{:S(2)}, u32[]{:S(2)}) %collective-permute-start.1) | collective-permute-done | bytes 215072 | tf_op jit(solution)/shard_map/ppermute | solution.py:316
  37.0 3.6 %collective-permute-start.4 = (f32[3,128,128]{2,1,0:T(8,128)S(1)}, f32[3,128,128]{2,1,0:T(8,128)S(1)}, u32[]{:S(2)}, u32[]{:S(2)}) collective-permute-start(f32[3,128,128]{2,1,0:T(8,128)S(1)} %pad_maximum_fusion.2), channel_id=1, source_target_pairs={{0,4},{4,8},{8,12},{12,16},{16,20},{20,24},{24,28},{1,5},{5,9},{9,... | collective-permute-start | bytes 589832 | tf_op jit(solution)/shard_map/ppermute | solution.py:429
  40.6 2.6 %fusion.76 = (bf16[512,2048]{1,0:T(8,128)(2,1)}, bf16[512,2048]{1,0:T(8,128)(2,1)}) fusion(bf16[1024,2048]{1,0:T(8,128)(2,1)S(1)} %bitcast.156), kind=kLoop, calls=%fused_computation.148 | loop fusion | bytes 8388608 | tf_op jit(solution)/shard_map/slice | solution.py:342
  43.3 1.6 collective-permute-start.3
  45.8 11.7 %cholesky.59 = f32[128,128]{1,0:T(8,128)S(1)} custom-call(f32[128,128]{1,0:T(8,128)S(1)} %copy.53), custom_call_target="Cholesky" | custom-call | tf_op jit(solution)/shard_map/jit(cholesky)/cholesky | solution.py:261
  58.2 0.7 fusion.25
  58.9 9.8 %custom-call.7 = f32[1,128,128]{1,2,0:T(8,128)S(1)} custom-call(f32[1,128,128]{2,1,0:T(8,128)S(1)} %fusion.25), custom_call_target="InvertDiagBlocksLowerTriangular" | custom-call | tf_op jit(solution)/shard_map/triangular_solve/custom-call.0 | solution.py:263
  70.0 4.7 %collective-permute-start.5 = (f32[3,128,128]{2,1,0:T(8,128)S(1)}, f32[3,128,128]{2,1,0:T(8,128)S(1)}, u32[]{:S(2)}, u32[]{:S(2)}) collective-permute-start(f32[3,128,128]{2,1,0:T(8,128)S(1)} %pad_maximum_fusion.3), channel_id=1, source_target_pairs={{0,8},{4,12},{8,16},{12,20},{16,24},{20,28},{1,9},{5,13},{9,17},{1... | collective-permute-start | bytes 589832 | tf_op jit(solution)/shard_map/ppermute | solution.py:429
  74.9 2.8 %collective-permute-done.5 = f32[3,128,128]{2,1,0:T(8,128)S(1)} collective-permute-done((f32[3,128,128]{2,1,0:T(8,128)S(1)}, f32[3,128,128]{2,1,0:T(8,128)S(1)}, u32[]{:S(2)}, u32[]{:S(2)}) %collective-permute-start.5) | collective-permute-done | bytes 196640 | tf_op jit(solution)/shard_map/ppermute | solution.py:429
  78.0 11.7 %cholesky.70 = f32[128,128]{1,0:T(8,128)S(1)} custom-call(f32[128,128]{1,0:T(8,128)S(1)} %fusion.40), custom_call_target="Cholesky" | custom-call | tf_op jit(solution)/shard_map/jit(cholesky)/cholesky | solution.py:261
  90.4 0.7 fusion.26
  91.0 9.8 %custom-call.8 = f32[1,128,128]{1,2,0:T(8,128)S(1)} custom-call(f32[1,128,128]{2,1,0:T(8,128)S(1)} %fusion.26), custom_call_target="InvertDiagBlocksLowerTriangular" | custom-call | tf_op jit(solution)/shard_map/triangular_solve/custom-call.0 | solution.py:263
  102.2 5.6 %collective-permute-start.6 = (f32[3,128,128]{2,1,0:T(8,128)S(1)}, f32[3,128,128]{2,1,0:T(8,128)S(1)}, u32[]{:S(2)}, u32[]{:S(2)}) collective-permute-start(f32[3,128,128]{2,1,0:T(8,128)S(1)} %pad_maximum_fusion.4), channel_id=1, source_target_pairs={{0,16},{4,20},{8,24},{12,28},{1,17},{5,21},{9,25},{13,29},{2,18},{... | collective-permute-start | bytes 589832 | tf_op jit(solution)/shard_map/ppermute | solution.py:429
  108.4 0.9 broadcast_in_dim.49.w_ref
  109.2 13.4 %shard_map.78 = (f32[512,2048]{1,0:T(8,128)}, f32[512,2048]{1,0:T(8,128)}) custom-call(s32[8]{0:T(128)} %get-tuple-element.34.src_left, s32[16]{0:T(128)} %copy-done, s32[8]{0:T(128)} %get-tuple-element.35.tile_ref, s32[64]{0:T(128)} %get-tuple-element.60.mask_ref, s32[8]{0:T(128)} %compare_convert_fusion.flag_ref, ...), custom_call_target="tpu_custom_call", output_to_operand_aliasing={{0}: (8, {}), {1}: (9, {})} | custom-call | tf_op jit(solution)/shard_map/pallas_call | solution.py:177
  123.0 11.7 %cholesky.81 = f32[128,128]{1,0:T(8,128)S(1)} custom-call(f32[128,128]{1,0:T(8,128)S(1)} %fusion.38), custom_call_target="Cholesky" | custom-call | tf_op jit(solution)/shard_map/jit(cholesky)/cholesky | solution.py:261
  135.4 0.7 fusion.27
  136.0 9.8 %custom-call.9 = f32[1,128,128]{1,2,0:T(8,128)S(1)} custom-call(f32[1,128,128]{2,1,0:T(8,128)S(1)} %fusion.27), custom_call_target="InvertDiagBlocksLowerTriangular" | custom-call | tf_op jit(solution)/shard_map/triangular_solve/custom-call.0 | solution.py:263
  149.8 0.7 maximum_bitcast_fusion
  150.5 1.0 collective-permute-done.7.g2_ref
  151.6 1.0 broadcast_in_dim.47.w_ref
  152.6 11.0 %shard_map.79 = f32[1,512,2048]{2,1,0:T(8,128)} custom-call(s32[4]{0:T(128)} %and_select_fusion.1.src_left, s32[16]{0:T(128)} %copy-done, s32[4]{0:T(128)} %copy-done.5, s32[128]{0:T(128)} %reshape.227.mask_ref, s32[4]{0:T(128)} %bitcast.179, bf16[512,2048]{1,0:T(8,128)(2,1)} %copy-done.3, ...), custom_call_target="tpu_custom_call", output_to_operand_aliasing={{}: (9, {})} | custom-call | tf_op jit(solution)/shard_map/pallas_call | solution.py:242
  (106 shorter events, 13.2 us)
Async XLA Ops:
  0.6 10.4 %copy-start.4 = (f32[1,1024]{1,0:T(1,128)S(1)}, f32[1,1024]{1,0:T(1,128)}, u32[]{:S(2)}) copy-start(f32[1,1024]{1,0:T(1,128)} %param.10) | copy-start | bytes 12292
  0.6 11.6 %copy-start.7 = (s32[16]{0:T(128)S(1)}, s32[16]{0:T(128)}, u32[]{:S(2)}) copy-start(s32[16]{0:T(128)} %param.13) | copy-start | bytes 196
  1.4 13.3 %copy-start = (s32[16]{0:T(128)}, s32[16]{0:T(128)S(1)}, u32[]{:S(2)}) copy-start(s32[16]{0:T(128)S(1)} %select_reduce_fusion.3.src_right) | copy-start | bytes 196
  6.7 8.1 %copy-start.6 = (s32[128]{0:T(128)}, s32[128]{0:T(128)S(1)}, u32[]{:S(2)}) copy-start(s32[128]{0:T(128)S(1)} %reshape_squeeze.4.mask_ref) | copy-start | bytes 1540
  11.2 17.1 %collective-permute-start = (f32[53760]{0:T(1024)S(1)}, f32[53760]{0:T(1024)S(1)}, u32[]{:S(2)}, u32[]{:S(2)}) collective-permute-start(f32[53760]{0:T(1024)S(1)} %pad_maximum_fusion), channel_id=1, source_target_pairs={{0,1},{1,0},{2,3},{3,2},{4,5},{5,4},{6,7},{7,6},{8,9},{9,8},{10,11... | collective-permute-start | bytes 645128 | tf_op jit(solution)/shard_map/ppermute | solution.py:316
  12.4 135.9 %copy-start.5 = (s32[4]{0:T(128)}, s32[4]{0:T(128)S(1)}, u32[]{:S(2)}) copy-start(s32[4]{0:T(128)S(1)} %get-tuple-element.41.tile_ref) | copy-start | bytes 52
  13.1 27.5 %copy-start.2 = (bf16[1,1024,2048]{2,1,0:T(8,128)(2,1)S(1)}, bf16[1,1024,2048]{2,1,0:T(8,128)(2,1)}, u32[]{:S(2)}) copy-start(bf16[1,1024,2048]{2,1,0:T(8,128)(2,1)} %param.9) | copy-start | bytes 12582916
  28.3 8.6 %collective-permute-start.1 = (f32[53760]{0:T(1024)S(1)}, f32[53760]{0:T(1024)S(1)}, u32[]{:S(2)}, u32[]{:S(2)}) collective-permute-start(f32[53760]{0:T(1024)S(1)} %fusion.75), channel_id=1, source_target_pairs={{0,2},{1,3},{2,0},{3,1},{4,6},{5,7},{6,4},{7,5},{8,10},{9,11},{10,... | collective-permute-start | bytes 645128 | tf_op jit(solution)/shard_map/ppermute | solution.py:316
  37.0 8.4 %collective-permute-start.4 = (f32[3,128,128]{2,1,0:T(8,128)S(1)}, f32[3,128,128]{2,1,0:T(8,128)S(1)}, u32[]{:S(2)}, u32[]{:S(2)}) collective-permute-start(f32[3,128,128]{2,1,0:T(8,128)S(1)} %pad_maximum_fusion.2), channel_id=1, source_target_pairs={{0,4},{4,8},{8,12},{12,16},{16,20},{20,24},{24,28},{1,5},{5,9},{9,... | collective-permute-start | bytes 589832 | tf_op jit(solution)/shard_map/ppermute | solution.py:429
  43.3 58.8 %collective-permute-start.3 = (bf16[512,2048]{1,0:T(8,128)(2,1)}, bf16[512,2048]{1,0:T(8,128)(2,1)}, u32[]{:S(2)}, u32[]{:S(2)}) collective-permute-start(bf16[512,2048]{1,0:T(8,128)(2,1)} %get-tuple-element.44), channel_id=1, source_target_pairs={{0,2},{1,3},{2,0},{3,1},{4,6},{5,7},{6,4},{7,5},{8,10},{9,11},{10,... | collective-permute-start | bytes 6291464 | tf_op jit(solution)/shard_map/ppermute | solution.py:316
  44.9 102.2 %collective-permute-start.2 = (bf16[512,2048]{1,0:T(8,128)(2,1)}, bf16[512,2048]{1,0:T(8,128)(2,1)S(1)}, u32[]{:S(2)}, u32[]{:S(2)}) collective-permute-start(bf16[512,2048]{1,0:T(8,128)(2,1)} %get-tuple-element.45), channel_id=1, source_target_pairs={{0,2},{1,3},{2,0},{3,1},{4,6},{5,7},{6,4},{7,5},{8,10},{9,11},{10,... | collective-permute-start | bytes 6291464 | tf_op jit(solution)/shard_map/ppermute | solution.py:316
  70.0 7.7 %collective-permute-start.5 = (f32[3,128,128]{2,1,0:T(8,128)S(1)}, f32[3,128,128]{2,1,0:T(8,128)S(1)}, u32[]{:S(2)}, u32[]{:S(2)}) collective-permute-start(f32[3,128,128]{2,1,0:T(8,128)S(1)} %pad_maximum_fusion.3), channel_id=1, source_target_pairs={{0,8},{4,12},{8,16},{12,20},{16,24},{20,28},{1,9},{5,13},{9,17},{1... | collective-permute-start | bytes 589832 | tf_op jit(solution)/shard_map/ppermute | solution.py:429
  102.2 20.4 %collective-permute-start.6 = (f32[3,128,128]{2,1,0:T(8,128)S(1)}, f32[3,128,128]{2,1,0:T(8,128)S(1)}, u32[]{:S(2)}, u32[]{:S(2)}) collective-permute-start(f32[3,128,128]{2,1,0:T(8,128)S(1)} %pad_maximum_fusion.4), channel_id=1, source_target_pairs={{0,16},{4,20},{8,24},{12,28},{1,17},{5,21},{9,25},{13,29},{2,18},{... | collective-permute-start | bytes 589832 | tf_op jit(solution)/shard_map/ppermute | solution.py:429
  109.2 38.4 %copy-start.1 = (s32[16]{0:T(128)S(1)}, s32[16]{0:T(128)}, u32[]{:S(2)}) copy-start(s32[16]{0:T(128)} %copy-done) | copy-start | bytes 196
  122.6 29.0 %collective-permute-start.8 = (f32[512,2048]{1,0:T(8,128)}, f32[512,2048]{1,0:T(8,128)}, u32[]{:S(2)}, u32[]{:S(2)}) collective-permute-start(f32[512,2048]{1,0:T(8,128)} %get-tuple-element.28), channel_id=1, source_target_pairs={{0,1},{1,0},{2,3},{3,2},{4,5},{5,4},{6,7},{7,6},{8,9},{9,8},{10,11... | collective-permute-start | bytes 12582920 | tf_op jit(solution)/shard_map/ppermute | solution.py:316
  147.1 5.5 %copy-start.3 = (bf16[512,2048]{1,0:T(8,128)(2,1)}, bf16[512,2048]{1,0:T(8,128)(2,1)S(1)}, u32[]{:S(2)}) copy-start(bf16[512,2048]{1,0:T(8,128)(2,1)S(1)} %collective-permute-done.2.g1_ref) | copy-start | bytes 6291460
  147.1 4.5 %collective-permute-start.7 = (bf16[512,2048]{1,0:T(8,128)(2,1)S(1)}, bf16[512,2048]{1,0:T(8,128)(2,1)}, u32[]{:S(2)}, u32[]{:S(2)}) collective-permute-start(bf16[512,2048]{1,0:T(8,128)(2,1)S(1)} %collective-permute-done.2.g1_ref), channel_id=1, source_target_pairs={{0,1},{1,0},{2,3},{3,2},{4,5},{5,4},{6,7},{7,6},{8,9},{9,8},{10,11... | collective-permute-start | bytes 6291464 | tf_op jit(solution)/shard_map/ppermute | solution.py:316

commit v23 on v22

--- a/solution.py
+++ b/solution.py
@@ -321,8 +321,8 @@
     piece_count = part_pieces.size
     summed_all = jnp.concatenate([part_pieces.reshape(-1), side_slots.reshape(-1)])
     if owners == 4:
+        summed_all = summed_all + exchange(summed_all, 2)
         summed_all = summed_all + exchange(summed_all, 1)
-        summed_all = summed_all + exchange(summed_all, 2)
     else:
         summed_all = lax.psum(summed_all, "row")
     kernel_slab, summed_all = lax.optimization_barrier((local_slab, summed_all))

time: 164 us -> 160 us (0.976)
  waiting for transfers between devices: 9.15 us -> 5.08 us
    ppermute x6, waiting for transfers between devices: 6.33 us -> 1.82 us  [exchange(): lax.ppermute(value, 'row', [(src, src ^ step) for src in range(owners)])]
  transfers between devices with their start and end apart: 9 -> 9, of which waited for: 3 -> 3; matrix products, arithmetic and copies ran while one was open for 51% -> 53% of each run, Pallas kernels for 16% -> 17%
where the time goes in v23:
time: 160 us
  other arithmetic  74.9 us (47%)
  Pallas kernels  37.9 us (24%)
  starting transfers between devices  20 us (12%)
  local copies, waits for them, and re-layouts  11.5 us (7%)
  between operations  6.43 us (4%)
  waiting for transfers between devices  5.08 us (3%)
  matrix products  3.87 us (2%)
    another operation x9, other arithmetic, join_segments(): factor = jnp.linalg.cholesky(middle)  37.2 us
    another operation x6, other arithmetic, join_segments(): lax.linalg.triangular_solve(factor, jnp.concatenate([cross_one.T, cross_t...  31.4 us
    pallas_call x2, Pallas kernels, split_rows(): pl.pallas_call(functools.partial(split_kernel, group=group, accumulate=ac...  26.8 us
    ppermute x3, starting transfers between devices, local(): moved = lax.ppermute(jnp.stack(running), 'tm', pairs)  14.2 us
    pallas_call x1, Pallas kernels, pair_rows(): pl.pallas_call(pair_kernel, grid_spec=grid_spec, out_shape=jax.ShapeDtype...  11 us
    ppermute x6, starting transfers between devices, exchange(): lax.ppermute(value, 'row', [(src, src ^ step) for src in range(owners)])  5.76 us
    ppermute x3, waiting for transfers between devices, local(): moved = lax.ppermute(jnp.stack(running), 'tm', pairs)  3.26 us
  transfers between devices with their start and end apart: 9, of which 3 were waited for; matrix products, arithmetic and copies ran while one was open for 53% of the time, Pallas kernels for 17%

profile of v23, /device:TPU:0, one launch (start us, length us, event | category | flops | bytes accessed | tf_op | source)
XLA Modules:
  0.0 159.7 jit_solution(15259082219016721932)
XLA Ops:
  0.7 0.8 select_reduce_fusion.3.src_right
  5.9 0.8 reshape_squeeze.4.mask_ref
  8.0 1.0 fusion.68
  9.0 1.5 multiply_convert_fusion.1
  11.2 3.0 %collective-permute-start = (f32[53760]{0:T(1024)S(1)}, f32[53760]{0:T(1024)S(1)}, u32[]{:S(2)}, u32[]{:S(2)}) collective-permute-start(f32[53760]{0:T(1024)S(1)} %pad_maximum_fusion), channel_id=1, source_target_pairs={{0,2},{1,3},{2,0},{3,1},{4,6},{5,7},{6,4},{7,5},{8,10},{9,11},{10,... | collective-permute-start | bytes 645128 | tf_op jit(solution)/shard_map/ppermute | solution.py:316
  15.0 0.6 gather_fusion.1
  15.6 0.6 and_select_fusion
  16.3 1.0 mul.105.w_ref
  17.3 13.5 %shard_map.77 = (f32[512,2048]{1,0:T(8,128)}, f32[512,2048]{1,0:T(8,128)}) custom-call(s32[8]{0:T(128)} %get-tuple-element.34.src_left, s32[16]{0:T(128)} %copy-done, s32[8]{0:T(128)} %get-tuple-element.35.tile_ref, s32[128]{0:T(128)} %copy-done.6, s32[8]{0:T(128)} %compare_convert_fusion.flag_ref, bf16[1024,2048]{1,0:T(8,128)(2,1)} %bitcast.155, ...), custom_call_target="tpu_custom_call" | custom-call | tf_op jit(solution)/shard_map/pallas_call | solution.py:177
  30.9 0.7 slice_bitcast_fusion.16
  31.5 0.8 collective-permute-done.1
  32.4 3.4 %collective-permute-start.4 = (f32[3,128,128]{2,1,0:T(8,128)S(1)}, f32[3,128,128]{2,1,0:T(8,128)S(1)}, u32[]{:S(2)}, u32[]{:S(2)}) collective-permute-start(f32[3,128,128]{2,1,0:T(8,128)S(1)} %pad_maximum_fusion.2), channel_id=1, source_target_pairs={{0,4},{4,8},{8,12},{12,16},{16,20},{20,24},{24,28},{1,5},{5,9},{9,... | collective-permute-start | bytes 589832 | tf_op jit(solution)/shard_map/ppermute | solution.py:429
  35.9 2.6 %fusion.76 = (bf16[512,2048]{1,0:T(8,128)(2,1)}, bf16[512,2048]{1,0:T(8,128)(2,1)}) fusion(bf16[1024,2048]{1,0:T(8,128)(2,1)S(1)} %bitcast.156), kind=kLoop, calls=%fused_computation.148 | loop fusion | bytes 8388608 | tf_op jit(solution)/shard_map/slice | solution.py:342
  39.2 1.5 collective-permute-start.2
  41.1 11.7 %cholesky.59 = f32[128,128]{1,0:T(8,128)S(1)} custom-call(f32[128,128]{1,0:T(8,128)S(1)} %copy.53), custom_call_target="Cholesky" | custom-call | tf_op jit(solution)/shard_map/jit(cholesky)/cholesky | solution.py:261
  53.5 0.7 fusion.25
  54.1 9.8 %custom-call.7 = f32[1,128,128]{1,2,0:T(8,128)S(1)} custom-call(f32[1,128,128]{2,1,0:T(8,128)S(1)} %fusion.25), custom_call_target="InvertDiagBlocksLowerTriangular" | custom-call | tf_op jit(solution)/shard_map/triangular_solve/custom-call.0 | solution.py:263
  65.3 5.2 %collective-permute-start.5 = (f32[3,128,128]{2,1,0:T(8,128)S(1)}, f32[3,128,128]{2,1,0:T(8,128)S(1)}, u32[]{:S(2)}, u32[]{:S(2)}) collective-permute-start(f32[3,128,128]{2,1,0:T(8,128)S(1)} %pad_maximum_fusion.3), channel_id=1, source_target_pairs={{0,8},{4,12},{8,16},{12,20},{16,24},{20,28},{1,9},{5,13},{9,17},{1... | collective-permute-start | bytes 589832 | tf_op jit(solution)/shard_map/ppermute | solution.py:429
  70.7 3.3 %collective-permute-done.5 = f32[3,128,128]{2,1,0:T(8,128)S(1)} collective-permute-done((f32[3,128,128]{2,1,0:T(8,128)S(1)}, f32[3,128,128]{2,1,0:T(8,128)S(1)}, u32[]{:S(2)}, u32[]{:S(2)}) %collective-permute-start.5) | collective-permute-done | bytes 196640 | tf_op jit(solution)/shard_map/ppermute | solution.py:429
  74.2 11.7 %cholesky.70 = f32[128,128]{1,0:T(8,128)S(1)} custom-call(f32[128,128]{1,0:T(8,128)S(1)} %fusion.40), custom_call_target="Cholesky" | custom-call | tf_op jit(solution)/shard_map/jit(cholesky)/cholesky | solution.py:261
  86.6 0.7 fusion.26
  87.2 9.8 %custom-call.8 = f32[1,128,128]{1,2,0:T(8,128)S(1)} custom-call(f32[1,128,128]{2,1,0:T(8,128)S(1)} %fusion.26), custom_call_target="InvertDiagBlocksLowerTriangular" | custom-call | tf_op jit(solution)/shard_map/triangular_solve/custom-call.0 | solution.py:263
  98.4 5.6 %collective-permute-start.6 = (f32[3,128,128]{2,1,0:T(8,128)S(1)}, f32[3,128,128]{2,1,0:T(8,128)S(1)}, u32[]{:S(2)}, u32[]{:S(2)}) collective-permute-start(f32[3,128,128]{2,1,0:T(8,128)S(1)} %pad_maximum_fusion.4), channel_id=1, source_target_pairs={{0,16},{4,20},{8,24},{12,28},{1,17},{5,21},{9,25},{13,29},{2,18},{... | collective-permute-start | bytes 589832 | tf_op jit(solution)/shard_map/ppermute | solution.py:429
  104.5 0.9 broadcast_in_dim.49.w_ref
  105.3 13.4 %shard_map.78 = (f32[512,2048]{1,0:T(8,128)}, f32[512,2048]{1,0:T(8,128)}) custom-call(s32[8]{0:T(128)} %get-tuple-element.34.src_left, s32[16]{0:T(128)} %copy-done, s32[8]{0:T(128)} %get-tuple-element.35.tile_ref, s32[64]{0:T(128)} %get-tuple-element.60.mask_ref, s32[8]{0:T(128)} %compare_convert_fusion.flag_ref, ...), custom_call_target="tpu_custom_call", output_to_operand_aliasing={{0}: (8, {}), {1}: (9, {})} | custom-call | tf_op jit(solution)/shard_map/pallas_call | solution.py:177
  119.1 11.7 %cholesky.81 = f32[128,128]{1,0:T(8,128)S(1)} custom-call(f32[128,128]{1,0:T(8,128)S(1)} %fusion.38), custom_call_target="Cholesky" | custom-call | tf_op jit(solution)/shard_map/jit(cholesky)/cholesky | solution.py:261
  131.4 0.7 fusion.27
  132.1 9.8 %custom-call.9 = f32[1,128,128]{1,2,0:T(8,128)S(1)} custom-call(f32[1,128,128]{2,1,0:T(8,128)S(1)} %fusion.27), custom_call_target="InvertDiagBlocksLowerTriangular" | custom-call | tf_op jit(solution)/shard_map/triangular_solve/custom-call.0 | solution.py:263
  145.9 0.7 maximum_bitcast_fusion
  146.6 1.0 collective-permute-done.7.g2_ref
  147.6 1.0 broadcast_in_dim.47.w_ref
  148.6 11.0 %shard_map.79 = f32[1,512,2048]{2,1,0:T(8,128)} custom-call(s32[4]{0:T(128)} %and_select_fusion.1.src_left, s32[16]{0:T(128)} %copy-done, s32[4]{0:T(128)} %copy-done.5, s32[128]{0:T(128)} %reshape.227.mask_ref, s32[4]{0:T(128)} %bitcast.179, bf16[512,2048]{1,0:T(8,128)(2,1)} %copy-done.3, ...), custom_call_target="tpu_custom_call", output_to_operand_aliasing={{}: (9, {})} | custom-call | tf_op jit(solution)/shard_map/pallas_call | solution.py:242
  (106 shorter events, 12.8 us)
Async XLA Ops:
  0.6 10.4 %copy-start.4 = (f32[1,1024]{1,0:T(1,128)S(1)}, f32[1,1024]{1,0:T(1,128)}, u32[]{:S(2)}) copy-start(f32[1,1024]{1,0:T(1,128)} %param.10) | copy-start | bytes 12292
  0.6 14.2 %copy-start.7 = (s32[16]{0:T(128)S(1)}, s32[16]{0:T(128)}, u32[]{:S(2)}) copy-start(s32[16]{0:T(128)} %param.13) | copy-start | bytes 196
  1.4 15.8 %copy-start = (s32[16]{0:T(128)}, s32[16]{0:T(128)S(1)}, u32[]{:S(2)}) copy-start(s32[16]{0:T(128)S(1)} %select_reduce_fusion.3.src_right) | copy-start | bytes 196
  6.7 10.6 %copy-start.6 = (s32[128]{0:T(128)}, s32[128]{0:T(128)S(1)}, u32[]{:S(2)}) copy-start(s32[128]{0:T(128)S(1)} %reshape_squeeze.4.mask_ref) | copy-start | bytes 1540
  11.2 19.6 %collective-permute-start = (f32[53760]{0:T(1024)S(1)}, f32[53760]{0:T(1024)S(1)}, u32[]{:S(2)}, u32[]{:S(2)}) collective-permute-start(f32[53760]{0:T(1024)S(1)} %pad_maximum_fusion), channel_id=1, source_target_pairs={{0,2},{1,3},{2,0},{3,1},{4,6},{5,7},{6,4},{7,5},{8,10},{9,11},{10,... | collective-permute-start | bytes 645128 | tf_op jit(solution)/shard_map/ppermute | solution.py:316
  14.9 129.5 %copy-start.5 = (s32[4]{0:T(128)}, s32[4]{0:T(128)S(1)}, u32[]{:S(2)}) copy-start(s32[4]{0:T(128)S(1)} %get-tuple-element.41.tile_ref) | copy-start | bytes 52
  15.6 20.3 %copy-start.2 = (bf16[1,1024,2048]{2,1,0:T(8,128)(2,1)S(1)}, bf16[1,1024,2048]{2,1,0:T(8,128)(2,1)}, u32[]{:S(2)}) copy-start(bf16[1,1024,2048]{2,1,0:T(8,128)(2,1)} %param.9) | copy-start | bytes 12582916
  30.8 1.5 collective-permute-start.1
  32.4 8.3 %collective-permute-start.4 = (f32[3,128,128]{2,1,0:T(8,128)S(1)}, f32[3,128,128]{2,1,0:T(8,128)S(1)}, u32[]{:S(2)}, u32[]{:S(2)}) collective-permute-start(f32[3,128,128]{2,1,0:T(8,128)S(1)} %pad_maximum_fusion.2), channel_id=1, source_target_pairs={{0,4},{4,8},{8,12},{12,16},{16,20},{20,24},{24,28},{1,5},{5,9},{9,... | collective-permute-start | bytes 589832 | tf_op jit(solution)/shard_map/ppermute | solution.py:429
  38.6 59.7 %collective-permute-start.3 = (bf16[512,2048]{1,0:T(8,128)(2,1)}, bf16[512,2048]{1,0:T(8,128)(2,1)}, u32[]{:S(2)}, u32[]{:S(2)}) collective-permute-start(bf16[512,2048]{1,0:T(8,128)(2,1)} %get-tuple-element.44), channel_id=1, source_target_pairs={{0,2},{1,3},{2,0},{3,1},{4,6},{5,7},{6,4},{7,5},{8,10},{9,11},{10,... | collective-permute-start | bytes 6291464 | tf_op jit(solution)/shard_map/ppermute | solution.py:316
  39.2 104.0 %collective-permute-start.2 = (bf16[512,2048]{1,0:T(8,128)(2,1)}, bf16[512,2048]{1,0:T(8,128)(2,1)S(1)}, u32[]{:S(2)}, u32[]{:S(2)}) collective-permute-start(bf16[512,2048]{1,0:T(8,128)(2,1)} %get-tuple-element.45), channel_id=1, source_target_pairs={{0,2},{1,3},{2,0},{3,1},{4,6},{5,7},{6,4},{7,5},{8,10},{9,11},{10,... | collective-permute-start | bytes 6291464 | tf_op jit(solution)/shard_map/ppermute | solution.py:316
  65.3 8.6 %collective-permute-start.5 = (f32[3,128,128]{2,1,0:T(8,128)S(1)}, f32[3,128,128]{2,1,0:T(8,128)S(1)}, u32[]{:S(2)}, u32[]{:S(2)}) collective-permute-start(f32[3,128,128]{2,1,0:T(8,128)S(1)} %pad_maximum_fusion.3), channel_id=1, source_target_pairs={{0,8},{4,12},{8,16},{12,20},{16,24},{20,28},{1,9},{5,13},{9,17},{1... | collective-permute-start | bytes 589832 | tf_op jit(solution)/shard_map/ppermute | solution.py:429
  98.4 20.3 %collective-permute-start.6 = (f32[3,128,128]{2,1,0:T(8,128)S(1)}, f32[3,128,128]{2,1,0:T(8,128)S(1)}, u32[]{:S(2)}, u32[]{:S(2)}) collective-permute-start(f32[3,128,128]{2,1,0:T(8,128)S(1)} %pad_maximum_fusion.4), channel_id=1, source_target_pairs={{0,16},{4,20},{8,24},{12,28},{1,17},{5,21},{9,25},{13,29},{2,18},{... | collective-permute-start | bytes 589832 | tf_op jit(solution)/shard_map/ppermute | solution.py:429
  105.3 38.4 %copy-start.1 = (s32[16]{0:T(128)S(1)}, s32[16]{0:T(128)}, u32[]{:S(2)}) copy-start(s32[16]{0:T(128)} %copy-done) | copy-start | bytes 196
  118.7 29.0 %collective-permute-start.8 = (f32[512,2048]{1,0:T(8,128)}, f32[512,2048]{1,0:T(8,128)}, u32[]{:S(2)}, u32[]{:S(2)}) collective-permute-start(f32[512,2048]{1,0:T(8,128)} %get-tuple-element.28), channel_id=1, source_target_pairs={{0,1},{1,0},{2,3},{3,2},{4,5},{5,4},{6,7},{7,6},{8,9},{9,8},{10,11... | collective-permute-start | bytes 12582920 | tf_op jit(solution)/shard_map/ppermute | solution.py:316
  143.2 5.5 %copy-start.3 = (bf16[512,2048]{1,0:T(8,128)(2,1)}, bf16[512,2048]{1,0:T(8,128)(2,1)S(1)}, u32[]{:S(2)}) copy-start(bf16[512,2048]{1,0:T(8,128)(2,1)S(1)} %collective-permute-done.2.g1_ref) | copy-start | bytes 6291460
  143.2 4.5 %collective-permute-start.7 = (bf16[512,2048]{1,0:T(8,128)(2,1)S(1)}, bf16[512,2048]{1,0:T(8,128)(2,1)}, u32[]{:S(2)}, u32[]{:S(2)}) collective-permute-start(bf16[512,2048]{1,0:T(8,128)(2,1)S(1)} %collective-permute-done.2.g1_ref), channel_id=1, source_target_pairs={{0,1},{1,0},{2,3},{3,2},{4,5},{5,4},{6,7},{7,6},{8,9},{9,8},{10,11... | collective-permute-start | bytes 6291464 | tf_op jit(solution)/shard_map/ppermute | solution.py:316

commit v24 on v23

--- a/solution.py
+++ b/solution.py
@@ -246,8 +246,7 @@
         input_output_aliases={9: 0},
         compiler_params=pltpu.CompilerParams(vmem_limit_bytes=56 * 1024 * 1024),
     )(src_left, src_right, out_tiles, live_blocks.reshape(-1), flags, slab_one, slab_two,
-      jnp.broadcast_to(weights.reshape(height, 1), (height, BLK)), diagonal.reshape(col_blocks, BLK),
-      acc, extra)
+      weights, diagonal.reshape(col_blocks, BLK), acc, extra)
 
 
 HIGHEST = lax.Precision.HIGHEST
@@ -380,7 +379,7 @@
 
         def last_part(slab_one, slab_two, mine, received):
             total = pair_rows(
-                slab_one, slab_two, last_weights, last_live, jnp.take(source, mine_order), source,
+                slab_one, slab_two, state["wide"], last_live, jnp.take(source, mine_order), source,
                 mine_order, diagonal, flags[:own_blocks], own_blocks, mine[None], received[None],
             )
             return total[0]
@@ -413,6 +412,8 @@
             state["partial"] = own_part(slab_in)
         elif kind == "across":
             mine, partners = across_part(slab_in, state["partial"], 0)
+            wide = jnp.broadcast_to(last_weights.reshape(-1, 1), (last_weights.shape[0], BLK))
+            state["wide"], mine = lax.optimization_barrier((wide, mine))
             state["mine"] = mine
             state["received"] = exchange(partners, 1)
         else:

time: 160 us -> 159 us (level)
  transfers between devices with their start and end apart: 9 -> 9, of which waited for: 3 -> 2; matrix products, arithmetic and copies ran while one was open for 53% -> 54% of each run, Pallas kernels for 17% -> 17%
where the time goes in v24:
time: 159 us
  other arithmetic  74.9 us (47%)
  Pallas kernels  37.9 us (24%)
  starting transfers between devices  20 us (13%)
  local copies, waits for them, and re-layouts  11.6 us (7%)
  between operations  6.44 us (4%)
  waiting for transfers between devices  4.05 us (3%)
  matrix products  3.87 us (2%)
    another operation x9, other arithmetic, join_segments(): factor = jnp.linalg.cholesky(middle)  37.2 us
    another operation x6, other arithmetic, join_segments(): lax.linalg.triangular_solve(factor, jnp.concatenate([cross_one.T, cross_t...  31.4 us
    pallas_call x2, Pallas kernels, split_rows(): pl.pallas_call(functools.partial(split_kernel, group=group, accumulate=ac...  26.9 us
    ppermute x3, starting transfers between devices, local(): moved = lax.ppermute(jnp.stack(running), 'tm', pairs)  14.3 us
    pallas_call x1, Pallas kernels, pair_rows(): pl.pallas_call(pair_kernel, grid_spec=grid_spec, out_shape=jax.ShapeDtype...  11 us
    ppermute x6, starting transfers between devices, exchange(): lax.ppermute(value, 'row', [(src, src ^ step) for src in range(owners)])  5.76 us
    ppermute x3, waiting for transfers between devices, local(): moved = lax.ppermute(jnp.stack(running), 'tm', pairs)  3.26 us
  transfers between devices with their start and end apart: 9, of which 2 were waited for; matrix products, arithmetic and copies ran while one was open for 54% of the time, Pallas kernels for 17%

profile of v24, /device:TPU:0, one launch (start us, length us, event | category | flops | bytes accessed | tf_op | source)
XLA Modules:
  0.0 158.8 jit_solution(9632654574465215311)
XLA Ops:
  0.7 0.8 select_reduce_fusion.3.src_right
  5.9 0.8 reshape_squeeze.4.mask_ref
  8.0 1.0 fusion.68
  9.0 1.5 multiply_convert_fusion.1
  11.2 3.0 %collective-permute-start = (f32[53760]{0:T(1024)S(1)}, f32[53760]{0:T(1024)S(1)}, u32[]{:S(2)}, u32[]{:S(2)}) collective-permute-start(f32[53760]{0:T(1024)S(1)} %pad_maximum_fusion), channel_id=1, source_target_pairs={{0,2},{1,3},{2,0},{3,1},{4,6},{5,7},{6,4},{7,5},{8,10},{9,11},{10,... | collective-permute-start | bytes 645128 | tf_op jit(solution)/shard_map/ppermute | solution.py:315
  14.9 0.6 gather_fusion.1
  15.6 0.6 and_select_fusion
  16.3 1.0 mul.105.w_ref
  17.3 13.5 %shard_map.77 = (f32[512,2048]{1,0:T(8,128)}, f32[512,2048]{1,0:T(8,128)}) custom-call(s32[8]{0:T(128)} %get-tuple-element.38.src_left, s32[16]{0:T(128)} %copy-done, s32[8]{0:T(128)} %get-tuple-element.39.tile_ref, s32[128]{0:T(128)} %copy-done.6, s32[8]{0:T(128)} %compare_convert_fusion.flag_ref, bf16[1024,2048]{1,0:T(8,128)(2,1)} %bitcast.155, ...), custom_call_target="tpu_custom_call" | custom-call | tf_op jit(solution)/shard_map/pallas_call | solution.py:177
  30.8 0.7 slice_bitcast_fusion.16
  31.5 0.8 collective-permute-done.1
  32.4 3.4 %collective-permute-start.4 = (f32[3,128,128]{2,1,0:T(8,128)S(1)}, f32[3,128,128]{2,1,0:T(8,128)S(1)}, u32[]{:S(2)}, u32[]{:S(2)}) collective-permute-start(f32[3,128,128]{2,1,0:T(8,128)S(1)} %pad_maximum_fusion.2), channel_id=1, source_target_pairs={{0,4},{4,8},{8,12},{12,16},{16,20},{20,24},{24,28},{1,5},{5,9},{9,... | collective-permute-start | bytes 589832 | tf_op jit(solution)/shard_map/ppermute | solution.py:430
  35.8 2.6 %fusion.76 = (bf16[512,2048]{1,0:T(8,128)(2,1)}, bf16[512,2048]{1,0:T(8,128)(2,1)}) fusion(bf16[1024,2048]{1,0:T(8,128)(2,1)S(1)} %bitcast.156), kind=kLoop, calls=%fused_computation.148 | loop fusion | bytes 8388608 | tf_op jit(solution)/shard_map/slice | solution.py:341
  39.1 1.5 collective-permute-start.2
  41.0 11.7 %cholesky.59 = f32[128,128]{1,0:T(8,128)S(1)} custom-call(f32[128,128]{1,0:T(8,128)S(1)} %copy.53), custom_call_target="Cholesky" | custom-call | tf_op jit(solution)/shard_map/jit(cholesky)/cholesky | solution.py:260
  53.4 0.7 fusion.25
  54.1 9.8 %custom-call.7 = f32[1,128,128]{1,2,0:T(8,128)S(1)} custom-call(f32[1,128,128]{2,1,0:T(8,128)S(1)} %fusion.25), custom_call_target="InvertDiagBlocksLowerTriangular" | custom-call | tf_op jit(solution)/shard_map/triangular_solve/custom-call.0 | solution.py:262
  65.3 5.2 %collective-permute-start.5 = (f32[3,128,128]{2,1,0:T(8,128)S(1)}, f32[3,128,128]{2,1,0:T(8,128)S(1)}, u32[]{:S(2)}, u32[]{:S(2)}) collective-permute-start(f32[3,128,128]{2,1,0:T(8,128)S(1)} %pad_maximum_fusion.3), channel_id=1, source_target_pairs={{0,8},{4,12},{8,16},{12,20},{16,24},{20,28},{1,9},{5,13},{9,17},{1... | collective-permute-start | bytes 589832 | tf_op jit(solution)/shard_map/ppermute | solution.py:430
  70.6 3.3 %collective-permute-done.5 = f32[3,128,128]{2,1,0:T(8,128)S(1)} collective-permute-done((f32[3,128,128]{2,1,0:T(8,128)S(1)}, f32[3,128,128]{2,1,0:T(8,128)S(1)}, u32[]{:S(2)}, u32[]{:S(2)}) %collective-permute-start.5) | collective-permute-done | bytes 196640 | tf_op jit(solution)/shard_map/ppermute | solution.py:430
  74.1 11.7 %cholesky.70 = f32[128,128]{1,0:T(8,128)S(1)} custom-call(f32[128,128]{1,0:T(8,128)S(1)} %fusion.40), custom_call_target="Cholesky" | custom-call | tf_op jit(solution)/shard_map/jit(cholesky)/cholesky | solution.py:260
  86.5 0.7 fusion.26
  87.2 9.8 %custom-call.8 = f32[1,128,128]{1,2,0:T(8,128)S(1)} custom-call(f32[1,128,128]{2,1,0:T(8,128)S(1)} %fusion.26), custom_call_target="InvertDiagBlocksLowerTriangular" | custom-call | tf_op jit(solution)/shard_map/triangular_solve/custom-call.0 | solution.py:262
  98.3 5.6 %collective-permute-start.6 = (f32[3,128,128]{2,1,0:T(8,128)S(1)}, f32[3,128,128]{2,1,0:T(8,128)S(1)}, u32[]{:S(2)}, u32[]{:S(2)}) collective-permute-start(f32[3,128,128]{2,1,0:T(8,128)S(1)} %pad_maximum_fusion.4), channel_id=1, source_target_pairs={{0,16},{4,20},{8,24},{12,28},{1,17},{5,21},{9,25},{13,29},{2,18},{... | collective-permute-start | bytes 589832 | tf_op jit(solution)/shard_map/ppermute | solution.py:430
  104.5 0.9 broadcast_in_dim.49.w_ref
  105.4 13.4 %shard_map.78 = (f32[512,2048]{1,0:T(8,128)}, f32[512,2048]{1,0:T(8,128)}) custom-call(s32[8]{0:T(128)} %get-tuple-element.38.src_left, s32[16]{0:T(128)} %copy-done, s32[8]{0:T(128)} %get-tuple-element.39.tile_ref, s32[64]{0:T(128)} %get-tuple-element.64.mask_ref, s32[8]{0:T(128)} %compare_convert_fusion.flag_ref, ...), custom_call_target="tpu_custom_call", output_to_operand_aliasing={{0}: (8, {}), {1}: (9, {})} | custom-call | tf_op jit(solution)/shard_map/pallas_call | solution.py:177
  119.1 11.7 %cholesky.81 = f32[128,128]{1,0:T(8,128)S(1)} custom-call(f32[128,128]{1,0:T(8,128)S(1)} %fusion.38), custom_call_target="Cholesky" | custom-call | tf_op jit(solution)/shard_map/jit(cholesky)/cholesky | solution.py:260
  131.5 0.7 fusion.27
  132.2 9.8 %custom-call.9 = f32[1,128,128]{1,2,0:T(8,128)S(1)} custom-call(f32[1,128,128]{2,1,0:T(8,128)S(1)} %fusion.27), custom_call_target="InvertDiagBlocksLowerTriangular" | custom-call | tf_op jit(solution)/shard_map/triangular_solve/custom-call.0 | solution.py:262
  145.3 0.7 reshape.227.mask_ref
  146.0 1.0 broadcast_in_dim.47.w_ref
  147.1 0.7 maximum_bitcast_fusion
  147.8 11.0 %shard_map.79 = f32[1,512,2048]{2,1,0:T(8,128)} custom-call(s32[4]{0:T(128)} %and_select_fusion.1.src_left, s32[16]{0:T(128)} %copy-done, s32[4]{0:T(128)} %copy-done.5, s32[128]{0:T(128)} %reshape.227.mask_ref, s32[4]{0:T(128)} %bitcast.179, bf16[512,2048]{1,0:T(8,128)(2,1)} %copy-done.3, ...), custom_call_target="tpu_custom_call", output_to_operand_aliasing={{}: (9, {})} | custom-call | tf_op jit(solution)/shard_map/pallas_call | solution.py:242
  (106 shorter events, 12.2 us)
Async XLA Ops:
  0.6 10.4 %copy-start.4 = (f32[1,1024]{1,0:T(1,128)S(1)}, f32[1,1024]{1,0:T(1,128)}, u32[]{:S(2)}) copy-start(f32[1,1024]{1,0:T(1,128)} %param.10) | copy-start | bytes 12292
  0.6 14.1 %copy-start.7 = (s32[16]{0:T(128)S(1)}, s32[16]{0:T(128)}, u32[]{:S(2)}) copy-start(s32[16]{0:T(128)} %param.13) | copy-start | bytes 196
  1.4 15.8 %copy-start = (s32[16]{0:T(128)}, s32[16]{0:T(128)S(1)}, u32[]{:S(2)}) copy-start(s32[16]{0:T(128)S(1)} %select_reduce_fusion.3.src_right) | copy-start | bytes 196
  6.7 10.6 %copy-start.6 = (s32[128]{0:T(128)}, s32[128]{0:T(128)S(1)}, u32[]{:S(2)}) copy-start(s32[128]{0:T(128)S(1)} %reshape_squeeze.4.mask_ref) | copy-start | bytes 1540
  11.2 19.6 %collective-permute-start = (f32[53760]{0:T(1024)S(1)}, f32[53760]{0:T(1024)S(1)}, u32[]{:S(2)}, u32[]{:S(2)}) collective-permute-start(f32[53760]{0:T(1024)S(1)} %pad_maximum_fusion), channel_id=1, source_target_pairs={{0,2},{1,3},{2,0},{3,1},{4,6},{5,7},{6,4},{7,5},{8,10},{9,11},{10,... | collective-permute-start | bytes 645128 | tf_op jit(solution)/shard_map/ppermute | solution.py:315
  14.9 129.6 %copy-start.5 = (s32[4]{0:T(128)}, s32[4]{0:T(128)S(1)}, u32[]{:S(2)}) copy-start(s32[4]{0:T(128)S(1)} %get-tuple-element.45.tile_ref) | copy-start | bytes 52
  15.6 20.2 %copy-start.2 = (bf16[1,1024,2048]{2,1,0:T(8,128)(2,1)S(1)}, bf16[1,1024,2048]{2,1,0:T(8,128)(2,1)}, u32[]{:S(2)}) copy-start(bf16[1,1024,2048]{2,1,0:T(8,128)(2,1)} %param.9) | copy-start | bytes 12582916
  30.8 1.5 collective-permute-start.1
  32.4 8.3 %collective-permute-start.4 = (f32[3,128,128]{2,1,0:T(8,128)S(1)}, f32[3,128,128]{2,1,0:T(8,128)S(1)}, u32[]{:S(2)}, u32[]{:S(2)}) collective-permute-start(f32[3,128,128]{2,1,0:T(8,128)S(1)} %pad_maximum_fusion.2), channel_id=1, source_target_pairs={{0,4},{4,8},{8,12},{12,16},{16,20},{20,24},{24,28},{1,5},{5,9},{9,... | collective-permute-start | bytes 589832 | tf_op jit(solution)/shard_map/ppermute | solution.py:430
  38.6 59.7 %collective-permute-start.3 = (bf16[512,2048]{1,0:T(8,128)(2,1)}, bf16[512,2048]{1,0:T(8,128)(2,1)}, u32[]{:S(2)}, u32[]{:S(2)}) collective-permute-start(bf16[512,2048]{1,0:T(8,128)(2,1)} %get-tuple-element.48), channel_id=1, source_target_pairs={{0,2},{1,3},{2,0},{3,1},{4,6},{5,7},{6,4},{7,5},{8,10},{9,11},{10,... | collective-permute-start | bytes 6291464 | tf_op jit(solution)/shard_map/ppermute | solution.py:315
  39.1 104.1 %collective-permute-start.2 = (bf16[512,2048]{1,0:T(8,128)(2,1)}, bf16[512,2048]{1,0:T(8,128)(2,1)S(1)}, u32[]{:S(2)}, u32[]{:S(2)}) collective-permute-start(bf16[512,2048]{1,0:T(8,128)(2,1)} %get-tuple-element.49), channel_id=1, source_target_pairs={{0,2},{1,3},{2,0},{3,1},{4,6},{5,7},{6,4},{7,5},{8,10},{9,11},{10,... | collective-permute-start | bytes 6291464 | tf_op jit(solution)/shard_map/ppermute | solution.py:315
  65.3 8.6 %collective-permute-start.5 = (f32[3,128,128]{2,1,0:T(8,128)S(1)}, f32[3,128,128]{2,1,0:T(8,128)S(1)}, u32[]{:S(2)}, u32[]{:S(2)}) collective-permute-start(f32[3,128,128]{2,1,0:T(8,128)S(1)} %pad_maximum_fusion.3), channel_id=1, source_target_pairs={{0,8},{4,12},{8,16},{12,20},{16,24},{20,28},{1,9},{5,13},{9,17},{1... | collective-permute-start | bytes 589832 | tf_op jit(solution)/shard_map/ppermute | solution.py:430
  98.3 20.4 %collective-permute-start.6 = (f32[3,128,128]{2,1,0:T(8,128)S(1)}, f32[3,128,128]{2,1,0:T(8,128)S(1)}, u32[]{:S(2)}, u32[]{:S(2)}) collective-permute-start(f32[3,128,128]{2,1,0:T(8,128)S(1)} %pad_maximum_fusion.4), channel_id=1, source_target_pairs={{0,16},{4,20},{8,24},{12,28},{1,17},{5,21},{9,25},{13,29},{2,18},{... | collective-permute-start | bytes 589832 | tf_op jit(solution)/shard_map/ppermute | solution.py:430
  105.4 38.5 %copy-start.1 = (s32[16]{0:T(128)S(1)}, s32[16]{0:T(128)}, u32[]{:S(2)}) copy-start(s32[16]{0:T(128)} %copy-done) | copy-start | bytes 196
  118.8 29.1 %collective-permute-start.8 = (f32[512,2048]{1,0:T(8,128)}, f32[512,2048]{1,0:T(8,128)}, u32[]{:S(2)}, u32[]{:S(2)}) collective-permute-start(f32[512,2048]{1,0:T(8,128)} %get-tuple-element.32), channel_id=1, source_target_pairs={{0,1},{1,0},{2,3},{3,2},{4,5},{5,4},{6,7},{7,6},{8,9},{9,8},{10,11... | collective-permute-start | bytes 12582920 | tf_op jit(solution)/shard_map/ppermute | solution.py:315
  143.2 4.6 %copy-start.3 = (bf16[512,2048]{1,0:T(8,128)(2,1)}, bf16[512,2048]{1,0:T(8,128)(2,1)S(1)}, u32[]{:S(2)}) copy-start(bf16[512,2048]{1,0:T(8,128)(2,1)S(1)} %collective-permute-done.2.g1_ref) | copy-start | bytes 6291460
  143.2 4.6 %collective-permute-start.7 = (bf16[512,2048]{1,0:T(8,128)(2,1)S(1)}, bf16[512,2048]{1,0:T(8,128)(2,1)}, u32[]{:S(2)}, u32[]{:S(2)}) collective-permute-start(bf16[512,2048]{1,0:T(8,128)(2,1)S(1)} %collective-permute-done.2.g1_ref), channel_id=1, source_target_pairs={{0,1},{1,0},{2,3},{3,2},{4,5},{5,4},{6,7},{7,6},{8,9},{9,8},{10,11... | collective-permute-start | bytes 6291464 | tf_op jit(solution)/shard_map/ppermute | solution.py:315
